TPU v7x, 32 devices: a whole 2x2x4 slice. The times are simulated.
32 devices in a mesh: wide: 8 (over y, x, core), lon: 4 (over z).
Axes of the slice: x: 2, y: 2, z: 4, core: 2. Of those that a mesh axis runs over, the one named last changes fastest.
Arguments:
- background_ensemble: bfloat16 [256, 64, 1024], P('wide', None, 'lon'), may hold values from -6 to 6
- innov: bfloat16 [256, 64, 1024], P(None, 'wide', 'lon'), may hold values from -6 to 6
- obs_index: int32 [4, 64, 1024], P(None, None, 'lon'), may hold values from 0 to 16383, as said below
- obs_weight: float32 [4, 64, 1024], P(None, None, 'lon'), may hold values from 0.05 to 0.5
- obs_list: int32 [4, 128, 16], P('lon', 'wide'), may hold values from 0 to 23, as said below
- tile_count: int32 [4, 128], P('lon', 'wide'), may hold values from 1 to 16
- taper_class: int32 [4, 128, 16], P('lon', 'wide'), may hold values from 0 to 3
Outputs:
- analysis: bfloat16 [256, 64, 1024], P('wide', None, 'lon')
Inputs may be any that keep to these rules, and one draw needn't show every extreme that they name: obs_index[k, i, c] = r * 256 + q names the cell in row r and column q of the observation's own longitude tile, and row r lies among the 8 rows of the region that holds row i. Each row of obs_list names 16 different candidates of its region.
All inputs are finite; a program needn't handle non-finite values.
Results may differ from a plain program's by a relative error of at most 0.0056.
Values may be sent and summed in bfloat16 or wider, within the bound.
No kernel may reach another device: no remote copies, remote signals or barrier semaphores. Data moves between devices by JAX's collectives and lax.ppermute only.
A program may use at most 64 MiB of HBM per device.

v0:
```python
import math

import jax
import jax.numpy as jnp
from jax import lax
from jax.sharding import PartitionSpec as P

BLK = 128
HALO_BLK = 4


def padded_2(value, sides, width):
    for axis, dim in sides:
        size, length = (lax.axis_size(axis), value.shape[dim])
        up = [(i, (i + 1) % size) for i in range(size)]
        down = [(j, i) for i, j in up]
        last = lax.slice_in_dim(value, length - width, length, axis=dim)
        first = lax.slice_in_dim(value, 0, width, axis=dim)
        before = lax.ppermute(last, axis, up)
        after = lax.ppermute(first, axis, down)
        value = jnp.concatenate([before, value, after], axis=dim)
    return value


def observe_region(state, index, weight):
    members, cells = state.shape
    width = math.gcd(512, cells)
    nblocks = cells // width
    index_blocks = index.reshape(4, nblocks, width).transpose(1, 0, 2)
    weight_blocks = weight.reshape(4, nblocks, width).transpose(1, 0, 2)
    cell_ids = lax.broadcasted_iota(jnp.int32, (cells, width), 0)

    def observe_one_block(pieces):
        index_here, weight_here = pieces
        summed = jnp.zeros((members, width), jnp.float32)
        for k in range(4):
            selector = (cell_ids == index_here[k][None, :]).astype(jnp.bfloat16)
            picked = jnp.dot(state, selector, preferred_element_type=jnp.float32)
            summed = summed + weight_here[k][None, :] * picked
        return summed.astype(jnp.bfloat16)

    result = lax.map(observe_one_block, (index_blocks, weight_blocks))
    return result.transpose(1, 0, 2).reshape(members, cells)


def anomaly_from_mean(state_values):
    centred = state_values.astype(jnp.float32)
    return (centred - jnp.mean(centred, axis=-2, keepdims=True)).astype(jnp.bfloat16)


def taper_tiles(classes, in_use, tile_width):
    row_ids = lax.broadcasted_iota(jnp.float32, (tile_width, tile_width), 0)
    col_ids = lax.broadcasted_iota(jnp.float32, (tile_width, tile_width), 1)
    offset = row_ids - col_ids
    length = 8.0 * jnp.exp2(classes.astype(jnp.float32))
    scaled = offset / length[..., None, None]
    return in_use[..., None, None] / (1.0 + scaled * scaled)


def body(background_ensemble, innov, obs_index, obs_weight, obs_list, tile_count, taper_class):
    padded = padded_2(background_ensemble, (("lon", 2),), 1)
    state_values = background_ensemble.astype(jnp.float32)
    east_neighbour = padded[:, :, 2:].astype(jnp.float32)
    west_neighbour = padded[:, :, :-2].astype(jnp.float32)
    northern = jnp.pad(state_values[:, 1:, :], ((0, 0), (0, 1), (0, 0)))
    southern = jnp.pad(state_values[:, :-1, :], ((0, 0), (1, 0), (0, 0)))
    member_spread = east_neighbour + west_neighbour + northern + southern - 4.0 * state_values
    prediction_increment = (
        state_values + 0.2 * member_spread - 0.3 * (east_neighbour - west_neighbour)
    ).astype(jnp.bfloat16)
    ensemble_lines_here, whole_parallel_set, patch_meridian_lines = prediction_increment.shape
    members = innov.shape[0]
    band_rows = innov.shape[1]
    patch_gridpoints = band_rows * patch_meridian_lines
    region = lax.all_to_all(prediction_increment, "wide", split_axis=1, concat_axis=0, tiled=True)
    region_state = region.reshape(members, patch_gridpoints)
    first_row = lax.axis_index("wide") * band_rows
    local_index = lax.dynamic_slice_in_dim(obs_index, first_row, band_rows, 1).reshape(
        4, patch_gridpoints
    )
    local_index = local_index - first_row * patch_meridian_lines
    local_weight = lax.dynamic_slice_in_dim(obs_weight, first_row, band_rows, 1).reshape(
        4, patch_gridpoints
    )
    region_obs = observe_region(region_state, local_index, local_weight)
    model_anomaly = anomaly_from_mean(region_state)
    obs_dev = anomaly_from_mean(region_obs)
    stacked = jnp.stack([obs_dev, innov.reshape(members, patch_gridpoints)])
    widened = padded_2(stacked, (("lon", 2),), HALO_BLK * BLK)
    candidate_count = widened.shape[2] // BLK
    cand = widened.reshape(2, members, candidate_count, BLK)
    block_count = patch_gridpoints // BLK
    candidate_ids = lax.broadcasted_iota(jnp.int32, (obs_list.shape[2], candidate_count), 1)

    def body_one_block(position, result):
        start = position * BLK
        state_tile = lax.dynamic_slice_in_dim(model_anomaly, start, BLK, 1)
        anchor = lax.dynamic_slice_in_dim(region_state, start, BLK, 1)
        listed = obs_list[0, position]
        classes = taper_class[0, position]
        live_count = tile_count[0, position]
        selector = (candidate_ids == listed[:, None]).astype(jnp.bfloat16)
        picked = jnp.einsum(
            "jk,smko->smjo", selector, cand, preferred_element_type=jnp.float32
        ).astype(jnp.bfloat16)
        covariance = jnp.einsum(
            "mc,mjo->jco", state_tile, picked[0], preferred_element_type=jnp.float32
        ) / (members - 1.0)
        in_use = (jnp.arange(listed.shape[0], dtype=jnp.int32) < live_count).astype(jnp.float32)
        tapered = (covariance * taper_tiles(classes, in_use, BLK)).astype(jnp.bfloat16)
        change = jnp.einsum("mjo,jco->mc", picked[1], tapered, preferred_element_type=jnp.float32)
        updated = (anchor.astype(jnp.float32) + change).astype(jnp.bfloat16)
        return lax.dynamic_update_slice_in_dim(result, updated, start, 1)

    result = lax.fori_loop(
        0, block_count, body_one_block, jnp.zeros((members, patch_gridpoints), jnp.bfloat16)
    )
    return lax.all_to_all(
        result.reshape(members, band_rows, patch_meridian_lines),
        "wide",
        split_axis=0,
        concat_axis=1,
        tiled=True,
    )


def solution(mesh):
    in_specs = (
        P("wide", None, "lon"),
        P(None, "wide", "lon"),
        P(None, None, "lon"),
        P(None, None, "lon"),
        P("lon", "wide", None),
        P("lon", "wide"),
        P("lon", "wide", None),
    )
    out_specs = P("wide", None, "lon")
    return jax.shard_map(body, mesh=mesh, in_specs=in_specs, out_specs=out_specs, check_vma=False)
```

profile of v0, /device:TPU:0, one launch (start us, length us, event | category | flops | bytes accessed | tf_op | source)
XLA Modules:
  0.0 259.9 jit_solution(14126926620454648274)
XLA Ops:
  0.0 1.9 fusion.95
  2.2 5.1 %collective-permute-start = (bf16[32,64,1]{2,0,1:T(8,128)(2,1)S(1)}, bf16[32,64,1]{2,0,1:T(8,128)(2,1)S(1)}, u32[]{:S(2)}, u32[]{:S(2)}) collective-permute-start(bf16[32,64,1]{2,0,1:T(8,128)(2,1)S(1)} %get-tuple-element.305), channel_id=1, source_target_pairs={{1,0},{2,1},{3,2},{0,3},{5,4},{6,5},{7,6},{4,7},{9,8},{10,9},{11,1... | collective-permute-start | bytes 12296 | tf_op jit(solution)/shard_map/ppermute | solution.py:20
  7.8 11.8 %collective-permute-done = bf16[32,64,1]{2,0,1:T(8,128)(2,1)S(1)} collective-permute-done((bf16[32,64,1]{2,0,1:T(8,128)(2,1)S(1)}, bf16[32,64,1]{2,0,1:T(8,128)(2,1)S(1)}, u32[]{:S(2)}, u32[]{:S(2)}) %collective-permute-start) | collective-permute-done | bytes 4128 | tf_op jit(solution)/shard_map/ppermute | solution.py:20
  19.6 11.0 %collective-permute-done.1 = bf16[32,64,1]{2,0,1:T(8,128)(2,1)S(1)} collective-permute-done((bf16[32,64,1]{2,0,1:T(8,128)(2,1)S(1)}, bf16[32,64,1]{2,0,1:T(8,128)(2,1)S(1)}, u32[]{:S(2)}, u32[]{:S(2)}) %collective-permute-start.1) | collective-permute-done | bytes 4128 | tf_op jit(solution)/shard_map/ppermute | solution.py:19
  30.6 2.9 %fusion.90 = bf16[32,64,256]{2,0,1:T(8,128)(2,1)} fusion(f32[32,63,256]{2,0,1:T(8,128)S(1)} %get-tuple-element.304, f32[32,63,256]{2,0,1:T(8,128)S(1)} %get-tuple-element.303, bf16[32,64,256]{2,0,1:T(8,128)(2,1)S(1)} %get-tuple-element.307, bf16[32,64,1]{2,0,1:T(8,128)(2,1)S(1)} %collective-permute-done.1, bf16[32,64,1]{2,0,1:T(8,128)(2,1)S(1)} %collective-permute-done), kind=kLoop, calls=%fused_computation.85 | loop fusion | flops 10485760 | bytes 6234112 | tf_op jit(solution)/shard_map/convert_element_type | solution.py:70
  33.5 3.7 %all-to-all-start = ((bf16[32,64,256]{2,0,1:T(8,128)(2,1)}), bf16[32,64,256]{2,0,1:T(8,128)(2,1)S(1)}, u32[]{:S(2)}, u32[]{:S(2)}) async-start(bf16[32,64,256]{2,0,1:T(8,128)(2,1)} %fusion.90), calls=%async_computation | async-start | bytes 2097152 | tf_op jit(solution)/shard_map/all_to_all | solution.py:75
  38.0 1.6 copy.43
  39.7 12.9 %all-to-all-done = bf16[32,64,256]{2,0,1:T(8,128)(2,1)S(1)} async-done(((bf16[32,64,256]{2,0,1:T(8,128)(2,1)}), bf16[32,64,256]{2,0,1:T(8,128)(2,1)S(1)}, u32[]{:S(2)}, u32[]{:S(2)}) %all-to-all-start) | async-done | bytes 1048608 | tf_op jit(solution)/shard_map/all_to_all | solution.py:75
  53.2 1.3 copy.55
  54.5 17.8 %while.27 = (s32[]{:T(128)}, bf16[4,256,512]{1,2,0:T(8,128)(2,1)S(1)}, f32[4,4,512]{2,0,1:T(4,128)S(1)}, s32[4,4,512]{2,0,1:T(4,128)S(1)}, bf16[256,2048]{1,0:T(...) while((s32[]{:T(128)}, bf16[4,256,512]{1,2,0:T(8,128)(2,1)S(1)}, ...), condition=%wide.region_2.3_spmd.clone.clone, body=%wide.region_1.2_spmd.clone.clone.sunk | while | flops 2156920832 | bytes 11845833 | solution.py:42
  54.6 2.1 fusion.135
  59.1 2.1 fusion.135
  63.5 2.1 fusion.135
  68.0 2.1 fusion.135
  73.6 1.7 collective-permute-start.2
  75.3 2.2 collective-permute-start.3
  77.5 1.2 subtract_convert_fusion
  78.7 11.6 %collective-permute-done.2 = bf16[2,256,512]{1,2,0:T(8,128)(2,1)S(1)} collective-permute-done((bf16[2,256,512]{1,2,0:T(8,128)(2,1)S(1)}, bf16[2,256,512]{1,2,0:T(8,128)(2,1)S(1)}, u32[]{:S(2)}, u32[]{:S(2)}) %collective-permute-start.2) | collective-permute-done | bytes 524320 | tf_op jit(solution)/shard_map/ppermute | solution.py:19
  90.3 6.8 %collective-permute-done.3 = bf16[2,256,512]{1,2,0:T(8,128)(2,1)S(1)} collective-permute-done((bf16[2,256,512]{1,2,0:T(8,128)(2,1)S(1)}, bf16[2,256,512]{1,2,0:T(8,128)(2,1)S(1)}, u32[]{:S(2)}, u32[]{:S(2)}) %collective-permute-start.3) | collective-permute-done | bytes 524320 | tf_op jit(solution)/shard_map/ppermute | solution.py:20
  97.1 1.8 pad_maximum_fusion
  98.9 3.6 %copy.44 = bf16[2,256,24,128]{3,2,1,0:T(8,128)(2,1)S(1)} copy(bf16[2,256,24,128]{1,3,2,0:T(8,128)(2,1)} %bitcast.156) | data formatting | bytes 6291456 | tf_op jit(solution)/shard_map/reshape | solution.py:91
  102.5 1.1 broadcast_in_dim.21
  103.6 133.7 %while.26 = (s32[]{:T(128)}, bf16[256,2048]{1,0:T(8,128)(2,1)}, bf16[256,2048]{1,0:T(8,128)(2,1)}, s32[1,16,16]{2,1,0:T(8,128)}, bf16[2,256,24,128]{3,2,1,0:T(8,...) while((s32[]{:T(128)}, bf16[256,2048]{1,0:T(8,128)(2,1)}, ...), condition=%wide.region_5.6_spmd.clone, body=%wide.region_4.5_spmd.clone.sunk | while | flops 321765856 | bytes 11863739 | solution.py:115
  105.1 1.7 slice_bitcast_fusion.3
  108.8 3.2 %fusion.126 = bf16[256,2048]{1,0:T(8,128)(2,1)} fusion(bf16[256,2048]{1,0:T(8,128)(2,1)} %get-tuple-element.452, s32[]{:T(128)S(6)} %select_n.23, bf16[256,16,128]{2,1,0:T(8,128)(2,1)} %get-tuple-element.394, bf16[256,16,128]{2,1,0:T(8,128)(2,1)} %get-tuple-element.395, f32[16]{0:T(128)S(1)} %multiply_bitcast_fusion.4, ...), kind=kOutput, calls=%fused_computation.11.clone.1 | convolution fusion | flops 270368768 | bytes 2360448 | tf_op jit(solution)/shard_map/while/body/eval_jaxpr/mjo,jco->mc/dot_general | solution.py:111
  112.7 0.8 convert_bitcast_fusion.2
  113.5 1.7 slice_bitcast_fusion.3
  117.2 3.2 %fusion.126 = bf16[256,2048]{1,0:T(8,128)(2,1)} fusion(bf16[256,2048]{1,0:T(8,128)(2,1)} %get-tuple-element.452, s32[]{:T(128)S(6)} %select_n.23, bf16[256,16,128]{2,1,0:T(8,128)(2,1)} %get-tuple-element.394, bf16[256,16,128]{2,1,0:T(8,128)(2,1)} %get-tuple-element.395, f32[16]{0:T(128)S(1)} %multiply_bitcast_fusion.4, ...), kind=kOutput, calls=%fused_computation.11.clone.1 | convolution fusion | flops 270368768 | bytes 2360448 | tf_op jit(solution)/shard_map/while/body/eval_jaxpr/mjo,jco->mc/dot_general | solution.py:111
  121.8 1.7 slice_bitcast_fusion.3
  125.5 3.2 %fusion.126 = bf16[256,2048]{1,0:T(8,128)(2,1)} fusion(bf16[256,2048]{1,0:T(8,128)(2,1)} %get-tuple-element.452, s32[]{:T(128)S(6)} %select_n.23, bf16[256,16,128]{2,1,0:T(8,128)(2,1)} %get-tuple-element.394, bf16[256,16,128]{2,1,0:T(8,128)(2,1)} %get-tuple-element.395, f32[16]{0:T(128)S(1)} %multiply_bitcast_fusion.4, ...), kind=kOutput, calls=%fused_computation.11.clone.1 | convolution fusion | flops 270368768 | bytes 2360448 | tf_op jit(solution)/shard_map/while/body/eval_jaxpr/mjo,jco->mc/dot_general | solution.py:111
  129.4 0.8 convert_bitcast_fusion.2
  130.2 1.7 slice_bitcast_fusion.3
  133.9 3.2 %fusion.126 = bf16[256,2048]{1,0:T(8,128)(2,1)} fusion(bf16[256,2048]{1,0:T(8,128)(2,1)} %get-tuple-element.452, s32[]{:T(128)S(6)} %select_n.23, bf16[256,16,128]{2,1,0:T(8,128)(2,1)} %get-tuple-element.394, bf16[256,16,128]{2,1,0:T(8,128)(2,1)} %get-tuple-element.395, f32[16]{0:T(128)S(1)} %multiply_bitcast_fusion.4, ...), kind=kOutput, calls=%fused_computation.11.clone.1 | convolution fusion | flops 270368768 | bytes 2360448 | tf_op jit(solution)/shard_map/while/body/eval_jaxpr/mjo,jco->mc/dot_general | solution.py:111
  138.5 1.7 slice_bitcast_fusion.3
  142.2 3.2 %fusion.126 = bf16[256,2048]{1,0:T(8,128)(2,1)} fusion(bf16[256,2048]{1,0:T(8,128)(2,1)} %get-tuple-element.452, s32[]{:T(128)S(6)} %select_n.23, bf16[256,16,128]{2,1,0:T(8,128)(2,1)} %get-tuple-element.394, bf16[256,16,128]{2,1,0:T(8,128)(2,1)} %get-tuple-element.395, f32[16]{0:T(128)S(1)} %multiply_bitcast_fusion.4, ...), kind=kOutput, calls=%fused_computation.11.clone.1 | convolution fusion | flops 270368768 | bytes 2360448 | tf_op jit(solution)/shard_map/while/body/eval_jaxpr/mjo,jco->mc/dot_general | solution.py:111
  146.1 0.8 convert_bitcast_fusion.2
  146.9 1.7 slice_bitcast_fusion.3
  150.6 3.2 %fusion.126 = bf16[256,2048]{1,0:T(8,128)(2,1)} fusion(bf16[256,2048]{1,0:T(8,128)(2,1)} %get-tuple-element.452, s32[]{:T(128)S(6)} %select_n.23, bf16[256,16,128]{2,1,0:T(8,128)(2,1)} %get-tuple-element.394, bf16[256,16,128]{2,1,0:T(8,128)(2,1)} %get-tuple-element.395, f32[16]{0:T(128)S(1)} %multiply_bitcast_fusion.4, ...), kind=kOutput, calls=%fused_computation.11.clone.1 | convolution fusion | flops 270368768 | bytes 2360448 | tf_op jit(solution)/shard_map/while/body/eval_jaxpr/mjo,jco->mc/dot_general | solution.py:111
  155.3 1.7 slice_bitcast_fusion.3
  158.9 3.2 %fusion.126 = bf16[256,2048]{1,0:T(8,128)(2,1)} fusion(bf16[256,2048]{1,0:T(8,128)(2,1)} %get-tuple-element.452, s32[]{:T(128)S(6)} %select_n.23, bf16[256,16,128]{2,1,0:T(8,128)(2,1)} %get-tuple-element.394, bf16[256,16,128]{2,1,0:T(8,128)(2,1)} %get-tuple-element.395, f32[16]{0:T(128)S(1)} %multiply_bitcast_fusion.4, ...), kind=kOutput, calls=%fused_computation.11.clone.1 | convolution fusion | flops 270368768 | bytes 2360448 | tf_op jit(solution)/shard_map/while/body/eval_jaxpr/mjo,jco->mc/dot_general | solution.py:111
  162.8 0.8 convert_bitcast_fusion.2
  163.6 1.7 slice_bitcast_fusion.3
  167.3 3.2 %fusion.126 = bf16[256,2048]{1,0:T(8,128)(2,1)} fusion(bf16[256,2048]{1,0:T(8,128)(2,1)} %get-tuple-element.452, s32[]{:T(128)S(6)} %select_n.23, bf16[256,16,128]{2,1,0:T(8,128)(2,1)} %get-tuple-element.394, bf16[256,16,128]{2,1,0:T(8,128)(2,1)} %get-tuple-element.395, f32[16]{0:T(128)S(1)} %multiply_bitcast_fusion.4, ...), kind=kOutput, calls=%fused_computation.11.clone.1 | convolution fusion | flops 270368768 | bytes 2360448 | tf_op jit(solution)/shard_map/while/body/eval_jaxpr/mjo,jco->mc/dot_general | solution.py:111
  172.0 1.7 slice_bitcast_fusion.3
  175.6 3.2 %fusion.126 = bf16[256,2048]{1,0:T(8,128)(2,1)} fusion(bf16[256,2048]{1,0:T(8,128)(2,1)} %get-tuple-element.452, s32[]{:T(128)S(6)} %select_n.23, bf16[256,16,128]{2,1,0:T(8,128)(2,1)} %get-tuple-element.394, bf16[256,16,128]{2,1,0:T(8,128)(2,1)} %get-tuple-element.395, f32[16]{0:T(128)S(1)} %multiply_bitcast_fusion.4, ...), kind=kOutput, calls=%fused_computation.11.clone.1 | convolution fusion | flops 270368768 | bytes 2360448 | tf_op jit(solution)/shard_map/while/body/eval_jaxpr/mjo,jco->mc/dot_general | solution.py:111
  179.5 0.8 convert_bitcast_fusion.2
  180.3 1.7 slice_bitcast_fusion.3
  184.0 3.2 %fusion.126 = bf16[256,2048]{1,0:T(8,128)(2,1)} fusion(bf16[256,2048]{1,0:T(8,128)(2,1)} %get-tuple-element.452, s32[]{:T(128)S(6)} %select_n.23, bf16[256,16,128]{2,1,0:T(8,128)(2,1)} %get-tuple-element.394, bf16[256,16,128]{2,1,0:T(8,128)(2,1)} %get-tuple-element.395, f32[16]{0:T(128)S(1)} %multiply_bitcast_fusion.4, ...), kind=kOutput, calls=%fused_computation.11.clone.1 | convolution fusion | flops 270368768 | bytes 2360448 | tf_op jit(solution)/shard_map/while/body/eval_jaxpr/mjo,jco->mc/dot_general | solution.py:111
  188.7 1.7 slice_bitcast_fusion.3
  192.3 3.2 %fusion.126 = bf16[256,2048]{1,0:T(8,128)(2,1)} fusion(bf16[256,2048]{1,0:T(8,128)(2,1)} %get-tuple-element.452, s32[]{:T(128)S(6)} %select_n.23, bf16[256,16,128]{2,1,0:T(8,128)(2,1)} %get-tuple-element.394, bf16[256,16,128]{2,1,0:T(8,128)(2,1)} %get-tuple-element.395, f32[16]{0:T(128)S(1)} %multiply_bitcast_fusion.4, ...), kind=kOutput, calls=%fused_computation.11.clone.1 | convolution fusion | flops 270368768 | bytes 2360448 | tf_op jit(solution)/shard_map/while/body/eval_jaxpr/mjo,jco->mc/dot_general | solution.py:111
  196.2 0.8 convert_bitcast_fusion.2
  197.0 1.7 slice_bitcast_fusion.3
  200.7 3.2 %fusion.126 = bf16[256,2048]{1,0:T(8,128)(2,1)} fusion(bf16[256,2048]{1,0:T(8,128)(2,1)} %get-tuple-element.452, s32[]{:T(128)S(6)} %select_n.23, bf16[256,16,128]{2,1,0:T(8,128)(2,1)} %get-tuple-element.394, bf16[256,16,128]{2,1,0:T(8,128)(2,1)} %get-tuple-element.395, f32[16]{0:T(128)S(1)} %multiply_bitcast_fusion.4, ...), kind=kOutput, calls=%fused_computation.11.clone.1 | convolution fusion | flops 270368768 | bytes 2360448 | tf_op jit(solution)/shard_map/while/body/eval_jaxpr/mjo,jco->mc/dot_general | solution.py:111
  205.4 1.7 slice_bitcast_fusion.3
  209.0 3.2 %fusion.126 = bf16[256,2048]{1,0:T(8,128)(2,1)} fusion(bf16[256,2048]{1,0:T(8,128)(2,1)} %get-tuple-element.452, s32[]{:T(128)S(6)} %select_n.23, bf16[256,16,128]{2,1,0:T(8,128)(2,1)} %get-tuple-element.394, bf16[256,16,128]{2,1,0:T(8,128)(2,1)} %get-tuple-element.395, f32[16]{0:T(128)S(1)} %multiply_bitcast_fusion.4, ...), kind=kOutput, calls=%fused_computation.11.clone.1 | convolution fusion | flops 270368768 | bytes 2360448 | tf_op jit(solution)/shard_map/while/body/eval_jaxpr/mjo,jco->mc/dot_general | solution.py:111
  213.7 1.7 slice_bitcast_fusion.3
  217.4 3.2 %fusion.126 = bf16[256,2048]{1,0:T(8,128)(2,1)} fusion(bf16[256,2048]{1,0:T(8,128)(2,1)} %get-tuple-element.452, s32[]{:T(128)S(6)} %select_n.23, bf16[256,16,128]{2,1,0:T(8,128)(2,1)} %get-tuple-element.394, bf16[256,16,128]{2,1,0:T(8,128)(2,1)} %get-tuple-element.395, f32[16]{0:T(128)S(1)} %multiply_bitcast_fusion.4, ...), kind=kOutput, calls=%fused_computation.11.clone.1 | convolution fusion | flops 270368768 | bytes 2360448 | tf_op jit(solution)/shard_map/while/body/eval_jaxpr/mjo,jco->mc/dot_general | solution.py:111
  222.1 1.7 slice_bitcast_fusion.3
  225.8 3.2 %fusion.126 = bf16[256,2048]{1,0:T(8,128)(2,1)} fusion(bf16[256,2048]{1,0:T(8,128)(2,1)} %get-tuple-element.452, s32[]{:T(128)S(6)} %select_n.23, bf16[256,16,128]{2,1,0:T(8,128)(2,1)} %get-tuple-element.394, bf16[256,16,128]{2,1,0:T(8,128)(2,1)} %get-tuple-element.395, f32[16]{0:T(128)S(1)} %multiply_bitcast_fusion.4, ...), kind=kOutput, calls=%fused_computation.11.clone.1 | convolution fusion | flops 270368768 | bytes 2360448 | tf_op jit(solution)/shard_map/while/body/eval_jaxpr/mjo,jco->mc/dot_general | solution.py:111
  230.4 1.7 slice_bitcast_fusion.3
  234.1 3.2 %fusion.126 = bf16[256,2048]{1,0:T(8,128)(2,1)} fusion(bf16[256,2048]{1,0:T(8,128)(2,1)} %get-tuple-element.452, s32[]{:T(128)S(6)} %select_n.23, bf16[256,16,128]{2,1,0:T(8,128)(2,1)} %get-tuple-element.394, bf16[256,16,128]{2,1,0:T(8,128)(2,1)} %get-tuple-element.395, f32[16]{0:T(128)S(1)} %multiply_bitcast_fusion.4, ...), kind=kOutput, calls=%fused_computation.11.clone.1 | convolution fusion | flops 270368768 | bytes 2360448 | tf_op jit(solution)/shard_map/while/body/eval_jaxpr/mjo,jco->mc/dot_general | solution.py:111
  237.3 1.5 copy.58
  238.8 19.9 %all_to_all.33 = bf16[256,8,256]{2,1,0:T(8,128)(2,1)S(1)} all-to-all(bf16[256,8,256]{2,1,0:T(8,128)(2,1)S(1)} %bitcast.164), channel_id=1, replica_groups=mesh['wide'=8,'lon'=4] {'wide'}, dimensions={0} | all-to-all | bytes 2097152 | tf_op jit(solution)/shard_map/all_to_all | solution.py:118
  258.8 1.1 copy.67
  (142 shorter events, 63.3 us)
Async XLA Ops:
  0.0 38.0 %copy-start = (f32[4,64,256]{2,1,0:T(8,128)S(1)}, f32[4,64,256]{2,1,0:T(8,128)}, u32[]{:S(2)}) copy-start(f32[4,64,256]{2,1,0:T(8,128)} %param.14) | copy-start | bytes 786436
  2.2 17.4 %collective-permute-start = (bf16[32,64,1]{2,0,1:T(8,128)(2,1)S(1)}, bf16[32,64,1]{2,0,1:T(8,128)(2,1)S(1)}, u32[]{:S(2)}, u32[]{:S(2)}) collective-permute-start(bf16[32,64,1]{2,0,1:T(8,128)(2,1)S(1)} %get-tuple-element.305), channel_id=1, source_target_pairs={{1,0},{2,1},{3,2},{0,3},{5,4},{6,5},{7,6},{4,7},{9,8},{10,9},{11,1... | collective-permute-start | bytes 12296 | tf_op jit(solution)/shard_map/ppermute | solution.py:20
  7.3 23.3 %collective-permute-start.1 = (bf16[32,64,1]{2,0,1:T(8,128)(2,1)S(1)}, bf16[32,64,1]{2,0,1:T(8,128)(2,1)S(1)}, u32[]{:S(2)}, u32[]{:S(2)}) collective-permute-start(bf16[32,64,1]{2,0,1:T(8,128)(2,1)S(1)} %get-tuple-element.306), channel_id=1, source_target_pairs={{0,1},{1,2},{2,3},{3,0},{4,5},{5,6},{6,7},{7,4},{8,9},{9,10},{10,1... | collective-permute-start | bytes 12296 | tf_op jit(solution)/shard_map/ppermute | solution.py:19
  33.5 19.1 %all-to-all-start = ((bf16[32,64,256]{2,0,1:T(8,128)(2,1)}), bf16[32,64,256]{2,0,1:T(8,128)(2,1)S(1)}, u32[]{:S(2)}, u32[]{:S(2)}) async-start(bf16[32,64,256]{2,0,1:T(8,128)(2,1)} %fusion.90), calls=%async_computation | async-start | bytes 2097152 | tf_op jit(solution)/shard_map/all_to_all | solution.py:75
  54.6 2.1 copy-start.1
  59.1 2.1 copy-start.1
  63.5 2.1 copy-start.1
  68.0 2.1 copy-start.1
  73.5 4.0 %copy-start.2 = (bf16[256,2048]{1,0:T(8,128)(2,1)S(1)}, bf16[256,2048]{1,0:T(8,128)(2,1)}, u32[]{:S(2)}) copy-start(bf16[256,2048]{1,0:T(8,128)(2,1)} %get-tuple-element.476) | copy-start | bytes 3145732
  73.6 16.7 %collective-permute-start.2 = (bf16[2,256,512]{1,2,0:T(8,128)(2,1)S(1)}, bf16[2,256,512]{1,2,0:T(8,128)(2,1)S(1)}, u32[]{:S(2)}, u32[]{:S(2)}) collective-permute-start(bf16[2,256,512]{1,2,0:T(8,128)(2,1)S(1)} %get-tuple-element.301), channel_id=1, source_target_pairs={{0,1},{1,2},{2,3},{3,0},{4,5},{5,6},{6,7},{7,4},{8,9},{9,10},{10,1... | collective-permute-start | bytes 1572872 | tf_op jit(solution)/shard_map/ppermute | solution.py:19
  75.3 21.9 %collective-permute-start.3 = (bf16[2,256,512]{1,2,0:T(8,128)(2,1)S(1)}, bf16[2,256,512]{1,2,0:T(8,128)(2,1)S(1)}, u32[]{:S(2)}, u32[]{:S(2)}) collective-permute-start(bf16[2,256,512]{1,2,0:T(8,128)(2,1)S(1)} %get-tuple-element.302), channel_id=1, source_target_pairs={{1,0},{2,1},{3,2},{0,3},{5,4},{6,5},{7,6},{4,7},{9,8},{10,9},{11,1... | collective-permute-start | bytes 1572872 | tf_op jit(solution)/shard_map/ppermute | solution.py:20
  98.9 4.7 %copy-start.3 = (s32[1,16]{1,0:T(1,128)S(1)}, s32[1,16]{1,0:T(1,128)}, u32[]{:S(2)}) copy-start(s32[1,16]{1,0:T(1,128)} %param.16) | copy-start | bytes 196
where the time goes:
time: 262 us; the launch traced here: 260 us
  matrix products  81.1 us (31%)
  local copies, waits for them, and re-layouts  59.7 us (23%)
  waiting for transfers between devices  54.1 us (21%)
  other arithmetic  31.5 us (12%)
  blocking collectives  19.9 us (8%)
  starting transfers between devices  12.7 us (5%)
    dot_general x16, matrix products, body_one_block(): jnp.einsum('mjo,jco->mc', picked[1], tapered, preferred_element_type=jnp....  50.8 us
    squeeze x16, local copies, waits for them, and re-layouts, body_one_block(): picked[0]  27 us
    ppermute x2, waiting for transfers between devices, padded_2(): before = lax.ppermute(last, axis, up)  22.6 us
    all_to_all x1, blocking collectives, body(): lax.all_to_all(result.reshape(members, band_rows, patch_meridian_lines),...  19.9 us
    ppermute x2, waiting for transfers between devices, padded_2(): after = lax.ppermute(first, axis, down)  18.6 us
    dot_general x16, matrix products, observe_one_block(): picked = jnp.dot(state, selector, preferred_element_type=jnp.float32)  17.4 us
    dot_general x16, matrix products, body_one_block(): jnp.einsum('jk,smko->smjo', selector, cand, preferred_element_type=jnp.fl...  13 us
    all_to_all x1, waiting for transfers between devices, body(): lax.all_to_all(prediction_increment, 'wide', split_axis=1, concat_axis=0,...  12.9 us
  transfers between devices with their start and end apart: 5, of which 5 were waited for; matrix products, arithmetic and copies ran while one was open for 2% of the time, Pallas kernels for 0%

commit v1 on v0

--- a/solution.py
+++ b/solution.py
@@ -4,6 +4,8 @@
 import jax.numpy as jnp
 from jax import lax
 from jax.sharding import PartitionSpec as P
+from jax.experimental import pallas as pl
+from jax.experimental.pallas import tpu as pltpu
 
 BLK = 128
 HALO_BLK = 4
@@ -88,33 +90,22 @@
     stacked = jnp.stack([obs_dev, innov.reshape(members, patch_gridpoints)])
     widened = padded_2(stacked, (("lon", 2),), HALO_BLK * BLK)
     candidate_count = widened.shape[2] // BLK
-    cand = widened.reshape(2, members, candidate_count, BLK)
     block_count = patch_gridpoints // BLK
-    candidate_ids = lax.broadcasted_iota(jnp.int32, (obs_list.shape[2], candidate_count), 1)
-
-    def body_one_block(position, result):
-        start = position * BLK
-        state_tile = lax.dynamic_slice_in_dim(model_anomaly, start, BLK, 1)
-        anchor = lax.dynamic_slice_in_dim(region_state, start, BLK, 1)
-        listed = obs_list[0, position]
-        classes = taper_class[0, position]
-        live_count = tile_count[0, position]
-        selector = (candidate_ids == listed[:, None]).astype(jnp.bfloat16)
-        picked = jnp.einsum(
-            "jk,smko->smjo", selector, cand, preferred_element_type=jnp.float32
-        ).astype(jnp.bfloat16)
-        covariance = jnp.einsum(
-            "mc,mjo->jco", state_tile, picked[0], preferred_element_type=jnp.float32
-        ) / (members - 1.0)
-        in_use = (jnp.arange(listed.shape[0], dtype=jnp.int32) < live_count).astype(jnp.float32)
-        tapered = (covariance * taper_tiles(classes, in_use, BLK)).astype(jnp.bfloat16)
-        change = jnp.einsum("mjo,jco->mc", picked[1], tapered, preferred_element_type=jnp.float32)
-        updated = (anchor.astype(jnp.float32) + change).astype(jnp.bfloat16)
-        return lax.dynamic_update_slice_in_dim(result, updated, start, 1)
-
-    result = lax.fori_loop(
-        0, block_count, body_one_block, jnp.zeros((members, patch_gridpoints), jnp.bfloat16)
+    code = block_codes(obs_list[0], tile_count[0], taper_class[0], candidate_count)
+    tiles = taper_table(BLK, members)
+    cand_obs = widened[0]
+    cand_innov_t = widened[1].T
+    result_t = update_call(
+        code.reshape(-1),
+        model_anomaly.T,
+        region_state.T,
+        cand_obs,
+        cand_innov_t,
+        tiles,
+        block_count,
+        candidate_count,
     )
+    result = result_t.T
     return lax.all_to_all(
         result.reshape(members, band_rows, patch_meridian_lines),
         "wide",
@@ -122,6 +113,68 @@
         concat_axis=1,
         tiled=True,
     )
+
+
+def block_codes(lists, counts, classes, candidate_count):
+    zero_code = 4
+    entries = jnp.arange(lists.shape[1], dtype=jnp.int32)
+    value = jnp.where(entries[None, :] < counts[:, None], classes, zero_code)
+    hit = lists[:, :, None] == jnp.arange(candidate_count, dtype=jnp.int32)[None, None, :]
+    code = zero_code + jnp.sum(jnp.where(hit, value[:, :, None] - zero_code, 0), axis=1)
+    return jnp.clip(code, 0, zero_code).astype(jnp.int32)
+
+
+def taper_table(tile_width, members):
+    row_ids = lax.broadcasted_iota(jnp.float32, (tile_width, tile_width), 0)
+    col_ids = lax.broadcasted_iota(jnp.float32, (tile_width, tile_width), 1)
+    offset = row_ids - col_ids
+    length = 8.0 * jnp.exp2(jnp.arange(4, dtype=jnp.float32))
+    scaled = offset[None] / length[:, None, None]
+    tiles = (1.0 / (1.0 + scaled * scaled)) / (members - 1.0)
+    return jnp.concatenate([tiles, jnp.zeros((1, tile_width, tile_width), jnp.float32)], axis=0)
+
+
+GROUP = 4
+
+
+def update_call(code, state_t, anchor_t, cand_obs, cand_innov_t, tiles, block_count, candidate_count):
+    cells, members = state_t.shape
+    rows = GROUP * BLK
+    width = candidate_count * BLK
+
+    def kernel(code_ref, st_ref, ft_ref, o_ref, it_ref, taper_ref, out_ref, cov_scr, tap_scr):
+        g = pl.program_id(0)
+        cov_scr[...] = jnp.dot(st_ref[...], o_ref[...], preferred_element_type=jnp.float32)
+        for sl in range(GROUP):
+            s = g * GROUP + sl
+            for b in range(candidate_count):
+                c = code_ref[s * candidate_count + b]
+                tile = cov_scr[sl * BLK:(sl + 1) * BLK, b * BLK:(b + 1) * BLK] * taper_ref[c]
+                tap_scr[sl * BLK:(sl + 1) * BLK, b * BLK:(b + 1) * BLK] = tile.astype(jnp.bfloat16)
+        change = jnp.dot(tap_scr[...], it_ref[...], preferred_element_type=jnp.float32)
+        out_ref[...] = (ft_ref[...].astype(jnp.float32) + change).astype(jnp.bfloat16)
+
+    grid_spec = pltpu.PrefetchScalarGridSpec(
+        num_scalar_prefetch=1,
+        grid=(block_count // GROUP,),
+        in_specs=[
+            pl.BlockSpec((rows, members), lambda g, code: (g, 0)),
+            pl.BlockSpec((rows, members), lambda g, code: (g, 0)),
+            pl.BlockSpec((members, width), lambda g, code: (0, 0)),
+            pl.BlockSpec((width, members), lambda g, code: (0, 0)),
+            pl.BlockSpec(tiles.shape, lambda g, code: (0, 0, 0)),
+        ],
+        out_specs=pl.BlockSpec((rows, members), lambda g, code: (g, 0)),
+        scratch_shapes=[
+            pltpu.VMEM((rows, width), jnp.float32),
+            pltpu.VMEM((rows, width), jnp.bfloat16),
+        ],
+    )
+    return pl.pallas_call(
+        kernel,
+        grid_spec=grid_spec,
+        out_shape=jax.ShapeDtypeStruct((cells, members), jnp.bfloat16),
+    )(code, state_t, anchor_t, cand_obs, cand_innov_t, tiles)
 
 
 def solution(mesh):

time: 262 us -> 144 us (0.55)
  matrix products: 81.1 us -> 17.4 us
  local copies, waits for them, and re-layouts: 59.7 us -> 16.4 us
  other arithmetic: 31.5 us -> 13.8 us
  Pallas kernels: 0 us -> 13.5 us
  waiting for transfers between devices: 54.1 us -> 49.4 us
    dot_general x32 -> x0, matrix products: 63.7 us -> none  [the longest x16 50.8 us: body_one_block(): jnp.einsum('mjo,jco->mc', picked[1], tapered, preferred_element_type=jnp....]
    squeeze x16 -> x1, local copies, waits for them, and re-layouts: 27 us -> 1.73 us  [body(): cand_obs = widened[0]]
    pallas_call x0 -> x1, Pallas kernels: none -> 13.5 us  [update_call(): pl.pallas_call(kernel, grid_spec=grid_spec, out_shape=jax.ShapeDtypeStruc...]
    mul x16 -> x1, other arithmetic: 11.3 us -> 0.01 us  [taper_table(): length = 8.0 * jnp.exp2(jnp.arange(4, dtype=jnp.float32))]
    eq x16 -> x0, local copies, waits for them, and re-layouts: 11.1 us -> none  [body_one_block(): selector = (candidate_ids == listed[:, None]).astype(jnp.bfloat16)]
    convert_element_type x16 -> x0, other arithmetic: 10.1 us -> none  [body_one_block(): (jnp.arange(listed.shape[0], dtype=jnp.int32) < live_count).astype(jnp.fl...]
    dynamic_slice x16 -> x0, local copies, waits for them, and re-layouts: 9.68 us -> none  [body_one_block(): live_count = tile_count[0, position]]
    ppermute x2, waiting for transfers between devices: 18.6 us -> 14.5 us  [padded_2(): after = lax.ppermute(first, axis, down)]
  transfers between devices with their start and end apart: 5 -> 5, of which waited for: 5 -> 5; matrix products, arithmetic and copies ran while one was open for 2% -> 7% of each run, Pallas kernels for 0% -> 0%
where the time goes in v1:
time: 144 us
  waiting for transfers between devices  49.4 us (34%)
  blocking collectives  20 us (14%)
  matrix products  17.4 us (12%)
  local copies, waits for them, and re-layouts  16.4 us (11%)
  other arithmetic  13.8 us (10%)
  Pallas kernels  13.5 us (9%)
  starting transfers between devices  12.7 us (9%)
    ppermute x2, waiting for transfers between devices, padded_2(): before = lax.ppermute(last, axis, up)  21.3 us
    all_to_all x1, blocking collectives, body(): lax.all_to_all(result.reshape(members, band_rows, patch_meridian_lines),...  20 us
    dot_general x16, matrix products, observe_one_block(): picked = jnp.dot(state, selector, preferred_element_type=jnp.float32)  17.4 us
    ppermute x2, waiting for transfers between devices, padded_2(): after = lax.ppermute(first, axis, down)  14.5 us
    pallas_call x1, Pallas kernels, update_call(): pl.pallas_call(kernel, grid_spec=grid_spec, out_shape=jax.ShapeDtypeStruc...  13.5 us
    all_to_all x1, waiting for transfers between devices, body(): lax.all_to_all(prediction_increment, 'wide', split_axis=1, concat_axis=0,...  13.5 us
    ppermute x2, starting transfers between devices, padded_2(): after = lax.ppermute(first, axis, down)  7.25 us
    convert_element_type x1, other arithmetic, body(): prediction_increment = (state_values + 0.2 * member_spread - 0.3 * (east_...  5.22 us
  transfers between devices with their start and end apart: 5, of which 5 were waited for; matrix products, arithmetic and copies ran while one was open for 7% of the time, Pallas kernels for 0%

profile of v1, /device:TPU:0, one launch (start us, length us, event | category | flops | bytes accessed | tf_op | source)
XLA Modules:
  0.0 143.7 jit_solution(4329772839119455210)
XLA Ops:
  0.0 0.0 copy-start
  0.0 1.9 %fusion.64 = (bf16[32,64,256]{2,0,1:T(8,128)(2,1)S(1)}, f32[32,64,256]{2,0,1:T(8,128)S(1)}) fusion(bf16[32,64,256]{2,1,0:T(8,128)(2,1)} %param.9), kind=kLoop, calls=%fused_computation.78 | loop fusion | flops 524288 | bytes 4194304 | tf_op args[0]
  1.9 1.2 fusion.63
  3.2 5.0 %collective-permute-start = (bf16[32,64,1]{2,0,1:T(8,128)(2,1)}, bf16[32,64,1]{2,0,1:T(8,128)(2,1)}, u32[]{:S(2)}, u32[]{:S(2)}) collective-permute-start(bf16[32,64,1]{2,0,1:T(8,128)(2,1)} %get-tuple-element.126), channel_id=1, source_target_pairs={{1,0},{2,1},{3,2},{0,3},{5,4},{6,5},{7,6},{4,7},{9,8},{10,9},{11,1... | collective-permute-start | bytes 12296 | tf_op jit(solution)/shard_map/ppermute | solution.py:22
  8.2 0.0 collective-permute-start.1
  8.2 2.4 %fusion.62 = (f32[32,63,256]{2,0,1:T(8,128)}, f32[32,63,256]{2,0,1:T(8,128)}) fusion(f32[32,64,256]{2,0,1:T(8,128)S(1)} %get-tuple-element.129), kind=kLoop, calls=%fused_computation.76 | loop fusion | bytes 8257536 | tf_op jit(solution)/shard_map/slice | solution.py:67
  10.7 0.0 copy-done
  10.7 0.8 dynamic-slice_subtract_fusion
  11.5 1.6 %copy.54 = bf16[256,8,256]{0,2,1:T(8,128)(2,1)S(1)} copy(bf16[256,8,256]{2,1,0:T(8,128)(2,1)} %param.10) | data formatting | bytes 2097152 | tf_op args[1]
  13.1 7.7 %collective-permute-done = bf16[32,64,1]{2,0,1:T(8,128)(2,1)} collective-permute-done((bf16[32,64,1]{2,0,1:T(8,128)(2,1)}, bf16[32,64,1]{2,0,1:T(8,128)(2,1)}, u32[]{:S(2)}, u32[]{:S(2)}) %collective-permute-start) | collective-permute-done | bytes 4128 | tf_op jit(solution)/shard_map/ppermute | solution.py:22
  20.9 11.0 %collective-permute-done.1 = bf16[32,64,1]{2,0,1:T(8,128)(2,1)} collective-permute-done((bf16[32,64,1]{2,0,1:T(8,128)(2,1)}, bf16[32,64,1]{2,0,1:T(8,128)(2,1)}, u32[]{:S(2)}, u32[]{:S(2)}) %collective-permute-start.1) | collective-permute-done | bytes 4128 | tf_op jit(solution)/shard_map/ppermute | solution.py:21
  31.8 5.2 %fusion.54 = bf16[32,64,256]{2,0,1:T(8,128)(2,1)} fusion(f32[32,63,256]{2,0,1:T(8,128)} %get-tuple-element.125, f32[32,63,256]{2,0,1:T(8,128)} %get-tuple-element.124, bf16[32,64,256]{2,0,1:T(8,128)(2,1)S(1)} %get-tuple-element.128, bf16[32,64,1]{2,0,1:T(8,128)(2,1)} %collective-permute-done.1, bf16[32,64,1]{2,0,1:T(8,128)(2,1)} %collective-permute-done), kind=kLoop, calls=%fused_computation.44 | loop fusion | flops 10485760 | bytes 6234112 | tf_op jit(solution)/shard_map/convert_element_type | solution.py:72
  37.1 3.9 %all-to-all-start = ((bf16[32,64,256]{2,0,1:T(8,128)(2,1)}), bf16[32,64,256]{2,0,1:T(8,128)(2,1)S(1)}, u32[]{:S(2)}, u32[]{:S(2)}) async-start(bf16[32,64,256]{2,0,1:T(8,128)(2,1)} %fusion.54), calls=%async_computation | async-start | bytes 2097152 | tf_op jit(solution)/shard_map/all_to_all | solution.py:77
  40.9 0.0 copy-done.4
  40.9 0.0 copy-done.5
  41.0 0.1 fusion.61
  41.0 0.1 select_reduce_fusion
  41.2 0.7 min.12.code_ref
  41.9 0.1 fusion.60
  42.0 0.8 concatenate.16.taper_ref
  42.8 13.5 %all-to-all-done = bf16[32,64,256]{2,0,1:T(8,128)(2,1)S(1)} async-done(((bf16[32,64,256]{2,0,1:T(8,128)(2,1)}), bf16[32,64,256]{2,0,1:T(8,128)(2,1)S(1)}, u32[]{:S(2)}, u32[]{:S(2)}) %all-to-all-start) | async-done | bytes 1048608 | tf_op jit(solution)/shard_map/all_to_all | solution.py:77
  56.4 0.6 copy.49
  57.0 1.3 copy.68
  58.3 17.9 %while.12 = (s32[]{:T(128)}, bf16[4,256,512]{1,2,0:T(8,128)(2,1)S(1)}, f32[4,4,512]{2,0,1:T(4,128)S(1)}, s32[4,4,512]{2,0,1:T(4,128)S(1)}, bf16[256,2048]{1,0:T(...) while((s32[]{:T(128)}, bf16[4,256,512]{1,2,0:T(8,128)(2,1)S(1)}, ...), condition=%wide.region_3.4_spmd.clone.clone, body=%wide.region_2.3_spmd.clone.clone.sunk | while | flops 2156920832 | bytes 11845833 | solution.py:44
  58.3 0.0 copy-start.2
  58.3 2.1 %fusion.89 = f32[512,256]{1,0:T(8,128)S(1)} fusion(bf16[256,2048]{1,0:T(8,128)(2,1)} %get-tuple-element.201, s32[512]{0:T(512)S(1)} %bitcast.123, f32[512]{0:T(512)S(1)} %bitcast.125), kind=kOutput, calls=%fused_computation.17.clone.1 | convolution fusion | flops 539099136 | bytes 1576960 | tf_op jit(solution)/shard_map/while/body/eval_jaxpr/dot_general | solution.py:40
  60.4 0.8 fusion.90
  61.2 0.8 fusion.91
  61.9 0.8 fusion.92
  62.8 0.0 copy-start.2
  62.8 2.1 %fusion.89 = f32[512,256]{1,0:T(8,128)S(1)} fusion(bf16[256,2048]{1,0:T(8,128)(2,1)} %get-tuple-element.201, s32[512]{0:T(512)S(1)} %bitcast.123, f32[512]{0:T(512)S(1)} %bitcast.125), kind=kOutput, calls=%fused_computation.17.clone.1 | convolution fusion | flops 539099136 | bytes 1576960 | tf_op jit(solution)/shard_map/while/body/eval_jaxpr/dot_general | solution.py:40
  64.9 0.0 copy-done.2
  64.9 0.8 fusion.90
  65.6 0.8 fusion.91
  66.4 0.8 fusion.92
  67.2 0.0 copy-start.2
  67.3 2.1 %fusion.89 = f32[512,256]{1,0:T(8,128)S(1)} fusion(bf16[256,2048]{1,0:T(8,128)(2,1)} %get-tuple-element.201, s32[512]{0:T(512)S(1)} %bitcast.123, f32[512]{0:T(512)S(1)} %bitcast.125), kind=kOutput, calls=%fused_computation.17.clone.1 | convolution fusion | flops 539099136 | bytes 1576960 | tf_op jit(solution)/shard_map/while/body/eval_jaxpr/dot_general | solution.py:40
  69.4 0.8 fusion.90
  70.1 0.8 fusion.91
  70.9 0.8 fusion.92
  71.7 0.0 copy-start.2
  71.7 2.1 %fusion.89 = f32[512,256]{1,0:T(8,128)S(1)} fusion(bf16[256,2048]{1,0:T(8,128)(2,1)} %get-tuple-element.201, s32[512]{0:T(512)S(1)} %bitcast.123, f32[512]{0:T(512)S(1)} %bitcast.125), kind=kOutput, calls=%fused_computation.17.clone.1 | convolution fusion | flops 539099136 | bytes 1576960 | tf_op jit(solution)/shard_map/while/body/eval_jaxpr/dot_general | solution.py:40
  73.8 0.0 copy-done.2
  73.8 0.8 fusion.90
  74.6 0.8 fusion.91
  75.3 0.8 fusion.92
  76.1 0.2 convert_element_type.73
  76.3 0.4 convert_reduce_fusion.1
  76.7 0.6 convert_reduce_fusion
  77.3 0.3 fusion.56
  77.7 1.0 pad_maximum_fusion.4
  78.7 1.6 %collective-permute-start.2 = (bf16[2,256,512]{1,2,0:T(8,128)(2,1)}, bf16[2,256,512]{1,2,0:T(8,128)(2,1)}, u32[]{:S(2)}, u32[]{:S(2)}) collective-permute-start(bf16[2,256,512]{1,2,0:T(8,128)(2,1)} %get-tuple-element.122), channel_id=1, source_target_pairs={{0,1},{1,2},{2,3},{3,0},{4,5},{5,6},{6,7},{7,4},{8,9},{9,10},{10,1... | collective-permute-start | bytes 1572872 | tf_op jit(solution)/shard_map/ppermute | solution.py:21
  80.3 2.2 %collective-permute-start.3 = (bf16[2,256,512]{1,2,0:T(8,128)(2,1)}, bf16[2,256,512]{1,2,0:T(8,128)(2,1)}, u32[]{:S(2)}, u32[]{:S(2)}) collective-permute-start(bf16[2,256,512]{1,2,0:T(8,128)(2,1)} %get-tuple-element.123), channel_id=1, source_target_pairs={{1,0},{2,1},{3,2},{0,3},{5,4},{6,5},{7,6},{4,7},{9,8},{10,9},{11,1... | collective-permute-start | bytes 1572872 | tf_op jit(solution)/shard_map/ppermute | solution.py:22
  82.5 1.5 %copy.50 = bf16[256,2048]{0,1:T(8,128)(2,1)S(1)} copy(bf16[256,2048]{1,0:T(8,128)(2,1)} %get-tuple-element.210) | data formatting | bytes 2097152 | tf_op jit(solution)/shard_map/reshape | solution.py:78
  84.0 1.3 fusion.57.st_ref
  85.3 10.3 %collective-permute-done.2 = bf16[2,256,512]{1,2,0:T(8,128)(2,1)} collective-permute-done((bf16[2,256,512]{1,2,0:T(8,128)(2,1)}, bf16[2,256,512]{1,2,0:T(8,128)(2,1)}, u32[]{:S(2)}, u32[]{:S(2)}) %collective-permute-start.2) | collective-permute-done | bytes 524320 | tf_op jit(solution)/shard_map/ppermute | solution.py:21
  95.7 6.8 %collective-permute-done.3 = bf16[2,256,512]{1,2,0:T(8,128)(2,1)} collective-permute-done((bf16[2,256,512]{1,2,0:T(8,128)(2,1)}, bf16[2,256,512]{1,2,0:T(8,128)(2,1)}, u32[]{:S(2)}, u32[]{:S(2)}) %collective-permute-start.3) | collective-permute-done | bytes 524320 | tf_op jit(solution)/shard_map/ppermute | solution.py:22
  102.5 1.6 %pad_maximum_fusion = bf16[2,256,3072]{1,2,0:T(8,128)(2,1)S(1)} fusion(bf16[2,256,512]{1,2,0:T(8,128)(2,1)} %collective-permute-done.3, bf16[1,256,2048]{1,2,0:T(8,128)(2,1)S(1)} %bitcast.107, bf16[1,256,2048]{1,2,0:T(8,128)(2,1)S(1)} %fusion.56, bf16[2,256,512]{1,2,0:T(8,128)(2,1)} %collective-permute-done.2), kind=kLoop, calls=%fused_computation.35 | loop fusion | flops 12582912 | bytes 6291456 | tf_op jit(solution)/shard_map/concatenate | solution.py:23
  104.1 1.4 slice_bitcast_fusion
  105.4 1.7 %copy.55.o_ref = bf16[256,3072]{1,0:T(8,128)(2,1)} copy(bf16[256,3072]{0,1:T(8,128)(2,1)S(1)} %get-tuple-element.121) | data formatting | bytes 3145728 | tf_op jit(solution)/shard_map/squeeze | solution.py:96
  107.2 13.5 %shard_map.73 = bf16[2048,256]{1,0:T(8,128)(2,1)} custom-call(s32[384]{0:T(512)} %min.12.code_ref, bf16[2048,256]{1,0:T(8,128)(2,1)} %fusion.57.st_ref, bf16[2048,256]{1,0:T(8,128)(2,1)} %bitcast.110, bf16[256,3072]{1,0:T(8,128)(2,1)} %copy.55.o_ref, bf16[3072,256]{1,0:T(8,128)(2,1)} %get-tuple-element.120.it_ref, f32[5,128,128]{2,1,0:T(8,128)} %concatenate.16.taper_ref), custom_call_target="tpu_custom_call" | custom-call | tf_op jit(solution)/shard_map/pallas_call | solution.py:173
  120.7 1.9 %copy.56 = bf16[256,8,256]{2,1,0:T(8,128)(2,1)S(1)} copy(bf16[256,8,256]{0,2,1:T(8,128)(2,1)} %bitcast.115) | data formatting | bytes 2097152 | tf_op jit(solution)/shard_map/reshape | solution.py:110
  122.6 20.0 %all_to_all.33 = bf16[256,8,256]{2,1,0:T(8,128)(2,1)S(1)} all-to-all(bf16[256,8,256]{2,1,0:T(8,128)(2,1)S(1)} %copy.56), channel_id=1, replica_groups=mesh['wide'=8,'lon'=4] {'wide'}, dimensions={0} | all-to-all | bytes 2097152 | tf_op jit(solution)/shard_map/all_to_all | solution.py:109
  142.6 1.1 copy.75
  (27 shorter events, 0.3 us)
Async XLA Ops:
  0.0 10.7 %copy-start = (f32[4,64,256]{2,1,0:T(8,128)S(1)}, f32[4,64,256]{2,1,0:T(8,128)}, u32[]{:S(2)}) copy-start(f32[4,64,256]{2,1,0:T(8,128)} %param.12) | copy-start | bytes 786436
  3.2 17.7 %collective-permute-start = (bf16[32,64,1]{2,0,1:T(8,128)(2,1)}, bf16[32,64,1]{2,0,1:T(8,128)(2,1)}, u32[]{:S(2)}, u32[]{:S(2)}) collective-permute-start(bf16[32,64,1]{2,0,1:T(8,128)(2,1)} %get-tuple-element.126), channel_id=1, source_target_pairs={{1,0},{2,1},{3,2},{0,3},{5,4},{6,5},{7,6},{4,7},{9,8},{10,9},{11,1... | collective-permute-start | bytes 12296 | tf_op jit(solution)/shard_map/ppermute | solution.py:22
  8.2 23.6 %collective-permute-start.1 = (bf16[32,64,1]{2,0,1:T(8,128)(2,1)}, bf16[32,64,1]{2,0,1:T(8,128)(2,1)}, u32[]{:S(2)}, u32[]{:S(2)}) collective-permute-start(bf16[32,64,1]{2,0,1:T(8,128)(2,1)} %get-tuple-element.127), channel_id=1, source_target_pairs={{0,1},{1,2},{2,3},{3,0},{4,5},{5,6},{6,7},{7,4},{8,9},{9,10},{10,1... | collective-permute-start | bytes 12296 | tf_op jit(solution)/shard_map/ppermute | solution.py:21
  37.1 3.9 %copy-start.4 = (s32[1,16,16]{2,1,0:T(8,128)S(1)}, s32[1,16,16]{2,1,0:T(8,128)}, u32[]{:S(2)}) copy-start(s32[1,16,16]{2,1,0:T(8,128)} %param.15) | copy-start | bytes 3076
  37.1 3.9 %copy-start.5 = (s32[1,16]{1,0:T(1,128)S(1)}, s32[1,16]{1,0:T(1,128)}, u32[]{:S(2)}) copy-start(s32[1,16]{1,0:T(1,128)} %param.14) | copy-start | bytes 196
  37.1 4.0 %copy-start.3 = (s32[1,16,16]{2,1,0:T(8,128)S(1)}, s32[1,16,16]{2,1,0:T(8,128)}, u32[]{:S(2)}) copy-start(s32[1,16,16]{2,1,0:T(8,128)} %param.13) | copy-start | bytes 3076
  37.1 19.3 %all-to-all-start = ((bf16[32,64,256]{2,0,1:T(8,128)(2,1)}), bf16[32,64,256]{2,0,1:T(8,128)(2,1)S(1)}, u32[]{:S(2)}, u32[]{:S(2)}) async-start(bf16[32,64,256]{2,0,1:T(8,128)(2,1)} %fusion.54), calls=%async_computation | async-start | bytes 2097152 | tf_op jit(solution)/shard_map/all_to_all | solution.py:77
  58.3 2.1 %copy-start.2 = (bf16[256,2048]{1,0:T(8,128)(2,1)S(1)}, bf16[256,2048]{1,0:T(8,128)(2,1)}, u32[]{:S(2)}) copy-start(bf16[256,2048]{1,0:T(8,128)(2,1)} %get-tuple-element.201) | copy-start | bytes 3145732 | tf_op jit(solution)/shard_map/while
  62.8 2.1 %copy-start.2 = (bf16[256,2048]{1,0:T(8,128)(2,1)S(1)}, bf16[256,2048]{1,0:T(8,128)(2,1)}, u32[]{:S(2)}) copy-start(bf16[256,2048]{1,0:T(8,128)(2,1)} %get-tuple-element.201) | copy-start | bytes 3145732 | tf_op jit(solution)/shard_map/while
  67.2 2.1 %copy-start.2 = (bf16[256,2048]{1,0:T(8,128)(2,1)S(1)}, bf16[256,2048]{1,0:T(8,128)(2,1)}, u32[]{:S(2)}) copy-start(bf16[256,2048]{1,0:T(8,128)(2,1)} %get-tuple-element.201) | copy-start | bytes 3145732 | tf_op jit(solution)/shard_map/while
  71.7 2.1 %copy-start.2 = (bf16[256,2048]{1,0:T(8,128)(2,1)S(1)}, bf16[256,2048]{1,0:T(8,128)(2,1)}, u32[]{:S(2)}) copy-start(bf16[256,2048]{1,0:T(8,128)(2,1)} %get-tuple-element.201) | copy-start | bytes 3145732 | tf_op jit(solution)/shard_map/while
  78.7 17.0 %collective-permute-start.2 = (bf16[2,256,512]{1,2,0:T(8,128)(2,1)}, bf16[2,256,512]{1,2,0:T(8,128)(2,1)}, u32[]{:S(2)}, u32[]{:S(2)}) collective-permute-start(bf16[2,256,512]{1,2,0:T(8,128)(2,1)} %get-tuple-element.122), channel_id=1, source_target_pairs={{0,1},{1,2},{2,3},{3,0},{4,5},{5,6},{6,7},{7,4},{8,9},{9,10},{10,1... | collective-permute-start | bytes 1572872 | tf_op jit(solution)/shard_map/ppermute | solution.py:21
  80.3 22.1 %collective-permute-start.3 = (bf16[2,256,512]{1,2,0:T(8,128)(2,1)}, bf16[2,256,512]{1,2,0:T(8,128)(2,1)}, u32[]{:S(2)}, u32[]{:S(2)}) collective-permute-start(bf16[2,256,512]{1,2,0:T(8,128)(2,1)} %get-tuple-element.123), channel_id=1, source_target_pairs={{1,0},{2,1},{3,2},{0,3},{5,4},{6,5},{7,6},{4,7},{9,8},{10,9},{11,1... | collective-permute-start | bytes 1572872 | tf_op jit(solution)/shard_map/ppermute | solution.py:22
  84.0 20.1 %copy-start.1 = (bf16[256,2048]{0,1:T(8,128)(2,1)}, bf16[256,2048]{0,1:T(8,128)(2,1)S(1)}, u32[]{:S(2)}) copy-start(bf16[256,2048]{0,1:T(8,128)(2,1)S(1)} %copy.50) | copy-start | bytes 3145732

commit v2 on v1

--- a/solution.py
+++ b/solution.py
@@ -24,6 +24,17 @@
     return value
 
 
+def column_halo(value, axis):
+    size = lax.axis_size(axis)
+    here = lax.axis_index(axis)
+    edges = jnp.concatenate([value[..., :1], value[..., -1:]], axis=-1)
+    spread = jnp.broadcast_to(edges[None], (size,) + edges.shape)
+    got = lax.all_to_all(spread, axis, 0, 0, tiled=False)
+    west = lax.dynamic_index_in_dim(got, (here - 1) % size, 0, keepdims=False)[..., 1:2]
+    east = lax.dynamic_index_in_dim(got, (here + 1) % size, 0, keepdims=False)[..., 0:1]
+    return jnp.concatenate([west, value, east], axis=-1)
+
+
 def observe_region(state, index, weight):
     members, cells = state.shape
     width = math.gcd(512, cells)
@@ -60,7 +71,7 @@
 
 
 def body(background_ensemble, innov, obs_index, obs_weight, obs_list, tile_count, taper_class):
-    padded = padded_2(background_ensemble, (("lon", 2),), 1)
+    padded = column_halo(background_ensemble, "lon")
     state_values = background_ensemble.astype(jnp.float32)
     east_neighbour = padded[:, :, 2:].astype(jnp.float32)
     west_neighbour = padded[:, :, :-2].astype(jnp.float32)

time: 144 us -> 132 us (0.917)
  waiting for transfers between devices: 49.4 us -> 31 us
  local copies, waits for them, and re-layouts: 16.4 us -> 20.9 us
    ppermute x2 -> x1, waiting for transfers between devices: 21.3 us -> 10.3 us  [padded_2(): before = lax.ppermute(last, axis, up)]
    ppermute x2 -> x1, waiting for transfers between devices: 14.5 us -> 7.19 us  [padded_2(): after = lax.ppermute(first, axis, down)]
    all_to_all x0 -> x1, starting transfers between devices: none -> 6.32 us  [column_halo(): got = lax.all_to_all(spread, axis, 0, 0, tiled=False)]
    ppermute x2 -> x1, starting transfers between devices: 7.25 us -> 1.8 us  [padded_2(): after = lax.ppermute(first, axis, down)]
    slice x1 -> x5, local copies, waits for them, and re-layouts: 1.22 us -> 4.87 us  [the longest x2 1.66 us: column_halo(): lax.dynamic_index_in_dim(got, (here - 1) % size, 0, keepdims=False)]
    unnamed x14 -> x23, local copies, waits for them, and re-layouts: 2.94 us -> 4.37 us
  transfers between devices with their start and end apart: 5 -> 4, of which waited for: 5 -> 3; matrix products, arithmetic and copies ran while one was open for 7% -> 8% of each run, Pallas kernels for 0% -> 0%
where the time goes in v2:
time: 132 us; the launch traced here: 131 us
  waiting for transfers between devices  31 us (23%)
  local copies, waits for them, and re-layouts  20.9 us (16%)
  blocking collectives  20 us (15%)
  matrix products  17.4 us (13%)
  starting transfers between devices  14 us (11%)
  other arithmetic  13.8 us (10%)
  Pallas kernels  13.6 us (10%)
    all_to_all x1, blocking collectives, body(): lax.all_to_all(result.reshape(members, band_rows, patch_meridian_lines),...  20 us
    dot_general x16, matrix products, observe_one_block(): picked = jnp.dot(state, selector, preferred_element_type=jnp.float32)  17.4 us
    pallas_call x1, Pallas kernels, update_call(): pl.pallas_call(kernel, grid_spec=grid_spec, out_shape=jax.ShapeDtypeStruc...  13.6 us
    all_to_all x1, waiting for transfers between devices, body(): lax.all_to_all(prediction_increment, 'wide', split_axis=1, concat_axis=0,...  13.5 us
    ppermute x1, waiting for transfers between devices, padded_2(): before = lax.ppermute(last, axis, up)  10.3 us
    ppermute x1, waiting for transfers between devices, padded_2(): after = lax.ppermute(first, axis, down)  7.19 us
    all_to_all x1, starting transfers between devices, column_halo(): got = lax.all_to_all(spread, axis, 0, 0, tiled=False)  6.32 us
    convert_element_type x1, other arithmetic, body(): prediction_increment = (state_values + 0.2 * member_spread - 0.3 * (east_...  5.56 us
  transfers between devices with their start and end apart: 4, of which 3 were waited for; matrix products, arithmetic and copies ran while one was open for 8% of the time, Pallas kernels for 0%

profile of v2, /device:TPU:0, one launch (start us, length us, event | category | flops | bytes accessed | tf_op | source)
XLA Modules:
  0.0 131.3 jit_solution(10904893451747456401)
XLA Ops:
  0.0 0.0 copy-start
  0.0 1.5 %fusion.63 = (bf16[32,64,1]{2,1,0:T(8,128)(2,1)S(1)}, bf16[32,64,1]{2,1,0:T(8,128)(2,1)S(1)}) fusion(bf16[32,64,256]{2,1,0:T(8,128)(2,1)} %param.9), kind=kLoop, calls=%fused_computation.80 | loop fusion | bytes 16384 | tf_op jit(solution)/shard_map/slice | solution.py:30
  1.6 0.3 copy.78
  1.8 0.3 copy.79
  2.1 0.7 reshape.144
  2.9 6.3 %all-to-all-start = ((bf16[4,2,2048]{2,1,0:T(2,128)(2,1)}), bf16[4,2,2048]{2,1,0:T(2,128)(2,1)S(1)}, u32[]{:S(2)}, u32[]{:S(2)}) async-start(bf16[4,2,2048]{2,1,0:T(2,128)(2,1)} %reshape.144), calls=%async_computation | async-start | bytes 65536 | tf_op jit(solution)/shard_map/all_to_all | solution.py:32
  9.2 0.0 copy-done.4
  9.2 1.6 %fusion.64 = (bf16[32,64,256]{2,0,1:T(8,128)(2,1)}, f32[32,64,256]{2,0,1:T(8,128)S(1)}) fusion(bf16[32,64,256]{2,1,0:T(8,128)(2,1)S(1)} %copy-done.4), kind=kLoop, calls=%fused_computation.81 | loop fusion | flops 524288 | bytes 4194304 | tf_op args[0]
  10.8 1.8 %fusion.62 = (f32[32,63,256]{2,0,1:T(8,128)S(1)}, f32[32,63,256]{2,0,1:T(8,128)}) fusion(f32[32,64,256]{2,0,1:T(8,128)S(1)} %get-tuple-element.134), kind=kLoop, calls=%fused_computation.79 | loop fusion | bytes 8257536 | tf_op jit(solution)/shard_map/slice | solution.py:78
  12.7 0.0 copy-done
  12.7 0.8 dynamic-slice_subtract_fusion
  13.5 1.6 %copy.72 = bf16[256,8,256]{0,2,1:T(8,128)(2,1)S(1)} copy(bf16[256,8,256]{2,1,0:T(8,128)(2,1)} %param.10) | data formatting | bytes 2097152 | tf_op args[1]
  15.1 0.0 all-to-all-done
  15.2 0.1 reshape.145
  15.3 1.7 %copy.64 = bf16[32,64,1]{2,0,1:T(8,128)(2,1)} copy(bf16[32,64,1]{1,0,2:T(8,128)(2,1)S(1)} %slice.98) | data formatting | bytes 8192 | tf_op jit(solution)/shard_map/slice | solution.py:34
  17.0 1.7 %copy.65 = bf16[32,64,1]{2,0,1:T(8,128)(2,1)} copy(bf16[32,64,1]{1,0,2:T(8,128)(2,1)S(1)} %slice.99) | data formatting | bytes 8192 | tf_op jit(solution)/shard_map/slice | solution.py:33
  18.6 5.6 %fusion.54 = bf16[32,64,256]{2,0,1:T(8,128)(2,1)} fusion(f32[32,63,256]{2,0,1:T(8,128)} %get-tuple-element.130, f32[32,63,256]{2,0,1:T(8,128)S(1)} %get-tuple-element.129, bf16[32,64,256]{2,0,1:T(8,128)(2,1)} %get-tuple-element.133, bf16[32,64,1]{2,0,1:T(8,128)(2,1)} %copy.65, bf16[32,64,1]{2,0,1:T(8,128)(2,1)} %copy.64), kind=kLoop, calls=%fused_computation.44 | loop fusion | flops 10485760 | bytes 6234112 | tf_op jit(solution)/shard_map/convert_element_type | solution.py:83
  24.2 3.9 %all-to-all-start.1 = ((bf16[32,64,256]{2,0,1:T(8,128)(2,1)}), bf16[32,64,256]{2,0,1:T(8,128)(2,1)S(1)}, u32[]{:S(2)}, u32[]{:S(2)}) async-start(bf16[32,64,256]{2,0,1:T(8,128)(2,1)} %fusion.54), calls=%async_computation.1 | async-start | bytes 2097152 | tf_op jit(solution)/shard_map/all_to_all | solution.py:88
  28.1 0.0 copy-done.7
  28.1 0.1 fusion.61
  28.2 0.1 select_reduce_fusion
  28.3 0.7 min.12.code_ref
  29.0 0.1 fusion.60
  29.2 0.8 concatenate.20.taper_ref
  29.9 13.5 %all-to-all-done.1 = bf16[32,64,256]{2,0,1:T(8,128)(2,1)S(1)} async-done(((bf16[32,64,256]{2,0,1:T(8,128)(2,1)}), bf16[32,64,256]{2,0,1:T(8,128)(2,1)S(1)}, u32[]{:S(2)}, u32[]{:S(2)}) %all-to-all-start.1) | async-done | bytes 1048608 | tf_op jit(solution)/shard_map/all_to_all | solution.py:88
  43.5 0.6 copy.67
  44.1 1.3 copy.88
  45.4 0.0 copy-done.2
  45.4 17.8 %while.12 = (s32[]{:T(128)}, bf16[4,256,512]{1,2,0:T(8,128)(2,1)S(1)}, f32[4,4,512]{2,0,1:T(4,128)S(1)}, s32[4,4,512]{2,0,1:T(4,128)S(1)}, bf16[256,2048]{1,0:T(...) while((s32[]{:T(128)}, bf16[4,256,512]{1,2,0:T(8,128)(2,1)S(1)}, ...), condition=%wide.region_3.4_spmd.clone.clone, body=%wide.region_2.3_spmd.clone.clone.sunk | while | flops 2156920832 | bytes 11845833 | solution.py:55
  45.5 2.1 %fusion.89 = f32[512,256]{1,0:T(8,128)S(1)} fusion(bf16[256,2048]{1,0:T(8,128)(2,1)} %get-tuple-element.208, s32[512]{0:T(512)S(1)} %bitcast.131, f32[512]{0:T(512)S(1)} %bitcast.133), kind=kOutput, calls=%fused_computation.17.clone.1 | convolution fusion | flops 539099136 | bytes 1576960 | tf_op jit(solution)/shard_map/while/body/eval_jaxpr/dot_general | solution.py:51
  47.5 0.8 fusion.90
  48.3 0.8 fusion.91
  49.1 0.8 fusion.92
  49.9 2.1 %fusion.89 = f32[512,256]{1,0:T(8,128)S(1)} fusion(bf16[256,2048]{1,0:T(8,128)(2,1)} %get-tuple-element.208, s32[512]{0:T(512)S(1)} %bitcast.131, f32[512]{0:T(512)S(1)} %bitcast.133), kind=kOutput, calls=%fused_computation.17.clone.1 | convolution fusion | flops 539099136 | bytes 1576960 | tf_op jit(solution)/shard_map/while/body/eval_jaxpr/dot_general | solution.py:51
  52.0 0.8 fusion.90
  52.8 0.8 fusion.91
  53.5 0.8 fusion.92
  54.4 2.1 %fusion.89 = f32[512,256]{1,0:T(8,128)S(1)} fusion(bf16[256,2048]{1,0:T(8,128)(2,1)} %get-tuple-element.208, s32[512]{0:T(512)S(1)} %bitcast.131, f32[512]{0:T(512)S(1)} %bitcast.133), kind=kOutput, calls=%fused_computation.17.clone.1 | convolution fusion | flops 539099136 | bytes 1576960 | tf_op jit(solution)/shard_map/while/body/eval_jaxpr/dot_general | solution.py:51
  56.5 0.8 fusion.90
  57.2 0.8 fusion.91
  58.0 0.8 fusion.92
  58.8 0.0 copy-start.3
  58.8 2.1 %fusion.89 = f32[512,256]{1,0:T(8,128)S(1)} fusion(bf16[256,2048]{1,0:T(8,128)(2,1)} %get-tuple-element.208, s32[512]{0:T(512)S(1)} %bitcast.131, f32[512]{0:T(512)S(1)} %bitcast.133), kind=kOutput, calls=%fused_computation.17.clone.1 | convolution fusion | flops 539099136 | bytes 1576960 | tf_op jit(solution)/shard_map/while/body/eval_jaxpr/dot_general | solution.py:51
  60.9 0.8 fusion.90
  61.7 0.8 fusion.91
  62.5 0.8 fusion.92
  63.2 0.2 convert_element_type.73
  63.4 0.4 convert_reduce_fusion.1
  63.8 0.6 convert_reduce_fusion
  64.4 0.3 fusion.56
  64.8 1.1 pad_maximum_fusion.4
  65.8 2.0 %collective-permute-start = (bf16[2,256,512]{1,2,0:T(8,128)(2,1)}, bf16[2,256,512]{1,2,0:T(8,128)(2,1)}, u32[]{:S(2)}, u32[]{:S(2)}) collective-permute-start(bf16[2,256,512]{1,2,0:T(8,128)(2,1)} %get-tuple-element.127), channel_id=1, source_target_pairs={{0,1},{1,2},{2,3},{3,0},{4,5},{5,6},{6,7},{7,4},{8,9},{9,10},{10,1... | collective-permute-start | bytes 1572872 | tf_op jit(solution)/shard_map/ppermute | solution.py:21
  67.9 1.8 %collective-permute-start.1 = (bf16[2,256,512]{1,2,0:T(8,128)(2,1)}, bf16[2,256,512]{1,2,0:T(8,128)(2,1)}, u32[]{:S(2)}, u32[]{:S(2)}) collective-permute-start(bf16[2,256,512]{1,2,0:T(8,128)(2,1)} %get-tuple-element.128), channel_id=1, source_target_pairs={{1,0},{2,1},{3,2},{0,3},{5,4},{6,5},{7,6},{4,7},{9,8},{10,9},{11,1... | collective-permute-start | bytes 1572872 | tf_op jit(solution)/shard_map/ppermute | solution.py:22
  69.7 1.5 %copy.68 = bf16[256,2048]{0,1:T(8,128)(2,1)S(1)} copy(bf16[256,2048]{1,0:T(8,128)(2,1)} %get-tuple-element.217) | data formatting | bytes 2097152 | tf_op jit(solution)/shard_map/reshape | solution.py:89
  71.2 1.3 fusion.57.st_ref
  72.5 10.3 %collective-permute-done = bf16[2,256,512]{1,2,0:T(8,128)(2,1)} collective-permute-done((bf16[2,256,512]{1,2,0:T(8,128)(2,1)}, bf16[2,256,512]{1,2,0:T(8,128)(2,1)}, u32[]{:S(2)}, u32[]{:S(2)}) %collective-permute-start) | collective-permute-done | bytes 524320 | tf_op jit(solution)/shard_map/ppermute | solution.py:21
  82.8 7.2 %collective-permute-done.1 = bf16[2,256,512]{1,2,0:T(8,128)(2,1)} collective-permute-done((bf16[2,256,512]{1,2,0:T(8,128)(2,1)}, bf16[2,256,512]{1,2,0:T(8,128)(2,1)}, u32[]{:S(2)}, u32[]{:S(2)}) %collective-permute-start.1) | collective-permute-done | bytes 524320 | tf_op jit(solution)/shard_map/ppermute | solution.py:22
  90.0 1.6 %pad_maximum_fusion = bf16[2,256,3072]{1,2,0:T(8,128)(2,1)S(1)} fusion(bf16[2,256,512]{1,2,0:T(8,128)(2,1)} %collective-permute-done.1, bf16[1,256,2048]{1,2,0:T(8,128)(2,1)S(1)} %bitcast.114, bf16[1,256,2048]{1,2,0:T(8,128)(2,1)S(1)} %fusion.56, bf16[2,256,512]{1,2,0:T(8,128)(2,1)} %collective-permute-done), kind=kLoop, calls=%fused_computation.35 | loop fusion | flops 12582912 | bytes 6291456 | tf_op jit(solution)/shard_map/concatenate | solution.py:23
  91.6 1.4 %slice_bitcast_fusion = (bf16[3072,256]{1,0:T(8,128)(2,1)}, bf16[256,3072]{0,1:T(8,128)(2,1)S(1)}) fusion(bf16[2,256,3072]{1,2,0:T(8,128)(2,1)S(1)} %pad_maximum_fusion), kind=kLoop, calls=%fused_computation.50 | loop fusion | bytes 6291456 | tf_op jit(solution)/shard_map/transpose | solution.py:108
  93.0 1.7 %copy.73.o_ref = bf16[256,3072]{1,0:T(8,128)(2,1)} copy(bf16[256,3072]{0,1:T(8,128)(2,1)S(1)} %get-tuple-element.126) | data formatting | bytes 3145728 | tf_op jit(solution)/shard_map/squeeze | solution.py:107
  94.8 13.6 %shard_map.73 = bf16[2048,256]{1,0:T(8,128)(2,1)} custom-call(s32[384]{0:T(512)} %min.12.code_ref, bf16[2048,256]{1,0:T(8,128)(2,1)} %fusion.57.st_ref, bf16[2048,256]{1,0:T(8,128)(2,1)} %bitcast.117, bf16[256,3072]{1,0:T(8,128)(2,1)} %copy.73.o_ref, bf16[3072,256]{1,0:T(8,128)(2,1)} %get-tuple-element.125.it_ref, f32[5,128,128]{2,1,0:T(8,128)} %concatenate.20.taper_ref), custom_call_target="tpu_custom_call" | custom-call | tf_op jit(solution)/shard_map/pallas_call | solution.py:184
  108.3 1.9 %copy.74 = bf16[256,8,256]{2,1,0:T(8,128)(2,1)S(1)} copy(bf16[256,8,256]{0,2,1:T(8,128)(2,1)} %bitcast.122) | data formatting | bytes 2097152 | tf_op jit(solution)/shard_map/reshape | solution.py:121
  110.2 20.0 %all_to_all.38 = bf16[256,8,256]{2,1,0:T(8,128)(2,1)S(1)} all-to-all(bf16[256,8,256]{2,1,0:T(8,128)(2,1)S(1)} %copy.74), channel_id=1, replica_groups=mesh['wide'=8,'lon'=4] {'wide'}, dimensions={0} | all-to-all | bytes 2097152 | tf_op jit(solution)/shard_map/all_to_all | solution.py:120
  130.2 1.1 copy.95
  (40 shorter events, 0.3 us)
Async XLA Ops:
  0.0 12.7 %copy-start = (f32[4,64,256]{2,1,0:T(8,128)S(1)}, f32[4,64,256]{2,1,0:T(8,128)}, u32[]{:S(2)}) copy-start(f32[4,64,256]{2,1,0:T(8,128)} %param.12) | copy-start | bytes 786436
  0.0 9.2 %copy-start.4 = (bf16[32,64,256]{2,1,0:T(8,128)(2,1)S(1)}, bf16[32,64,256]{2,1,0:T(8,128)(2,1)}, u32[]{:S(2)}) copy-start(bf16[32,64,256]{2,1,0:T(8,128)(2,1)} %param.9) | copy-start | bytes 3145732
  2.9 12.3 %all-to-all-start = ((bf16[4,2,2048]{2,1,0:T(2,128)(2,1)}), bf16[4,2,2048]{2,1,0:T(2,128)(2,1)S(1)}, u32[]{:S(2)}, u32[]{:S(2)}) async-start(bf16[4,2,2048]{2,1,0:T(2,128)(2,1)} %reshape.144), calls=%async_computation | async-start | bytes 65536 | tf_op jit(solution)/shard_map/all_to_all | solution.py:32
  24.2 3.9 %copy-start.6 = (s32[1,16,16]{2,1,0:T(8,128)S(1)}, s32[1,16,16]{2,1,0:T(8,128)}, u32[]{:S(2)}) copy-start(s32[1,16,16]{2,1,0:T(8,128)} %param.15) | copy-start | bytes 3076
  24.2 3.9 %copy-start.7 = (s32[1,16]{1,0:T(1,128)S(1)}, s32[1,16]{1,0:T(1,128)}, u32[]{:S(2)}) copy-start(s32[1,16]{1,0:T(1,128)} %param.14) | copy-start | bytes 196
  24.2 4.0 %copy-start.5 = (s32[1,16,16]{2,1,0:T(8,128)S(1)}, s32[1,16,16]{2,1,0:T(8,128)}, u32[]{:S(2)}) copy-start(s32[1,16,16]{2,1,0:T(8,128)} %param.13) | copy-start | bytes 3076
  24.2 19.3 %all-to-all-start.1 = ((bf16[32,64,256]{2,0,1:T(8,128)(2,1)}), bf16[32,64,256]{2,0,1:T(8,128)(2,1)S(1)}, u32[]{:S(2)}, u32[]{:S(2)}) async-start(bf16[32,64,256]{2,0,1:T(8,128)(2,1)} %fusion.54), calls=%async_computation.1 | async-start | bytes 2097152 | tf_op jit(solution)/shard_map/all_to_all | solution.py:88
  43.5 1.9 %copy-start.2 = (bf16[4,256,512]{1,2,0:T(8,128)(2,1)S(1)}, bf16[4,256,512]{1,2,0:T(8,128)(2,1)}, u32[]{:S(2)}) copy-start(bf16[4,256,512]{1,2,0:T(8,128)(2,1)} %custom-call) | copy-start | bytes 3145732
  45.4 2.1 %copy-start.3 = (bf16[256,2048]{1,0:T(8,128)(2,1)S(1)}, bf16[256,2048]{1,0:T(8,128)(2,1)}, u32[]{:S(2)}) copy-start(bf16[256,2048]{1,0:T(8,128)(2,1)} %get-tuple-element.208) | copy-start | bytes 3145732 | tf_op jit(solution)/shard_map/while
  49.9 2.1 %copy-start.3 = (bf16[256,2048]{1,0:T(8,128)(2,1)S(1)}, bf16[256,2048]{1,0:T(8,128)(2,1)}, u32[]{:S(2)}) copy-start(bf16[256,2048]{1,0:T(8,128)(2,1)} %get-tuple-element.208) | copy-start | bytes 3145732 | tf_op jit(solution)/shard_map/while
  54.4 2.1 %copy-start.3 = (bf16[256,2048]{1,0:T(8,128)(2,1)S(1)}, bf16[256,2048]{1,0:T(8,128)(2,1)}, u32[]{:S(2)}) copy-start(bf16[256,2048]{1,0:T(8,128)(2,1)} %get-tuple-element.208) | copy-start | bytes 3145732 | tf_op jit(solution)/shard_map/while
  58.8 2.1 %copy-start.3 = (bf16[256,2048]{1,0:T(8,128)(2,1)S(1)}, bf16[256,2048]{1,0:T(8,128)(2,1)}, u32[]{:S(2)}) copy-start(bf16[256,2048]{1,0:T(8,128)(2,1)} %get-tuple-element.208) | copy-start | bytes 3145732 | tf_op jit(solution)/shard_map/while
  65.8 17.0 %collective-permute-start = (bf16[2,256,512]{1,2,0:T(8,128)(2,1)}, bf16[2,256,512]{1,2,0:T(8,128)(2,1)}, u32[]{:S(2)}, u32[]{:S(2)}) collective-permute-start(bf16[2,256,512]{1,2,0:T(8,128)(2,1)} %get-tuple-element.127), channel_id=1, source_target_pairs={{0,1},{1,2},{2,3},{3,0},{4,5},{5,6},{6,7},{7,4},{8,9},{9,10},{10,1... | collective-permute-start | bytes 1572872 | tf_op jit(solution)/shard_map/ppermute | solution.py:21
  67.9 22.1 %collective-permute-start.1 = (bf16[2,256,512]{1,2,0:T(8,128)(2,1)}, bf16[2,256,512]{1,2,0:T(8,128)(2,1)}, u32[]{:S(2)}, u32[]{:S(2)}) collective-permute-start(bf16[2,256,512]{1,2,0:T(8,128)(2,1)} %get-tuple-element.128), channel_id=1, source_target_pairs={{1,0},{2,1},{3,2},{0,3},{5,4},{6,5},{7,6},{4,7},{9,8},{10,9},{11,1... | collective-permute-start | bytes 1572872 | tf_op jit(solution)/shard_map/ppermute | solution.py:22
  71.2 20.5 %copy-start.1 = (bf16[256,2048]{0,1:T(8,128)(2,1)}, bf16[256,2048]{0,1:T(8,128)(2,1)S(1)}, u32[]{:S(2)}) copy-start(bf16[256,2048]{0,1:T(8,128)(2,1)S(1)} %copy.68) | copy-start | bytes 3145732

commit v3 on v2

--- a/solution.py
+++ b/solution.py
@@ -37,8 +37,9 @@
 
 def observe_region(state, index, weight):
     members, cells = state.shape
-    width = math.gcd(512, cells)
-    nblocks = cells // width
+    count = index.shape[1]
+    width = math.gcd(512, count)
+    nblocks = count // width
     index_blocks = index.reshape(4, nblocks, width).transpose(1, 0, 2)
     weight_blocks = weight.reshape(4, nblocks, width).transpose(1, 0, 2)
     cell_ids = lax.broadcasted_iota(jnp.int32, (cells, width), 0)
@@ -53,7 +54,7 @@
         return summed.astype(jnp.bfloat16)
 
     result = lax.map(observe_one_block, (index_blocks, weight_blocks))
-    return result.transpose(1, 0, 2).reshape(members, cells)
+    return result.transpose(1, 0, 2).reshape(members, count)
 
 
 def anomaly_from_mean(state_values):
@@ -95,26 +96,46 @@
     local_weight = lax.dynamic_slice_in_dim(obs_weight, first_row, band_rows, 1).reshape(
         4, patch_gridpoints
     )
-    region_obs = observe_region(region_state, local_index, local_weight)
+    halo = HALO_BLK * BLK
+    innov_flat = innov.reshape(members, patch_gridpoints)
+    edge_index = jnp.concatenate([local_index[:, :halo], local_index[:, -halo:]], axis=1)
+    edge_weight = jnp.concatenate([local_weight[:, :halo], local_weight[:, -halo:]], axis=1)
+    edge_dev = anomaly_from_mean(observe_region(region_state, edge_index, edge_weight))
+    edge_innov = jnp.concatenate([innov_flat[:, :halo], innov_flat[:, -halo:]], axis=1)
+    edges = jnp.stack([edge_dev, edge_innov])
+    lon_size = lax.axis_size("lon")
+    up = [(i, (i + 1) % lon_size) for i in range(lon_size)]
+    down = [(j, i) for i, j in up]
+    west = lax.ppermute(edges[:, :, halo:], "lon", up)
+    east = lax.ppermute(edges[:, :, :halo], "lon", down)
+    middle_dev = anomaly_from_mean(
+        observe_region(region_state, local_index[:, halo:-halo], local_weight[:, halo:-halo])
+    )
+    obs_dev = jnp.concatenate([edge_dev[:, :halo], middle_dev, edge_dev[:, halo:]], axis=1)
     model_anomaly = anomaly_from_mean(region_state)
-    obs_dev = anomaly_from_mean(region_obs)
-    stacked = jnp.stack([obs_dev, innov.reshape(members, patch_gridpoints)])
-    widened = padded_2(stacked, (("lon", 2),), HALO_BLK * BLK)
-    candidate_count = widened.shape[2] // BLK
+    halo_blocks = halo // BLK
     block_count = patch_gridpoints // BLK
+    candidate_count = block_count + 2 * halo_blocks
     code = block_codes(obs_list[0], tile_count[0], taper_class[0], candidate_count)
+    own_code = code[:, halo_blocks:halo_blocks + block_count]
+    halo_code = jnp.concatenate([code[:, :halo_blocks], code[:, halo_blocks + block_count:]], axis=1)
     tiles = taper_table(BLK, members)
-    cand_obs = widened[0]
-    cand_innov_t = widened[1].T
+    state_t = model_anomaly.T
+    partial = update_call(
+        own_code.reshape(-1), state_t, None, None, obs_dev, innov_flat.T, tiles, block_count, block_count
+    )
+    halo_obs = jnp.concatenate([west[0], east[0]], axis=1)
+    halo_innov = jnp.concatenate([west[1], east[1]], axis=1)
     result_t = update_call(
-        code.reshape(-1),
-        model_anomaly.T,
+        halo_code.reshape(-1),
+        state_t,
+        partial,
         region_state.T,
-        cand_obs,
-        cand_innov_t,
+        halo_obs,
+        halo_innov.T,
         tiles,
         block_count,
-        candidate_count,
+        2 * halo_blocks,
     )
     result = result_t.T
     return lax.all_to_all(
@@ -148,12 +169,17 @@
 GROUP = 4
 
 
-def update_call(code, state_t, anchor_t, cand_obs, cand_innov_t, tiles, block_count, candidate_count):
+def update_call(code, state_t, partial, anchor_t, cand_obs, cand_innov_t, tiles, block_count, candidate_count):
     cells, members = state_t.shape
     rows = GROUP * BLK
     width = candidate_count * BLK
-
-    def kernel(code_ref, st_ref, ft_ref, o_ref, it_ref, taper_ref, out_ref, cov_scr, tap_scr):
+    final = anchor_t is not None
+
+    def kernel(code_ref, st_ref, o_ref, it_ref, taper_ref, *rest):
+        if final:
+            part_ref, ft_ref, out_ref, cov_scr, tap_scr = rest
+        else:
+            out_ref, cov_scr, tap_scr = rest
         g = pl.program_id(0)
         cov_scr[...] = jnp.dot(st_ref[...], o_ref[...], preferred_element_type=jnp.float32)
         for sl in range(GROUP):
@@ -163,29 +189,40 @@
                 tile = cov_scr[sl * BLK:(sl + 1) * BLK, b * BLK:(b + 1) * BLK] * taper_ref[c]
                 tap_scr[sl * BLK:(sl + 1) * BLK, b * BLK:(b + 1) * BLK] = tile.astype(jnp.bfloat16)
         change = jnp.dot(tap_scr[...], it_ref[...], preferred_element_type=jnp.float32)
-        out_ref[...] = (ft_ref[...].astype(jnp.float32) + change).astype(jnp.bfloat16)
-
+        if final:
+            total = part_ref[...] + change
+            out_ref[...] = (ft_ref[...].astype(jnp.float32) + total).astype(jnp.bfloat16)
+        else:
+            out_ref[...] = change
+
+    row_spec = pl.BlockSpec((rows, members), lambda g, code: (g, 0))
+    in_specs = [
+        row_spec,
+        pl.BlockSpec((members, width), lambda g, code: (0, 0)),
+        pl.BlockSpec((width, members), lambda g, code: (0, 0)),
+        pl.BlockSpec(tiles.shape, lambda g, code: (0, 0, 0)),
+    ]
+    operands = [state_t, cand_obs, cand_innov_t, tiles]
+    if final:
+        in_specs += [row_spec, row_spec]
+        operands += [partial, anchor_t]
     grid_spec = pltpu.PrefetchScalarGridSpec(
         num_scalar_prefetch=1,
         grid=(block_count // GROUP,),
-        in_specs=[
-            pl.BlockSpec((rows, members), lambda g, code: (g, 0)),
-            pl.BlockSpec((rows, members), lambda g, code: (g, 0)),
-            pl.BlockSpec((members, width), lambda g, code: (0, 0)),
-            pl.BlockSpec((width, members), lambda g, code: (0, 0)),
-            pl.BlockSpec(tiles.shape, lambda g, code: (0, 0, 0)),
-        ],
-        out_specs=pl.BlockSpec((rows, members), lambda g, code: (g, 0)),
+        in_specs=in_specs,
+        out_specs=row_spec,
         scratch_shapes=[
             pltpu.VMEM((rows, width), jnp.float32),
             pltpu.VMEM((rows, width), jnp.bfloat16),
         ],
     )
+    out_type = jnp.bfloat16 if final else jnp.float32
     return pl.pallas_call(
         kernel,
         grid_spec=grid_spec,
-        out_shape=jax.ShapeDtypeStruct((cells, members), jnp.bfloat16),
-    )(code, state_t, anchor_t, cand_obs, cand_innov_t, tiles)
+        out_shape=jax.ShapeDtypeStruct((cells, members), out_type),
+        cost_estimate=pl.CostEstimate(flops=4 * cells * members * width, transcendentals=0, bytes_accessed=8 * cells * members),
+    )(code, *operands)
 
 
 def solution(mesh):

time: 132 us -> 122 us (0.924)
  waiting for transfers between devices: 31 us -> 15 us
  Pallas kernels: 13.6 us -> 17.8 us
  local copies, waits for them, and re-layouts: 20.9 us -> 23.5 us
  matrix products: 17.4 us -> 14.8 us
  other arithmetic: 13.8 us -> 16 us
    ppermute x2, waiting for transfers between devices: 17.5 us -> 3.25 us  [the longest x1 3.25 us: body(): west = lax.ppermute(edges[:, :, halo:], 'lon', up)]
    pallas_call x1 -> x2, Pallas kernels: 13.6 us -> 17.8 us  [update_call(): pl.pallas_call(kernel, grid_spec=grid_spec, out_shape=jax.ShapeDtypeStruc...]
    dot_general x16, matrix products: 17.4 us -> 14.8 us  [observe_one_block(): picked = jnp.dot(state, selector, preferred_element_type=jnp.float32)]
    all_to_all x1, waiting for transfers between devices: 13.5 us -> 11.2 us  [body(): lax.all_to_all(prediction_increment, 'wide', split_axis=1, concat_axis=0,...]
    convert_element_type x0 -> x2, local copies, waits for them, and re-layouts: none -> 1.64 us  [anomaly_from_mean(): centred = state_values.astype(jnp.float32)]
    transpose x1 -> x0, local copies, waits for them, and re-layouts: 1.37 us -> none  [body(): cand_innov_t = widened[1].T]
    reshape x0 -> x2, local copies, waits for them, and re-layouts: none -> 1.36 us  [the longest x1 0.76 us: body(): own_code.reshape(-1)]
    unnamed x23 -> x39, local copies, waits for them, and re-layouts: 4.37 us -> 3.57 us
  transfers between devices with their start and end apart: 4 -> 4, of which waited for: 3 -> 3; matrix products, arithmetic and copies ran while one was open for 8% -> 14% of each run, Pallas kernels for 0% -> 8%
where the time goes in v3:
time: 122 us; the launch traced here: 121 us
  local copies, waits for them, and re-layouts  23.5 us (19%)
  blocking collectives  20 us (16%)
  Pallas kernels  17.8 us (15%)
  other arithmetic  16 us (13%)
  waiting for transfers between devices  15 us (12%)
  matrix products  14.8 us (12%)
  starting transfers between devices  13.5 us (11%)
    all_to_all x1, blocking collectives, body(): lax.all_to_all(result.reshape(members, band_rows, patch_meridian_lines),...  20 us
    pallas_call x2, Pallas kernels, update_call(): pl.pallas_call(kernel, grid_spec=grid_spec, out_shape=jax.ShapeDtypeStruc...  17.8 us
    dot_general x16, matrix products, observe_one_block(): picked = jnp.dot(state, selector, preferred_element_type=jnp.float32)  14.8 us
    all_to_all x1, waiting for transfers between devices, body(): lax.all_to_all(prediction_increment, 'wide', split_axis=1, concat_axis=0,...  11.2 us
    all_to_all x1, starting transfers between devices, column_halo(): got = lax.all_to_all(spread, axis, 0, 0, tiled=False)  6.32 us
    convert_element_type x1, other arithmetic, body(): prediction_increment = (state_values + 0.2 * member_spread - 0.3 * (east_...  4.6 us
    all_to_all x1, starting transfers between devices, body(): lax.all_to_all(prediction_increment, 'wide', split_axis=1, concat_axis=0,...  3.87 us
    unnamed x39, local copies, waits for them, and re-layouts  3.57 us
  transfers between devices with their start and end apart: 4, of which 3 were waited for; matrix products, arithmetic and copies ran while one was open for 14% of the time, Pallas kernels for 8%

profile of v3, /device:TPU:0, one launch (start us, length us, event | category | flops | bytes accessed | tf_op | source)
XLA Modules:
  0.0 121.2 jit_solution(8748316491477614212)
XLA Ops:
  0.0 1.5 %fusion.113 = (bf16[32,64,1]{2,1,0:T(8,128)(2,1)S(1)}, bf16[32,64,1]{2,1,0:T(8,128)(2,1)S(1)}) fusion(bf16[32,64,256]{2,1,0:T(8,128)(2,1)} %param.11), kind=kLoop, calls=%fused_computation.130 | loop fusion | bytes 16384 | tf_op jit(solution)/shard_map/slice | solution.py:30
  1.6 0.3 copy.82
  1.8 0.3 copy.81
  2.1 0.7 reshape.200
  2.9 6.3 %all-to-all-start = ((bf16[4,2,2048]{2,1,0:T(2,128)(2,1)}), bf16[4,2,2048]{2,1,0:T(2,128)(2,1)S(1)}, u32[]{:S(2)}, u32[]{:S(2)}) async-start(bf16[4,2,2048]{2,1,0:T(2,128)(2,1)} %reshape.200), calls=%async_computation | async-start | bytes 65536 | tf_op jit(solution)/shard_map/all_to_all | solution.py:32
  9.2 0.7 fusion.114
  9.9 0.6 exponential_multiply_fusion
  10.8 1.8 %fusion.111 = (f32[32,63,256]{2,0,1:T(8,128)S(1)}, f32[32,63,256]{2,0,1:T(8,128)}) fusion(f32[32,64,256]{2,0,1:T(8,128)S(1)} %get-tuple-element.204), kind=kLoop, calls=%fused_computation.128 | loop fusion | bytes 8257536 | tf_op jit(solution)/shard_map/slice | solution.py:79
  12.7 0.8 fusion.109
  13.7 0.6 reshape.187.code_ref
  14.3 0.6 all-to-all-done
  15.0 1.7 %copy.68 = bf16[32,64,1]{2,0,1:T(8,128)(2,1)} copy(bf16[32,64,1]{1,0,2:T(8,128)(2,1)S(1)} %slice.209) | data formatting | bytes 8192 | tf_op jit(solution)/shard_map/slice | solution.py:33
  16.7 1.7 %copy.67 = bf16[32,64,1]{2,0,1:T(8,128)(2,1)} copy(bf16[32,64,1]{1,0,2:T(8,128)(2,1)S(1)} %slice.208) | data formatting | bytes 8192 | tf_op jit(solution)/shard_map/slice | solution.py:34
  18.3 4.6 %fusion.102 = bf16[32,64,256]{2,0,1:T(8,128)(2,1)} fusion(f32[32,63,256]{2,0,1:T(8,128)} %get-tuple-element.196, f32[32,63,256]{2,0,1:T(8,128)S(1)} %get-tuple-element.195, bf16[32,64,256]{2,0,1:T(8,128)(2,1)S(1)} %get-tuple-element.203, bf16[32,64,1]{2,0,1:T(8,128)(2,1)} %copy.68, bf16[32,64,1]{2,0,1:T(8,128)(2,1)} %copy.67), kind=kLoop, calls=%fused_computation.78 | loop fusion | flops 10485760 | bytes 6234112 | tf_op jit(solution)/shard_map/convert_element_type | solution.py:84
  22.9 3.9 %all-to-all-start.1 = ((bf16[32,64,256]{2,0,1:T(8,128)(2,1)}), bf16[32,64,256]{2,0,1:T(8,128)(2,1)S(1)}, u32[]{:S(2)}, u32[]{:S(2)}) async-start(bf16[32,64,256]{2,0,1:T(8,128)(2,1)} %fusion.102), calls=%async_computation.1 | async-start | bytes 2097152 | tf_op jit(solution)/shard_map/all_to_all | solution.py:89
  26.8 0.8 subtract_bitcast_fusion
  27.6 0.8 copy.72
  28.4 0.8 reshape.193.code_ref
  29.2 1.7 %concatenate.43.taper_ref = f32[5,128,128]{2,1,0:T(8,128)} pad(f32[4,128,128]{2,1,0:T(8,128)} %fusion.109, f32[]{:T(128)} %constant.79.clone.1), padding=0_1x0_0x0_0 | pad | bytes 589828 | tf_op jit(solution)/shard_map/concatenate | solution.py:166
  31.0 11.2 %all-to-all-done.1 = bf16[32,64,256]{2,0,1:T(8,128)(2,1)S(1)} async-done(((bf16[32,64,256]{2,0,1:T(8,128)(2,1)}), bf16[32,64,256]{2,0,1:T(8,128)(2,1)S(1)}, u32[]{:S(2)}, u32[]{:S(2)}) %all-to-all-start.1) | async-done | bytes 1048608 | tf_op jit(solution)/shard_map/all_to_all | solution.py:89
  42.2 0.6 copy.70
  42.8 0.6 convert_reduce_fusion
  43.5 0.3 copy.83
  43.8 0.5 copy.71
  44.4 6.3 %while.24 = (s32[]{:T(128)}, bf16[2,256,512]{1,2,0:T(8,128)(2,1)S(1)}, f32[2,4,512]{2,1,0:T(4,128)S(1)}, s32[2,4,512]{2,1,0:T(4,128)S(1)}, bf16[256,2048]{1,0:T(...) while((s32[]{:T(128)}, bf16[2,256,512]{1,2,0:T(8,128)(2,1)S(1)}, ...), condition=%wide.region_3.4_spmd.clone.clone, body=%wide.region_2.3_spmd.clone.clone.sunk | while | flops 2156920832 | bytes 7651509 | solution.py:56
  44.4 0.8 fusion.159
  45.2 0.8 fusion.160
  45.9 0.8 fusion.161
  46.7 0.8 fusion.162
  47.5 0.8 fusion.159
  48.3 0.8 fusion.160
  49.1 0.8 fusion.161
  49.8 0.8 fusion.162
  50.6 1.0 copy-done.2
  51.6 0.2 convert_reduce_fusion.2
  51.9 8.9 %while.25 = (s32[]{:T(128)}, bf16[2,256,512]{1,2,0:T(8,128)(2,1)S(1)}, f32[2,4,512]{2,1,0:T(4,128)S(1)}, s32[2,4,512]{2,1,0:T(4,128)S(1)}, bf16[256,2048]{1,0:T(...) while((s32[]{:T(128)}, bf16[2,256,512]{1,2,0:T(8,128)(2,1)S(1)}, ...), condition=%wide.region_6.7_spmd.clone.clone, body=%wide.region_5.6_spmd.clone.clone.sunk | while | flops 2156920832 | bytes 11845841 | solution.py:56
  52.0 2.1 %fusion.171 = f32[512,256]{1,0:T(8,128)S(1)} fusion(bf16[256,2048]{1,0:T(8,128)(2,1)} %get-tuple-element.369, s32[512]{0:T(512)S(1)} %bitcast.206, f32[512]{0:T(512)S(1)} %bitcast.210), kind=kOutput, calls=%fused_computation.52.clone.1 | convolution fusion | flops 539099136 | bytes 1576960 | tf_op jit(solution)/shard_map/while/body/eval_jaxpr/dot_general | solution.py:52
  54.1 0.8 fusion.172
  54.9 0.8 fusion.173
  55.6 0.8 fusion.174
  56.5 2.1 %fusion.171 = f32[512,256]{1,0:T(8,128)S(1)} fusion(bf16[256,2048]{1,0:T(8,128)(2,1)} %get-tuple-element.369, s32[512]{0:T(512)S(1)} %bitcast.206, f32[512]{0:T(512)S(1)} %bitcast.210), kind=kOutput, calls=%fused_computation.52.clone.1 | convolution fusion | flops 539099136 | bytes 1576960 | tf_op jit(solution)/shard_map/while/body/eval_jaxpr/dot_general | solution.py:52
  58.6 0.8 fusion.172
  59.3 0.8 fusion.173
  60.1 0.8 fusion.174
  60.9 1.1 convert_element_type.114
  62.0 0.2 convert_reduce_fusion.1
  62.5 1.0 fusion.106
  63.5 3.3 %collective-permute-start.1 = (bf16[2,256,512]{1,2,0:T(8,128)(2,1)}, bf16[2,256,512]{1,2,0:T(8,128)(2,1)}, u32[]{:S(2)}, u32[]{:S(2)}) collective-permute-start(bf16[2,256,512]{1,2,0:T(8,128)(2,1)} %get-tuple-element.198), channel_id=1, source_target_pairs={{1,0},{2,1},{3,2},{0,3},{5,4},{6,5},{7,6},{4,7},{9,8},{10,9},{11,1... | collective-permute-start | bytes 1572872 | tf_op jit(solution)/shard_map/ppermute | solution.py:110
  66.8 1.3 %copy.79 = f32[256,1024]{1,0:T(8,128)} copy(f32[256,1024]{0,1:T(8,128)S(1)} %bitcast.174) | data formatting | bytes 2097152 | tf_op jit(solution)/shard_map/convert_element_type | solution.py:61
  68.1 1.3 %subtract_convert_fusion.2 = bf16[256,1024]{1,0:T(8,128)(2,1)S(1)} fusion(f32[256,1024]{1,0:T(8,128)} %copy.79, f32[1024]{0:T(1024)S(1)} %bitcast.212), kind=kLoop, calls=%fused_computation.92 | loop fusion | flops 524288 | bytes 1576960 | tf_op jit(solution)/shard_map/convert_element_type | solution.py:62
  69.4 0.8 fusion.115
  70.2 0.3 copy.80
  70.6 1.3 %fusion.104.st_ref = bf16[2048,256]{1,0:T(8,128)(2,1)} fusion(bf16[256,2048]{0,1:T(8,128)(2,1)S(1)} %copy.71, f32[2048]{0:T(1024)S(1)} %bitcast.213), kind=kLoop, calls=%fused_computation.82 | loop fusion | flops 1572864 | bytes 2105344 | tf_op jit(solution)/shard_map/transpose | solution.py:123
  72.0 1.1 pad_maximum_fusion.2.o_ref
  73.2 10.3 %shard_map.73.rest_0_ = f32[2048,256]{1,0:T(8,128)} custom-call(s32[256]{0:T(256)} %reshape.193.code_ref, bf16[2048,256]{1,0:T(8,128)(2,1)} %fusion.104.st_ref, bf16[256,2048]{1,0:T(8,128)(2,1)} %pad_maximum_fusion.2.o_ref, bf16[2048,256]{1,0:T(8,128)(2,1)} %bitcast.184, f32[5,128,128]{2,1,0:T(8,128)} %concatenate.43.taper_ref), custom_call_target="tpu_custom_call" | custom-call | flops 4294967296 | bytes 4194304 | tf_op jit(solution)/shard_map/pallas_call | solution.py:220
  83.4 1.1 slice_bitcast_fusion
  84.5 3.3 %collective-permute-done = bf16[2,256,512]{1,2,0:T(8,128)(2,1)} collective-permute-done((bf16[2,256,512]{1,2,0:T(8,128)(2,1)}, bf16[2,256,512]{1,2,0:T(8,128)(2,1)}, u32[]{:S(2)}, u32[]{:S(2)}) %collective-permute-start) | collective-permute-done | bytes 524320 | tf_op jit(solution)/shard_map/ppermute | solution.py:109
  87.7 1.1 slice_bitcast_fusion.1
  88.8 0.9 pad_maximum_fusion.4
  89.7 1.0 copy.76.o_ref
  90.7 7.6 %shard_map.74 = bf16[2048,256]{1,0:T(8,128)(2,1)} custom-call(s32[128]{0:T(128)} %reshape.187.code_ref, bf16[2048,256]{1,0:T(8,128)(2,1)} %fusion.104.st_ref, bf16[256,1024]{1,0:T(8,128)(2,1)} %copy.76.o_ref, bf16[1024,256]{1,0:T(8,128)(2,1)} %get-tuple-element.220.it_ref, f32[5,128,128]{2,1,0:T(8,128)} %concatenate.43.taper_ref, ...), custom_call_target="tpu_custom_call" | custom-call | flops 2147483648 | bytes 4194304 | tf_op jit(solution)/shard_map/pallas_call | solution.py:220
  98.3 1.9 %copy.77 = bf16[256,8,256]{2,1,0:T(8,128)(2,1)S(1)} copy(bf16[256,8,256]{0,2,1:T(8,128)(2,1)} %bitcast.185) | data formatting | bytes 2097152 | tf_op jit(solution)/shard_map/reshape | solution.py:142
  100.1 20.0 %all_to_all.38 = bf16[256,8,256]{2,1,0:T(8,128)(2,1)S(1)} all-to-all(bf16[256,8,256]{2,1,0:T(8,128)(2,1)S(1)} %copy.77), channel_id=1, replica_groups=mesh['wide'=8,'lon'=4] {'wide'}, dimensions={0} | all-to-all | bytes 2097152 | tf_op jit(solution)/shard_map/all_to_all | solution.py:141
  120.1 1.1 copy.93
  (74 shorter events, 1.4 us)
Async XLA Ops:
  0.0 12.7 %copy-start = (f32[4,64,256]{2,1,0:T(8,128)S(1)}, f32[4,64,256]{2,1,0:T(8,128)}, u32[]{:S(2)}) copy-start(f32[4,64,256]{2,1,0:T(8,128)} %param.14) | copy-start | bytes 786436
  0.0 9.2 %copy-start.5 = (bf16[32,64,256]{2,1,0:T(8,128)(2,1)S(1)}, bf16[32,64,256]{2,1,0:T(8,128)(2,1)}, u32[]{:S(2)}) copy-start(bf16[32,64,256]{2,1,0:T(8,128)(2,1)} %param.11) | copy-start | bytes 3145732
  2.9 12.0 %all-to-all-start = ((bf16[4,2,2048]{2,1,0:T(2,128)(2,1)}), bf16[4,2,2048]{2,1,0:T(2,128)(2,1)S(1)}, u32[]{:S(2)}, u32[]{:S(2)}) async-start(bf16[4,2,2048]{2,1,0:T(2,128)(2,1)} %reshape.200), calls=%async_computation | async-start | bytes 65536 | tf_op jit(solution)/shard_map/all_to_all | solution.py:32
  9.2 1.3 %copy-start.11 = (s32[1,16,16]{2,1,0:T(8,128)S(1)}, s32[1,16,16]{2,1,0:T(8,128)}, u32[]{:S(2)}) copy-start(s32[1,16,16]{2,1,0:T(8,128)} %param.17) | copy-start | bytes 3076
  9.2 1.3 %copy-start.13 = (s32[1,16]{1,0:T(1,128)S(1)}, s32[1,16]{1,0:T(1,128)}, u32[]{:S(2)}) copy-start(s32[1,16]{1,0:T(1,128)} %param.16) | copy-start | bytes 196
  9.2 1.4 %copy-start.10 = (s32[1,16,16]{2,1,0:T(8,128)S(1)}, s32[1,16,16]{2,1,0:T(8,128)}, u32[]{:S(2)}) copy-start(s32[1,16,16]{2,1,0:T(8,128)} %param.15) | copy-start | bytes 3076
  10.8 1.9 %copy-start.12 = (f32[4]{0:T(128)S(1)}, f32[4]{0:T(128)}, u32[]{:S(2)}) copy-start(f32[4]{0:T(128)} %exponential_multiply_fusion) | copy-start | bytes 52
  22.9 4.7 %copy-start.7 = (bf16[256,8,256]{2,1,0:T(8,128)(2,1)S(1)}, bf16[256,8,256]{2,1,0:T(8,128)(2,1)}, u32[]{:S(2)}) copy-start(bf16[256,8,256]{2,1,0:T(8,128)(2,1)} %param.12) | copy-start | bytes 3145732
  22.9 19.3 %all-to-all-start.1 = ((bf16[32,64,256]{2,0,1:T(8,128)(2,1)}), bf16[32,64,256]{2,0,1:T(8,128)(2,1)S(1)}, u32[]{:S(2)}, u32[]{:S(2)}) async-start(bf16[32,64,256]{2,0,1:T(8,128)(2,1)} %fusion.102), calls=%async_computation.1 | async-start | bytes 2097152 | tf_op jit(solution)/shard_map/all_to_all | solution.py:89
  28.4 14.4 %copy-start.6 = (bf16[256,8,256]{0,2,1:T(8,128)(2,1)}, bf16[256,8,256]{0,2,1:T(8,128)(2,1)S(1)}, u32[]{:S(2)}) copy-start(bf16[256,8,256]{0,2,1:T(8,128)(2,1)S(1)} %copy.72) | copy-start | bytes 3145732
  44.3 26.3 %copy-start.1 = (bf16[256,2048]{0,1:T(8,128)(2,1)}, bf16[256,2048]{0,1:T(8,128)(2,1)S(1)}, u32[]{:S(2)}) copy-start(bf16[256,2048]{0,1:T(8,128)(2,1)S(1)} %copy.71) | copy-start | bytes 3145732
  50.6 1.0 copy-start.2
  52.0 2.1 %copy-start.3 = (bf16[256,2048]{1,0:T(8,128)(2,1)S(1)}, bf16[256,2048]{1,0:T(8,128)(2,1)}, u32[]{:S(2)}) copy-start(bf16[256,2048]{1,0:T(8,128)(2,1)} %get-tuple-element.369) | copy-start | bytes 3145732 | tf_op jit(solution)/shard_map/while
  56.5 2.1 %copy-start.3 = (bf16[256,2048]{1,0:T(8,128)(2,1)S(1)}, bf16[256,2048]{1,0:T(8,128)(2,1)}, u32[]{:S(2)}) copy-start(bf16[256,2048]{1,0:T(8,128)(2,1)} %get-tuple-element.369) | copy-start | bytes 3145732 | tf_op jit(solution)/shard_map/while
  63.5 19.9 %collective-permute-start.1 = (bf16[2,256,512]{1,2,0:T(8,128)(2,1)}, bf16[2,256,512]{1,2,0:T(8,128)(2,1)}, u32[]{:S(2)}, u32[]{:S(2)}) collective-permute-start(bf16[2,256,512]{1,2,0:T(8,128)(2,1)} %get-tuple-element.198), channel_id=1, source_target_pairs={{1,0},{2,1},{3,2},{0,3},{5,4},{6,5},{7,6},{4,7},{9,8},{10,9},{11,1... | collective-permute-start | bytes 1572872 | tf_op jit(solution)/shard_map/ppermute | solution.py:110
  66.8 21.0 %collective-permute-start = (bf16[2,256,512]{1,2,0:T(8,128)(2,1)}, bf16[2,256,512]{1,2,0:T(8,128)(2,1)}, u32[]{:S(2)}, u32[]{:S(2)}) collective-permute-start(bf16[2,256,512]{1,2,0:T(8,128)(2,1)} %get-tuple-element.197), channel_id=1, source_target_pairs={{0,1},{1,2},{2,3},{3,0},{4,5},{5,6},{6,7},{7,4},{8,9},{9,10},{10,1... | collective-permute-start | bytes 1572872 | tf_op jit(solution)/shard_map/ppermute | solution.py:109
  66.8 3.5 %copy-start.4 = (f32[2,256,512]{1,2,0:T(8,128)S(1)}, f32[2,256,512]{1,2,0:T(8,128)}, u32[]{:S(2)}) copy-start(f32[2,256,512]{1,2,0:T(8,128)} %convert_element_type.114) | copy-start | bytes 3145732
  70.6 1.5 %copy-start.8 = (bf16[256,512]{1,0:T(8,128)(2,1)S(1)}, bf16[256,512]{1,0:T(8,128)(2,1)}, u32[]{:S(2)}) copy-start(bf16[256,512]{1,0:T(8,128)(2,1)} %get-tuple-element.205) | copy-start | bytes 786436
  70.6 1.5 %copy-start.9 = (bf16[256,512]{1,0:T(8,128)(2,1)S(1)}, bf16[256,512]{1,0:T(8,128)(2,1)}, u32[]{:S(2)}) copy-start(bf16[256,512]{1,0:T(8,128)(2,1)} %get-tuple-element.206) | copy-start | bytes 786436

commit v4 on v3

--- a/solution.py
+++ b/solution.py
@@ -38,23 +38,15 @@
 def observe_region(state, index, weight):
     members, cells = state.shape
     count = index.shape[1]
-    width = math.gcd(512, count)
-    nblocks = count // width
-    index_blocks = index.reshape(4, nblocks, width).transpose(1, 0, 2)
-    weight_blocks = weight.reshape(4, nblocks, width).transpose(1, 0, 2)
-    cell_ids = lax.broadcasted_iota(jnp.int32, (cells, width), 0)
-
-    def observe_one_block(pieces):
-        index_here, weight_here = pieces
-        summed = jnp.zeros((members, width), jnp.float32)
-        for k in range(4):
-            selector = (cell_ids == index_here[k][None, :]).astype(jnp.bfloat16)
-            picked = jnp.dot(state, selector, preferred_element_type=jnp.float32)
-            summed = summed + weight_here[k][None, :] * picked
-        return summed.astype(jnp.bfloat16)
-
-    result = lax.map(observe_one_block, (index_blocks, weight_blocks))
-    return result.transpose(1, 0, 2).reshape(members, count)
+    cell_ids = lax.broadcasted_iota(jnp.int32, (cells, count), 0)
+    combined = jnp.zeros((cells, count), jnp.float32)
+    for k in range(4):
+        combined = combined + jnp.where(cell_ids == index[k][None, :], weight[k][None, :], 0.0)
+    high = combined.astype(jnp.bfloat16)
+    low = (combined - high.astype(jnp.float32)).astype(jnp.bfloat16)
+    summed = jnp.dot(state, high, preferred_element_type=jnp.float32)
+    summed = summed + jnp.dot(state, low, preferred_element_type=jnp.float32)
+    return summed.astype(jnp.bfloat16)
 
 
 def anomaly_from_mean(state_values):

time: 122 us -> 125 us (1.025)
  matrix products: 14.8 us -> 19.3 us
  blocking collectives: 20 us -> 17.8 us
    dot_general x16 -> x4, matrix products: 14.8 us -> 19.3 us  [the longest x2 9.67 us: observe_region(): summed = summed + jnp.dot(state, low, preferred_element_type=jnp.float32)]
    all_to_all x1, waiting for transfers between devices: 11.2 us -> 15.2 us  [body(): lax.all_to_all(prediction_increment, 'wide', split_axis=1, concat_axis=0,...]
    ppermute x1, waiting for transfers between devices: 3.25 us -> 0.01 us  [body(): west = lax.ppermute(edges[:, :, halo:], 'lon', up)]
    all_to_all x1, blocking collectives: 20 us -> 17.8 us  [body(): lax.all_to_all(result.reshape(members, band_rows, patch_meridian_lines),...]
    convert_element_type x2 -> x0, local copies, waits for them, and re-layouts: 1.64 us -> none  [anomaly_from_mean(): centred = state_values.astype(jnp.float32)]
    concatenate x1, other arithmetic: 0.01 us -> 1.47 us  [body(): jnp.concatenate([local_weight[:, :halo], local_weight[:, -halo:]], axis=1)]
    convert_element_type x3 -> x2, other arithmetic: 1.59 us -> 0.3 us  [anomaly_from_mean(): (centred - jnp.mean(centred, axis=-2, keepdims=True)).astype(jnp.bfloat16)]
  transfers between devices with their start and end apart: 4 -> 4, of which waited for: 3 -> 1; matrix products, arithmetic and copies ran while one was open for 14% -> 23% of each run, Pallas kernels for 8% -> 8%
where the time goes in v4:
time: 125 us; the launch traced here: 124 us
  local copies, waits for them, and re-layouts  23.5 us (19%)
  matrix products  19.3 us (15%)
  Pallas kernels  17.8 us (14%)
  blocking collectives  17.8 us (14%)
  other arithmetic  16 us (13%)
  waiting for transfers between devices  15.2 us (12%)
  starting transfers between devices  14 us (11%)
    pallas_call x2, Pallas kernels, update_call(): pl.pallas_call(kernel, grid_spec=grid_spec, out_shape=jax.ShapeDtypeStruc...  17.8 us
    all_to_all x1, blocking collectives, body(): lax.all_to_all(result.reshape(members, band_rows, patch_meridian_lines),...  17.8 us
    all_to_all x1, waiting for transfers between devices, body(): lax.all_to_all(prediction_increment, 'wide', split_axis=1, concat_axis=0,...  15.2 us
    dot_general x2, matrix products, observe_region(): summed = summed + jnp.dot(state, low, preferred_element_type=jnp.float32)  9.67 us
    dot_general x2, matrix products, observe_region(): summed = jnp.dot(state, high, preferred_element_type=jnp.float32)  9.65 us
    all_to_all x1, starting transfers between devices, column_halo(): got = lax.all_to_all(spread, axis, 0, 0, tiled=False)  6.32 us
    convert_element_type x1, other arithmetic, body(): prediction_increment = (state_values + 0.2 * member_spread - 0.3 * (east_...  4.6 us
    unnamed x39, local copies, waits for them, and re-layouts  4.24 us
  transfers between devices with their start and end apart: 4, of which 1 were waited for; matrix products, arithmetic and copies ran while one was open for 23% of the time, Pallas kernels for 8%

profile of v4, /device:TPU:0, one launch (start us, length us, event | category | flops | bytes accessed | tf_op | source)
XLA Modules:
  0.0 124.0 jit_solution(7655492727125656358)
XLA Ops:
  0.0 0.0 copy-start
  0.0 1.5 %fusion.50 = (bf16[32,64,1]{2,1,0:T(8,128)(2,1)S(1)}, bf16[32,64,1]{2,1,0:T(8,128)(2,1)S(1)}) fusion(bf16[32,64,256]{2,1,0:T(8,128)(2,1)} %param.7), kind=kLoop, calls=%fused_computation.104 | loop fusion | bytes 16384 | tf_op jit(solution)/shard_map/slice | solution.py:30
  1.6 0.3 copy.92
  1.8 0.3 copy.91
  2.1 0.7 reshape.92
  2.9 6.3 %all-to-all-start = ((bf16[4,2,2048]{2,1,0:T(2,128)(2,1)}), bf16[4,2,2048]{2,1,0:T(2,128)(2,1)S(1)}, u32[]{:S(2)}, u32[]{:S(2)}) async-start(bf16[4,2,2048]{2,1,0:T(2,128)(2,1)} %reshape.92), calls=%async_computation | async-start | bytes 65536 | tf_op jit(solution)/shard_map/all_to_all | solution.py:32
  9.2 0.0 copy-done.2
  9.2 0.0 copy-start.7
  9.2 0.7 fusion.51
  9.9 0.5 exponential_multiply_fusion
  10.4 0.0 copy-done.8
  10.5 0.1 fusion.37
  10.5 0.1 select_reduce_fusion
  10.7 0.7 fusion.57
  11.4 1.8 %fusion.48 = (f32[32,63,256]{2,0,1:T(8,128)S(1)}, f32[32,63,256]{2,0,1:T(8,128)}) fusion(f32[32,64,256]{2,0,1:T(8,128)S(1)} %get-tuple-element.14), kind=kLoop, calls=%fused_computation.102 | loop fusion | bytes 8257536 | tf_op jit(solution)/shard_map/slice | solution.py:71
  13.2 0.6 fusion.56
  13.8 0.8 subtract_bitcast_fusion
  14.6 0.6 fusion.55
  15.2 1.5 %fusion.39 = (f32[1,1024]{1,0:T(1,128)}, f32[1,1024]{1,0:T(1,128)}, f32[1,1024]{1,0:T(1,128)}, f32[1,1024]{1,0:T(1,128)}) fusion(f32[4,512]{1,0:T(4,128)} %get-tuple-element.33, f32[4,512]{1,0:T(4,128)} %get-tuple-element.34), kind=kLoop, calls=%fused_computation.87 | loop fusion | flops 4096 | bytes 32768 | tf_op jit(solution)/shard_map/concatenate | solution.py:94
  16.7 1.4 %fusion.36 = f32[4,128,128]{2,1,0:T(8,128)} fusion(f32[4]{0:T(128)} %exponential_multiply_fusion, f32[128,128]{1,0:T(8,128)S(1)} %iota_subtract_fusion), kind=kLoop, calls=%fused_computation.55 | loop fusion | flops 327680 | bytes 327696 | tf_op jit(solution)/shard_map/div | solution.py:157
  18.1 0.8 pad_add_fusion
  18.9 0.1 slice.206
  18.9 0.6 reshape.86.code_ref
  19.5 2.4 %copy.82 = bf16[256,8,256]{0,2,1:T(8,128)(2,1)} copy(bf16[256,8,256]{2,1,0:T(8,128)(2,1)} %param.8) | data formatting | bytes 2097152 | tf_op args[1]
  22.0 0.7 reshape.90.code_ref
  22.6 1.7 %concatenate.43.taper_ref = f32[5,128,128]{2,1,0:T(8,128)} pad(f32[4,128,128]{2,1,0:T(8,128)} %fusion.36, f32[]{:T(128)} %constant.59.clone.1), padding=0_1x0_0x0_0 | pad | bytes 589828 | tf_op jit(solution)/shard_map/concatenate | solution.py:158
  24.3 0.0 all-to-all-done
  24.3 0.1 reshape.93
  24.5 1.7 %copy.76 = bf16[32,64,1]{2,0,1:T(8,128)(2,1)} copy(bf16[32,64,1]{1,0,2:T(8,128)(2,1)S(1)} %slice.179) | data formatting | bytes 8192 | tf_op jit(solution)/shard_map/slice | solution.py:33
  26.1 1.7 %copy.75 = bf16[32,64,1]{2,0,1:T(8,128)(2,1)} copy(bf16[32,64,1]{1,0,2:T(8,128)(2,1)S(1)} %slice.178) | data formatting | bytes 8192 | tf_op jit(solution)/shard_map/slice | solution.py:34
  27.8 4.6 %fusion.10 = bf16[32,64,256]{2,0,1:T(8,128)(2,1)} fusion(f32[32,63,256]{2,0,1:T(8,128)} %get-tuple-element.6, f32[32,63,256]{2,0,1:T(8,128)S(1)} %get-tuple-element.5, bf16[32,64,256]{2,0,1:T(8,128)(2,1)S(1)} %get-tuple-element.13, bf16[32,64,1]{2,0,1:T(8,128)(2,1)} %copy.76, bf16[32,64,1]{2,0,1:T(8,128)(2,1)} %copy.75), kind=kLoop, calls=%fused_computation.24 | loop fusion | flops 10485760 | bytes 6234112 | tf_op jit(solution)/shard_map/convert_element_type | solution.py:76
  32.4 3.9 %all-to-all-start.1 = ((bf16[32,64,256]{2,0,1:T(8,128)(2,1)}), bf16[32,64,256]{2,0,1:T(8,128)(2,1)S(1)}, u32[]{:S(2)}, u32[]{:S(2)}) async-start(bf16[32,64,256]{2,0,1:T(8,128)(2,1)} %fusion.10), calls=%async_computation.1 | async-start | bytes 2097152 | tf_op jit(solution)/shard_map/all_to_all | solution.py:81
  36.3 0.0 copy-done.3
  36.5 15.2 %all-to-all-done.1 = bf16[32,64,256]{2,0,1:T(8,128)(2,1)S(1)} async-done(((bf16[32,64,256]{2,0,1:T(8,128)(2,1)}), bf16[32,64,256]{2,0,1:T(8,128)(2,1)S(1)}, u32[]{:S(2)}, u32[]{:S(2)}) %all-to-all-start.1) | async-done | bytes 1048608 | tf_op jit(solution)/shard_map/all_to_all | solution.py:81
  51.7 0.6 copy.78
  52.3 0.6 convert_reduce_fusion
  53.0 0.3 copy.93
  53.3 0.5 copy.79
  53.9 5.1 %fusion.2 = f32[256,1024]{0,1:T(8,128)S(1)} fusion(bf16[256,2048]{1,0:T(8,128)(2,1)S(1)} %bitcast.81, f32[1024]{0:T(1024)S(1)} %bitcast.101, s32[1024]{0:T(1024)S(1)} %bitcast.125, f32[1024]{0:T(1024)S(1)} %bitcast.103, s32[1024]{0:T(1024)S(1)} %bitcast.127, f32[1024]{0:T(1024)S(1)} %bitcast.99, s32[1024]{0:T(1024)S(1)} %bitcast.123, ...), kind=kOutput, calls=%fused_computation.14 | convolution fusion | flops 1105199104 | bytes 2129920 | tf_op jit(solution)/shard_map/dot_general | solution.py:48
  59.0 5.1 %convert_reduce_fusion.2 = (f32[1024]{0:T(1024)S(1)}, bf16[256,1024]{0,1:T(8,128)(2,1)S(1)}) fusion(f32[256,1024]{0,1:T(8,128)S(1)} %fusion.2, bf16[256,2048]{1,0:T(8,128)(2,1)S(1)} %bitcast.82, f32[1024]{0:T(1024)S(1)} %bitcast.102, s32[1024]{0:T(1024)S(1)} %bitcast.126, f32[1024]{0:T(1024)S(1)} %bitcast.104, s32[1024]{0:T(1024)S(1)} %bitcast.128, ...), kind=kOutput, calls=%fused_computation.35 | convolution fusion | flops 1099955200 | bytes 2658304 | tf_op jit(solution)/shard_map/dot_general | solution.py:47
  64.1 0.2 fusion.62
  64.3 0.2 fusion.30
  64.5 1.0 fusion.33
  65.6 3.8 %collective-permute-start.1 = (bf16[2,256,512]{1,2,0:T(8,128)(2,1)}, bf16[2,256,512]{1,2,0:T(8,128)(2,1)}, u32[]{:S(2)}, u32[]{:S(2)}) collective-permute-start(bf16[2,256,512]{1,2,0:T(8,128)(2,1)} %get-tuple-element.8), channel_id=1, source_target_pairs={{1,0},{2,1},{3,2},{0,3},{5,4},{6,5},{7,6},{4,7},{9,8},{10,9},{11,1... | collective-permute-start | bytes 1572872 | tf_op jit(solution)/shard_map/ppermute | solution.py:102
  69.4 0.0 collective-permute-start
  69.4 0.1 copy.84
  69.6 4.6 %fusion.3 = f32[256,1024]{1,0:T(8,128)S(1)} fusion(bf16[256,2048]{1,0:T(8,128)(2,1)S(1)} %bitcast.83, f32[1024]{0:T(1024)S(1)} %bitcast.107, s32[1024]{0:T(1024)S(1)} %bitcast.115, f32[1024]{0:T(1024)S(1)} %bitcast.109, s32[1024]{0:T(1024)S(1)} %bitcast.117, f32[1024]{0:T(1024)S(1)} %bitcast.111, s32[1024]{0:T(1024)S(1)} %bitcast.119, ...), kind=kOutput, calls=%fused_computation.15 | convolution fusion | flops 1105199104 | bytes 2129920 | tf_op jit(solution)/shard_map/dot_general | solution.py:48
  74.1 4.6 %convert_reduce_fusion.1 = (f32[1024]{0:T(1024)S(1)}, bf16[256,1024]{1,0:T(8,128)(2,1)}) fusion(f32[256,1024]{1,0:T(8,128)S(1)} %fusion.3, bf16[256,2048]{1,0:T(8,128)(2,1)S(1)} %bitcast.84, f32[1024]{0:T(1024)S(1)} %bitcast.108, s32[1024]{0:T(1024)S(1)} %bitcast.116, f32[1024]{0:T(1024)S(1)} %bitcast.110, s32[1024]{0:T(1024)S(1)} %bitcast.118, ...), kind=kOutput, calls=%fused_computation.33 | convolution fusion | flops 1099955200 | bytes 2658304 | tf_op jit(solution)/shard_map/dot_general | solution.py:47
  78.7 0.1 copy.83
  78.9 0.0 copy-done.1
  78.9 1.3 %fusion.32.st_ref = bf16[2048,256]{1,0:T(8,128)(2,1)} fusion(bf16[256,2048]{0,1:T(8,128)(2,1)S(1)} %copy.79, f32[2048]{0:T(1024)S(1)} %bitcast.95), kind=kLoop, calls=%fused_computation.40 | loop fusion | flops 1572864 | bytes 2105344 | tf_op jit(solution)/shard_map/transpose | solution.py:115
  80.2 0.1 fusion.31
  80.3 1.1 pad_maximum_fusion.2.o_ref
  81.4 10.3 %shard_map.73.rest_0_ = f32[2048,256]{1,0:T(8,128)} custom-call(s32[256]{0:T(256)} %reshape.90.code_ref, bf16[2048,256]{1,0:T(8,128)(2,1)} %fusion.32.st_ref, bf16[256,2048]{1,0:T(8,128)(2,1)} %pad_maximum_fusion.2.o_ref, bf16[2048,256]{1,0:T(8,128)(2,1)} %bitcast.87, f32[5,128,128]{2,1,0:T(8,128)} %concatenate.43.taper_ref), custom_call_target="tpu_custom_call" | custom-call | flops 4294967296 | bytes 4194304 | tf_op jit(solution)/shard_map/pallas_call | solution.py:212
  91.7 0.0 collective-permute-done.1
  91.7 1.1 slice_bitcast_fusion
  92.7 0.0 collective-permute-done
  92.7 1.1 slice_bitcast_fusion.1
  93.8 0.9 pad_maximum_fusion.4
  94.7 1.0 copy.86.o_ref
  95.7 7.6 %shard_map.74 = bf16[2048,256]{1,0:T(8,128)(2,1)} custom-call(s32[128]{0:T(128)} %reshape.86.code_ref, bf16[2048,256]{1,0:T(8,128)(2,1)} %fusion.32.st_ref, bf16[256,1024]{1,0:T(8,128)(2,1)} %copy.86.o_ref, bf16[1024,256]{1,0:T(8,128)(2,1)} %get-tuple-element.50.it_ref, f32[5,128,128]{2,1,0:T(8,128)} %concatenate.43.taper_ref, ...), custom_call_target="tpu_custom_call" | custom-call | flops 2147483648 | bytes 4194304 | tf_op jit(solution)/shard_map/pallas_call | solution.py:212
  103.3 1.9 %copy.87 = bf16[256,8,256]{2,1,0:T(8,128)(2,1)S(1)} copy(bf16[256,8,256]{0,2,1:T(8,128)(2,1)} %bitcast.89) | data formatting | bytes 2097152 | tf_op jit(solution)/shard_map/reshape | solution.py:134
  105.1 17.8 %all_to_all.38 = bf16[256,8,256]{2,1,0:T(8,128)(2,1)S(1)} all-to-all(bf16[256,8,256]{2,1,0:T(8,128)(2,1)S(1)} %copy.87), channel_id=1, replica_groups=mesh['wide'=8,'lon'=4] {'wide'}, dimensions={0} | all-to-all | bytes 2097152 | tf_op jit(solution)/shard_map/all_to_all | solution.py:133
  122.9 1.1 copy.101
  (42 shorter events, 0.3 us)
Async XLA Ops:
  0.0 13.2 %copy-start = (f32[4,64,256]{2,1,0:T(8,128)S(1)}, f32[4,64,256]{2,1,0:T(8,128)}, u32[]{:S(2)}) copy-start(f32[4,64,256]{2,1,0:T(8,128)} %param.10) | copy-start | bytes 786436
  0.0 9.2 %copy-start.2 = (bf16[32,64,256]{2,1,0:T(8,128)(2,1)S(1)}, bf16[32,64,256]{2,1,0:T(8,128)(2,1)}, u32[]{:S(2)}) copy-start(bf16[32,64,256]{2,1,0:T(8,128)(2,1)} %param.7) | copy-start | bytes 3145732
  2.9 21.5 %all-to-all-start = ((bf16[4,2,2048]{2,1,0:T(2,128)(2,1)}), bf16[4,2,2048]{2,1,0:T(2,128)(2,1)S(1)}, u32[]{:S(2)}, u32[]{:S(2)}) async-start(bf16[4,2,2048]{2,1,0:T(2,128)(2,1)} %reshape.92), calls=%async_computation | async-start | bytes 65536 | tf_op jit(solution)/shard_map/all_to_all | solution.py:32
  9.2 1.2 %copy-start.8 = (s32[1,16,16]{2,1,0:T(8,128)S(1)}, s32[1,16,16]{2,1,0:T(8,128)}, u32[]{:S(2)}) copy-start(s32[1,16,16]{2,1,0:T(8,128)} %param.13) | copy-start | bytes 3076
  9.2 1.2 %copy-start.13 = (s32[1,16]{1,0:T(1,128)S(1)}, s32[1,16]{1,0:T(1,128)}, u32[]{:S(2)}) copy-start(s32[1,16]{1,0:T(1,128)} %param.12) | copy-start | bytes 196
  9.2 1.3 %copy-start.7 = (s32[1,16,16]{2,1,0:T(8,128)S(1)}, s32[1,16,16]{2,1,0:T(8,128)}, u32[]{:S(2)}) copy-start(s32[1,16,16]{2,1,0:T(8,128)} %param.11) | copy-start | bytes 3076
  32.4 3.9 %copy-start.5 = (s32[4,512]{1,0:T(4,128)S(1)}, s32[4,512]{1,0:T(4,128)}, u32[]{:S(2)}) copy-start(s32[4,512]{1,0:T(4,128)} %get-tuple-element.31) | copy-start | bytes 24580
  32.4 3.9 %copy-start.6 = (s32[4,512]{1,0:T(4,128)S(1)}, s32[4,512]{1,0:T(4,128)}, u32[]{:S(2)}) copy-start(s32[4,512]{1,0:T(4,128)} %get-tuple-element.32) | copy-start | bytes 24580
  32.4 3.9 %copy-start.3 = (bf16[256,8,256]{0,2,1:T(8,128)(2,1)S(1)}, bf16[256,8,256]{0,2,1:T(8,128)(2,1)}, u32[]{:S(2)}) copy-start(bf16[256,8,256]{0,2,1:T(8,128)(2,1)} %copy.82) | copy-start | bytes 3145732
  32.4 19.3 %all-to-all-start.1 = ((bf16[32,64,256]{2,0,1:T(8,128)(2,1)}), bf16[32,64,256]{2,0,1:T(8,128)(2,1)S(1)}, u32[]{:S(2)}, u32[]{:S(2)}) async-start(bf16[32,64,256]{2,0,1:T(8,128)(2,1)} %fusion.10), calls=%async_computation.1 | async-start | bytes 2097152 | tf_op jit(solution)/shard_map/all_to_all | solution.py:81
  52.9 0.9 copy-start.9
  52.9 0.9 copy-start.10
  52.9 0.9 copy-start.11
  53.0 0.9 copy-start.12
  53.8 25.1 %copy-start.1 = (bf16[256,2048]{0,1:T(8,128)(2,1)}, bf16[256,2048]{0,1:T(8,128)(2,1)S(1)}, u32[]{:S(2)}) copy-start(bf16[256,2048]{0,1:T(8,128)(2,1)S(1)} %copy.79) | copy-start | bytes 3145732
  65.6 26.1 %collective-permute-start.1 = (bf16[2,256,512]{1,2,0:T(8,128)(2,1)}, bf16[2,256,512]{1,2,0:T(8,128)(2,1)}, u32[]{:S(2)}, u32[]{:S(2)}) collective-permute-start(bf16[2,256,512]{1,2,0:T(8,128)(2,1)} %get-tuple-element.8), channel_id=1, source_target_pairs={{1,0},{2,1},{3,2},{0,3},{5,4},{6,5},{7,6},{4,7},{9,8},{10,9},{11,1... | collective-permute-start | bytes 1572872 | tf_op jit(solution)/shard_map/ppermute | solution.py:102
  69.4 23.4 %collective-permute-start = (bf16[2,256,512]{1,2,0:T(8,128)(2,1)}, bf16[2,256,512]{1,2,0:T(8,128)(2,1)}, u32[]{:S(2)}, u32[]{:S(2)}) collective-permute-start(bf16[2,256,512]{1,2,0:T(8,128)(2,1)} %get-tuple-element.7), channel_id=1, source_target_pairs={{0,1},{1,2},{2,3},{3,0},{4,5},{5,6},{6,7},{7,4},{8,9},{9,10},{10,1... | collective-permute-start | bytes 1572872 | tf_op jit(solution)/shard_map/ppermute | solution.py:101
  78.7 1.5 %copy-start.4 = (bf16[256,1024]{1,0:T(8,128)(2,1)S(1)}, bf16[256,1024]{1,0:T(8,128)(2,1)}, u32[]{:S(2)}) copy-start(bf16[256,1024]{1,0:T(8,128)(2,1)} %get-tuple-element.48) | copy-start | bytes 1572868

commit v5 on v4

--- a/solution.py
+++ b/solution.py
@@ -39,13 +39,11 @@
     members, cells = state.shape
     count = index.shape[1]
     cell_ids = lax.broadcasted_iota(jnp.int32, (cells, count), 0)
-    combined = jnp.zeros((cells, count), jnp.float32)
+    summed = jnp.zeros((members, count), jnp.float32)
     for k in range(4):
-        combined = combined + jnp.where(cell_ids == index[k][None, :], weight[k][None, :], 0.0)
-    high = combined.astype(jnp.bfloat16)
-    low = (combined - high.astype(jnp.float32)).astype(jnp.bfloat16)
-    summed = jnp.dot(state, high, preferred_element_type=jnp.float32)
-    summed = summed + jnp.dot(state, low, preferred_element_type=jnp.float32)
+        selector = (cell_ids == index[k][None, :]).astype(jnp.bfloat16)
+        picked = jnp.dot(state, selector, preferred_element_type=jnp.float32)
+        summed = summed + weight[k][None, :] * picked
     return summed.astype(jnp.bfloat16)
 
 

time: 125 us -> 129 us (1.032)
  waiting for transfers between devices: 15.2 us -> 22.6 us
  local copies, waits for them, and re-layouts: 23.5 us -> 20.4 us
  blocking collectives: 17.8 us -> 20 us
  matrix products: 19.3 us -> 18 us
    ppermute x1, waiting for transfers between devices: 0.01 us -> 7.15 us  [body(): east = lax.ppermute(edges[:, :, :halo], 'lon', down)]
    all_to_all x1, blocking collectives: 17.8 us -> 20 us  [body(): lax.all_to_all(result.reshape(members, band_rows, patch_meridian_lines),...]
    squeeze x2, local copies, waits for them, and re-layouts: 2.13 us -> 0.07 us  [body(): halo_innov = jnp.concatenate([west[1], east[1]], axis=1)]
    ppermute x1, starting transfers between devices: 0.01 us -> 2.03 us  [body(): west = lax.ppermute(edges[:, :, halo:], 'lon', up)]
    ppermute x1, starting transfers between devices: 3.82 us -> 1.8 us  [body(): east = lax.ppermute(edges[:, :, :halo], 'lon', down)]
    concatenate x1, other arithmetic: 1.47 us -> 0.02 us  [body(): jnp.concatenate([local_weight[:, :halo], local_weight[:, -halo:]], axis=1)]
    dot_general x4 -> x8, matrix products: 19.3 us -> 18 us  [observe_region(): picked = jnp.dot(state, selector, preferred_element_type=jnp.float32)]
    unnamed x39 -> x33, local copies, waits for them, and re-layouts: 4.24 us -> 4.22 us
  transfers between devices with their start and end apart: 4 -> 4, of which waited for: 1 -> 3; matrix products, arithmetic and copies ran while one was open for 23% -> 12% of each run, Pallas kernels for 8% -> 8%
where the time goes in v5:
time: 129 us
  waiting for transfers between devices  22.6 us (18%)
  local copies, waits for them, and re-layouts  20.4 us (16%)
  blocking collectives  20 us (16%)
  matrix products  18 us (14%)
  Pallas kernels  17.9 us (14%)
  other arithmetic  15.3 us (12%)
  starting transfers between devices  14 us (11%)
    all_to_all x1, blocking collectives, body(): lax.all_to_all(result.reshape(members, band_rows, patch_meridian_lines),...  20 us
    dot_general x8, matrix products, observe_region(): picked = jnp.dot(state, selector, preferred_element_type=jnp.float32)  18 us
    pallas_call x2, Pallas kernels, update_call(): pl.pallas_call(kernel, grid_spec=grid_spec, out_shape=jax.ShapeDtypeStruc...  17.9 us
    all_to_all x1, waiting for transfers between devices, body(): lax.all_to_all(prediction_increment, 'wide', split_axis=1, concat_axis=0,...  15.2 us
    ppermute x1, waiting for transfers between devices, body(): east = lax.ppermute(edges[:, :, :halo], 'lon', down)  7.15 us
    all_to_all x1, starting transfers between devices, column_halo(): got = lax.all_to_all(spread, axis, 0, 0, tiled=False)  6.32 us
    convert_element_type x1, other arithmetic, body(): prediction_increment = (state_values + 0.2 * member_spread - 0.3 * (east_...  4.6 us
    unnamed x33, local copies, waits for them, and re-layouts  4.22 us
  transfers between devices with their start and end apart: 4, of which 3 were waited for; matrix products, arithmetic and copies ran while one was open for 12% of the time, Pallas kernels for 8%

profile of v5, /device:TPU:0, one launch (start us, length us, event | category | flops | bytes accessed | tf_op | source)
XLA Modules:
  0.0 128.6 jit_solution(17203691400118383046)
XLA Ops:
  0.0 1.5 %fusion.56 = (bf16[32,64,1]{2,1,0:T(8,128)(2,1)S(1)}, bf16[32,64,1]{2,1,0:T(8,128)(2,1)S(1)}) fusion(bf16[32,64,256]{2,1,0:T(8,128)(2,1)} %param.7), kind=kLoop, calls=%fused_computation.118 | loop fusion | bytes 16384 | tf_op jit(solution)/shard_map/slice | solution.py:30
  1.6 0.3 copy.105
  1.8 0.3 copy.106
  2.1 0.7 reshape.92
  2.9 6.3 %all-to-all-start = ((bf16[4,2,2048]{2,1,0:T(2,128)(2,1)}), bf16[4,2,2048]{2,1,0:T(2,128)(2,1)S(1)}, u32[]{:S(2)}, u32[]{:S(2)}) async-start(bf16[4,2,2048]{2,1,0:T(2,128)(2,1)} %reshape.92), calls=%async_computation | async-start | bytes 65536 | tf_op jit(solution)/shard_map/all_to_all | solution.py:32
  9.2 0.0 copy-done.2
  9.2 0.7 fusion.57
  9.9 0.6 exponential_multiply_fusion
  10.5 1.8 %fusion.54 = (f32[32,63,256]{2,0,1:T(8,128)S(1)}, f32[32,63,256]{2,0,1:T(8,128)}) fusion(f32[32,64,256]{2,0,1:T(8,128)S(1)} %get-tuple-element.14), kind=kLoop, calls=%fused_computation.116 | loop fusion | bytes 8257536 | tf_op jit(solution)/shard_map/slice | solution.py:69
  12.3 0.8 subtract_bitcast_fusion
  13.2 0.6 fusion.61
  13.8 0.8 fusion.47
  14.6 0.1 select_reduce_fusion
  14.7 0.1 fusion.63
  14.8 0.6 fusion.49
  15.4 1.5 %fusion.46 = f32[4,128,128]{2,1,0:T(8,128)} fusion(f32[4]{0:T(128)} %exponential_multiply_fusion, f32[128,128]{1,0:T(8,128)S(1)} %iota_subtract_fusion), kind=kLoop, calls=%fused_computation.73 | loop fusion | flops 327680 | bytes 327696 | tf_op jit(solution)/shard_map/div | solution.py:155
  16.9 0.1 pad_add_fusion
  17.0 0.1 slice.206
  17.1 2.4 %copy.94 = bf16[256,8,256]{0,2,1:T(8,128)(2,1)} copy(bf16[256,8,256]{2,1,0:T(8,128)(2,1)} %param.8) | data formatting | bytes 2097152 | tf_op args[1]
  19.5 0.6 reshape.90.code_ref
  20.1 0.7 reshape.86.code_ref
  20.8 1.7 %concatenate.43.taper_ref = f32[5,128,128]{2,1,0:T(8,128)} pad(f32[4,128,128]{2,1,0:T(8,128)} %fusion.46, f32[]{:T(128)} %constant.59.clone.1), padding=0_1x0_0x0_0 | pad | bytes 589828 | tf_op jit(solution)/shard_map/concatenate | solution.py:156
  22.4 0.0 all-to-all-done
  22.5 0.1 reshape.93
  22.6 1.7 %copy.85 = bf16[32,64,1]{2,0,1:T(8,128)(2,1)} copy(bf16[32,64,1]{1,0,2:T(8,128)(2,1)S(1)} %slice.178) | data formatting | bytes 8192 | tf_op jit(solution)/shard_map/slice | solution.py:34
  24.3 1.7 %copy.86 = bf16[32,64,1]{2,0,1:T(8,128)(2,1)} copy(bf16[32,64,1]{1,0,2:T(8,128)(2,1)S(1)} %slice.179) | data formatting | bytes 8192 | tf_op jit(solution)/shard_map/slice | solution.py:33
  25.9 4.6 %fusion.22 = bf16[32,64,256]{2,0,1:T(8,128)(2,1)} fusion(f32[32,63,256]{2,0,1:T(8,128)} %get-tuple-element.6, f32[32,63,256]{2,0,1:T(8,128)S(1)} %get-tuple-element.5, bf16[32,64,256]{2,0,1:T(8,128)(2,1)S(1)} %get-tuple-element.13, bf16[32,64,1]{2,0,1:T(8,128)(2,1)} %copy.86, bf16[32,64,1]{2,0,1:T(8,128)(2,1)} %copy.85), kind=kLoop, calls=%fused_computation.32 | loop fusion | flops 10485760 | bytes 6234112 | tf_op jit(solution)/shard_map/convert_element_type | solution.py:74
  30.5 3.9 %all-to-all-start.1 = ((bf16[32,64,256]{2,0,1:T(8,128)(2,1)}), bf16[32,64,256]{2,0,1:T(8,128)(2,1)S(1)}, u32[]{:S(2)}, u32[]{:S(2)}) async-start(bf16[32,64,256]{2,0,1:T(8,128)(2,1)} %fusion.22), calls=%async_computation.1 | async-start | bytes 2097152 | tf_op jit(solution)/shard_map/all_to_all | solution.py:79
  34.4 0.0 copy-done.3
  34.6 15.2 %all-to-all-done.1 = bf16[32,64,256]{2,0,1:T(8,128)(2,1)S(1)} async-done(((bf16[32,64,256]{2,0,1:T(8,128)(2,1)}), bf16[32,64,256]{2,0,1:T(8,128)(2,1)S(1)}, u32[]{:S(2)}, u32[]{:S(2)}) %all-to-all-start.1) | async-done | bytes 1048608 | tf_op jit(solution)/shard_map/all_to_all | solution.py:79
  49.8 0.6 copy.88
  50.4 0.6 convert_reduce_fusion
  51.0 0.0 copy-start.10
  51.1 0.3 copy.107
  51.4 0.7 copy.89
  52.1 2.4 %fusion.28 = f32[256,1024]{0,1:T(8,128)S(1)} fusion(bf16[256,2048]{1,0:T(8,128)(2,1)S(1)} %bitcast.85, s32[1024]{0:T(1024)S(1)} %bitcast.108, f32[1024]{0:T(1024)S(1)} %bitcast.120), kind=kOutput, calls=%fused_computation.40 | convolution fusion | flops 1076101120 | bytes 2105344 | tf_op jit(solution)/shard_map/dot_general | solution.py:45
  54.5 2.4 %fusion.29 = f32[256,1024]{0,1:T(8,128)S(1)} fusion(bf16[256,2048]{1,0:T(8,128)(2,1)S(1)} %bitcast.86, s32[1024]{0:T(1024)S(1)} %bitcast.107, f32[1024]{0:T(1024)S(1)} %bitcast.119), kind=kOutput, calls=%fused_computation.41 | convolution fusion | flops 1076101120 | bytes 2105344 | tf_op jit(solution)/shard_map/dot_general | solution.py:45
  56.9 2.4 %fusion.30 = f32[256,1024]{0,1:T(8,128)S(1)} fusion(bf16[256,2048]{1,0:T(8,128)(2,1)S(1)} %bitcast.87, s32[1024]{0:T(1024)S(1)} %bitcast.106, f32[1024]{0:T(1024)S(1)} %bitcast.118), kind=kOutput, calls=%fused_computation.42 | convolution fusion | flops 1076101120 | bytes 2105344 | tf_op jit(solution)/shard_map/dot_general | solution.py:45
  59.3 0.0 copy-done.7
  59.3 2.6 %convert_reduce_fusion.2 = (f32[1024]{0:T(1024)S(1)}, bf16[256,1024]{0,1:T(8,128)(2,1)S(1)}) fusion(f32[256,1024]{0,1:T(8,128)S(1)} %fusion.28, f32[256,1024]{0,1:T(8,128)S(1)} %fusion.29, f32[256,1024]{0,1:T(8,128)S(1)} %fusion.30, bf16[256,2048]{1,0:T(8,128)(2,1)S(1)} %bitcast.88, s32[1024]{0:T(1024)S(1)} %bitcast.105, f32[1024]{0:T(1024)S(1)} %bitcast.115), kind=kOutput, calls=%fused_computation.47 | convolution fusion | flops 1077672960 | bytes 4730880 | tf_op jit(solution)/shard_map/dot_general | solution.py:45
  61.9 0.2 fusion.40
  62.1 0.2 fusion.72
  62.4 1.8 %fusion.24 = f32[256,1024]{1,0:T(8,128)S(1)} fusion(bf16[256,2048]{1,0:T(8,128)(2,1)S(1)} %bitcast.89, s32[1024]{0:T(1024)S(1)} %bitcast.113, f32[1024]{0:T(1024)S(1)} %bitcast.117), kind=kOutput, calls=%fused_computation.36 | convolution fusion | flops 1076101120 | bytes 2105344 | tf_op jit(solution)/shard_map/dot_general | solution.py:45
  64.1 2.0 %fusion.25 = f32[256,1024]{1,0:T(8,128)S(1)} fusion(bf16[256,2048]{1,0:T(8,128)(2,1)S(1)} %bitcast.90, s32[1024]{0:T(1024)S(1)} %bitcast.112, f32[1024]{0:T(1024)S(1)} %bitcast.116), kind=kOutput, calls=%fused_computation.37 | convolution fusion | flops 1076101120 | bytes 2105344 | tf_op jit(solution)/shard_map/dot_general | solution.py:45
  66.2 1.8 %fusion.26 = f32[256,1024]{1,0:T(8,128)S(1)} fusion(bf16[256,2048]{1,0:T(8,128)(2,1)S(1)} %bitcast.91, s32[1024]{0:T(1024)S(1)} %bitcast.110, f32[1024]{0:T(1024)S(1)} %bitcast.114), kind=kOutput, calls=%fused_computation.38 | convolution fusion | flops 1076101120 | bytes 2105344 | tf_op jit(solution)/shard_map/dot_general | solution.py:45
  67.9 2.7 %convert_reduce_fusion.1 = (f32[1024]{0:T(1024)S(1)}, bf16[256,1024]{1,0:T(8,128)(2,1)}) fusion(f32[256,1024]{1,0:T(8,128)S(1)} %fusion.24, f32[256,1024]{1,0:T(8,128)S(1)} %fusion.25, f32[256,1024]{1,0:T(8,128)S(1)} %fusion.26, bf16[256,2048]{1,0:T(8,128)(2,1)S(1)} %bitcast.92, s32[1024]{0:T(1024)S(1)} %bitcast.109, f32[1024]{0:T(1024)S(1)} %bitcast.111), kind=kOutput, calls=%fused_computation.45 | convolution fusion | flops 1077672960 | bytes 4730880 | tf_op jit(solution)/shard_map/dot_general | solution.py:45
  70.7 0.1 copy.95
  70.9 0.1 copy.96
  71.0 0.0 copy-start.4
  71.0 1.1 fusion.43
  72.1 2.0 %collective-permute-start = (bf16[2,256,512]{1,2,0:T(8,128)(2,1)}, bf16[2,256,512]{1,2,0:T(8,128)(2,1)S(1)}, u32[]{:S(2)}, u32[]{:S(2)}) collective-permute-start(bf16[2,256,512]{1,2,0:T(8,128)(2,1)} %get-tuple-element.7), channel_id=1, source_target_pairs={{0,1},{1,2},{2,3},{3,0},{4,5},{5,6},{6,7},{7,4},{8,9},{9,10},{10,1... | collective-permute-start | bytes 1572872 | tf_op jit(solution)/shard_map/ppermute | solution.py:99
  74.1 1.8 %collective-permute-start.1 = (bf16[2,256,512]{1,2,0:T(8,128)(2,1)}, bf16[2,256,512]{1,2,0:T(8,128)(2,1)S(1)}, u32[]{:S(2)}, u32[]{:S(2)}) collective-permute-start(bf16[2,256,512]{1,2,0:T(8,128)(2,1)} %get-tuple-element.8), channel_id=1, source_target_pairs={{1,0},{2,1},{3,2},{0,3},{5,4},{6,5},{7,6},{4,7},{9,8},{10,9},{11,1... | collective-permute-start | bytes 1572872 | tf_op jit(solution)/shard_map/ppermute | solution.py:100
  75.9 0.1 fusion.41
  76.1 1.3 %fusion.42.st_ref = bf16[2048,256]{1,0:T(8,128)(2,1)} fusion(bf16[256,2048]{0,1:T(8,128)(2,1)S(1)} %copy.89, f32[2048]{0:T(1024)S(1)} %bitcast.103), kind=kLoop, calls=%fused_computation.58 | loop fusion | flops 1572864 | bytes 2105344 | tf_op jit(solution)/shard_map/transpose | solution.py:113
  77.4 1.1 pad_maximum_fusion.2.o_ref
  78.5 10.3 %shard_map.73.rest_0_ = f32[2048,256]{1,0:T(8,128)} custom-call(s32[256]{0:T(256)} %reshape.90.code_ref, bf16[2048,256]{1,0:T(8,128)(2,1)} %fusion.42.st_ref, bf16[256,2048]{1,0:T(8,128)(2,1)} %pad_maximum_fusion.2.o_ref, bf16[2048,256]{1,0:T(8,128)(2,1)} %bitcast.95, f32[5,128,128]{2,1,0:T(8,128)} %concatenate.43.taper_ref), custom_call_target="tpu_custom_call" | custom-call | flops 4294967296 | bytes 4194304 | tf_op jit(solution)/shard_map/pallas_call | solution.py:210
  88.8 0.2 collective-permute-done
  89.0 7.2 %collective-permute-done.1 = bf16[2,256,512]{1,2,0:T(8,128)(2,1)S(1)} collective-permute-done((bf16[2,256,512]{1,2,0:T(8,128)(2,1)}, bf16[2,256,512]{1,2,0:T(8,128)(2,1)S(1)}, u32[]{:S(2)}, u32[]{:S(2)}) %collective-permute-start.1) | collective-permute-done | bytes 524320 | tf_op jit(solution)/shard_map/ppermute | solution.py:100
  96.2 0.9 pad_maximum_fusion.4
  97.1 1.0 copy.98.o_ref
  98.1 7.6 %shard_map.74 = bf16[2048,256]{1,0:T(8,128)(2,1)} custom-call(s32[128]{0:T(128)} %reshape.86.code_ref, bf16[2048,256]{1,0:T(8,128)(2,1)} %fusion.42.st_ref, bf16[256,1024]{1,0:T(8,128)(2,1)} %copy.98.o_ref, bf16[1024,256]{1,0:T(8,128)(2,1)} %get-tuple-element.50.it_ref, f32[5,128,128]{2,1,0:T(8,128)} %concatenate.43.taper_ref, ...), custom_call_target="tpu_custom_call" | custom-call | flops 2147483648 | bytes 4194304 | tf_op jit(solution)/shard_map/pallas_call | solution.py:210
  105.7 1.9 %copy.99 = bf16[256,8,256]{2,1,0:T(8,128)(2,1)S(1)} copy(bf16[256,8,256]{0,2,1:T(8,128)(2,1)} %bitcast.97) | data formatting | bytes 2097152 | tf_op jit(solution)/shard_map/reshape | solution.py:132
  107.6 20.0 %all_to_all.38 = bf16[256,8,256]{2,1,0:T(8,128)(2,1)S(1)} all-to-all(bf16[256,8,256]{2,1,0:T(8,128)(2,1)S(1)} %copy.99), channel_id=1, replica_groups=mesh['wide'=8,'lon'=4] {'wide'}, dimensions={0} | all-to-all | bytes 2097152 | tf_op jit(solution)/shard_map/all_to_all | solution.py:131
  127.5 1.1 copy.115
  (40 shorter events, 0.4 us)
Async XLA Ops:
  0.0 13.1 %copy-start = (f32[4,64,256]{2,1,0:T(8,128)S(1)}, f32[4,64,256]{2,1,0:T(8,128)}, u32[]{:S(2)}) copy-start(f32[4,64,256]{2,1,0:T(8,128)} %param.10) | copy-start | bytes 786436
  0.0 9.2 %copy-start.2 = (bf16[32,64,256]{2,1,0:T(8,128)(2,1)S(1)}, bf16[32,64,256]{2,1,0:T(8,128)(2,1)}, u32[]{:S(2)}) copy-start(bf16[32,64,256]{2,1,0:T(8,128)(2,1)} %param.7) | copy-start | bytes 3145732
  2.9 19.6 %all-to-all-start = ((bf16[4,2,2048]{2,1,0:T(2,128)(2,1)}), bf16[4,2,2048]{2,1,0:T(2,128)(2,1)S(1)}, u32[]{:S(2)}, u32[]{:S(2)}) async-start(bf16[4,2,2048]{2,1,0:T(2,128)(2,1)} %reshape.92), calls=%async_computation | async-start | bytes 65536 | tf_op jit(solution)/shard_map/all_to_all | solution.py:32
  10.5 4.1 %copy-start.6 = (s32[1,16,16]{2,1,0:T(8,128)S(1)}, s32[1,16,16]{2,1,0:T(8,128)}, u32[]{:S(2)}) copy-start(s32[1,16,16]{2,1,0:T(8,128)} %param.11) | copy-start | bytes 3076
  30.5 3.9 %copy-start.5 = (f32[4,512]{1,0:T(4,128)S(1)}, f32[4,512]{1,0:T(4,128)}, u32[]{:S(2)}) copy-start(f32[4,512]{1,0:T(4,128)} %get-tuple-element.32) | copy-start | bytes 24580
  30.5 3.9 %copy-start.3 = (bf16[256,8,256]{0,2,1:T(8,128)(2,1)S(1)}, bf16[256,8,256]{0,2,1:T(8,128)(2,1)}, u32[]{:S(2)}) copy-start(bf16[256,8,256]{0,2,1:T(8,128)(2,1)} %copy.94) | copy-start | bytes 3145732
  30.5 19.3 %all-to-all-start.1 = ((bf16[32,64,256]{2,0,1:T(8,128)(2,1)}), bf16[32,64,256]{2,0,1:T(8,128)(2,1)S(1)}, u32[]{:S(2)}, u32[]{:S(2)}) async-start(bf16[32,64,256]{2,0,1:T(8,128)(2,1)} %fusion.22), calls=%async_computation.1 | async-start | bytes 2097152 | tf_op jit(solution)/shard_map/all_to_all | solution.py:79
  51.0 1.0 copy-start.10
  52.1 24.0 %copy-start.1 = (bf16[256,2048]{0,1:T(8,128)(2,1)}, bf16[256,2048]{0,1:T(8,128)(2,1)S(1)}, u32[]{:S(2)}) copy-start(bf16[256,2048]{0,1:T(8,128)(2,1)S(1)} %copy.89) | copy-start | bytes 3145732
  52.1 2.4 %copy-start.9 = (s32[1,1024]{1,0:T(1,128)S(1)}, s32[1,1024]{1,0:T(1,128)}, u32[]{:S(2)}) copy-start(s32[1,1024]{1,0:T(1,128)} %get-tuple-element.42) | copy-start | bytes 12292
  54.5 2.4 %copy-start.8 = (s32[1,1024]{1,0:T(1,128)S(1)}, s32[1,1024]{1,0:T(1,128)}, u32[]{:S(2)}) copy-start(s32[1,1024]{1,0:T(1,128)} %get-tuple-element.40) | copy-start | bytes 12292
  56.9 2.4 %copy-start.7 = (s32[1,1024]{1,0:T(1,128)S(1)}, s32[1,1024]{1,0:T(1,128)}, u32[]{:S(2)}) copy-start(s32[1,1024]{1,0:T(1,128)} %get-tuple-element.39) | copy-start | bytes 12292
  71.0 4.9 %copy-start.4 = (bf16[256,1024]{1,0:T(8,128)(2,1)S(1)}, bf16[256,1024]{1,0:T(8,128)(2,1)}, u32[]{:S(2)}) copy-start(bf16[256,1024]{1,0:T(8,128)(2,1)} %get-tuple-element.48) | copy-start | bytes 1572868
  72.1 16.9 %collective-permute-start = (bf16[2,256,512]{1,2,0:T(8,128)(2,1)}, bf16[2,256,512]{1,2,0:T(8,128)(2,1)S(1)}, u32[]{:S(2)}, u32[]{:S(2)}) collective-permute-start(bf16[2,256,512]{1,2,0:T(8,128)(2,1)} %get-tuple-element.7), channel_id=1, source_target_pairs={{0,1},{1,2},{2,3},{3,0},{4,5},{5,6},{6,7},{7,4},{8,9},{9,10},{10,1... | collective-permute-start | bytes 1572872 | tf_op jit(solution)/shard_map/ppermute | solution.py:99
  74.1 22.0 %collective-permute-start.1 = (bf16[2,256,512]{1,2,0:T(8,128)(2,1)}, bf16[2,256,512]{1,2,0:T(8,128)(2,1)S(1)}, u32[]{:S(2)}, u32[]{:S(2)}) collective-permute-start(bf16[2,256,512]{1,2,0:T(8,128)(2,1)} %get-tuple-element.8), channel_id=1, source_target_pairs={{1,0},{2,1},{3,2},{0,3},{5,4},{6,5},{7,6},{4,7},{9,8},{10,9},{11,1... | collective-permute-start | bytes 1572872 | tf_op jit(solution)/shard_map/ppermute | solution.py:100

commit v6 on v3

--- a/solution.py
+++ b/solution.py
@@ -32,7 +32,12 @@
     got = lax.all_to_all(spread, axis, 0, 0, tiled=False)
     west = lax.dynamic_index_in_dim(got, (here - 1) % size, 0, keepdims=False)[..., 1:2]
     east = lax.dynamic_index_in_dim(got, (here + 1) % size, 0, keepdims=False)[..., 0:1]
-    return jnp.concatenate([west, value, east], axis=-1)
+    return west, east
+
+
+def stencil(state, east, west, northern, southern):
+    member_spread = east + west + northern + southern - 4.0 * state
+    return (state + 0.2 * member_spread - 0.3 * (east - west)).astype(jnp.bfloat16)
 
 
 def observe_region(state, index, weight):
@@ -72,16 +77,22 @@
 
 
 def body(background_ensemble, innov, obs_index, obs_weight, obs_list, tile_count, taper_class):
-    padded = column_halo(background_ensemble, "lon")
     state_values = background_ensemble.astype(jnp.float32)
-    east_neighbour = padded[:, :, 2:].astype(jnp.float32)
-    west_neighbour = padded[:, :, :-2].astype(jnp.float32)
     northern = jnp.pad(state_values[:, 1:, :], ((0, 0), (0, 1), (0, 0)))
     southern = jnp.pad(state_values[:, :-1, :], ((0, 0), (1, 0), (0, 0)))
-    member_spread = east_neighbour + west_neighbour + northern + southern - 4.0 * state_values
-    prediction_increment = (
-        state_values + 0.2 * member_spread - 0.3 * (east_neighbour - west_neighbour)
-    ).astype(jnp.bfloat16)
+    inner_east = jnp.pad(state_values[:, :, 1:], ((0, 0), (0, 0), (0, 1)))
+    inner_west = jnp.pad(state_values[:, :, :-1], ((0, 0), (0, 0), (1, 0)))
+    inner = stencil(state_values, inner_east, inner_west, northern, southern)
+    west_col, east_col = column_halo(background_ensemble, "lon")
+    first = stencil(
+        state_values[..., :1], state_values[..., 1:2], west_col.astype(jnp.float32),
+        northern[..., :1], southern[..., :1],
+    )
+    last = stencil(
+        state_values[..., -1:], east_col.astype(jnp.float32), state_values[..., -2:-1],
+        northern[..., -1:], southern[..., -1:],
+    )
+    prediction_increment = jnp.concatenate([first, inner[..., 1:-1], last], axis=-1)
     ensemble_lines_here, whole_parallel_set, patch_meridian_lines = prediction_increment.shape
     members = innov.shape[0]
     band_rows = innov.shape[1]

time: 122 us -> 149 us (1.22)
  local copies, waits for them, and re-layouts: 23.5 us -> 35.2 us
  other arithmetic: 16 us -> 26.4 us
  waiting for transfers between devices: 15 us -> 19.5 us
    ppermute x1, waiting for transfers between devices: 0.01 us -> 7.16 us  [body(): east = lax.ppermute(edges[:, :, :halo], 'lon', down)]
    unnamed x39 -> x38, local copies, waits for them, and re-layouts: 3.57 us -> 10.5 us
    add x0 -> x1, other arithmetic: none -> 6.45 us  [stencil(): member_spread = east + west + northern + southern - 4.0 * state]
    convert_element_type x1 -> x3, other arithmetic: 4.6 us -> 8.31 us  [the longest x2 5.73 us: stencil(): (state + 0.2 * member_spread - 0.3 * (east - west)).astype(jnp.bfloat16)]
    concatenate x0 -> x1, local copies, waits for them, and re-layouts: none -> 3.55 us  [body(): jnp.concatenate([first, inner[..., 1:-1], last], axis=-1)]
    ppermute x1, waiting for transfers between devices: 3.25 us -> 0.32 us  [body(): west = lax.ppermute(edges[:, :, halo:], 'lon', up)]
    slice x1, local copies, waits for them, and re-layouts: 1.84 us -> 4.22 us  [body(): northern = jnp.pad(state_values[:, 1:, :], ((0, 0), (0, 1), (0, 0)))]
    squeeze x2, local copies, waits for them, and re-layouts: 2.13 us -> 0.07 us  [body(): halo_innov = jnp.concatenate([west[1], east[1]], axis=1)]
  transfers between devices with their start and end apart: 4 -> 4, of which waited for: 3 -> 3; matrix products, arithmetic and copies ran while one was open for 14% -> 22% of each run, Pallas kernels for 8% -> 7%
where the time goes in v6:
time: 149 us; the launch traced here: 148 us
  local copies, waits for them, and re-layouts  35.2 us (24%)
  other arithmetic  26.4 us (18%)
  blocking collectives  20 us (13%)
  waiting for transfers between devices  19.5 us (13%)
  Pallas kernels  17.8 us (12%)
  matrix products  14.8 us (10%)
  starting transfers between devices  13.9 us (9%)
    all_to_all x1, blocking collectives, body(): lax.all_to_all(result.reshape(members, band_rows, patch_meridian_lines),...  20 us
    pallas_call x2, Pallas kernels, update_call(): pl.pallas_call(kernel, grid_spec=grid_spec, out_shape=jax.ShapeDtypeStruc...  17.8 us
    dot_general x16, matrix products, observe_one_block(): picked = jnp.dot(state, selector, preferred_element_type=jnp.float32)  14.8 us
    all_to_all x1, waiting for transfers between devices, body(): lax.all_to_all(prediction_increment, 'wide', split_axis=1, concat_axis=0,...  12 us
    unnamed x38, local copies, waits for them, and re-layouts  10.5 us
    ppermute x1, waiting for transfers between devices, body(): east = lax.ppermute(edges[:, :, :halo], 'lon', down)  7.16 us
    add x1, other arithmetic, stencil(): member_spread = east + west + northern + southern - 4.0 * state  6.45 us
    all_to_all x1, starting transfers between devices, column_halo(): got = lax.all_to_all(spread, axis, 0, 0, tiled=False)  6.32 us
  transfers between devices with their start and end apart: 4, of which 3 were waited for; matrix products, arithmetic and copies ran while one was open for 22% of the time, Pallas kernels for 7%

profile of v6, /device:TPU:0, one launch (start us, length us, event | category | flops | bytes accessed | tf_op | source)
XLA Modules:
  0.0 148.2 jit_solution(7895462566551652939)
XLA Ops:
  0.0 4.0 %copy.58 = bf16[32,64,256]{1,0,2:T(8,128)(2,1)S(1)} copy(bf16[32,64,256]{2,1,0:T(8,128)(2,1)} %param.11) | data formatting | bytes 2097152 | tf_op args[0]
  4.0 0.7 reshape.200
  4.7 6.3 %all-to-all-start = ((bf16[4,2,2048]{2,1,0:T(2,128)(2,1)}), bf16[4,2,2048]{2,1,0:T(2,128)(2,1)S(1)}, u32[]{:S(2)}, u32[]{:S(2)}) async-start(bf16[4,2,2048]{2,1,0:T(2,128)(2,1)} %reshape.200), calls=%async_computation | async-start | bytes 65536 | tf_op jit(solution)/shard_map/all_to_all | solution.py:32
  11.1 4.2 %fusion.123 = (f32[32,63,256]{1,0,2:T(8,128)}, f32[32,63,256]{1,0,2:T(8,128)}) fusion(bf16[32,64,256]{1,0,2:T(8,128)(2,1)S(1)} %copy.58), kind=kLoop, calls=%fused_computation.147 | loop fusion | bytes 8257536 | tf_op jit(solution)/shard_map/slice | solution.py:81
  15.3 2.6 %convert_element_type.99 = f32[32,64,256]{1,0,2:T(8,128)} convert(bf16[32,64,256]{1,0,2:T(8,128)(2,1)S(1)} %copy.58) | non-fusion elementwise | flops 524288 | bytes 3145728 | tf_op jit(solution)/shard_map/convert_element_type | solution.py:80
  17.9 4.3 %fusion.121 = (f32[32,64,255]{1,0,2:T(8,128)}, f32[32,64,255]{1,0,2:T(8,128)}) fusion(bf16[32,64,256]{1,0,2:T(8,128)(2,1)S(1)} %copy.58), kind=kLoop, calls=%fused_computation.145 | loop fusion | bytes 8355840 | tf_op jit(solution)/shard_map/slice | solution.py:83
  22.2 0.8 subtract_bitcast_fusion
  23.4 0.8 fusion.107
  24.2 6.4 %add_add_fusion = f32[32,64,256]{1,0,2:T(8,128)S(1)} fusion(f32[32,64,255]{1,0,2:T(8,128)} %get-tuple-element.198, f32[32,64,255]{1,0,2:T(8,128)} %get-tuple-element.197, f32[32,63,256]{1,0,2:T(8,128)} %get-tuple-element.201), kind=kLoop, calls=%fused_computation.70 | loop fusion | flops 1048576 | bytes 8339456 | tf_op jit(solution)/shard_map/add | solution.py:39
  30.7 0.6 copy-done.2
  31.3 1.2 copy-done.3
  32.5 1.2 copy-done.4
  33.7 4.7 %fusion.98 = bf16[32,64,254]{1,0,2:T(8,128)(2,1)} fusion(f32[32,64,255]{1,0,2:T(8,128)S(1)} %copy-done.3, f32[32,64,255]{1,0,2:T(8,128)S(1)} %copy-done.2, f32[32,63,256]{1,0,2:T(8,128)S(1)} %copy-done.1, f32[32,64,256]{1,0,2:T(8,128)S(1)} %add_add_fusion, f32[32,64,256]{1,0,2:T(8,128)S(1)} %copy-done.4), kind=kLoop, calls=%fused_computation.74 | loop fusion | flops 4681728 | bytes 11444224 | tf_op jit(solution)/shard_map/convert_element_type | solution.py:40
  38.5 1.6 %copy.64 = bf16[256,8,256]{0,2,1:T(8,128)(2,1)S(1)} copy(bf16[256,8,256]{2,1,0:T(8,128)(2,1)} %param.12) | data formatting | bytes 2097152 | tf_op args[1]
  40.1 0.8 reshape.193.code_ref
  41.0 1.1 fusion.116
  42.1 0.6 copy-done.5
  42.7 0.5 pad_maximum_fusion
  43.2 3.6 %copy.61 = bf16[32,64,256]{2,0,1:T(8,128)(2,1)} copy(bf16[32,64,256]{1,0,2:T(8,128)(2,1)S(1)} %pad_maximum_fusion) | data formatting | bytes 2097152 | tf_op jit(solution)/shard_map/concatenate | solution.py:95
  46.8 3.7 %all-to-all-start.1 = ((bf16[32,64,256]{2,0,1:T(8,128)(2,1)}), bf16[32,64,256]{2,0,1:T(8,128)(2,1)S(1)}, u32[]{:S(2)}, u32[]{:S(2)}) async-start(bf16[32,64,256]{2,0,1:T(8,128)(2,1)} %copy.61), calls=%async_computation.1 | async-start | bytes 2097152 | tf_op jit(solution)/shard_map/all_to_all | solution.py:100
  50.6 0.7 reshape.187.code_ref
  51.3 1.7 %concatenate.38.taper_ref = f32[5,128,128]{2,1,0:T(8,128)} pad(f32[4,128,128]{2,1,0:T(8,128)} %fusion.107, f32[]{:T(128)} %constant.81.clone.1), padding=0_1x0_0x0_0 | pad | bytes 589828 | tf_op jit(solution)/shard_map/concatenate | solution.py:177
  53.0 0.8 maximum_bitcast_fusion
  53.9 12.0 %all-to-all-done.1 = bf16[32,64,256]{2,0,1:T(8,128)(2,1)S(1)} async-done(((bf16[32,64,256]{2,0,1:T(8,128)(2,1)}), bf16[32,64,256]{2,0,1:T(8,128)(2,1)S(1)}, u32[]{:S(2)}, u32[]{:S(2)}) %all-to-all-start.1) | async-done | bytes 1048608 | tf_op jit(solution)/shard_map/all_to_all | solution.py:100
  65.9 0.6 copy.62
  66.5 0.3 copy.73
  66.9 6.3 %while.25 = (s32[]{:T(128)}, bf16[2,256,512]{1,2,0:T(8,128)(2,1)S(1)}, f32[2,4,512]{2,1,0:T(4,128)S(1)}, s32[2,4,512]{2,1,0:T(4,128)S(1)}, bf16[256,2048]{1,0:T(...) while((s32[]{:T(128)}, bf16[2,256,512]{1,2,0:T(8,128)(2,1)S(1)}, ...), condition=%wide.region_6.7_spmd.clone.clone, body=%wide.region_5.6_spmd.clone.clone.sunk | while | flops 2156920832 | bytes 7651501 | solution.py:61
  66.9 0.8 fusion.181
  67.7 0.8 fusion.182
  68.5 0.8 fusion.183
  69.2 0.8 fusion.184
  70.1 0.8 fusion.181
  70.8 0.8 fusion.182
  71.6 0.8 fusion.183
  72.4 0.8 fusion.184
  73.2 1.2 convert_element_type.126
  74.6 8.9 %while.24 = (s32[]{:T(128)}, bf16[2,256,512]{1,2,0:T(8,128)(2,1)S(1)}, f32[2,4,512]{2,1,0:T(4,128)S(1)}, s32[2,4,512]{2,1,0:T(4,128)S(1)}, bf16[256,2048]{1,0:T(...) while((s32[]{:T(128)}, bf16[2,256,512]{1,2,0:T(8,128)(2,1)S(1)}, ...), condition=%wide.region_3.4_spmd.clone.clone, body=%wide.region_2.3_spmd.clone.clone.sunk | while | flops 2156920832 | bytes 11845833 | solution.py:61
  74.7 2.1 %fusion.169 = f32[512,256]{1,0:T(8,128)S(1)} fusion(bf16[256,2048]{1,0:T(8,128)(2,1)} %get-tuple-element.341, s32[512]{0:T(512)S(1)} %bitcast.205, f32[512]{0:T(512)S(1)} %bitcast.209), kind=kOutput, calls=%fused_computation.18.clone.1 | convolution fusion | flops 539099136 | bytes 1576960 | tf_op jit(solution)/shard_map/while/body/eval_jaxpr/dot_general | solution.py:57
  76.8 0.8 fusion.170
  77.6 0.8 fusion.171
  78.3 0.8 fusion.172
  79.2 2.1 %fusion.169 = f32[512,256]{1,0:T(8,128)S(1)} fusion(bf16[256,2048]{1,0:T(8,128)(2,1)} %get-tuple-element.341, s32[512]{0:T(512)S(1)} %bitcast.205, f32[512]{0:T(512)S(1)} %bitcast.209), kind=kOutput, calls=%fused_computation.18.clone.1 | convolution fusion | flops 539099136 | bytes 1576960 | tf_op jit(solution)/shard_map/while/body/eval_jaxpr/dot_general | solution.py:57
  81.3 0.8 fusion.170
  82.0 0.8 fusion.171
  82.8 0.8 fusion.172
  83.9 1.5 copy.63
  85.4 0.6 convert_reduce_fusion
  86.0 1.6 %copy.72 = f32[256,1024]{1,0:T(8,128)S(1)} copy(f32[256,1024]{0,1:T(8,128)} %bitcast.178) | data formatting | bytes 2097152 | tf_op jit(solution)/shard_map/convert_element_type | solution.py:66
  87.6 1.3 copy.71
  88.9 1.4 subtract_convert_fusion.2
  90.6 1.1 fusion.104
  91.6 2.0 %collective-permute-start = (bf16[2,256,512]{1,2,0:T(8,128)(2,1)}, bf16[2,256,512]{1,2,0:T(8,128)(2,1)S(1)}, u32[]{:S(2)}, u32[]{:S(2)}) collective-permute-start(bf16[2,256,512]{1,2,0:T(8,128)(2,1)} %get-tuple-element.203), channel_id=1, source_target_pairs={{0,1},{1,2},{2,3},{3,0},{4,5},{5,6},{6,7},{7,4},{8,9},{9,10},{10,1... | collective-permute-start | bytes 1572872 | tf_op jit(solution)/shard_map/ppermute | solution.py:120
  93.7 1.8 %collective-permute-start.1 = (bf16[2,256,512]{1,2,0:T(8,128)(2,1)}, bf16[2,256,512]{1,2,0:T(8,128)(2,1)S(1)}, u32[]{:S(2)}, u32[]{:S(2)}) collective-permute-start(bf16[2,256,512]{1,2,0:T(8,128)(2,1)} %get-tuple-element.204), channel_id=1, source_target_pairs={{1,0},{2,1},{3,2},{0,3},{5,4},{6,5},{7,6},{4,7},{9,8},{10,9},{11,1... | collective-permute-start | bytes 1572872 | tf_op jit(solution)/shard_map/ppermute | solution.py:121
  95.6 1.3 fusion.102.st_ref
  96.9 1.1 pad_maximum_fusion.1.o_ref
  98.0 10.2 %shard_map.73.rest_0_ = f32[2048,256]{1,0:T(8,128)} custom-call(s32[256]{0:T(256)} %reshape.193.code_ref, bf16[2048,256]{1,0:T(8,128)(2,1)} %fusion.102.st_ref, bf16[256,2048]{1,0:T(8,128)(2,1)} %pad_maximum_fusion.1.o_ref, bf16[2048,256]{1,0:T(8,128)(2,1)} %bitcast.183, f32[5,128,128]{2,1,0:T(8,128)} %concatenate.38.taper_ref), custom_call_target="tpu_custom_call" | custom-call | flops 4294967296 | bytes 4194304 | tf_op jit(solution)/shard_map/pallas_call | solution.py:231
  108.2 0.3 collective-permute-done
  108.6 7.2 %collective-permute-done.1 = bf16[2,256,512]{1,2,0:T(8,128)(2,1)S(1)} collective-permute-done((bf16[2,256,512]{1,2,0:T(8,128)(2,1)}, bf16[2,256,512]{1,2,0:T(8,128)(2,1)S(1)}, u32[]{:S(2)}, u32[]{:S(2)}) %collective-permute-start.1) | collective-permute-done | bytes 524320 | tf_op jit(solution)/shard_map/ppermute | solution.py:121
  115.8 0.9 pad_maximum_fusion.3
  116.6 1.0 copy.68.o_ref
  117.6 7.6 %shard_map.74 = bf16[2048,256]{1,0:T(8,128)(2,1)} custom-call(s32[128]{0:T(128)} %reshape.187.code_ref, bf16[2048,256]{1,0:T(8,128)(2,1)} %fusion.102.st_ref, bf16[256,1024]{1,0:T(8,128)(2,1)} %copy.68.o_ref, bf16[1024,256]{1,0:T(8,128)(2,1)} %get-tuple-element.222.it_ref, f32[5,128,128]{2,1,0:T(8,128)} %concatenate.38.taper_ref, ...), custom_call_target="tpu_custom_call" | custom-call | flops 2147483648 | bytes 4194304 | tf_op jit(solution)/shard_map/pallas_call | solution.py:231
  125.2 1.9 %copy.69 = bf16[256,8,256]{2,1,0:T(8,128)(2,1)S(1)} copy(bf16[256,8,256]{0,2,1:T(8,128)(2,1)} %bitcast.184) | data formatting | bytes 2097152 | tf_op jit(solution)/shard_map/reshape | solution.py:153
  127.1 20.0 %all_to_all.38 = bf16[256,8,256]{2,1,0:T(8,128)(2,1)S(1)} all-to-all(bf16[256,8,256]{2,1,0:T(8,128)(2,1)S(1)} %copy.69), channel_id=1, replica_groups=mesh['wide'=8,'lon'=4] {'wide'}, dimensions={0} | all-to-all | bytes 2097152 | tf_op jit(solution)/shard_map/all_to_all | solution.py:152
  147.1 1.1 copy.81
  (74 shorter events, 1.9 us)
Async XLA Ops:
  0.0 38.4 %copy-start = (f32[4,64,256]{2,1,0:T(8,128)S(1)}, f32[4,64,256]{2,1,0:T(8,128)}, u32[]{:S(2)}) copy-start(f32[4,64,256]{2,1,0:T(8,128)} %param.14) | copy-start | bytes 786436
  4.7 36.1 %all-to-all-start = ((bf16[4,2,2048]{2,1,0:T(2,128)(2,1)}), bf16[4,2,2048]{2,1,0:T(2,128)(2,1)S(1)}, u32[]{:S(2)}, u32[]{:S(2)}) async-start(bf16[4,2,2048]{2,1,0:T(2,128)(2,1)} %reshape.200), calls=%async_computation | async-start | bytes 65536 | tf_op jit(solution)/shard_map/all_to_all | solution.py:32
  17.9 5.2 %copy-start.12 = (s32[1,16,16]{2,1,0:T(8,128)S(1)}, s32[1,16,16]{2,1,0:T(8,128)}, u32[]{:S(2)}) copy-start(s32[1,16,16]{2,1,0:T(8,128)} %param.17) | copy-start | bytes 3076
  17.9 5.2 %copy-start.13 = (s32[1,16]{1,0:T(1,128)S(1)}, s32[1,16]{1,0:T(1,128)}, u32[]{:S(2)}) copy-start(s32[1,16]{1,0:T(1,128)} %param.16) | copy-start | bytes 196
  17.9 5.3 %copy-start.11 = (s32[1,16,16]{2,1,0:T(8,128)S(1)}, s32[1,16,16]{2,1,0:T(8,128)}, u32[]{:S(2)}) copy-start(s32[1,16,16]{2,1,0:T(8,128)} %param.15) | copy-start | bytes 3076
  24.2 6.5 %copy-start.1 = (f32[32,63,256]{1,0,2:T(8,128)S(1)}, f32[32,63,256]{1,0,2:T(8,128)}, u32[]{:S(2)}) copy-start(f32[32,63,256]{1,0,2:T(8,128)} %get-tuple-element.202) | copy-start | bytes 6193156
  24.2 7.1 %copy-start.2 = (f32[32,64,255]{1,0,2:T(8,128)S(1)}, f32[32,64,255]{1,0,2:T(8,128)}, u32[]{:S(2)}) copy-start(f32[32,64,255]{1,0,2:T(8,128)} %get-tuple-element.197) | copy-start | bytes 6266884
  24.2 8.3 %copy-start.3 = (f32[32,64,255]{1,0,2:T(8,128)S(1)}, f32[32,64,255]{1,0,2:T(8,128)}, u32[]{:S(2)}) copy-start(f32[32,64,255]{1,0,2:T(8,128)} %get-tuple-element.198) | copy-start | bytes 6266884
  24.2 9.5 %copy-start.4 = (f32[32,64,256]{1,0,2:T(8,128)S(1)}, f32[32,64,256]{1,0,2:T(8,128)}, u32[]{:S(2)}) copy-start(f32[32,64,256]{1,0,2:T(8,128)} %convert_element_type.99) | copy-start | bytes 6291460
  40.1 12.9 %copy-start.9 = (bf16[256,8,256]{0,2,1:T(8,128)(2,1)}, bf16[256,8,256]{0,2,1:T(8,128)(2,1)S(1)}, u32[]{:S(2)}) copy-start(bf16[256,8,256]{0,2,1:T(8,128)(2,1)S(1)} %copy.64) | copy-start | bytes 3145732
  41.0 1.7 %copy-start.5 = (bf16[32,64,254]{1,0,2:T(8,128)(2,1)S(1)}, bf16[32,64,254]{1,0,2:T(8,128)(2,1)}, u32[]{:S(2)}) copy-start(bf16[32,64,254]{1,0,2:T(8,128)(2,1)} %fusion.98) | copy-start | bytes 3121156
  46.8 19.1 %all-to-all-start.1 = ((bf16[32,64,256]{2,0,1:T(8,128)(2,1)}), bf16[32,64,256]{2,0,1:T(8,128)(2,1)S(1)}, u32[]{:S(2)}, u32[]{:S(2)}) async-start(bf16[32,64,256]{2,0,1:T(8,128)(2,1)} %copy.61), calls=%async_computation.1 | async-start | bytes 2097152 | tf_op jit(solution)/shard_map/all_to_all | solution.py:100
  73.2 1.4 copy-start.6
  74.7 2.1 %copy-start.7 = (bf16[256,2048]{1,0:T(8,128)(2,1)S(1)}, bf16[256,2048]{1,0:T(8,128)(2,1)}, u32[]{:S(2)}) copy-start(bf16[256,2048]{1,0:T(8,128)(2,1)} %get-tuple-element.341) | copy-start | bytes 3145732 | tf_op jit(solution)/shard_map/while
  79.1 2.1 %copy-start.7 = (bf16[256,2048]{1,0:T(8,128)(2,1)S(1)}, bf16[256,2048]{1,0:T(8,128)(2,1)}, u32[]{:S(2)}) copy-start(bf16[256,2048]{1,0:T(8,128)(2,1)} %get-tuple-element.341) | copy-start | bytes 3145732 | tf_op jit(solution)/shard_map/while
  85.4 10.2 %copy-start.8 = (bf16[256,2048]{0,1:T(8,128)(2,1)}, bf16[256,2048]{0,1:T(8,128)(2,1)S(1)}, u32[]{:S(2)}) copy-start(bf16[256,2048]{0,1:T(8,128)(2,1)S(1)} %copy.63) | copy-start | bytes 3145732
  88.9 1.7 %copy-start.10 = (bf16[1,256,1024]{1,2,0:T(8,128)(2,1)S(1)}, bf16[1,256,1024]{1,2,0:T(8,128)(2,1)}, u32[]{:S(2)}) copy-start(bf16[1,256,1024]{1,2,0:T(8,128)(2,1)} %maximum_bitcast_fusion) | copy-start | bytes 1572868
  91.6 16.9 %collective-permute-start = (bf16[2,256,512]{1,2,0:T(8,128)(2,1)}, bf16[2,256,512]{1,2,0:T(8,128)(2,1)S(1)}, u32[]{:S(2)}, u32[]{:S(2)}) collective-permute-start(bf16[2,256,512]{1,2,0:T(8,128)(2,1)} %get-tuple-element.203), channel_id=1, source_target_pairs={{0,1},{1,2},{2,3},{3,0},{4,5},{5,6},{6,7},{7,4},{8,9},{9,10},{10,1... | collective-permute-start | bytes 1572872 | tf_op jit(solution)/shard_map/ppermute | solution.py:120
  93.7 22.0 %collective-permute-start.1 = (bf16[2,256,512]{1,2,0:T(8,128)(2,1)}, bf16[2,256,512]{1,2,0:T(8,128)(2,1)S(1)}, u32[]{:S(2)}, u32[]{:S(2)}) collective-permute-start(bf16[2,256,512]{1,2,0:T(8,128)(2,1)} %get-tuple-element.204), channel_id=1, source_target_pairs={{1,0},{2,1},{3,2},{0,3},{5,4},{6,5},{7,6},{4,7},{9,8},{10,9},{11,1... | collective-permute-start | bytes 1572872 | tf_op jit(solution)/shard_map/ppermute | solution.py:121

commit v7 on v3

--- a/solution.py
+++ b/solution.py
@@ -32,7 +32,29 @@
     got = lax.all_to_all(spread, axis, 0, 0, tiled=False)
     west = lax.dynamic_index_in_dim(got, (here - 1) % size, 0, keepdims=False)[..., 1:2]
     east = lax.dynamic_index_in_dim(got, (here + 1) % size, 0, keepdims=False)[..., 0:1]
-    return jnp.concatenate([west, value, east], axis=-1)
+    return west, east
+
+
+def forecast_call(state, west, east):
+    members, rows, cols = state.shape
+
+    def kernel(x_ref, w_ref, e_ref, o_ref):
+        col = lax.broadcasted_iota(jnp.int32, (rows, cols), 1)
+        row = lax.broadcasted_iota(jnp.int32, (rows, cols), 0)
+
+        def one(m, carry):
+            x = x_ref[m].astype(jnp.float32)
+            east_n = jnp.where(col == cols - 1, e_ref[m].astype(jnp.float32), pltpu.roll(x, cols - 1, 1))
+            west_n = jnp.where(col == 0, w_ref[m].astype(jnp.float32), pltpu.roll(x, 1, 1))
+            north = jnp.where(row == rows - 1, 0.0, pltpu.roll(x, rows - 1, 0))
+            south = jnp.where(row == 0, 0.0, pltpu.roll(x, 1, 0))
+            spread = east_n + west_n + north + south - 4.0 * x
+            o_ref[m] = (x + 0.2 * spread - 0.3 * (east_n - west_n)).astype(jnp.bfloat16)
+            return carry
+
+        lax.fori_loop(0, members, one, 0)
+
+    return pl.pallas_call(kernel, out_shape=jax.ShapeDtypeStruct(state.shape, jnp.bfloat16))(state, west, east)
 
 
 def observe_region(state, index, weight):
@@ -72,16 +94,8 @@
 
 
 def body(background_ensemble, innov, obs_index, obs_weight, obs_list, tile_count, taper_class):
-    padded = column_halo(background_ensemble, "lon")
-    state_values = background_ensemble.astype(jnp.float32)
-    east_neighbour = padded[:, :, 2:].astype(jnp.float32)
-    west_neighbour = padded[:, :, :-2].astype(jnp.float32)
-    northern = jnp.pad(state_values[:, 1:, :], ((0, 0), (0, 1), (0, 0)))
-    southern = jnp.pad(state_values[:, :-1, :], ((0, 0), (1, 0), (0, 0)))
-    member_spread = east_neighbour + west_neighbour + northern + southern - 4.0 * state_values
-    prediction_increment = (
-        state_values + 0.2 * member_spread - 0.3 * (east_neighbour - west_neighbour)
-    ).astype(jnp.bfloat16)
+    west_col, east_col = column_halo(background_ensemble, "lon")
+    prediction_increment = forecast_call(background_ensemble, west_col, east_col)
     ensemble_lines_here, whole_parallel_set, patch_meridian_lines = prediction_increment.shape
     members = innov.shape[0]
     band_rows = innov.shape[1]

time: 122 us -> 123 us (level)
  Pallas kernels: 17.8 us -> 24.2 us
  other arithmetic: 16 us -> 10.8 us
  matrix products: 14.8 us -> 12.1 us
  waiting for transfers between devices: 15 us -> 17.6 us
    pallas_call x0 -> x1, Pallas kernels: none -> 6.33 us  [forecast_call(): pl.pallas_call(kernel, out_shape=jax.ShapeDtypeStruct(state.shape, jnp.bf...]
    convert_element_type x1 -> x0, other arithmetic: 4.6 us -> none  [body(): prediction_increment = (state_values + 0.2 * member_spread - 0.3 * (east_...]
    ppermute x1, waiting for transfers between devices: 0.01 us -> 3.74 us  [body(): east = lax.ppermute(edges[:, :, :halo], 'lon', down)]
    slice x3 -> x0, local copies, waits for them, and re-layouts: 3.51 us -> none  [the longest x1 1.84 us: body(): northern = jnp.pad(state_values[:, 1:, :], ((0, 0), (0, 1), (0, 0)))]
    ppermute x1, waiting for transfers between devices: 3.25 us -> 0.01 us  [body(): west = lax.ppermute(edges[:, :, halo:], 'lon', up)]
    pallas_call x0 -> x1, local copies, waits for them, and re-layouts: none -> 2.87 us  [forecast_call(): pl.pallas_call(kernel, out_shape=jax.ShapeDtypeStruct(state.shape, jnp.bf...]
    dot_general x16, matrix products: 14.8 us -> 12.1 us  [observe_one_block(): picked = jnp.dot(state, selector, preferred_element_type=jnp.float32)]
    another operation x2, other arithmetic: 1.08 us -> 2.99 us  [body(): edges = jnp.stack([edge_dev, edge_innov])]
  transfers between devices with their start and end apart: 4 -> 4, of which waited for: 3 -> 3; matrix products, arithmetic and copies ran while one was open for 14% -> 9% of each run, Pallas kernels for 8% -> 8%
where the time goes in v7:
time: 123 us; the launch traced here: 122 us
  Pallas kernels  24.2 us (20%)
  local copies, waits for them, and re-layouts  22.8 us (19%)
  blocking collectives  19.9 us (16%)
  waiting for transfers between devices  17.6 us (14%)
  starting transfers between devices  13.9 us (11%)
  matrix products  12.1 us (10%)
  other arithmetic  10.8 us (9%)
    all_to_all x1, blocking collectives, body(): lax.all_to_all(result.reshape(members, band_rows, patch_meridian_lines),...  19.9 us
    pallas_call x2, Pallas kernels, update_call(): pl.pallas_call(kernel, grid_spec=grid_spec, out_shape=jax.ShapeDtypeStruc...  17.9 us
    dot_general x16, matrix products, observe_one_block(): picked = jnp.dot(state, selector, preferred_element_type=jnp.float32)  12.1 us
    all_to_all x1, waiting for transfers between devices, body(): lax.all_to_all(prediction_increment, 'wide', split_axis=1, concat_axis=0,...  11.7 us
    pallas_call x1, Pallas kernels, forecast_call(): pl.pallas_call(kernel, out_shape=jax.ShapeDtypeStruct(state.shape, jnp.bf...  6.33 us
    all_to_all x1, starting transfers between devices, column_halo(): got = lax.all_to_all(spread, axis, 0, 0, tiled=False)  6.32 us
    ppermute x1, waiting for transfers between devices, body(): east = lax.ppermute(edges[:, :, :halo], 'lon', down)  3.74 us
    all_to_all x1, starting transfers between devices, body(): lax.all_to_all(prediction_increment, 'wide', split_axis=1, concat_axis=0,...  3.74 us
  transfers between devices with their start and end apart: 4, of which 3 were waited for; matrix products, arithmetic and copies ran while one was open for 9% of the time, Pallas kernels for 8%

profile of v7, /device:TPU:0, one launch (start us, length us, event | category | flops | bytes accessed | tf_op | source)
XLA Modules:
  0.0 121.9 jit_solution(2318675837194928473)
XLA Ops:
  0.0 1.5 %fusion.104 = (bf16[32,64,1]{2,1,0:T(8,128)(2,1)S(1)}, bf16[32,64,1]{2,1,0:T(8,128)(2,1)S(1)}) fusion(bf16[32,64,256]{2,1,0:T(8,128)(2,1)} %x_ref.1), kind=kLoop, calls=%fused_computation.116 | loop fusion | bytes 16384 | tf_op jit(solution)/shard_map/slice | solution.py:30
  1.5 0.3 copy.63
  1.8 0.3 copy.64
  2.1 0.7 reshape.200
  2.8 6.3 %all-to-all-start = ((bf16[4,2,2048]{2,1,0:T(2,128)(2,1)}), bf16[4,2,2048]{2,1,0:T(2,128)(2,1)S(1)}, u32[]{:S(2)}, u32[]{:S(2)}) async-start(bf16[4,2,2048]{2,1,0:T(2,128)(2,1)} %reshape.200), calls=%async_computation | async-start | bytes 65536 | tf_op jit(solution)/shard_map/all_to_all | solution.py:32
  9.5 0.8 subtract_bitcast_fusion
  10.3 0.8 fusion.101
  11.3 0.7 reshape.193.code_ref
  12.0 0.7 reshape.187.code_ref
  12.7 2.1 %all-to-all-done = bf16[4,2,2048]{2,1,0:T(2,128)(2,1)S(1)} async-done(((bf16[4,2,2048]{2,1,0:T(2,128)(2,1)}), bf16[4,2,2048]{2,1,0:T(2,128)(2,1)S(1)}, u32[]{:S(2)}, u32[]{:S(2)}) %all-to-all-start) | async-done | bytes 32800 | tf_op jit(solution)/shard_map/all_to_all | solution.py:32
  14.9 1.1 copy.50
  16.0 0.3 copy.49
  16.4 1.0 slice.190.w_ref
  17.4 6.3 %shard_map.73 = bf16[32,64,256]{2,1,0:T(8,128)(2,1)} custom-call(bf16[32,64,256]{2,1,0:T(8,128)(2,1)} %x_ref.1, bf16[32,64,1]{2,1,0:T(8,128)(2,1)} %slice.190.w_ref, bf16[32,64,1]{2,1,0:T(8,128)(2,1)} %bitcast.184), custom_call_target="tpu_custom_call" | custom-call | tf_op jit(solution)/shard_map/pallas_call | solution.py:57
  23.7 2.9 %copy.51 = bf16[32,64,256]{2,0,1:T(8,128)(2,1)} copy(bf16[32,64,256]{2,1,0:T(8,128)(2,1)} %shard_map.73) | data formatting | bytes 2097152 | tf_op jit(solution)/shard_map/pallas_call | solution.py:57
  26.6 3.7 %all-to-all-start.1 = ((bf16[32,64,256]{2,0,1:T(8,128)(2,1)}), bf16[32,64,256]{2,0,1:T(8,128)(2,1)S(1)}, u32[]{:S(2)}, u32[]{:S(2)}) async-start(bf16[32,64,256]{2,0,1:T(8,128)(2,1)} %copy.51), calls=%async_computation.1 | async-start | bytes 2097152 | tf_op jit(solution)/shard_map/all_to_all | solution.py:103
  30.4 0.8 copy.54
  31.2 1.9 %concatenate.34.taper_ref = f32[5,128,128]{2,1,0:T(8,128)} pad(f32[4,128,128]{2,1,0:T(8,128)} %fusion.101, f32[]{:T(128)} %constant.75.clone.1), padding=0_1x0_0x0_0 | pad | bytes 589828 | tf_op jit(solution)/shard_map/concatenate | solution.py:180
  33.2 0.9 maximum_bitcast_fusion
  34.0 11.7 %all-to-all-done.1 = bf16[32,64,256]{2,0,1:T(8,128)(2,1)S(1)} async-done(((bf16[32,64,256]{2,0,1:T(8,128)(2,1)}), bf16[32,64,256]{2,0,1:T(8,128)(2,1)S(1)}, u32[]{:S(2)}, u32[]{:S(2)}) %all-to-all-start.1) | async-done | bytes 1048608 | tf_op jit(solution)/shard_map/all_to_all | solution.py:103
  45.7 0.6 convert_reduce_fusion
  46.4 0.6 copy.52
  47.0 0.3 copy.65
  47.3 6.3 %while.24 = (s32[]{:T(128)}, bf16[2,256,512]{1,2,0:T(8,128)(2,1)S(1)}, f32[2,4,512]{2,1,0:T(4,128)S(1)}, s32[2,4,512]{2,1,0:T(4,128)S(1)}, bf16[256,2048]{1,0:T(...) while((s32[]{:T(128)}, bf16[2,256,512]{1,2,0:T(8,128)(2,1)S(1)}, ...), condition=%wide.region_3.4_spmd.clone.clone, body=%wide.region_2.3_spmd.clone.clone.sunk | while | flops 2156920832 | bytes 7651509 | solution.py:78
  47.4 0.8 fusion.149
  48.2 0.8 fusion.150
  48.9 0.8 fusion.151
  49.7 0.8 fusion.152
  50.5 0.8 fusion.149
  51.3 0.8 fusion.150
  52.1 0.8 fusion.151
  52.8 0.8 fusion.152
  53.6 0.2 convert_reduce_fusion.2
  54.0 6.3 %while.25 = (s32[]{:T(128)}, bf16[2,256,512]{1,2,0:T(8,128)(2,1)S(1)}, f32[2,4,512]{2,1,0:T(4,128)S(1)}, s32[2,4,512]{2,1,0:T(4,128)S(1)}, bf16[256,2048]{1,0:T(...) while((s32[]{:T(128)}, bf16[2,256,512]{1,2,0:T(8,128)(2,1)S(1)}, ...), condition=%wide.region_6.7_spmd.clone.clone, body=%wide.region_5.6_spmd.clone.clone.sunk | while | flops 2156920832 | bytes 7651509 | solution.py:78
  54.0 0.8 fusion.161
  54.8 0.8 fusion.162
  55.6 0.8 fusion.163
  56.3 0.8 fusion.164
  57.2 0.8 fusion.161
  57.9 0.8 fusion.162
  58.7 0.8 fusion.163
  59.5 0.8 fusion.164
  60.3 0.2 convert_reduce_fusion.1
  60.5 1.1 convert_element_type.94
  61.5 1.3 %copy.53 = bf16[256,2048]{0,1:T(8,128)(2,1)} copy(bf16[256,2048]{1,0:T(8,128)(2,1)S(1)} %get-tuple-element.373) | data formatting | bytes 2097152 | tf_op jit(solution)/shard_map/reshape | solution.py:104
  62.9 0.3 copy.62
  63.2 0.2 fusion.97
  63.4 2.1 %fusion.98 = (bf16[2,256,512]{1,2,0:T(8,128)(2,1)}, bf16[2,256,512]{1,2,0:T(8,128)(2,1)}) fusion(bf16[1,256,1024]{1,2,0:T(8,128)(2,1)S(1)} %fusion.97, bf16[1,256,1024]{1,2,0:T(8,128)(2,1)} %maximum_bitcast_fusion), kind=kLoop, calls=%fused_computation.81 | loop fusion | flops 2097152 | bytes 2097152 | tf_op jit(solution)/shard_map/stack | solution.py:119
  65.6 0.7 collective-permute-start
  66.3 3.1 %collective-permute-start.1 = (bf16[2,256,512]{1,2,0:T(8,128)(2,1)}, bf16[2,256,512]{1,2,0:T(8,128)(2,1)}, u32[]{:S(2)}, u32[]{:S(2)}) collective-permute-start(bf16[2,256,512]{1,2,0:T(8,128)(2,1)} %get-tuple-element.196), channel_id=1, source_target_pairs={{1,0},{2,1},{3,2},{0,3},{5,4},{6,5},{7,6},{4,7},{9,8},{10,9},{11,1... | collective-permute-start | bytes 1572872 | tf_op jit(solution)/shard_map/ppermute | solution.py:124
  69.4 0.3 copy.61
  70.0 1.0 copy-done.1
  71.0 1.3 %fusion.96.st_ref = bf16[2048,256]{1,0:T(8,128)(2,1)} fusion(bf16[256,2048]{0,1:T(8,128)(2,1)S(1)} %copy-done.1, f32[2048]{0:T(1024)S(1)} %bitcast.213), kind=kLoop, calls=%fused_computation.72 | loop fusion | flops 1572864 | bytes 2105344 | tf_op jit(solution)/shard_map/transpose | solution.py:137
  72.3 1.1 pad_maximum_fusion.o_ref
  73.4 10.3 %shard_map.74.rest_0_ = f32[2048,256]{1,0:T(8,128)} custom-call(s32[256]{0:T(256)} %reshape.193.code_ref, bf16[2048,256]{1,0:T(8,128)(2,1)} %fusion.96.st_ref, bf16[256,2048]{1,0:T(8,128)(2,1)} %pad_maximum_fusion.o_ref, bf16[2048,256]{1,0:T(8,128)(2,1)} %bitcast.182, f32[5,128,128]{2,1,0:T(8,128)} %concatenate.34.taper_ref), custom_call_target="tpu_custom_call" | custom-call | flops 4294967296 | bytes 4194304 | tf_op jit(solution)/shard_map/pallas_call | solution.py:234
  83.7 1.1 slice_bitcast_fusion.1
  84.7 3.7 %collective-permute-done.1 = bf16[2,256,512]{1,2,0:T(8,128)(2,1)} collective-permute-done((bf16[2,256,512]{1,2,0:T(8,128)(2,1)}, bf16[2,256,512]{1,2,0:T(8,128)(2,1)}, u32[]{:S(2)}, u32[]{:S(2)}) %collective-permute-start.1) | collective-permute-done | bytes 524320 | tf_op jit(solution)/shard_map/ppermute | solution.py:124
  88.5 1.1 slice_bitcast_fusion
  89.6 0.9 pad_maximum_fusion.2
  90.4 1.0 copy.58.o_ref
  91.4 7.6 %shard_map.75 = bf16[2048,256]{1,0:T(8,128)(2,1)} custom-call(s32[128]{0:T(128)} %reshape.187.code_ref, bf16[2048,256]{1,0:T(8,128)(2,1)} %fusion.96.st_ref, bf16[256,1024]{1,0:T(8,128)(2,1)} %copy.58.o_ref, bf16[1024,256]{1,0:T(8,128)(2,1)} %get-tuple-element.216.it_ref, f32[5,128,128]{2,1,0:T(8,128)} %concatenate.34.taper_ref, ...), custom_call_target="tpu_custom_call" | custom-call | flops 2147483648 | bytes 4194304 | tf_op jit(solution)/shard_map/pallas_call | solution.py:234
  99.0 1.9 %copy.59 = bf16[256,8,256]{2,1,0:T(8,128)(2,1)S(1)} copy(bf16[256,8,256]{0,2,1:T(8,128)(2,1)} %bitcast.185) | data formatting | bytes 2097152 | tf_op jit(solution)/shard_map/reshape | solution.py:156
  100.9 19.9 %all_to_all.38 = bf16[256,8,256]{2,1,0:T(8,128)(2,1)S(1)} all-to-all(bf16[256,8,256]{2,1,0:T(8,128)(2,1)S(1)} %copy.59), channel_id=1, replica_groups=mesh['wide'=8,'lon'=4] {'wide'}, dimensions={0} | all-to-all | bytes 2097152 | tf_op jit(solution)/shard_map/all_to_all | solution.py:155
  120.8 1.1 copy.73
  (58 shorter events, 1.3 us)
Async XLA Ops:
  0.0 30.3 %copy-start = (f32[4,64,256]{2,1,0:T(8,128)S(1)}, f32[4,64,256]{2,1,0:T(8,128)}, u32[]{:S(2)}) copy-start(f32[4,64,256]{2,1,0:T(8,128)} %param.14) | copy-start | bytes 786436
  0.0 9.2 %copy-start.6 = (s32[1,16,16]{2,1,0:T(8,128)S(1)}, s32[1,16,16]{2,1,0:T(8,128)}, u32[]{:S(2)}) copy-start(s32[1,16,16]{2,1,0:T(8,128)} %param.17) | copy-start | bytes 3076
  0.0 9.2 %copy-start.7 = (s32[1,16]{1,0:T(1,128)S(1)}, s32[1,16]{1,0:T(1,128)}, u32[]{:S(2)}) copy-start(s32[1,16]{1,0:T(1,128)} %param.16) | copy-start | bytes 196
  0.0 9.3 %copy-start.5 = (s32[1,16,16]{2,1,0:T(8,128)S(1)}, s32[1,16,16]{2,1,0:T(8,128)}, u32[]{:S(2)}) copy-start(s32[1,16,16]{2,1,0:T(8,128)} %param.15) | copy-start | bytes 3076
  2.8 12.0 %all-to-all-start = ((bf16[4,2,2048]{2,1,0:T(2,128)(2,1)}), bf16[4,2,2048]{2,1,0:T(2,128)(2,1)S(1)}, u32[]{:S(2)}, u32[]{:S(2)}) async-start(bf16[4,2,2048]{2,1,0:T(2,128)(2,1)} %reshape.200), calls=%async_computation | async-start | bytes 65536 | tf_op jit(solution)/shard_map/all_to_all | solution.py:32
  23.7 6.7 %copy-start.4 = (bf16[256,8,256]{2,1,0:T(8,128)(2,1)S(1)}, bf16[256,8,256]{2,1,0:T(8,128)(2,1)}, u32[]{:S(2)}) copy-start(bf16[256,8,256]{2,1,0:T(8,128)(2,1)} %param.12) | copy-start | bytes 3145732
  26.6 19.1 %all-to-all-start.1 = ((bf16[32,64,256]{2,0,1:T(8,128)(2,1)}), bf16[32,64,256]{2,0,1:T(8,128)(2,1)S(1)}, u32[]{:S(2)}, u32[]{:S(2)}) async-start(bf16[32,64,256]{2,0,1:T(8,128)(2,1)} %copy.51), calls=%async_computation.1 | async-start | bytes 2097152 | tf_op jit(solution)/shard_map/all_to_all | solution.py:103
  31.2 15.8 %copy-start.3 = (bf16[256,8,256]{0,2,1:T(8,128)(2,1)}, bf16[256,8,256]{0,2,1:T(8,128)(2,1)S(1)}, u32[]{:S(2)}) copy-start(bf16[256,8,256]{0,2,1:T(8,128)(2,1)S(1)} %copy.54) | copy-start | bytes 3145732
  61.5 1.4 %copy-start.2 = (f32[2,256,512]{1,2,0:T(8,128)S(1)}, f32[2,256,512]{1,2,0:T(8,128)}, u32[]{:S(2)}) copy-start(f32[2,256,512]{1,2,0:T(8,128)} %convert_element_type.94) | copy-start | bytes 3145732
  65.6 18.1 %collective-permute-start = (bf16[2,256,512]{1,2,0:T(8,128)(2,1)}, bf16[2,256,512]{1,2,0:T(8,128)(2,1)}, u32[]{:S(2)}, u32[]{:S(2)}) collective-permute-start(bf16[2,256,512]{1,2,0:T(8,128)(2,1)} %get-tuple-element.195), channel_id=1, source_target_pairs={{0,1},{1,2},{2,3},{3,0},{4,5},{5,6},{6,7},{7,4},{8,9},{9,10},{10,1... | collective-permute-start | bytes 1572872 | tf_op jit(solution)/shard_map/ppermute | solution.py:123
  66.3 22.2 %collective-permute-start.1 = (bf16[2,256,512]{1,2,0:T(8,128)(2,1)}, bf16[2,256,512]{1,2,0:T(8,128)(2,1)}, u32[]{:S(2)}, u32[]{:S(2)}) collective-permute-start(bf16[2,256,512]{1,2,0:T(8,128)(2,1)} %get-tuple-element.196), channel_id=1, source_target_pairs={{1,0},{2,1},{3,2},{0,3},{5,4},{6,5},{7,6},{4,7},{9,8},{10,9},{11,1... | collective-permute-start | bytes 1572872 | tf_op jit(solution)/shard_map/ppermute | solution.py:124
  69.7 1.2 %copy-start.1 = (bf16[256,2048]{0,1:T(8,128)(2,1)S(1)}, bf16[256,2048]{0,1:T(8,128)(2,1)}, u32[]{:S(2)}) copy-start(bf16[256,2048]{0,1:T(8,128)(2,1)} %copy.53) | copy-start | bytes 3145732

commit v8 on v7

--- a/solution.py
+++ b/solution.py
@@ -134,24 +134,22 @@
     own_code = code[:, halo_blocks:halo_blocks + block_count]
     halo_code = jnp.concatenate([code[:, :halo_blocks], code[:, halo_blocks + block_count:]], axis=1)
     tiles = taper_table(BLK, members)
-    state_t = model_anomaly.T
     partial = update_call(
-        own_code.reshape(-1), state_t, None, None, obs_dev, innov_flat.T, tiles, block_count, block_count
+        own_code.reshape(-1), model_anomaly, None, None, obs_dev, innov_flat, tiles, block_count, block_count
     )
     halo_obs = jnp.concatenate([west[0], east[0]], axis=1)
     halo_innov = jnp.concatenate([west[1], east[1]], axis=1)
-    result_t = update_call(
+    result = update_call(
         halo_code.reshape(-1),
-        state_t,
+        model_anomaly,
         partial,
-        region_state.T,
+        region_state,
         halo_obs,
-        halo_innov.T,
+        halo_innov,
         tiles,
         block_count,
         2 * halo_blocks,
     )
-    result = result_t.T
     return lax.all_to_all(
         result.reshape(members, band_rows, patch_meridian_lines),
         "wide",
@@ -183,48 +181,52 @@
 GROUP = 4
 
 
-def update_call(code, state_t, partial, anchor_t, cand_obs, cand_innov_t, tiles, block_count, candidate_count):
-    cells, members = state_t.shape
+def update_call(code, state, partial, anchor, cand_obs, cand_innov, tiles, block_count, candidate_count):
+    members, cells = state.shape
     rows = GROUP * BLK
     width = candidate_count * BLK
-    final = anchor_t is not None
-
-    def kernel(code_ref, st_ref, o_ref, it_ref, taper_ref, *rest):
+    final = anchor is not None
+
+    def kernel(code_ref, s_ref, o_ref, i_ref, taper_ref, *rest):
         if final:
-            part_ref, ft_ref, out_ref, cov_scr, tap_scr = rest
+            part_ref, f_ref, out_ref, cov_scr, tap_scr = rest
         else:
             out_ref, cov_scr, tap_scr = rest
         g = pl.program_id(0)
-        cov_scr[...] = jnp.dot(st_ref[...], o_ref[...], preferred_element_type=jnp.float32)
+        cov_scr[...] = lax.dot_general(
+            s_ref[...], o_ref[...], (((0,), (0,)), ((), ())), preferred_element_type=jnp.float32
+        )
         for sl in range(GROUP):
             s = g * GROUP + sl
             for b in range(candidate_count):
                 c = code_ref[s * candidate_count + b]
                 tile = cov_scr[sl * BLK:(sl + 1) * BLK, b * BLK:(b + 1) * BLK] * taper_ref[c]
                 tap_scr[sl * BLK:(sl + 1) * BLK, b * BLK:(b + 1) * BLK] = tile.astype(jnp.bfloat16)
-        change = jnp.dot(tap_scr[...], it_ref[...], preferred_element_type=jnp.float32)
+        change = lax.dot_general(
+            i_ref[...], tap_scr[...], (((1,), (1,)), ((), ())), preferred_element_type=jnp.float32
+        )
         if final:
             total = part_ref[...] + change
-            out_ref[...] = (ft_ref[...].astype(jnp.float32) + total).astype(jnp.bfloat16)
+            out_ref[...] = (f_ref[...].astype(jnp.float32) + total).astype(jnp.bfloat16)
         else:
             out_ref[...] = change
 
-    row_spec = pl.BlockSpec((rows, members), lambda g, code: (g, 0))
+    col_spec = pl.BlockSpec((members, rows), lambda g, code: (0, g))
     in_specs = [
-        row_spec,
+        col_spec,
         pl.BlockSpec((members, width), lambda g, code: (0, 0)),
-        pl.BlockSpec((width, members), lambda g, code: (0, 0)),
+        pl.BlockSpec((members, width), lambda g, code: (0, 0)),
         pl.BlockSpec(tiles.shape, lambda g, code: (0, 0, 0)),
     ]
-    operands = [state_t, cand_obs, cand_innov_t, tiles]
+    operands = [state, cand_obs, cand_innov, tiles]
     if final:
-        in_specs += [row_spec, row_spec]
-        operands += [partial, anchor_t]
+        in_specs += [col_spec, col_spec]
+        operands += [partial, anchor]
     grid_spec = pltpu.PrefetchScalarGridSpec(
         num_scalar_prefetch=1,
         grid=(block_count // GROUP,),
         in_specs=in_specs,
-        out_specs=row_spec,
+        out_specs=col_spec,
         scratch_shapes=[
             pltpu.VMEM((rows, width), jnp.float32),
             pltpu.VMEM((rows, width), jnp.bfloat16),
@@ -234,7 +236,7 @@
     return pl.pallas_call(
         kernel,
         grid_spec=grid_spec,
-        out_shape=jax.ShapeDtypeStruct((cells, members), out_type),
+        out_shape=jax.ShapeDtypeStruct((members, cells), out_type),
         cost_estimate=pl.CostEstimate(flops=4 * cells * members * width, transcendentals=0, bytes_accessed=8 * cells * members),
     )(code, *operands)
 

time: 123 us -> 120 us (0.976)
  waiting for transfers between devices: 17.6 us -> 21.3 us
  Pallas kernels: 24.2 us -> 21.4 us
  local copies, waits for them, and re-layouts: 22.8 us -> 20.1 us
  starting transfers between devices: 13.9 us -> 12.1 us
    ppermute x1, waiting for transfers between devices: 0.01 us -> 6.46 us  [body(): west = lax.ppermute(edges[:, :, halo:], 'lon', up)]
    ppermute x1, waiting for transfers between devices: 3.74 us -> 0.32 us  [body(): east = lax.ppermute(edges[:, :, :halo], 'lon', down)]
    reshape x2 -> x0, local copies, waits for them, and re-layouts: 3.16 us -> none  [the longest x1 1.86 us: body(): result.reshape(members, band_rows, patch_meridian_lines)]
    pallas_call x2, Pallas kernels: 17.9 us -> 15 us  [update_call(): pl.pallas_call(kernel, grid_spec=grid_spec, out_shape=jax.ShapeDtypeStruc...]
    ppermute x1, starting transfers between devices: 3.08 us -> 0.66 us  [body(): east = lax.ppermute(edges[:, :, :halo], 'lon', down)]
    all_to_all x1, waiting for transfers between devices: 2.14 us -> 3.64 us  [column_halo(): got = lax.all_to_all(spread, axis, 0, 0, tiled=False)]
    transpose x1 -> x0, other arithmetic: 1.33 us -> none  [body(): state_t = model_anomaly.T]
    unnamed x29 -> x28, local copies, waits for them, and re-layouts: 3.57 us -> 4.06 us
  transfers between devices with their start and end apart: 4 -> 4, of which waited for: 3 -> 4; matrix products, arithmetic and copies ran while one was open for 9% -> 9% of each run, Pallas kernels for 8% -> 7%
where the time goes in v8:
time: 120 us; the launch traced here: 119 us
  Pallas kernels  21.4 us (18%)
  waiting for transfers between devices  21.3 us (18%)
  local copies, waits for them, and re-layouts  20.1 us (17%)
  blocking collectives  20 us (17%)
  starting transfers between devices  12.1 us (10%)
  matrix products  12.1 us (10%)
  other arithmetic  11.9 us (10%)
    all_to_all x1, blocking collectives, body(): lax.all_to_all(result.reshape(members, band_rows, patch_meridian_lines),...  20 us
    pallas_call x2, Pallas kernels, update_call(): pl.pallas_call(kernel, grid_spec=grid_spec, out_shape=jax.ShapeDtypeStruc...  15 us
    dot_general x16, matrix products, observe_one_block(): picked = jnp.dot(state, selector, preferred_element_type=jnp.float32)  12.1 us
    all_to_all x1, waiting for transfers between devices, body(): lax.all_to_all(prediction_increment, 'wide', split_axis=1, concat_axis=0,...  10.9 us
    ppermute x1, waiting for transfers between devices, body(): west = lax.ppermute(edges[:, :, halo:], 'lon', up)  6.46 us
    pallas_call x1, Pallas kernels, forecast_call(): pl.pallas_call(kernel, out_shape=jax.ShapeDtypeStruct(state.shape, jnp.bf...  6.33 us
    all_to_all x1, starting transfers between devices, column_halo(): got = lax.all_to_all(spread, axis, 0, 0, tiled=False)  6.32 us
    unnamed x28, local copies, waits for them, and re-layouts  4.06 us
  transfers between devices with their start and end apart: 4, of which 4 were waited for; matrix products, arithmetic and copies ran while one was open for 9% of the time, Pallas kernels for 7%

profile of v8, /device:TPU:0, one launch (start us, length us, event | category | flops | bytes accessed | tf_op | source)
XLA Modules:
  0.0 119.4 jit_solution(9741795070537170318)
XLA Ops:
  0.0 1.5 %fusion.102 = (bf16[32,64,1]{2,1,0:T(8,128)(2,1)S(1)}, bf16[32,64,1]{2,1,0:T(8,128)(2,1)S(1)}) fusion(bf16[32,64,256]{2,1,0:T(8,128)(2,1)} %x_ref.1), kind=kLoop, calls=%fused_computation.114 | loop fusion | bytes 16384 | tf_op jit(solution)/shard_map/slice | solution.py:30
  1.5 0.3 copy.42
  1.8 0.3 copy.41
  2.1 0.7 reshape.200
  2.8 6.3 %all-to-all-start = ((bf16[4,2,2048]{2,1,0:T(2,128)(2,1)}), bf16[4,2,2048]{2,1,0:T(2,128)(2,1)S(1)}, u32[]{:S(2)}, u32[]{:S(2)}) async-start(bf16[4,2,2048]{2,1,0:T(2,128)(2,1)} %reshape.200), calls=%async_computation | async-start | bytes 65536 | tf_op jit(solution)/shard_map/all_to_all | solution.py:32
  9.6 0.8 fusion.99
  10.6 0.6 reshape.187.code_ref
  11.2 3.6 %all-to-all-done = bf16[4,2,2048]{2,1,0:T(2,128)(2,1)S(1)} async-done(((bf16[4,2,2048]{2,1,0:T(2,128)(2,1)}), bf16[4,2,2048]{2,1,0:T(2,128)(2,1)S(1)}, u32[]{:S(2)}, u32[]{:S(2)}) %all-to-all-start) | async-done | bytes 32800 | tf_op jit(solution)/shard_map/all_to_all | solution.py:32
  14.9 0.3 copy.30
  15.3 1.0 slice.190.w_ref
  16.3 1.1 copy.31
  17.4 6.3 %shard_map.73 = bf16[32,64,256]{2,1,0:T(8,128)(2,1)} custom-call(bf16[32,64,256]{2,1,0:T(8,128)(2,1)} %x_ref.1, bf16[32,64,1]{2,1,0:T(8,128)(2,1)} %slice.190.w_ref, bf16[32,64,1]{2,1,0:T(8,128)(2,1)} %bitcast.173), custom_call_target="tpu_custom_call" | custom-call | tf_op jit(solution)/shard_map/pallas_call | solution.py:57
  23.7 2.9 %copy.32 = bf16[32,64,256]{2,0,1:T(8,128)(2,1)} copy(bf16[32,64,256]{2,1,0:T(8,128)(2,1)} %shard_map.73) | data formatting | bytes 2097152 | tf_op jit(solution)/shard_map/pallas_call | solution.py:57
  26.6 3.7 %all-to-all-start.1 = ((bf16[32,64,256]{2,0,1:T(8,128)(2,1)}), bf16[32,64,256]{2,0,1:T(8,128)(2,1)S(1)}, u32[]{:S(2)}, u32[]{:S(2)}) async-start(bf16[32,64,256]{2,0,1:T(8,128)(2,1)} %copy.32), calls=%async_computation.1 | async-start | bytes 2097152 | tf_op jit(solution)/shard_map/all_to_all | solution.py:103
  30.4 0.8 subtract_bitcast_fusion
  31.2 0.3 copy.48
  31.5 0.7 reshape.193.code_ref
  32.2 1.7 %concatenate.34.taper_ref = f32[5,128,128]{2,1,0:T(8,128)} pad(f32[4,128,128]{2,1,0:T(8,128)} %fusion.99, f32[]{:T(128)} %constant.75.clone.1), padding=0_1x0_0x0_0 | pad | bytes 589828 | tf_op jit(solution)/shard_map/concatenate | solution.py:178
  34.0 0.9 maximum_bitcast_fusion
  34.9 10.9 %all-to-all-done.1 = bf16[32,64,256]{2,0,1:T(8,128)(2,1)S(1)} async-done(((bf16[32,64,256]{2,0,1:T(8,128)(2,1)}), bf16[32,64,256]{2,0,1:T(8,128)(2,1)S(1)}, u32[]{:S(2)}, u32[]{:S(2)}) %all-to-all-start.1) | async-done | bytes 1048608 | tf_op jit(solution)/shard_map/all_to_all | solution.py:103
  45.7 0.6 copy.33
  46.4 0.6 convert_reduce_fusion
  47.0 0.3 copy.43
  47.4 6.3 %while.24 = (s32[]{:T(128)}, bf16[2,256,512]{1,2,0:T(8,128)(2,1)S(1)}, f32[2,4,512]{2,1,0:T(4,128)S(1)}, s32[2,4,512]{2,1,0:T(4,128)S(1)}, bf16[256,2048]{1,0:T(...) while((s32[]{:T(128)}, bf16[2,256,512]{1,2,0:T(8,128)(2,1)S(1)}, ...), condition=%wide.region_3.4_spmd.clone.clone, body=%wide.region_2.3_spmd.clone.clone.sunk | while | flops 2156920832 | bytes 7651509 | solution.py:78
  47.4 0.8 fusion.147
  48.2 0.8 fusion.148
  49.0 0.8 fusion.149
  49.7 0.8 fusion.150
  50.6 0.8 fusion.147
  51.3 0.8 fusion.148
  52.1 0.8 fusion.149
  52.8 0.8 fusion.150
  53.7 0.2 convert_reduce_fusion.2
  54.0 6.3 %while.25 = (s32[]{:T(128)}, bf16[2,256,512]{1,2,0:T(8,128)(2,1)S(1)}, f32[2,4,512]{2,1,0:T(4,128)S(1)}, s32[2,4,512]{2,1,0:T(4,128)S(1)}, bf16[256,2048]{1,0:T(...) while((s32[]{:T(128)}, bf16[2,256,512]{1,2,0:T(8,128)(2,1)S(1)}, ...), condition=%wide.region_6.7_spmd.clone.clone, body=%wide.region_5.6_spmd.clone.clone.sunk | while | flops 2156920832 | bytes 7651509 | solution.py:78
  54.0 0.8 fusion.159
  54.8 0.8 fusion.160
  55.6 0.8 fusion.161
  56.3 0.8 fusion.162
  57.2 0.8 fusion.159
  57.9 0.8 fusion.160
  58.7 0.8 fusion.161
  59.5 0.8 fusion.162
  60.2 1.1 convert_element_type.94
  61.3 0.2 convert_reduce_fusion.1
  61.5 1.2 %subtract_convert_fusion.s_ref = bf16[256,2048]{1,0:T(8,128)(2,1)} fusion(bf16[256,2048]{1,0:T(8,128)(2,1)S(1)} %get-tuple-element.363, f32[2048]{0:T(1024)S(1)} %bitcast.203), kind=kLoop, calls=%fused_computation.70 | loop fusion | flops 1572864 | bytes 2105344 | tf_op jit(solution)/shard_map/convert_element_type | solution.py:84
  62.7 0.3 copy.38
  63.2 2.1 %fusion.96 = (bf16[2,256,512]{2,1,0:T(8,128)(2,1)}, bf16[2,256,512]{2,1,0:T(8,128)(2,1)}) fusion(bf16[1,256,1024]{2,1,0:T(8,128)(2,1)S(1)} %subtract_convert_fusion.3, bf16[1,256,1024]{2,1,0:T(8,128)(2,1)} %maximum_bitcast_fusion), kind=kLoop, calls=%fused_computation.79 | loop fusion | flops 2097152 | bytes 2097152 | tf_op jit(solution)/shard_map/stack | solution.py:119
  65.3 0.7 collective-permute-start.1
  66.0 1.4 %collective-permute-start = (bf16[2,256,512]{2,1,0:T(8,128)(2,1)}, bf16[2,256,512]{2,1,0:T(8,128)(2,1)}, u32[]{:S(2)}, u32[]{:S(2)}) collective-permute-start(bf16[2,256,512]{2,1,0:T(8,128)(2,1)} %get-tuple-element.185), channel_id=1, source_target_pairs={{0,1},{1,2},{2,3},{3,0},{4,5},{5,6},{6,7},{7,4},{8,9},{9,10},{10,1... | collective-permute-start | bytes 1572872 | tf_op jit(solution)/shard_map/ppermute | solution.py:123
  67.3 0.3 copy.39
  67.8 0.9 fusion.103
  68.6 0.4 copy-done.1
  69.1 0.3 copy.40
  69.5 2.1 %pad_maximum_fusion.o_ref = bf16[256,2048]{1,0:T(8,128)(2,1)} fusion(bf16[256,512]{1,0:T(8,128)(2,1)} %get-tuple-element.192, bf16[256,1024]{1,0:T(8,128)(2,1)S(1)} %subtract_convert_fusion.1, bf16[256,512]{1,0:T(8,128)(2,1)} %get-tuple-element.191), kind=kLoop, calls=%fused_computation.74 | loop fusion | flops 3145728 | bytes 2097152 | tf_op jit(solution)/shard_map/concatenate | solution.py:128
  71.7 8.4 %shard_map.74.rest_0_ = f32[256,2048]{1,0:T(8,128)} custom-call(s32[256]{0:T(256)} %reshape.193.code_ref, bf16[256,2048]{1,0:T(8,128)(2,1)} %subtract_convert_fusion.s_ref, bf16[256,2048]{1,0:T(8,128)(2,1)} %pad_maximum_fusion.o_ref, bf16[256,2048]{1,0:T(8,128)(2,1)} %bitcast.171, f32[5,128,128]{2,1,0:T(8,128)} %concatenate.34.taper_ref), custom_call_target="tpu_custom_call" | custom-call | flops 4294967296 | bytes 4194304 | tf_op jit(solution)/shard_map/pallas_call | solution.py:236
  80.1 0.3 collective-permute-done.1
  80.4 1.1 slice_bitcast_fusion
  81.5 6.5 %collective-permute-done = bf16[2,256,512]{2,1,0:T(8,128)(2,1)} collective-permute-done((bf16[2,256,512]{2,1,0:T(8,128)(2,1)}, bf16[2,256,512]{2,1,0:T(8,128)(2,1)}, u32[]{:S(2)}, u32[]{:S(2)}) %collective-permute-start) | collective-permute-done | bytes 524320 | tf_op jit(solution)/shard_map/ppermute | solution.py:123
  87.9 1.1 slice_bitcast_fusion.1
  89.0 1.2 pad_maximum_fusion.2
  90.2 6.6 %shard_map.75 = bf16[256,2048]{1,0:T(8,128)(2,1)} custom-call(s32[128]{0:T(128)} %reshape.187.code_ref, bf16[256,2048]{1,0:T(8,128)(2,1)} %subtract_convert_fusion.s_ref, bf16[256,1024]{1,0:T(8,128)(2,1)} %get-tuple-element.205.o_ref, bf16[256,1024]{1,0:T(8,128)(2,1)} %get-tuple-element.206.i_ref, f32[5,128,128]{2,1,0:T(8,128)} %concatenate.34.taper_ref, ...), custom_call_target="tpu_custom_call" | custom-call | flops 2147483648 | bytes 4194304 | tf_op jit(solution)/shard_map/pallas_call | solution.py:236
  96.8 1.5 %copy.50 = bf16[32,8,8,256]{3,2,1,0:T(8,128)(2,1)S(1)} copy(bf16[32,8,8,256]{3,1,2,0:T(8,128)(2,1)} %bitcast.175) | data formatting | bytes 2097152
  98.3 20.0 %all_to_all.38 = bf16[256,8,256]{2,1,0:T(8,128)(2,1)S(1)} all-to-all(bf16[256,8,256]{2,1,0:T(8,128)(2,1)S(1)} %bitcast.168), channel_id=1, replica_groups=mesh['wide'=8,'lon'=4] {'wide'}, dimensions={0} | all-to-all | bytes 2097152 | tf_op jit(solution)/shard_map/all_to_all | solution.py:153
  118.3 1.1 copy.53
  (55 shorter events, 1.3 us)
Async XLA Ops:
  0.0 9.5 %copy-start = (f32[4,64,256]{2,1,0:T(8,128)S(1)}, f32[4,64,256]{2,1,0:T(8,128)}, u32[]{:S(2)}) copy-start(f32[4,64,256]{2,1,0:T(8,128)} %param.14) | copy-start | bytes 786436
  0.0 9.2 %copy-start.5 = (s32[1,16,16]{2,1,0:T(8,128)S(1)}, s32[1,16,16]{2,1,0:T(8,128)}, u32[]{:S(2)}) copy-start(s32[1,16,16]{2,1,0:T(8,128)} %param.17) | copy-start | bytes 3076
  0.0 9.2 %copy-start.6 = (s32[1,16]{1,0:T(1,128)S(1)}, s32[1,16]{1,0:T(1,128)}, u32[]{:S(2)}) copy-start(s32[1,16]{1,0:T(1,128)} %param.16) | copy-start | bytes 196
  0.0 9.3 %copy-start.4 = (s32[1,16,16]{2,1,0:T(8,128)S(1)}, s32[1,16,16]{2,1,0:T(8,128)}, u32[]{:S(2)}) copy-start(s32[1,16,16]{2,1,0:T(8,128)} %param.15) | copy-start | bytes 3076
  2.8 12.0 %all-to-all-start = ((bf16[4,2,2048]{2,1,0:T(2,128)(2,1)}), bf16[4,2,2048]{2,1,0:T(2,128)(2,1)S(1)}, u32[]{:S(2)}, u32[]{:S(2)}) async-start(bf16[4,2,2048]{2,1,0:T(2,128)(2,1)} %reshape.200), calls=%async_computation | async-start | bytes 65536 | tf_op jit(solution)/shard_map/all_to_all | solution.py:32
  23.7 7.4 %copy-start.3 = (bf16[256,8,256]{2,1,0:T(8,128)(2,1)S(1)}, bf16[256,8,256]{2,1,0:T(8,128)(2,1)}, u32[]{:S(2)}) copy-start(bf16[256,8,256]{2,1,0:T(8,128)(2,1)} %param.12) | copy-start | bytes 3145732
  26.6 19.1 %all-to-all-start.1 = ((bf16[32,64,256]{2,0,1:T(8,128)(2,1)}), bf16[32,64,256]{2,0,1:T(8,128)(2,1)S(1)}, u32[]{:S(2)}, u32[]{:S(2)}) async-start(bf16[32,64,256]{2,0,1:T(8,128)(2,1)} %copy.32), calls=%async_computation.1 | async-start | bytes 2097152 | tf_op jit(solution)/shard_map/all_to_all | solution.py:103
  31.5 14.9 %copy-start.2 = (bf16[32,8,8,256]{3,1,2,0:T(8,128)(2,1)}, bf16[32,8,8,256]{3,1,2,0:T(8,128)(2,1)S(1)}, u32[]{:S(2)}) copy-start(bf16[32,8,8,256]{3,1,2,0:T(8,128)(2,1)S(1)} %copy.48) | copy-start | bytes 3145732
  65.3 15.1 %collective-permute-start.1 = (bf16[2,256,512]{2,1,0:T(8,128)(2,1)}, bf16[2,256,512]{2,1,0:T(8,128)(2,1)}, u32[]{:S(2)}, u32[]{:S(2)}) collective-permute-start(bf16[2,256,512]{2,1,0:T(8,128)(2,1)} %get-tuple-element.186), channel_id=1, source_target_pairs={{1,0},{2,1},{3,2},{0,3},{5,4},{6,5},{7,6},{4,7},{9,8},{10,9},{11,1... | collective-permute-start | bytes 1572872 | tf_op jit(solution)/shard_map/ppermute | solution.py:124
  66.0 22.0 %collective-permute-start = (bf16[2,256,512]{2,1,0:T(8,128)(2,1)}, bf16[2,256,512]{2,1,0:T(8,128)(2,1)}, u32[]{:S(2)}, u32[]{:S(2)}) collective-permute-start(bf16[2,256,512]{2,1,0:T(8,128)(2,1)} %get-tuple-element.185), channel_id=1, source_target_pairs={{0,1},{1,2},{2,3},{3,0},{4,5},{5,6},{6,7},{7,4},{8,9},{9,10},{10,1... | collective-permute-start | bytes 1572872 | tf_op jit(solution)/shard_map/ppermute | solution.py:123
  67.7 1.4 %copy-start.1 = (f32[2,256,512]{1,2,0:T(8,128)S(1)}, f32[2,256,512]{1,2,0:T(8,128)}, u32[]{:S(2)}) copy-start(f32[2,256,512]{1,2,0:T(8,128)} %convert_element_type.94) | copy-start | bytes 3145732

commit v9 on v8

--- a/solution.py
+++ b/solution.py
@@ -79,6 +79,32 @@
     return result.transpose(1, 0, 2).reshape(members, count)
 
 
+OBS_STEP = 256
+def observe_dev_call(state, index, weight):
+    members, cells = state.shape
+    count = index.shape[1]
+    def kernel(f_ref, i_ref, w_ref, o_ref):
+        cell_ids = lax.broadcasted_iota(jnp.int32, (cells, OBS_STEP), 0)
+        f = f_ref[...]
+        summed = jnp.zeros((members, OBS_STEP), jnp.float32)
+        for k in range(4):
+            selector = (cell_ids == i_ref[k:k + 1, :]).astype(jnp.bfloat16)
+            picked = jnp.dot(f, selector, preferred_element_type=jnp.float32)
+            summed = summed + w_ref[k:k + 1, :] * picked
+        ens = summed.astype(jnp.bfloat16).astype(jnp.float32)
+        mean = jnp.sum(ens, axis=0, keepdims=True) / members
+        o_ref[...] = (ens - mean).astype(jnp.bfloat16)
+    return pl.pallas_call(
+        kernel,
+        grid=(count // OBS_STEP,),
+        in_specs=[
+            pl.BlockSpec((members, cells), lambda j: (0, 0)),
+            pl.BlockSpec((4, OBS_STEP), lambda j: (0, j)),
+            pl.BlockSpec((4, OBS_STEP), lambda j: (0, j)),
+        ],
+        out_specs=pl.BlockSpec((members, OBS_STEP), lambda j: (0, j)),
+        out_shape=jax.ShapeDtypeStruct((members, count), jnp.bfloat16),
+    )(state, index, weight)
 def anomaly_from_mean(state_values):
     centred = state_values.astype(jnp.float32)
     return (centred - jnp.mean(centred, axis=-2, keepdims=True)).astype(jnp.bfloat16)
@@ -114,7 +140,7 @@
     innov_flat = innov.reshape(members, patch_gridpoints)
     edge_index = jnp.concatenate([local_index[:, :halo], local_index[:, -halo:]], axis=1)
     edge_weight = jnp.concatenate([local_weight[:, :halo], local_weight[:, -halo:]], axis=1)
-    edge_dev = anomaly_from_mean(observe_region(region_state, edge_index, edge_weight))
+    edge_dev = observe_dev_call(region_state, edge_index, edge_weight)
     edge_innov = jnp.concatenate([innov_flat[:, :halo], innov_flat[:, -halo:]], axis=1)
     edges = jnp.stack([edge_dev, edge_innov])
     lon_size = lax.axis_size("lon")
@@ -122,9 +148,7 @@
     down = [(j, i) for i, j in up]
     west = lax.ppermute(edges[:, :, halo:], "lon", up)
     east = lax.ppermute(edges[:, :, :halo], "lon", down)
-    middle_dev = anomaly_from_mean(
-        observe_region(region_state, local_index[:, halo:-halo], local_weight[:, halo:-halo])
-    )
+    middle_dev = observe_dev_call(region_state, local_index[:, halo:-halo], local_weight[:, halo:-halo])
     obs_dev = jnp.concatenate([edge_dev[:, :halo], middle_dev, edge_dev[:, halo:]], axis=1)
     model_anomaly = anomaly_from_mean(region_state)
     halo_blocks = halo // BLK

time: 120 us -> 112 us (0.933)
  Pallas kernels: 21.4 us -> 36.5 us
  matrix products: 12.1 us -> 0 us
  waiting for transfers between devices: 21.3 us -> 14.7 us
  other arithmetic: 11.9 us -> 8.45 us
  local copies, waits for them, and re-layouts: 20.1 us -> 17.8 us
  starting transfers between devices: 12.1 us -> 13.9 us
    pallas_call x0 -> x2, Pallas kernels: none -> 14.8 us  [observe_dev_call(): pl.pallas_call(kernel, grid=(count // OBS_STEP,), in_specs=[pl.BlockSpec(...]
    dot_general x16 -> x0, matrix products: 12.1 us -> none  [observe_one_block(): picked = jnp.dot(state, selector, preferred_element_type=jnp.float32)]
    ppermute x1, waiting for transfers between devices: 6.46 us -> 0.01 us  [body(): west = lax.ppermute(edges[:, :, halo:], 'lon', up)]
    another operation x2, other arithmetic: 2.99 us -> 0.14 us  [body(): edges = jnp.stack([edge_dev, edge_innov])]
    ppermute x1, starting transfers between devices: 0.66 us -> 3.08 us  [body(): east = lax.ppermute(edges[:, :, :halo], 'lon', down)]
    all_to_all x1, waiting for transfers between devices: 3.64 us -> 1.33 us  [column_halo(): got = lax.all_to_all(spread, axis, 0, 0, tiled=False)]
    squeeze x2, local copies, waits for them, and re-layouts: 2.13 us -> 0.07 us  [body(): halo_innov = jnp.concatenate([west[1], east[1]], axis=1)]
    all_to_all x1, waiting for transfers between devices: 10.9 us -> 12.6 us  [body(): lax.all_to_all(prediction_increment, 'wide', split_axis=1, concat_axis=0,...]
  transfers between devices with their start and end apart: 4 -> 4, of which waited for: 4 -> 3; matrix products, arithmetic and copies ran while one was open for 9% -> 8% of each run, Pallas kernels for 7% -> 14%
where the time goes in v9:
time: 112 us
  Pallas kernels  36.5 us (33%)
  blocking collectives  20 us (18%)
  local copies, waits for them, and re-layouts  17.8 us (16%)
  waiting for transfers between devices  14.7 us (13%)
  starting transfers between devices  13.9 us (12%)
  other arithmetic  8.45 us (8%)
    all_to_all x1, blocking collectives, body(): lax.all_to_all(result.reshape(members, band_rows, patch_meridian_lines),...  20 us
    pallas_call x2, Pallas kernels, update_call(): pl.pallas_call(kernel, grid_spec=grid_spec, out_shape=jax.ShapeDtypeStruc...  15.3 us
    pallas_call x2, Pallas kernels, observe_dev_call(): pl.pallas_call(kernel, grid=(count // OBS_STEP,), in_specs=[pl.BlockSpec(...  14.8 us
    all_to_all x1, waiting for transfers between devices, body(): lax.all_to_all(prediction_increment, 'wide', split_axis=1, concat_axis=0,...  12.6 us
    pallas_call x1, Pallas kernels, forecast_call(): pl.pallas_call(kernel, out_shape=jax.ShapeDtypeStruct(state.shape, jnp.bf...  6.33 us
    all_to_all x1, starting transfers between devices, column_halo(): got = lax.all_to_all(spread, axis, 0, 0, tiled=False)  6.32 us
    unnamed x30, local copies, waits for them, and re-layouts  4.59 us
    all_to_all x1, starting transfers between devices, body(): lax.all_to_all(prediction_increment, 'wide', split_axis=1, concat_axis=0,...  3.72 us
  transfers between devices with their start and end apart: 4, of which 3 were waited for; matrix products, arithmetic and copies ran while one was open for 8% of the time, Pallas kernels for 14%

profile of v9, /device:TPU:0, one launch (start us, length us, event | category | flops | bytes accessed | tf_op | source)
XLA Modules:
  0.0 111.5 jit_solution(485029348644276692)
XLA Ops:
  0.0 0.0 copy-start
  0.0 0.0 copy-start.8
  0.0 0.0 copy-start.7
  0.0 0.0 copy-start.6
  0.0 0.0 copy-start.4
  0.0 1.5 %fusion.6 = (bf16[32,64,1]{2,1,0:T(8,128)(2,1)S(1)}, bf16[32,64,1]{2,1,0:T(8,128)(2,1)S(1)}) fusion(bf16[32,64,256]{2,1,0:T(8,128)(2,1)} %x_ref.1), kind=kLoop, calls=%fused_computation.37 | loop fusion | bytes 16384 | tf_op jit(solution)/shard_map/slice | solution.py:30
  1.6 0.3 copy.26
  1.9 0.3 copy.27
  2.2 0.7 reshape.84
  2.9 6.3 %all-to-all-start = ((bf16[4,2,2048]{2,1,0:T(2,128)(2,1)}), bf16[4,2,2048]{2,1,0:T(2,128)(2,1)S(1)}, u32[]{:S(2)}, u32[]{:S(2)}) async-start(bf16[4,2,2048]{2,1,0:T(2,128)(2,1)} %reshape.84), calls=%async_computation | async-start | bytes 65536 | tf_op jit(solution)/shard_map/all_to_all | solution.py:32
  9.3 0.8 subtract_bitcast_fusion
  10.1 0.0 copy-done.8
  10.1 0.0 copy-done.7
  10.1 0.1 fusion.4
  10.2 0.0 copy-done.6
  10.2 0.1 select_reduce_fusion
  10.3 0.1 fusion.10
  10.4 0.8 fusion.3
  11.2 0.0 copy-done
  11.3 0.6 slice.110.i_ref
  11.9 0.1 slice.108
  11.9 0.6 slice.111.w_ref
  12.5 0.0 copy-done.4
  12.6 0.3 copy.32
  12.9 0.0 copy-start.3
  12.9 0.7 reshape.82.code_ref
  13.5 1.3 %all-to-all-done = bf16[4,2,2048]{2,1,0:T(2,128)(2,1)S(1)} async-done(((bf16[4,2,2048]{2,1,0:T(2,128)(2,1)}), bf16[4,2,2048]{2,1,0:T(2,128)(2,1)S(1)}, u32[]{:S(2)}, u32[]{:S(2)}) %all-to-all-start) | async-done | bytes 32800 | tf_op jit(solution)/shard_map/all_to_all | solution.py:32
  14.9 0.1 reshape.85
  15.0 0.3 copy.21
  15.3 1.0 slice.94.w_ref
  16.4 1.1 copy.22
  17.4 6.3 %shard_map.73 = bf16[32,64,256]{2,1,0:T(8,128)(2,1)} custom-call(bf16[32,64,256]{2,1,0:T(8,128)(2,1)} %x_ref.1, bf16[32,64,1]{2,1,0:T(8,128)(2,1)} %slice.94.w_ref, bf16[32,64,1]{2,1,0:T(8,128)(2,1)} %bitcast.61), custom_call_target="tpu_custom_call" | custom-call | tf_op jit(solution)/shard_map/pallas_call | solution.py:57
  23.8 2.8 %copy.23 = bf16[32,64,256]{2,0,1:T(8,128)(2,1)} copy(bf16[32,64,256]{2,1,0:T(8,128)(2,1)} %shard_map.73) | data formatting | bytes 2097152 | tf_op jit(solution)/shard_map/pallas_call | solution.py:57
  26.6 3.7 %all-to-all-start.1 = ((bf16[32,64,256]{2,0,1:T(8,128)(2,1)}), bf16[32,64,256]{2,0,1:T(8,128)(2,1)S(1)}, u32[]{:S(2)}, u32[]{:S(2)}) async-start(bf16[32,64,256]{2,0,1:T(8,128)(2,1)} %copy.23), calls=%async_computation.1 | async-start | bytes 2097152 | tf_op jit(solution)/shard_map/all_to_all | solution.py:129
  30.3 0.1 pad_add_fusion.1
  30.4 0.6 reshape.78.code_ref
  31.0 0.0 copy-done.5
  31.0 0.8 concatenate.34.taper_ref
  31.8 0.6 pad_add_fusion.i_ref
  32.4 0.6 pad_maximum_fusion.5.w_ref
  33.0 0.0 copy-done.3
  33.1 0.1 maximum_bitcast_fusion
  33.1 12.6 %all-to-all-done.1 = bf16[32,64,256]{2,0,1:T(8,128)(2,1)S(1)} async-done(((bf16[32,64,256]{2,0,1:T(8,128)(2,1)}), bf16[32,64,256]{2,0,1:T(8,128)(2,1)S(1)}, u32[]{:S(2)}, u32[]{:S(2)}) %all-to-all-start.1) | async-done | bytes 1048608 | tf_op jit(solution)/shard_map/all_to_all | solution.py:129
  45.8 0.6 copy.24
  46.4 0.6 convert_reduce_fusion
  47.0 1.3 %copy.28 = bf16[32,8,8,256]{3,1,2,0:T(8,128)(2,1)} copy(bf16[32,8,8,256]{3,2,1,0:T(8,128)(2,1)S(1)} %bitcast.55) | data formatting | bytes 2097152
  48.3 7.5 %shard_map.74 = bf16[256,1024]{1,0:T(8,128)(2,1)} custom-call(bf16[256,2048]{1,0:T(8,128)(2,1)} %bitcast.48, s32[4,1024]{1,0:T(4,128)} %pad_add_fusion.i_ref, f32[4,1024]{1,0:T(4,128)} %pad_maximum_fusion.5.w_ref), custom_call_target="tpu_custom_call" | custom-call | tf_op jit(solution)/shard_map/pallas_call | solution.py:97
  55.8 1.1 %fusion.7 = (bf16[256,512]{1,0:T(8,128)(2,1)S(1)}, bf16[256,512]{1,0:T(8,128)(2,1)S(1)}) fusion(bf16[256,1024]{1,0:T(8,128)(2,1)} %shard_map.74), kind=kLoop, calls=%fused_computation.38 | loop fusion | bytes 1048576 | tf_op jit(solution)/shard_map/slice | solution.py:152
  56.9 0.0 copy-done.1
  56.9 1.2 %subtract_convert_fusion.s_ref = bf16[256,2048]{1,0:T(8,128)(2,1)} fusion(bf16[256,2048]{1,0:T(8,128)(2,1)S(1)} %bitcast.51, f32[2048]{0:T(1024)S(1)} %bitcast.69), kind=kLoop, calls=%fused_computation | loop fusion | flops 1572864 | bytes 2105344 | tf_op jit(solution)/shard_map/convert_element_type | solution.py:110
  58.1 0.0 copy-done.2
  58.1 0.1 fusion
  58.2 0.8 collective-permute-start
  59.0 3.1 %collective-permute-start.1 = (bf16[2,256,512]{2,1,0:T(8,128)(2,1)S(1)}, bf16[2,256,512]{2,1,0:T(8,128)(2,1)S(1)}, u32[]{:S(2)}, u32[]{:S(2)}) collective-permute-start(bf16[2,256,512]{2,1,0:T(8,128)(2,1)S(1)} %get-tuple-element.6), channel_id=1, source_target_pairs={{1,0},{2,1},{3,2},{0,3},{5,4},{6,5},{7,6},{4,7},{9,8},{10,9},{11,1... | collective-permute-start | bytes 1572872 | tf_op jit(solution)/shard_map/ppermute | solution.py:150
  62.1 7.4 %shard_map.75 = bf16[256,1024]{1,0:T(8,128)(2,1)} custom-call(bf16[256,2048]{1,0:T(8,128)(2,1)} %bitcast.49, s32[4,1024]{1,0:T(4,128)} %slice.110.i_ref, f32[4,1024]{1,0:T(4,128)} %slice.111.w_ref), custom_call_target="tpu_custom_call" | custom-call | tf_op jit(solution)/shard_map/pallas_call | solution.py:97
  69.5 2.2 %pad_maximum_fusion.o_ref = bf16[256,2048]{1,0:T(8,128)(2,1)} fusion(bf16[256,512]{1,0:T(8,128)(2,1)S(1)} %get-tuple-element.12, bf16[256,1024]{1,0:T(8,128)(2,1)} %shard_map.75, bf16[256,512]{1,0:T(8,128)(2,1)S(1)} %get-tuple-element.11), kind=kLoop, calls=%fused_computation.4 | loop fusion | flops 3145728 | bytes 2097152 | tf_op jit(solution)/shard_map/concatenate | solution.py:152
  71.6 8.4 %shard_map.76.rest_0_ = f32[256,2048]{1,0:T(8,128)} custom-call(s32[256]{0:T(256)} %reshape.82.code_ref, bf16[256,2048]{1,0:T(8,128)(2,1)} %subtract_convert_fusion.s_ref, bf16[256,2048]{1,0:T(8,128)(2,1)} %pad_maximum_fusion.o_ref, bf16[256,2048]{1,0:T(8,128)(2,1)} %bitcast.59, f32[5,128,128]{2,1,0:T(8,128)} %concatenate.34.taper_ref), custom_call_target="tpu_custom_call" | custom-call | flops 4294967296 | bytes 4194304 | tf_op jit(solution)/shard_map/pallas_call | solution.py:260
  80.0 0.0 collective-permute-done
  80.1 0.8 collective-permute-done.1
  80.9 1.1 %pad_maximum_fusion.2 = (bf16[256,1024]{1,0:T(8,128)(2,1)}, bf16[256,1024]{1,0:T(8,128)(2,1)}) fusion(bf16[256,512]{1,0:T(8,128)(2,1)S(1)} %get-tuple-element.16, bf16[256,512]{1,0:T(8,128)(2,1)S(1)} %get-tuple-element.14, bf16[256,512]{1,0:T(8,128)(2,1)S(1)} %get-tuple-element.15, bf16[256,512]{1,0:T(8,128)(2,1)S(1)} %get-tuple-element.13), kind=kLoop, calls=%fused_computation.9 | loop fusion | flops 2097152 | bytes 2097152 | tf_op jit(solution)/shard_map/concatenate | solution.py:164
  82.0 6.9 %shard_map.77 = bf16[256,2048]{1,0:T(8,128)(2,1)} custom-call(s32[128]{0:T(128)} %reshape.78.code_ref, bf16[256,2048]{1,0:T(8,128)(2,1)} %subtract_convert_fusion.s_ref, bf16[256,1024]{1,0:T(8,128)(2,1)} %get-tuple-element.25.o_ref, bf16[256,1024]{1,0:T(8,128)(2,1)} %get-tuple-element.26.i_ref, f32[5,128,128]{2,1,0:T(8,128)} %concatenate.34.taper_ref, ...), custom_call_target="tpu_custom_call" | custom-call | flops 2147483648 | bytes 4194304 | tf_op jit(solution)/shard_map/pallas_call | solution.py:260
  88.9 1.5 %copy.33 = bf16[32,8,8,256]{3,2,1,0:T(8,128)(2,1)S(1)} copy(bf16[32,8,8,256]{3,1,2,0:T(8,128)(2,1)} %bitcast.63) | data formatting | bytes 2097152
  90.5 20.0 %all_to_all.38 = bf16[256,8,256]{2,1,0:T(8,128)(2,1)S(1)} all-to-all(bf16[256,8,256]{2,1,0:T(8,128)(2,1)S(1)} %bitcast.56), channel_id=1, replica_groups=mesh['wide'=8,'lon'=4] {'wide'}, dimensions={0} | all-to-all | bytes 2097152 | tf_op jit(solution)/shard_map/all_to_all | solution.py:177
  110.5 1.1 copy.36
  (19 shorter events, 0.2 us)
Async XLA Ops:
  0.0 11.2 %copy-start = (f32[4,64,256]{2,1,0:T(8,128)S(1)}, f32[4,64,256]{2,1,0:T(8,128)}, u32[]{:S(2)}) copy-start(f32[4,64,256]{2,1,0:T(8,128)} %param.10) | copy-start | bytes 786436
  0.0 10.1 %copy-start.8 = (s32[1,16]{1,0:T(1,128)S(1)}, s32[1,16]{1,0:T(1,128)}, u32[]{:S(2)}) copy-start(s32[1,16]{1,0:T(1,128)} %param.12) | copy-start | bytes 196
  0.0 10.1 %copy-start.7 = (s32[1,16,16]{2,1,0:T(8,128)S(1)}, s32[1,16,16]{2,1,0:T(8,128)}, u32[]{:S(2)}) copy-start(s32[1,16,16]{2,1,0:T(8,128)} %param.13) | copy-start | bytes 3076
  0.0 10.2 %copy-start.6 = (s32[1,16,16]{2,1,0:T(8,128)S(1)}, s32[1,16,16]{2,1,0:T(8,128)}, u32[]{:S(2)}) copy-start(s32[1,16,16]{2,1,0:T(8,128)} %param.11) | copy-start | bytes 3076
  0.0 12.5 %copy-start.4 = (bf16[256,8,256]{2,1,0:T(8,128)(2,1)S(1)}, bf16[256,8,256]{2,1,0:T(8,128)(2,1)}, u32[]{:S(2)}) copy-start(bf16[256,8,256]{2,1,0:T(8,128)(2,1)} %param.8) | copy-start | bytes 3145732
  2.9 12.0 %all-to-all-start = ((bf16[4,2,2048]{2,1,0:T(2,128)(2,1)}), bf16[4,2,2048]{2,1,0:T(2,128)(2,1)S(1)}, u32[]{:S(2)}, u32[]{:S(2)}) async-start(bf16[4,2,2048]{2,1,0:T(2,128)(2,1)} %reshape.84), calls=%async_computation | async-start | bytes 65536 | tf_op jit(solution)/shard_map/all_to_all | solution.py:32
  12.9 20.1 %copy-start.3 = (bf16[32,8,8,256]{3,1,2,0:T(8,128)(2,1)}, bf16[32,8,8,256]{3,1,2,0:T(8,128)(2,1)S(1)}, u32[]{:S(2)}) copy-start(bf16[32,8,8,256]{3,1,2,0:T(8,128)(2,1)S(1)} %copy.32) | copy-start | bytes 3145732
  23.8 7.3 %copy-start.5 = (f32[4,128,128]{2,1,0:T(8,128)S(1)}, f32[4,128,128]{2,1,0:T(8,128)}, u32[]{:S(2)}) copy-start(f32[4,128,128]{2,1,0:T(8,128)} %fusion.3) | copy-start | bytes 786436
  26.6 19.1 %all-to-all-start.1 = ((bf16[32,64,256]{2,0,1:T(8,128)(2,1)}), bf16[32,64,256]{2,0,1:T(8,128)(2,1)S(1)}, u32[]{:S(2)}, u32[]{:S(2)}) async-start(bf16[32,64,256]{2,0,1:T(8,128)(2,1)} %copy.23), calls=%async_computation.1 | async-start | bytes 2097152 | tf_op jit(solution)/shard_map/all_to_all | solution.py:129
  48.3 8.6 %copy-start.1 = (bf16[32,8,8,256]{3,1,2,0:T(8,128)(2,1)S(1)}, bf16[32,8,8,256]{3,1,2,0:T(8,128)(2,1)}, u32[]{:S(2)}) copy-start(bf16[32,8,8,256]{3,1,2,0:T(8,128)(2,1)} %copy.28) | copy-start | bytes 3145732
  55.8 2.4 %copy-start.2 = (bf16[256,1024]{1,0:T(8,128)(2,1)S(1)}, bf16[256,1024]{1,0:T(8,128)(2,1)}, u32[]{:S(2)}) copy-start(bf16[256,1024]{1,0:T(8,128)(2,1)} %shard_map.74) | copy-start | bytes 1572868
  58.2 21.8 %collective-permute-start = (bf16[2,256,512]{2,1,0:T(8,128)(2,1)S(1)}, bf16[2,256,512]{2,1,0:T(8,128)(2,1)S(1)}, u32[]{:S(2)}, u32[]{:S(2)}) collective-permute-start(bf16[2,256,512]{2,1,0:T(8,128)(2,1)S(1)} %get-tuple-element.5), channel_id=1, source_target_pairs={{0,1},{1,2},{2,3},{3,0},{4,5},{5,6},{6,7},{7,4},{8,9},{9,10},{10,1... | collective-permute-start | bytes 1572872 | tf_op jit(solution)/shard_map/ppermute | solution.py:149
  59.0 21.8 %collective-permute-start.1 = (bf16[2,256,512]{2,1,0:T(8,128)(2,1)S(1)}, bf16[2,256,512]{2,1,0:T(8,128)(2,1)S(1)}, u32[]{:S(2)}, u32[]{:S(2)}) collective-permute-start(bf16[2,256,512]{2,1,0:T(8,128)(2,1)S(1)} %get-tuple-element.6), channel_id=1, source_target_pairs={{1,0},{2,1},{3,2},{0,3},{5,4},{6,5},{7,6},{4,7},{9,8},{10,9},{11,1... | collective-permute-start | bytes 1572872 | tf_op jit(solution)/shard_map/ppermute | solution.py:150

commit v10 on v9

--- a/solution.py
+++ b/solution.py
@@ -52,7 +52,7 @@
             o_ref[m] = (x + 0.2 * spread - 0.3 * (east_n - west_n)).astype(jnp.bfloat16)
             return carry
 
-        lax.fori_loop(0, members, one, 0)
+        lax.fori_loop(0, members, one, 0, unroll=4)
 
     return pl.pallas_call(kernel, out_shape=jax.ShapeDtypeStruct(state.shape, jnp.bfloat16))(state, west, east)
 

time: 112 us -> 110 us (0.982)
  Pallas kernels: 36.5 us -> 34.6 us
    pallas_call x1, Pallas kernels: 6.33 us -> 4.46 us  [forecast_call(): pl.pallas_call(kernel, out_shape=jax.ShapeDtypeStruct(state.shape, jnp.bf...]
where the time goes in v10:
time: 110 us
  Pallas kernels  34.6 us (31%)
  blocking collectives  20 us (18%)
  local copies, waits for them, and re-layouts  17.8 us (16%)
  waiting for transfers between devices  14.8 us (13%)
  starting transfers between devices  13.9 us (13%)
  other arithmetic  8.45 us (8%)
    all_to_all x1, blocking collectives, body(): lax.all_to_all(result.reshape(members, band_rows, patch_meridian_lines),...  20 us
    pallas_call x2, Pallas kernels, update_call(): pl.pallas_call(kernel, grid_spec=grid_spec, out_shape=jax.ShapeDtypeStruc...  15.3 us
    pallas_call x2, Pallas kernels, observe_dev_call(): pl.pallas_call(kernel, grid=(count // OBS_STEP,), in_specs=[pl.BlockSpec(...  14.8 us
    all_to_all x1, waiting for transfers between devices, body(): lax.all_to_all(prediction_increment, 'wide', split_axis=1, concat_axis=0,...  12.6 us
    all_to_all x1, starting transfers between devices, column_halo(): got = lax.all_to_all(spread, axis, 0, 0, tiled=False)  6.32 us
    unnamed x30, local copies, waits for them, and re-layouts  4.59 us
    pallas_call x1, Pallas kernels, forecast_call(): pl.pallas_call(kernel, out_shape=jax.ShapeDtypeStruct(state.shape, jnp.bf...  4.46 us
    all_to_all x1, starting transfers between devices, body(): lax.all_to_all(prediction_increment, 'wide', split_axis=1, concat_axis=0,...  3.72 us
  transfers between devices with their start and end apart: 4, of which 3 were waited for; matrix products, arithmetic and copies ran while one was open for 8% of the time, Pallas kernels for 14%

profile of v10, /device:TPU:0, one launch (start us, length us, event | category | flops | bytes accessed | tf_op | source)
XLA Modules:
  0.0 109.7 jit_solution(3337062092450290387)
XLA Ops:
  0.0 0.0 copy-start
  0.0 0.0 copy-start.8
  0.0 0.0 copy-start.7
  0.0 0.0 copy-start.6
  0.0 0.0 copy-start.4
  0.0 1.5 %fusion.6 = (bf16[32,64,1]{2,1,0:T(8,128)(2,1)S(1)}, bf16[32,64,1]{2,1,0:T(8,128)(2,1)S(1)}) fusion(bf16[32,64,256]{2,1,0:T(8,128)(2,1)} %x_ref.1), kind=kLoop, calls=%fused_computation.37 | loop fusion | bytes 16384 | tf_op jit(solution)/shard_map/slice | solution.py:30
  1.6 0.3 copy.26
  1.9 0.3 copy.27
  2.2 0.7 reshape.84
  2.9 6.3 %all-to-all-start = ((bf16[4,2,2048]{2,1,0:T(2,128)(2,1)}), bf16[4,2,2048]{2,1,0:T(2,128)(2,1)S(1)}, u32[]{:S(2)}, u32[]{:S(2)}) async-start(bf16[4,2,2048]{2,1,0:T(2,128)(2,1)} %reshape.84), calls=%async_computation | async-start | bytes 65536 | tf_op jit(solution)/shard_map/all_to_all | solution.py:32
  9.3 0.8 subtract_bitcast_fusion
  10.1 0.0 copy-done.8
  10.1 0.0 copy-done.7
  10.1 0.1 fusion.4
  10.2 0.0 copy-done.6
  10.2 0.1 select_reduce_fusion
  10.3 0.1 fusion.10
  10.4 0.8 fusion.3
  11.2 0.0 copy-done
  11.3 0.6 slice.110.i_ref
  11.9 0.1 slice.108
  11.9 0.6 slice.111.w_ref
  12.5 0.0 copy-done.4
  12.6 0.3 copy.32
  12.9 0.0 copy-start.3
  12.9 0.7 reshape.82.code_ref
  13.5 1.3 %all-to-all-done = bf16[4,2,2048]{2,1,0:T(2,128)(2,1)S(1)} async-done(((bf16[4,2,2048]{2,1,0:T(2,128)(2,1)}), bf16[4,2,2048]{2,1,0:T(2,128)(2,1)S(1)}, u32[]{:S(2)}, u32[]{:S(2)}) %all-to-all-start) | async-done | bytes 32800 | tf_op jit(solution)/shard_map/all_to_all | solution.py:32
  14.9 0.1 reshape.85
  15.0 0.3 copy.21
  15.3 1.0 slice.94.w_ref
  16.4 1.1 copy.22
  17.4 4.5 %shard_map.73 = bf16[32,64,256]{2,1,0:T(8,128)(2,1)} custom-call(bf16[32,64,256]{2,1,0:T(8,128)(2,1)} %x_ref.1, bf16[32,64,1]{2,1,0:T(8,128)(2,1)} %slice.94.w_ref, bf16[32,64,1]{2,1,0:T(8,128)(2,1)} %bitcast.61), custom_call_target="tpu_custom_call" | custom-call | tf_op jit(solution)/shard_map/pallas_call | solution.py:57
  21.9 2.8 %copy.23 = bf16[32,64,256]{2,0,1:T(8,128)(2,1)} copy(bf16[32,64,256]{2,1,0:T(8,128)(2,1)} %shard_map.73) | data formatting | bytes 2097152 | tf_op jit(solution)/shard_map/pallas_call | solution.py:57
  24.8 3.7 %all-to-all-start.1 = ((bf16[32,64,256]{2,0,1:T(8,128)(2,1)}), bf16[32,64,256]{2,0,1:T(8,128)(2,1)S(1)}, u32[]{:S(2)}, u32[]{:S(2)}) async-start(bf16[32,64,256]{2,0,1:T(8,128)(2,1)} %copy.23), calls=%async_computation.1 | async-start | bytes 2097152 | tf_op jit(solution)/shard_map/all_to_all | solution.py:129
  28.5 0.1 pad_add_fusion.1
  28.6 0.6 reshape.78.code_ref
  29.2 0.0 copy-done.5
  29.2 0.8 concatenate.34.taper_ref
  29.9 0.6 pad_add_fusion.i_ref
  30.5 0.6 pad_maximum_fusion.5.w_ref
  31.1 0.0 copy-done.3
  31.2 0.1 maximum_bitcast_fusion
  31.3 12.6 %all-to-all-done.1 = bf16[32,64,256]{2,0,1:T(8,128)(2,1)S(1)} async-done(((bf16[32,64,256]{2,0,1:T(8,128)(2,1)}), bf16[32,64,256]{2,0,1:T(8,128)(2,1)S(1)}, u32[]{:S(2)}, u32[]{:S(2)}) %all-to-all-start.1) | async-done | bytes 1048608 | tf_op jit(solution)/shard_map/all_to_all | solution.py:129
  43.9 0.6 copy.24
  44.5 0.6 convert_reduce_fusion
  45.1 1.3 %copy.28 = bf16[32,8,8,256]{3,1,2,0:T(8,128)(2,1)} copy(bf16[32,8,8,256]{3,2,1,0:T(8,128)(2,1)S(1)} %bitcast.55) | data formatting | bytes 2097152
  46.4 7.5 %shard_map.74 = bf16[256,1024]{1,0:T(8,128)(2,1)} custom-call(bf16[256,2048]{1,0:T(8,128)(2,1)} %bitcast.48, s32[4,1024]{1,0:T(4,128)} %pad_add_fusion.i_ref, f32[4,1024]{1,0:T(4,128)} %pad_maximum_fusion.5.w_ref), custom_call_target="tpu_custom_call" | custom-call | tf_op jit(solution)/shard_map/pallas_call | solution.py:97
  53.9 1.1 %fusion.7 = (bf16[256,512]{1,0:T(8,128)(2,1)S(1)}, bf16[256,512]{1,0:T(8,128)(2,1)S(1)}) fusion(bf16[256,1024]{1,0:T(8,128)(2,1)} %shard_map.74), kind=kLoop, calls=%fused_computation.38 | loop fusion | bytes 1048576 | tf_op jit(solution)/shard_map/slice | solution.py:152
  55.0 0.0 copy-done.1
  55.0 1.2 %subtract_convert_fusion.s_ref = bf16[256,2048]{1,0:T(8,128)(2,1)} fusion(bf16[256,2048]{1,0:T(8,128)(2,1)S(1)} %bitcast.51, f32[2048]{0:T(1024)S(1)} %bitcast.69), kind=kLoop, calls=%fused_computation | loop fusion | flops 1572864 | bytes 2105344 | tf_op jit(solution)/shard_map/convert_element_type | solution.py:110
  56.3 0.0 copy-done.2
  56.3 0.1 fusion
  56.4 0.8 collective-permute-start
  57.1 3.1 %collective-permute-start.1 = (bf16[2,256,512]{2,1,0:T(8,128)(2,1)S(1)}, bf16[2,256,512]{2,1,0:T(8,128)(2,1)S(1)}, u32[]{:S(2)}, u32[]{:S(2)}) collective-permute-start(bf16[2,256,512]{2,1,0:T(8,128)(2,1)S(1)} %get-tuple-element.6), channel_id=1, source_target_pairs={{1,0},{2,1},{3,2},{0,3},{5,4},{6,5},{7,6},{4,7},{9,8},{10,9},{11,1... | collective-permute-start | bytes 1572872 | tf_op jit(solution)/shard_map/ppermute | solution.py:150
  60.2 7.4 %shard_map.75 = bf16[256,1024]{1,0:T(8,128)(2,1)} custom-call(bf16[256,2048]{1,0:T(8,128)(2,1)} %bitcast.49, s32[4,1024]{1,0:T(4,128)} %slice.110.i_ref, f32[4,1024]{1,0:T(4,128)} %slice.111.w_ref), custom_call_target="tpu_custom_call" | custom-call | tf_op jit(solution)/shard_map/pallas_call | solution.py:97
  67.6 2.2 %pad_maximum_fusion.o_ref = bf16[256,2048]{1,0:T(8,128)(2,1)} fusion(bf16[256,512]{1,0:T(8,128)(2,1)S(1)} %get-tuple-element.12, bf16[256,1024]{1,0:T(8,128)(2,1)} %shard_map.75, bf16[256,512]{1,0:T(8,128)(2,1)S(1)} %get-tuple-element.11), kind=kLoop, calls=%fused_computation.4 | loop fusion | flops 3145728 | bytes 2097152 | tf_op jit(solution)/shard_map/concatenate | solution.py:152
  69.8 8.4 %shard_map.76.rest_0_ = f32[256,2048]{1,0:T(8,128)} custom-call(s32[256]{0:T(256)} %reshape.82.code_ref, bf16[256,2048]{1,0:T(8,128)(2,1)} %subtract_convert_fusion.s_ref, bf16[256,2048]{1,0:T(8,128)(2,1)} %pad_maximum_fusion.o_ref, bf16[256,2048]{1,0:T(8,128)(2,1)} %bitcast.59, f32[5,128,128]{2,1,0:T(8,128)} %concatenate.34.taper_ref), custom_call_target="tpu_custom_call" | custom-call | flops 4294967296 | bytes 4194304 | tf_op jit(solution)/shard_map/pallas_call | solution.py:260
  78.2 0.0 collective-permute-done
  78.2 0.8 collective-permute-done.1
  79.0 1.1 %pad_maximum_fusion.2 = (bf16[256,1024]{1,0:T(8,128)(2,1)}, bf16[256,1024]{1,0:T(8,128)(2,1)}) fusion(bf16[256,512]{1,0:T(8,128)(2,1)S(1)} %get-tuple-element.16, bf16[256,512]{1,0:T(8,128)(2,1)S(1)} %get-tuple-element.14, bf16[256,512]{1,0:T(8,128)(2,1)S(1)} %get-tuple-element.15, bf16[256,512]{1,0:T(8,128)(2,1)S(1)} %get-tuple-element.13), kind=kLoop, calls=%fused_computation.9 | loop fusion | flops 2097152 | bytes 2097152 | tf_op jit(solution)/shard_map/concatenate | solution.py:164
  80.2 6.9 %shard_map.77 = bf16[256,2048]{1,0:T(8,128)(2,1)} custom-call(s32[128]{0:T(128)} %reshape.78.code_ref, bf16[256,2048]{1,0:T(8,128)(2,1)} %subtract_convert_fusion.s_ref, bf16[256,1024]{1,0:T(8,128)(2,1)} %get-tuple-element.25.o_ref, bf16[256,1024]{1,0:T(8,128)(2,1)} %get-tuple-element.26.i_ref, f32[5,128,128]{2,1,0:T(8,128)} %concatenate.34.taper_ref, ...), custom_call_target="tpu_custom_call" | custom-call | flops 2147483648 | bytes 4194304 | tf_op jit(solution)/shard_map/pallas_call | solution.py:260
  87.1 1.5 %copy.33 = bf16[32,8,8,256]{3,2,1,0:T(8,128)(2,1)S(1)} copy(bf16[32,8,8,256]{3,1,2,0:T(8,128)(2,1)} %bitcast.63) | data formatting | bytes 2097152
  88.6 20.0 %all_to_all.38 = bf16[256,8,256]{2,1,0:T(8,128)(2,1)S(1)} all-to-all(bf16[256,8,256]{2,1,0:T(8,128)(2,1)S(1)} %bitcast.56), channel_id=1, replica_groups=mesh['wide'=8,'lon'=4] {'wide'}, dimensions={0} | all-to-all | bytes 2097152 | tf_op jit(solution)/shard_map/all_to_all | solution.py:177
  108.6 1.1 %copy.36 = bf16[8,32,8,256]{3,2,0,1:T(8,128)(2,1)} copy(bf16[8,32,8,256]{3,2,1,0:T(8,128)(2,1)S(1)} %bitcast.57) | data formatting | bytes 2097152 | tf_op jit(solution)/shard_map/all_to_all | solution.py:177
  (19 shorter events, 0.2 us)
Async XLA Ops:
  0.0 11.2 %copy-start = (f32[4,64,256]{2,1,0:T(8,128)S(1)}, f32[4,64,256]{2,1,0:T(8,128)}, u32[]{:S(2)}) copy-start(f32[4,64,256]{2,1,0:T(8,128)} %param.10) | copy-start | bytes 786436
  0.0 10.1 %copy-start.8 = (s32[1,16]{1,0:T(1,128)S(1)}, s32[1,16]{1,0:T(1,128)}, u32[]{:S(2)}) copy-start(s32[1,16]{1,0:T(1,128)} %param.12) | copy-start | bytes 196
  0.0 10.1 %copy-start.7 = (s32[1,16,16]{2,1,0:T(8,128)S(1)}, s32[1,16,16]{2,1,0:T(8,128)}, u32[]{:S(2)}) copy-start(s32[1,16,16]{2,1,0:T(8,128)} %param.13) | copy-start | bytes 3076
  0.0 10.2 %copy-start.6 = (s32[1,16,16]{2,1,0:T(8,128)S(1)}, s32[1,16,16]{2,1,0:T(8,128)}, u32[]{:S(2)}) copy-start(s32[1,16,16]{2,1,0:T(8,128)} %param.11) | copy-start | bytes 3076
  0.0 12.5 %copy-start.4 = (bf16[256,8,256]{2,1,0:T(8,128)(2,1)S(1)}, bf16[256,8,256]{2,1,0:T(8,128)(2,1)}, u32[]{:S(2)}) copy-start(bf16[256,8,256]{2,1,0:T(8,128)(2,1)} %param.8) | copy-start | bytes 3145732
  2.9 12.0 %all-to-all-start = ((bf16[4,2,2048]{2,1,0:T(2,128)(2,1)}), bf16[4,2,2048]{2,1,0:T(2,128)(2,1)S(1)}, u32[]{:S(2)}, u32[]{:S(2)}) async-start(bf16[4,2,2048]{2,1,0:T(2,128)(2,1)} %reshape.84), calls=%async_computation | async-start | bytes 65536 | tf_op jit(solution)/shard_map/all_to_all | solution.py:32
  12.9 18.3 %copy-start.3 = (bf16[32,8,8,256]{3,1,2,0:T(8,128)(2,1)}, bf16[32,8,8,256]{3,1,2,0:T(8,128)(2,1)S(1)}, u32[]{:S(2)}) copy-start(bf16[32,8,8,256]{3,1,2,0:T(8,128)(2,1)S(1)} %copy.32) | copy-start | bytes 3145732
  21.9 7.3 %copy-start.5 = (f32[4,128,128]{2,1,0:T(8,128)S(1)}, f32[4,128,128]{2,1,0:T(8,128)}, u32[]{:S(2)}) copy-start(f32[4,128,128]{2,1,0:T(8,128)} %fusion.3) | copy-start | bytes 786436
  24.8 19.1 %all-to-all-start.1 = ((bf16[32,64,256]{2,0,1:T(8,128)(2,1)}), bf16[32,64,256]{2,0,1:T(8,128)(2,1)S(1)}, u32[]{:S(2)}, u32[]{:S(2)}) async-start(bf16[32,64,256]{2,0,1:T(8,128)(2,1)} %copy.23), calls=%async_computation.1 | async-start | bytes 2097152 | tf_op jit(solution)/shard_map/all_to_all | solution.py:129
  46.4 8.6 %copy-start.1 = (bf16[32,8,8,256]{3,1,2,0:T(8,128)(2,1)S(1)}, bf16[32,8,8,256]{3,1,2,0:T(8,128)(2,1)}, u32[]{:S(2)}) copy-start(bf16[32,8,8,256]{3,1,2,0:T(8,128)(2,1)} %copy.28) | copy-start | bytes 3145732
  53.9 2.4 %copy-start.2 = (bf16[256,1024]{1,0:T(8,128)(2,1)S(1)}, bf16[256,1024]{1,0:T(8,128)(2,1)}, u32[]{:S(2)}) copy-start(bf16[256,1024]{1,0:T(8,128)(2,1)} %shard_map.74) | copy-start | bytes 1572868
  56.4 21.8 %collective-permute-start = (bf16[2,256,512]{2,1,0:T(8,128)(2,1)S(1)}, bf16[2,256,512]{2,1,0:T(8,128)(2,1)S(1)}, u32[]{:S(2)}, u32[]{:S(2)}) collective-permute-start(bf16[2,256,512]{2,1,0:T(8,128)(2,1)S(1)} %get-tuple-element.5), channel_id=1, source_target_pairs={{0,1},{1,2},{2,3},{3,0},{4,5},{5,6},{6,7},{7,4},{8,9},{9,10},{10,1... | collective-permute-start | bytes 1572872 | tf_op jit(solution)/shard_map/ppermute | solution.py:149
  57.1 21.8 %collective-permute-start.1 = (bf16[2,256,512]{2,1,0:T(8,128)(2,1)S(1)}, bf16[2,256,512]{2,1,0:T(8,128)(2,1)S(1)}, u32[]{:S(2)}, u32[]{:S(2)}) collective-permute-start(bf16[2,256,512]{2,1,0:T(8,128)(2,1)S(1)} %get-tuple-element.6), channel_id=1, source_target_pairs={{1,0},{2,1},{3,2},{0,3},{5,4},{6,5},{7,6},{4,7},{9,8},{10,9},{11,1... | collective-permute-start | bytes 1572872 | tf_op jit(solution)/shard_map/ppermute | solution.py:150

commit v11 on v10

--- a/solution.py
+++ b/solution.py
@@ -173,6 +173,7 @@
         tiles,
         block_count,
         2 * halo_blocks,
+        group=8,
     )
     return lax.all_to_all(
         result.reshape(members, band_rows, patch_meridian_lines),
@@ -205,9 +206,9 @@
 GROUP = 4
 
 
-def update_call(code, state, partial, anchor, cand_obs, cand_innov, tiles, block_count, candidate_count):
+def update_call(code, state, partial, anchor, cand_obs, cand_innov, tiles, block_count, candidate_count, group=GROUP):
     members, cells = state.shape
-    rows = GROUP * BLK
+    rows = group * BLK
     width = candidate_count * BLK
     final = anchor is not None
 
@@ -220,8 +221,8 @@
         cov_scr[...] = lax.dot_general(
             s_ref[...], o_ref[...], (((0,), (0,)), ((), ())), preferred_element_type=jnp.float32
         )
-        for sl in range(GROUP):
-            s = g * GROUP + sl
+        for sl in range(group):
+            s = g * group + sl
             for b in range(candidate_count):
                 c = code_ref[s * candidate_count + b]
                 tile = cov_scr[sl * BLK:(sl + 1) * BLK, b * BLK:(b + 1) * BLK] * taper_ref[c]
@@ -248,7 +249,7 @@
         operands += [partial, anchor]
     grid_spec = pltpu.PrefetchScalarGridSpec(
         num_scalar_prefetch=1,
-        grid=(block_count // GROUP,),
+        grid=(block_count // group,),
         in_specs=in_specs,
         out_specs=col_spec,
         scratch_shapes=[

time: 110 us -> 110 us (level)
  no operation moved by 1% of the time
where the time goes in v11:
time: 110 us; the launch traced here: 109 us
  Pallas kernels  34.1 us (31%)
  blocking collectives  20 us (18%)
  local copies, waits for them, and re-layouts  17.8 us (16%)
  waiting for transfers between devices  14.8 us (13%)
  starting transfers between devices  13.9 us (13%)
  other arithmetic  8.45 us (8%)
    all_to_all x1, blocking collectives, body(): lax.all_to_all(result.reshape(members, band_rows, patch_meridian_lines),...  20 us
    pallas_call x2, Pallas kernels, observe_dev_call(): pl.pallas_call(kernel, grid=(count // OBS_STEP,), in_specs=[pl.BlockSpec(...  14.8 us
    pallas_call x2, Pallas kernels, update_call(): pl.pallas_call(kernel, grid_spec=grid_spec, out_shape=jax.ShapeDtypeStruc...  14.8 us
    all_to_all x1, waiting for transfers between devices, body(): lax.all_to_all(prediction_increment, 'wide', split_axis=1, concat_axis=0,...  12.6 us
    all_to_all x1, starting transfers between devices, column_halo(): got = lax.all_to_all(spread, axis, 0, 0, tiled=False)  6.32 us
    unnamed x30, local copies, waits for them, and re-layouts  4.59 us
    pallas_call x1, Pallas kernels, forecast_call(): pl.pallas_call(kernel, out_shape=jax.ShapeDtypeStruct(state.shape, jnp.bf...  4.46 us
    all_to_all x1, starting transfers between devices, body(): lax.all_to_all(prediction_increment, 'wide', split_axis=1, concat_axis=0,...  3.72 us
  transfers between devices with their start and end apart: 4, of which 3 were waited for; matrix products, arithmetic and copies ran while one was open for 8% of the time, Pallas kernels for 14%

profile of v11, /device:TPU:0, one launch (start us, length us, event | category | flops | bytes accessed | tf_op | source)
XLA Modules:
  0.0 109.1 jit_solution(14839361854847886658)
XLA Ops:
  0.0 0.0 copy-start
  0.0 0.0 copy-start.8
  0.0 0.0 copy-start.7
  0.0 0.0 copy-start.6
  0.0 0.0 copy-start.4
  0.0 1.5 %fusion.6 = (bf16[32,64,1]{2,1,0:T(8,128)(2,1)S(1)}, bf16[32,64,1]{2,1,0:T(8,128)(2,1)S(1)}) fusion(bf16[32,64,256]{2,1,0:T(8,128)(2,1)} %x_ref.1), kind=kLoop, calls=%fused_computation.37 | loop fusion | bytes 16384 | tf_op jit(solution)/shard_map/slice | solution.py:30
  1.6 0.3 copy.26
  1.9 0.3 copy.27
  2.2 0.7 reshape.84
  2.9 6.3 %all-to-all-start = ((bf16[4,2,2048]{2,1,0:T(2,128)(2,1)}), bf16[4,2,2048]{2,1,0:T(2,128)(2,1)S(1)}, u32[]{:S(2)}, u32[]{:S(2)}) async-start(bf16[4,2,2048]{2,1,0:T(2,128)(2,1)} %reshape.84), calls=%async_computation | async-start | bytes 65536 | tf_op jit(solution)/shard_map/all_to_all | solution.py:32
  9.3 0.8 subtract_bitcast_fusion
  10.1 0.0 copy-done.8
  10.1 0.0 copy-done.7
  10.1 0.1 fusion.4
  10.2 0.0 copy-done.6
  10.2 0.1 select_reduce_fusion
  10.3 0.1 fusion.10
  10.4 0.8 fusion.3
  11.2 0.0 copy-done
  11.3 0.6 slice.110.i_ref
  11.9 0.1 slice.108
  11.9 0.6 slice.111.w_ref
  12.5 0.0 copy-done.4
  12.6 0.3 copy.32
  12.9 0.0 copy-start.3
  12.9 0.7 reshape.82.code_ref
  13.5 1.3 %all-to-all-done = bf16[4,2,2048]{2,1,0:T(2,128)(2,1)S(1)} async-done(((bf16[4,2,2048]{2,1,0:T(2,128)(2,1)}), bf16[4,2,2048]{2,1,0:T(2,128)(2,1)S(1)}, u32[]{:S(2)}, u32[]{:S(2)}) %all-to-all-start) | async-done | bytes 32800 | tf_op jit(solution)/shard_map/all_to_all | solution.py:32
  14.9 0.1 reshape.85
  15.0 0.3 copy.21
  15.3 1.0 slice.94.w_ref
  16.4 1.1 copy.22
  17.4 4.5 %shard_map.73 = bf16[32,64,256]{2,1,0:T(8,128)(2,1)} custom-call(bf16[32,64,256]{2,1,0:T(8,128)(2,1)} %x_ref.1, bf16[32,64,1]{2,1,0:T(8,128)(2,1)} %slice.94.w_ref, bf16[32,64,1]{2,1,0:T(8,128)(2,1)} %bitcast.61), custom_call_target="tpu_custom_call" | custom-call | tf_op jit(solution)/shard_map/pallas_call | solution.py:57
  21.9 2.8 %copy.23 = bf16[32,64,256]{2,0,1:T(8,128)(2,1)} copy(bf16[32,64,256]{2,1,0:T(8,128)(2,1)} %shard_map.73) | data formatting | bytes 2097152 | tf_op jit(solution)/shard_map/pallas_call | solution.py:57
  24.8 3.7 %all-to-all-start.1 = ((bf16[32,64,256]{2,0,1:T(8,128)(2,1)}), bf16[32,64,256]{2,0,1:T(8,128)(2,1)S(1)}, u32[]{:S(2)}, u32[]{:S(2)}) async-start(bf16[32,64,256]{2,0,1:T(8,128)(2,1)} %copy.23), calls=%async_computation.1 | async-start | bytes 2097152 | tf_op jit(solution)/shard_map/all_to_all | solution.py:129
  28.5 0.1 pad_add_fusion.1
  28.6 0.6 reshape.78.code_ref
  29.2 0.0 copy-done.5
  29.2 0.8 concatenate.34.taper_ref
  29.9 0.6 pad_add_fusion.i_ref
  30.5 0.6 pad_maximum_fusion.5.w_ref
  31.1 0.0 copy-done.3
  31.2 0.1 maximum_bitcast_fusion
  31.3 12.6 %all-to-all-done.1 = bf16[32,64,256]{2,0,1:T(8,128)(2,1)S(1)} async-done(((bf16[32,64,256]{2,0,1:T(8,128)(2,1)}), bf16[32,64,256]{2,0,1:T(8,128)(2,1)S(1)}, u32[]{:S(2)}, u32[]{:S(2)}) %all-to-all-start.1) | async-done | bytes 1048608 | tf_op jit(solution)/shard_map/all_to_all | solution.py:129
  43.9 0.6 copy.24
  44.5 0.6 convert_reduce_fusion
  45.1 1.3 %copy.28 = bf16[32,8,8,256]{3,1,2,0:T(8,128)(2,1)} copy(bf16[32,8,8,256]{3,2,1,0:T(8,128)(2,1)S(1)} %bitcast.55) | data formatting | bytes 2097152
  46.4 7.5 %shard_map.74 = bf16[256,1024]{1,0:T(8,128)(2,1)} custom-call(bf16[256,2048]{1,0:T(8,128)(2,1)} %bitcast.48, s32[4,1024]{1,0:T(4,128)} %pad_add_fusion.i_ref, f32[4,1024]{1,0:T(4,128)} %pad_maximum_fusion.5.w_ref), custom_call_target="tpu_custom_call" | custom-call | tf_op jit(solution)/shard_map/pallas_call | solution.py:97
  53.9 1.1 %fusion.7 = (bf16[256,512]{1,0:T(8,128)(2,1)S(1)}, bf16[256,512]{1,0:T(8,128)(2,1)S(1)}) fusion(bf16[256,1024]{1,0:T(8,128)(2,1)} %shard_map.74), kind=kLoop, calls=%fused_computation.38 | loop fusion | bytes 1048576 | tf_op jit(solution)/shard_map/slice | solution.py:152
  55.0 0.0 copy-done.1
  55.0 1.2 %subtract_convert_fusion.s_ref = bf16[256,2048]{1,0:T(8,128)(2,1)} fusion(bf16[256,2048]{1,0:T(8,128)(2,1)S(1)} %bitcast.51, f32[2048]{0:T(1024)S(1)} %bitcast.69), kind=kLoop, calls=%fused_computation | loop fusion | flops 1572864 | bytes 2105344 | tf_op jit(solution)/shard_map/convert_element_type | solution.py:110
  56.3 0.0 copy-done.2
  56.3 0.1 fusion
  56.4 0.8 collective-permute-start
  57.1 3.1 %collective-permute-start.1 = (bf16[2,256,512]{2,1,0:T(8,128)(2,1)S(1)}, bf16[2,256,512]{2,1,0:T(8,128)(2,1)S(1)}, u32[]{:S(2)}, u32[]{:S(2)}) collective-permute-start(bf16[2,256,512]{2,1,0:T(8,128)(2,1)S(1)} %get-tuple-element.6), channel_id=1, source_target_pairs={{1,0},{2,1},{3,2},{0,3},{5,4},{6,5},{7,6},{4,7},{9,8},{10,9},{11,1... | collective-permute-start | bytes 1572872 | tf_op jit(solution)/shard_map/ppermute | solution.py:150
  60.2 7.4 %shard_map.75 = bf16[256,1024]{1,0:T(8,128)(2,1)} custom-call(bf16[256,2048]{1,0:T(8,128)(2,1)} %bitcast.49, s32[4,1024]{1,0:T(4,128)} %slice.110.i_ref, f32[4,1024]{1,0:T(4,128)} %slice.111.w_ref), custom_call_target="tpu_custom_call" | custom-call | tf_op jit(solution)/shard_map/pallas_call | solution.py:97
  67.6 2.2 %pad_maximum_fusion.o_ref = bf16[256,2048]{1,0:T(8,128)(2,1)} fusion(bf16[256,512]{1,0:T(8,128)(2,1)S(1)} %get-tuple-element.12, bf16[256,1024]{1,0:T(8,128)(2,1)} %shard_map.75, bf16[256,512]{1,0:T(8,128)(2,1)S(1)} %get-tuple-element.11), kind=kLoop, calls=%fused_computation.4 | loop fusion | flops 3145728 | bytes 2097152 | tf_op jit(solution)/shard_map/concatenate | solution.py:152
  69.8 8.4 %shard_map.76.rest_0_ = f32[256,2048]{1,0:T(8,128)} custom-call(s32[256]{0:T(256)} %reshape.82.code_ref, bf16[256,2048]{1,0:T(8,128)(2,1)} %subtract_convert_fusion.s_ref, bf16[256,2048]{1,0:T(8,128)(2,1)} %pad_maximum_fusion.o_ref, bf16[256,2048]{1,0:T(8,128)(2,1)} %bitcast.59, f32[5,128,128]{2,1,0:T(8,128)} %concatenate.34.taper_ref), custom_call_target="tpu_custom_call" | custom-call | flops 4294967296 | bytes 4194304 | tf_op jit(solution)/shard_map/pallas_call | solution.py:261
  78.2 0.0 collective-permute-done
  78.2 0.8 collective-permute-done.1
  79.0 1.1 %pad_maximum_fusion.2 = (bf16[256,1024]{1,0:T(8,128)(2,1)}, bf16[256,1024]{1,0:T(8,128)(2,1)}) fusion(bf16[256,512]{1,0:T(8,128)(2,1)S(1)} %get-tuple-element.16, bf16[256,512]{1,0:T(8,128)(2,1)S(1)} %get-tuple-element.14, bf16[256,512]{1,0:T(8,128)(2,1)S(1)} %get-tuple-element.15, bf16[256,512]{1,0:T(8,128)(2,1)S(1)} %get-tuple-element.13), kind=kLoop, calls=%fused_computation.9 | loop fusion | flops 2097152 | bytes 2097152 | tf_op jit(solution)/shard_map/concatenate | solution.py:164
  80.2 6.4 %shard_map.77 = bf16[256,2048]{1,0:T(8,128)(2,1)} custom-call(s32[128]{0:T(128)} %reshape.78.code_ref, bf16[256,2048]{1,0:T(8,128)(2,1)} %subtract_convert_fusion.s_ref, bf16[256,1024]{1,0:T(8,128)(2,1)} %get-tuple-element.25.o_ref, bf16[256,1024]{1,0:T(8,128)(2,1)} %get-tuple-element.26.i_ref, f32[5,128,128]{2,1,0:T(8,128)} %concatenate.34.taper_ref, ...), custom_call_target="tpu_custom_call" | custom-call | flops 2147483648 | bytes 4194304 | tf_op jit(solution)/shard_map/pallas_call | solution.py:261
  86.6 1.5 %copy.33 = bf16[32,8,8,256]{3,2,1,0:T(8,128)(2,1)S(1)} copy(bf16[32,8,8,256]{3,1,2,0:T(8,128)(2,1)} %bitcast.63) | data formatting | bytes 2097152
  88.1 20.0 %all_to_all.38 = bf16[256,8,256]{2,1,0:T(8,128)(2,1)S(1)} all-to-all(bf16[256,8,256]{2,1,0:T(8,128)(2,1)S(1)} %bitcast.56), channel_id=1, replica_groups=mesh['wide'=8,'lon'=4] {'wide'}, dimensions={0} | all-to-all | bytes 2097152 | tf_op jit(solution)/shard_map/all_to_all | solution.py:178
  108.0 1.1 %copy.36 = bf16[8,32,8,256]{3,2,0,1:T(8,128)(2,1)} copy(bf16[8,32,8,256]{3,2,1,0:T(8,128)(2,1)S(1)} %bitcast.57) | data formatting | bytes 2097152 | tf_op jit(solution)/shard_map/all_to_all | solution.py:178
  (19 shorter events, 0.2 us)
Async XLA Ops:
  0.0 11.2 %copy-start = (f32[4,64,256]{2,1,0:T(8,128)S(1)}, f32[4,64,256]{2,1,0:T(8,128)}, u32[]{:S(2)}) copy-start(f32[4,64,256]{2,1,0:T(8,128)} %param.10) | copy-start | bytes 786436
  0.0 10.1 %copy-start.8 = (s32[1,16]{1,0:T(1,128)S(1)}, s32[1,16]{1,0:T(1,128)}, u32[]{:S(2)}) copy-start(s32[1,16]{1,0:T(1,128)} %param.12) | copy-start | bytes 196
  0.0 10.1 %copy-start.7 = (s32[1,16,16]{2,1,0:T(8,128)S(1)}, s32[1,16,16]{2,1,0:T(8,128)}, u32[]{:S(2)}) copy-start(s32[1,16,16]{2,1,0:T(8,128)} %param.13) | copy-start | bytes 3076
  0.0 10.2 %copy-start.6 = (s32[1,16,16]{2,1,0:T(8,128)S(1)}, s32[1,16,16]{2,1,0:T(8,128)}, u32[]{:S(2)}) copy-start(s32[1,16,16]{2,1,0:T(8,128)} %param.11) | copy-start | bytes 3076
  0.0 12.5 %copy-start.4 = (bf16[256,8,256]{2,1,0:T(8,128)(2,1)S(1)}, bf16[256,8,256]{2,1,0:T(8,128)(2,1)}, u32[]{:S(2)}) copy-start(bf16[256,8,256]{2,1,0:T(8,128)(2,1)} %param.8) | copy-start | bytes 3145732
  2.9 12.0 %all-to-all-start = ((bf16[4,2,2048]{2,1,0:T(2,128)(2,1)}), bf16[4,2,2048]{2,1,0:T(2,128)(2,1)S(1)}, u32[]{:S(2)}, u32[]{:S(2)}) async-start(bf16[4,2,2048]{2,1,0:T(2,128)(2,1)} %reshape.84), calls=%async_computation | async-start | bytes 65536 | tf_op jit(solution)/shard_map/all_to_all | solution.py:32
  12.9 18.3 %copy-start.3 = (bf16[32,8,8,256]{3,1,2,0:T(8,128)(2,1)}, bf16[32,8,8,256]{3,1,2,0:T(8,128)(2,1)S(1)}, u32[]{:S(2)}) copy-start(bf16[32,8,8,256]{3,1,2,0:T(8,128)(2,1)S(1)} %copy.32) | copy-start | bytes 3145732
  21.9 7.3 %copy-start.5 = (f32[4,128,128]{2,1,0:T(8,128)S(1)}, f32[4,128,128]{2,1,0:T(8,128)}, u32[]{:S(2)}) copy-start(f32[4,128,128]{2,1,0:T(8,128)} %fusion.3) | copy-start | bytes 786436
  24.8 19.1 %all-to-all-start.1 = ((bf16[32,64,256]{2,0,1:T(8,128)(2,1)}), bf16[32,64,256]{2,0,1:T(8,128)(2,1)S(1)}, u32[]{:S(2)}, u32[]{:S(2)}) async-start(bf16[32,64,256]{2,0,1:T(8,128)(2,1)} %copy.23), calls=%async_computation.1 | async-start | bytes 2097152 | tf_op jit(solution)/shard_map/all_to_all | solution.py:129
  46.4 8.6 %copy-start.1 = (bf16[32,8,8,256]{3,1,2,0:T(8,128)(2,1)S(1)}, bf16[32,8,8,256]{3,1,2,0:T(8,128)(2,1)}, u32[]{:S(2)}) copy-start(bf16[32,8,8,256]{3,1,2,0:T(8,128)(2,1)} %copy.28) | copy-start | bytes 3145732
  53.9 2.4 %copy-start.2 = (bf16[256,1024]{1,0:T(8,128)(2,1)S(1)}, bf16[256,1024]{1,0:T(8,128)(2,1)}, u32[]{:S(2)}) copy-start(bf16[256,1024]{1,0:T(8,128)(2,1)} %shard_map.74) | copy-start | bytes 1572868
  56.4 21.8 %collective-permute-start = (bf16[2,256,512]{2,1,0:T(8,128)(2,1)S(1)}, bf16[2,256,512]{2,1,0:T(8,128)(2,1)S(1)}, u32[]{:S(2)}, u32[]{:S(2)}) collective-permute-start(bf16[2,256,512]{2,1,0:T(8,128)(2,1)S(1)} %get-tuple-element.5), channel_id=1, source_target_pairs={{0,1},{1,2},{2,3},{3,0},{4,5},{5,6},{6,7},{7,4},{8,9},{9,10},{10,1... | collective-permute-start | bytes 1572872 | tf_op jit(solution)/shard_map/ppermute | solution.py:149
  57.1 21.8 %collective-permute-start.1 = (bf16[2,256,512]{2,1,0:T(8,128)(2,1)S(1)}, bf16[2,256,512]{2,1,0:T(8,128)(2,1)S(1)}, u32[]{:S(2)}, u32[]{:S(2)}) collective-permute-start(bf16[2,256,512]{2,1,0:T(8,128)(2,1)S(1)} %get-tuple-element.6), channel_id=1, source_target_pairs={{1,0},{2,1},{3,2},{0,3},{5,4},{6,5},{7,6},{4,7},{9,8},{10,9},{11,1... | collective-permute-start | bytes 1572872 | tf_op jit(solution)/shard_map/ppermute | solution.py:150

commit v12 on v11

--- a/solution.py
+++ b/solution.py
@@ -35,17 +35,27 @@
     return west, east
 
 
-def forecast_call(state, west, east):
+def stencil(state, east, west, northern, southern):
+    member_spread = east + west + northern + southern - 4.0 * state
+    return (state + 0.2 * member_spread - 0.3 * (east - west)).astype(jnp.bfloat16)
+
+
+def rows_beside(column):
+    northern = jnp.pad(column[:, 1:, :], ((0, 0), (0, 1), (0, 0)))
+    southern = jnp.pad(column[:, :-1, :], ((0, 0), (1, 0), (0, 0)))
+    return northern, southern
+
+
+def forecast_call(state):
     members, rows, cols = state.shape
 
-    def kernel(x_ref, w_ref, e_ref, o_ref):
-        col = lax.broadcasted_iota(jnp.int32, (rows, cols), 1)
+    def kernel(x_ref, o_ref):
         row = lax.broadcasted_iota(jnp.int32, (rows, cols), 0)
 
         def one(m, carry):
             x = x_ref[m].astype(jnp.float32)
-            east_n = jnp.where(col == cols - 1, e_ref[m].astype(jnp.float32), pltpu.roll(x, cols - 1, 1))
-            west_n = jnp.where(col == 0, w_ref[m].astype(jnp.float32), pltpu.roll(x, 1, 1))
+            east_n = pltpu.roll(x, cols - 1, 1)
+            west_n = pltpu.roll(x, 1, 1)
             north = jnp.where(row == rows - 1, 0.0, pltpu.roll(x, rows - 1, 0))
             south = jnp.where(row == 0, 0.0, pltpu.roll(x, 1, 0))
             spread = east_n + west_n + north + south - 4.0 * x
@@ -54,7 +64,7 @@
 
         lax.fori_loop(0, members, one, 0, unroll=4)
 
-    return pl.pallas_call(kernel, out_shape=jax.ShapeDtypeStruct(state.shape, jnp.bfloat16))(state, west, east)
+    return pl.pallas_call(kernel, out_shape=jax.ShapeDtypeStruct(state.shape, jnp.bfloat16))(state)
 
 
 def observe_region(state, index, weight):
@@ -120,8 +130,13 @@
 
 
 def body(background_ensemble, innov, obs_index, obs_weight, obs_list, tile_count, taper_class):
+    inner = forecast_call(background_ensemble)
     west_col, east_col = column_halo(background_ensemble, "lon")
-    prediction_increment = forecast_call(background_ensemble, west_col, east_col)
+    near = background_ensemble[..., :2].astype(jnp.float32)
+    far = background_ensemble[..., -2:].astype(jnp.float32)
+    first = stencil(near[..., :1], near[..., 1:2], west_col.astype(jnp.float32), *rows_beside(near[..., :1]))
+    last = stencil(far[..., 1:], east_col.astype(jnp.float32), far[..., :1], *rows_beside(far[..., 1:]))
+    prediction_increment = jnp.concatenate([first, inner[..., 1:-1], last], axis=-1)
     ensemble_lines_here, whole_parallel_set, patch_meridian_lines = prediction_increment.shape
     members = innov.shape[0]
     band_rows = innov.shape[1]

time: 110 us -> 121 us (1.10)
  local copies, waits for them, and re-layouts: 17.8 us -> 23.6 us
  other arithmetic: 8.45 us -> 14.2 us
    convert_element_type x0 -> x4, other arithmetic: none -> 4.33 us  [the longest x1 4.04 us: stencil(): (state + 0.2 * member_spread - 0.3 * (east - west)).astype(jnp.bfloat16)]
    slice x1 -> x3, local copies, waits for them, and re-layouts: 1.01 us -> 5.15 us  [the longest x2 3.49 us: rows_beside(): northern = jnp.pad(column[:, 1:, :], ((0, 0), (0, 1), (0, 0)))]
    pallas_call x1 -> x0, local copies, waits for them, and re-layouts: 2.84 us -> none  [forecast_call(): pl.pallas_call(kernel, out_shape=jax.ShapeDtypeStruct(state.shape, jnp.bf...]
    convert_element_type x0 -> x2, local copies, waits for them, and re-layouts: none -> 2.77 us  [the longest x1 1.39 us: body(): west_col.astype(jnp.float32)]
    concatenate x0 -> x2, other arithmetic: none -> 1.66 us  [the longest x1 0.87 us: body(): halo_innov = jnp.concatenate([west[1], east[1]], axis=1)]
    concatenate x0 -> x1, local copies, waits for them, and re-layouts: none -> 1.56 us  [body(): jnp.concatenate([first, inner[..., 1:-1], last], axis=-1)]
    dynamic_slice x3 -> x0, local copies, waits for them, and re-layouts: 1.44 us -> none  [the longest x2 1.1 us: column_halo(): lax.dynamic_index_in_dim(got, (here + 1) % size, 0, keepdims=False)]
    all_to_all x1, waiting for transfers between devices: 1.33 us -> 0.01 us  [column_halo(): got = lax.all_to_all(spread, axis, 0, 0, tiled=False)]
  transfers between devices with their start and end apart: 4 -> 4, of which waited for: 3 -> 2; matrix products, arithmetic and copies ran while one was open for 8% -> 14% of each run, Pallas kernels for 14% -> 16%
where the time goes in v12:
time: 121 us; the launch traced here: 120 us
  Pallas kernels  33.6 us (28%)
  local copies, waits for them, and re-layouts  23.6 us (20%)
  blocking collectives  20 us (17%)
  waiting for transfers between devices  14.4 us (12%)
  other arithmetic  14.2 us (12%)
  starting transfers between devices  14.2 us (12%)
    all_to_all x1, blocking collectives, body(): lax.all_to_all(result.reshape(members, band_rows, patch_meridian_lines),...  20 us
    pallas_call x2, Pallas kernels, observe_dev_call(): pl.pallas_call(kernel, grid=(count // OBS_STEP,), in_specs=[pl.BlockSpec(...  14.8 us
    pallas_call x2, Pallas kernels, update_call(): pl.pallas_call(kernel, grid_spec=grid_spec, out_shape=jax.ShapeDtypeStruc...  14.8 us
    all_to_all x1, waiting for transfers between devices, body(): lax.all_to_all(prediction_increment, 'wide', split_axis=1, concat_axis=0,...  12.6 us
    all_to_all x1, starting transfers between devices, column_halo(): got = lax.all_to_all(spread, axis, 0, 0, tiled=False)  6.32 us
    unnamed x36, local copies, waits for them, and re-layouts  5.59 us
    convert_element_type x1, other arithmetic, stencil(): (state + 0.2 * member_spread - 0.3 * (east - west)).astype(jnp.bfloat16)  4.04 us
    pallas_call x1, Pallas kernels, forecast_call(): pl.pallas_call(kernel, out_shape=jax.ShapeDtypeStruct(state.shape, jnp.bf...  3.98 us
  transfers between devices with their start and end apart: 4, of which 2 were waited for; matrix products, arithmetic and copies ran while one was open for 14% of the time, Pallas kernels for 16%

profile of v12, /device:TPU:0, one launch (start us, length us, event | category | flops | bytes accessed | tf_op | source)
XLA Modules:
  0.0 120.1 jit_solution(16711410912764450915)
XLA Ops:
  0.0 1.5 %fusion.8 = (bf16[32,64,1]{2,1,0:T(8,128)(2,1)S(1)}, bf16[32,64,1]{2,1,0:T(8,128)(2,1)S(1)}) fusion(bf16[32,64,256]{2,1,0:T(8,128)(2,1)} %x_ref.1), kind=kLoop, calls=%fused_computation.46 | loop fusion | bytes 16384 | tf_op jit(solution)/shard_map/slice | solution.py:30
  1.6 0.3 copy.35
  1.8 0.3 copy.36
  2.1 0.7 reshape.84
  2.9 6.3 %all-to-all-start = ((bf16[4,2,2048]{2,1,0:T(2,128)(2,1)}), bf16[4,2,2048]{2,1,0:T(2,128)(2,1)S(1)}, u32[]{:S(2)}, u32[]{:S(2)}) async-start(bf16[4,2,2048]{2,1,0:T(2,128)(2,1)} %reshape.84), calls=%async_computation | async-start | bytes 65536 | tf_op jit(solution)/shard_map/all_to_all | solution.py:32
  9.2 0.3 slice_convert_fusion.1
  9.5 1.5 %fusion.6 = (f32[32,63,1]{2,1,0:T(8,128)}, f32[32,63,1]{2,1,0:T(8,128)}) fusion(f32[32,64,2]{2,1,0:T(8,128)S(1)} %get-tuple-element.11), kind=kLoop, calls=%fused_computation.44 | loop fusion | bytes 32256 | tf_op jit(solution)/shard_map/slice | solution.py:44
  11.1 1.9 %fusion.7 = (f32[32,63,1]{2,1,0:T(8,128)}, f32[32,63,1]{2,1,0:T(8,128)}) fusion(f32[32,64,2]{2,1,0:T(8,128)S(1)} %get-tuple-element.12), kind=kLoop, calls=%fused_computation.45 | loop fusion | bytes 32256 | tf_op jit(solution)/shard_map/slice | solution.py:44
  13.0 0.8 subtract_bitcast_fusion
  13.8 0.6 fusion.11
  14.4 0.0 copy-done.10
  14.4 0.1 fusion.4
  14.5 0.1 select_reduce_fusion
  14.7 0.1 fusion.12
  14.7 0.8 fusion.3
  15.6 4.0 %shard_map.73 = bf16[32,64,256]{2,1,0:T(8,128)(2,1)} custom-call(bf16[32,64,256]{2,1,0:T(8,128)(2,1)} %x_ref.1), custom_call_target="tpu_custom_call" | custom-call | tf_op jit(solution)/shard_map/pallas_call | solution.py:67
  19.6 0.6 slice.169.i_ref
  20.2 0.1 slice.167
  20.2 1.7 %slice.149 = bf16[32,64,254]{2,1,0:T(8,128)(2,1)S(1)} slice(bf16[32,64,256]{2,1,0:T(8,128)(2,1)} %shard_map.73), slice={[0:32], [0:64], [1:255]} | slice | bytes 2080768 | tf_op jit(solution)/shard_map/slice | solution.py:139
  21.9 0.6 slice.170.w_ref
  22.5 0.0 copy-done.5
  22.5 1.3 %copy.41 = bf16[32,8,8,256]{3,1,2,0:T(8,128)(2,1)} copy(bf16[32,8,8,256]{3,2,1,0:T(8,128)(2,1)S(1)} %bitcast.61) | data formatting | bytes 2097152
  23.8 0.7 reshape.82.code_ref
  24.5 0.0 all-to-all-done
  24.5 0.1 reshape.85
  24.6 1.4 %copy.28 = f32[32,64,1]{2,1,0:T(8,128)} copy(f32[32,64,1]{1,0,2:T(8,128)S(1)} %slice_convert_fusion.3) | data formatting | bytes 16384 | tf_op jit(solution)/shard_map/convert_element_type | solution.py:137
  26.0 1.4 %copy.30 = f32[32,64,1]{2,1,0:T(8,128)} copy(f32[32,64,1]{1,0,2:T(8,128)S(1)} %slice_convert_fusion.2) | data formatting | bytes 16384 | tf_op jit(solution)/shard_map/convert_element_type | solution.py:138
  27.4 4.0 %subtract_convert_fusion.1 = (bf16[32,64,1]{2,1,0:T(8,128)(2,1)S(1)}, bf16[32,64,1]{2,1,0:T(8,128)(2,1)S(1)}) fusion(f32[32,64,1]{2,1,0:T(8,128)} %copy.30, f32[32,64,2]{2,1,0:T(8,128)S(1)} %get-tuple-element.12, f32[32,63,1]{2,1,0:T(8,128)} %get-tuple-element.14, f32[32,63,1]{2,1,0:T(8,128)} %get-tuple-element.13, f32[32,64,1]{2,1,0:T(8,128)} %copy.28, ...), kind=kLoop, calls=%fused_computation.7 | loop fusion | flops 45056 | bytes 89600 | tf_op jit(solution)/shard_map/convert_element_type | solution.py:40
  31.5 0.8 pad_maximum_fusion
  32.3 0.0 copy-start.6
  32.3 0.0 copy-start.7
  32.3 0.0 copy-start.8
  32.3 0.0 copy-start.4
  32.3 1.6 %copy.32 = bf16[32,64,256]{2,0,1:T(8,128)(2,1)} copy(bf16[32,64,256]{2,1,0:T(8,128)(2,1)S(1)} %pad_maximum_fusion) | data formatting | bytes 2097152 | tf_op jit(solution)/shard_map/concatenate | solution.py:139
  33.9 3.7 %all-to-all-start.1 = ((bf16[32,64,256]{2,0,1:T(8,128)(2,1)}), bf16[32,64,256]{2,0,1:T(8,128)(2,1)S(1)}, u32[]{:S(2)}, u32[]{:S(2)}) async-start(bf16[32,64,256]{2,0,1:T(8,128)(2,1)} %copy.32), calls=%async_computation.1 | async-start | bytes 2097152 | tf_op jit(solution)/shard_map/all_to_all | solution.py:144
  37.6 0.1 pad_add_fusion.1
  37.7 0.6 reshape.78.code_ref
  38.3 0.0 copy-done.6
  38.3 0.8 concatenate.38.taper_ref
  39.1 0.6 pad_add_fusion.i_ref
  39.7 0.6 pad_maximum_fusion.6.w_ref
  40.3 0.1 maximum_bitcast_fusion
  40.4 12.6 %all-to-all-done.1 = bf16[32,64,256]{2,0,1:T(8,128)(2,1)S(1)} async-done(((bf16[32,64,256]{2,0,1:T(8,128)(2,1)}), bf16[32,64,256]{2,0,1:T(8,128)(2,1)S(1)}, u32[]{:S(2)}, u32[]{:S(2)}) %all-to-all-start.1) | async-done | bytes 1048608 | tf_op jit(solution)/shard_map/all_to_all | solution.py:144
  53.0 0.6 copy.33
  53.6 0.6 convert_reduce_fusion
  54.3 1.3 %copy.37 = bf16[32,8,8,256]{3,1,2,0:T(8,128)(2,1)} copy(bf16[32,8,8,256]{3,2,1,0:T(8,128)(2,1)S(1)} %bitcast.56) | data formatting | bytes 2097152
  55.5 7.5 %shard_map.74 = bf16[256,1024]{1,0:T(8,128)(2,1)} custom-call(bf16[256,2048]{1,0:T(8,128)(2,1)} %bitcast.49, s32[4,1024]{1,0:T(4,128)} %pad_add_fusion.i_ref, f32[4,1024]{1,0:T(4,128)} %pad_maximum_fusion.6.w_ref), custom_call_target="tpu_custom_call" | custom-call | tf_op jit(solution)/shard_map/pallas_call | solution.py:107
  63.0 1.1 fusion.9
  64.1 0.0 copy-done.1
  64.1 1.2 subtract_convert_fusion.s_ref
  65.3 0.1 fusion
  65.4 2.1 %collective-permute-start = (bf16[2,256,512]{2,1,0:T(8,128)(2,1)S(1)}, bf16[2,256,512]{2,1,0:T(8,128)(2,1)S(1)}, u32[]{:S(2)}, u32[]{:S(2)}) collective-permute-start(bf16[2,256,512]{2,1,0:T(8,128)(2,1)S(1)} %get-tuple-element.5), channel_id=1, source_target_pairs={{0,1},{1,2},{2,3},{3,0},{4,5},{5,6},{6,7},{7,4},{8,9},{9,10},{10,1... | collective-permute-start | bytes 1572872 | tf_op jit(solution)/shard_map/ppermute | solution.py:164
  67.5 2.0 %collective-permute-start.1 = (bf16[2,256,512]{2,1,0:T(8,128)(2,1)S(1)}, bf16[2,256,512]{2,1,0:T(8,128)(2,1)S(1)}, u32[]{:S(2)}, u32[]{:S(2)}) collective-permute-start(bf16[2,256,512]{2,1,0:T(8,128)(2,1)S(1)} %get-tuple-element.6), channel_id=1, source_target_pairs={{1,0},{2,1},{3,2},{0,3},{5,4},{6,5},{7,6},{4,7},{9,8},{10,9},{11,1... | collective-permute-start | bytes 1572872 | tf_op jit(solution)/shard_map/ppermute | solution.py:165
  69.5 7.4 %shard_map.75 = bf16[256,1024]{1,0:T(8,128)(2,1)} custom-call(bf16[256,2048]{1,0:T(8,128)(2,1)} %bitcast.50, s32[4,1024]{1,0:T(4,128)} %slice.169.i_ref, f32[4,1024]{1,0:T(4,128)} %slice.170.w_ref), custom_call_target="tpu_custom_call" | custom-call | tf_op jit(solution)/shard_map/pallas_call | solution.py:107
  76.9 2.2 %pad_maximum_fusion.1.o_ref = bf16[256,2048]{1,0:T(8,128)(2,1)} fusion(bf16[256,512]{1,0:T(8,128)(2,1)S(1)} %get-tuple-element.18, bf16[256,1024]{1,0:T(8,128)(2,1)} %shard_map.75, bf16[256,512]{1,0:T(8,128)(2,1)S(1)} %get-tuple-element.17), kind=kLoop, calls=%fused_computation.5 | loop fusion | flops 3145728 | bytes 2097152 | tf_op jit(solution)/shard_map/concatenate | solution.py:167
  79.1 8.4 %shard_map.76.rest_0_ = f32[256,2048]{1,0:T(8,128)} custom-call(s32[256]{0:T(256)} %reshape.82.code_ref, bf16[256,2048]{1,0:T(8,128)(2,1)} %subtract_convert_fusion.s_ref, bf16[256,2048]{1,0:T(8,128)(2,1)} %pad_maximum_fusion.1.o_ref, bf16[256,2048]{1,0:T(8,128)(2,1)} %bitcast.59, f32[5,128,128]{2,1,0:T(8,128)} %concatenate.38.taper_ref), custom_call_target="tpu_custom_call" | custom-call | flops 4294967296 | bytes 4194304 | tf_op jit(solution)/shard_map/pallas_call | solution.py:276
  87.5 0.0 collective-permute-done
  87.6 1.8 %collective-permute-done.1 = bf16[2,256,512]{2,1,0:T(8,128)(2,1)S(1)} collective-permute-done((bf16[2,256,512]{2,1,0:T(8,128)(2,1)S(1)}, bf16[2,256,512]{2,1,0:T(8,128)(2,1)S(1)}, u32[]{:S(2)}, u32[]{:S(2)}) %collective-permute-start.1) | collective-permute-done | bytes 524320 | tf_op jit(solution)/shard_map/ppermute | solution.py:165
  89.4 0.9 pad_maximum_fusion.4.i_ref
  90.2 0.9 pad_maximum_fusion.3.o_ref
  91.1 6.4 %shard_map.77 = bf16[256,2048]{1,0:T(8,128)(2,1)} custom-call(s32[128]{0:T(128)} %reshape.78.code_ref, bf16[256,2048]{1,0:T(8,128)(2,1)} %subtract_convert_fusion.s_ref, bf16[256,1024]{1,0:T(8,128)(2,1)} %pad_maximum_fusion.3.o_ref, bf16[256,1024]{1,0:T(8,128)(2,1)} %pad_maximum_fusion.4.i_ref, f32[5,128,128]{2,1,0:T(8,128)} %concatenate.38.taper_ref, ...), custom_call_target="tpu_custom_call" | custom-call | flops 2147483648 | bytes 4194304 | tf_op jit(solution)/shard_map/pallas_call | solution.py:276
  97.5 1.5 %copy.42 = bf16[32,8,8,256]{3,2,1,0:T(8,128)(2,1)S(1)} copy(bf16[32,8,8,256]{3,1,2,0:T(8,128)(2,1)} %bitcast.62) | data formatting | bytes 2097152
  99.0 20.0 %all_to_all.38 = bf16[256,8,256]{2,1,0:T(8,128)(2,1)S(1)} all-to-all(bf16[256,8,256]{2,1,0:T(8,128)(2,1)S(1)} %bitcast.57), channel_id=1, replica_groups=mesh['wide'=8,'lon'=4] {'wide'}, dimensions={0} | all-to-all | bytes 2097152 | tf_op jit(solution)/shard_map/all_to_all | solution.py:193
  119.0 1.1 copy.45
  (33 shorter events, 0.3 us)
Async XLA Ops:
  0.0 15.6 %copy-start = (f32[4,64,256]{2,1,0:T(8,128)S(1)}, f32[4,64,256]{2,1,0:T(8,128)}, u32[]{:S(2)}) copy-start(f32[4,64,256]{2,1,0:T(8,128)} %param.10) | copy-start | bytes 786436
  0.0 9.2 %copy-start.2 = (bf16[32,64,256]{2,1,0:T(8,128)(2,1)S(1)}, bf16[32,64,256]{2,1,0:T(8,128)(2,1)}, u32[]{:S(2)}) copy-start(bf16[32,64,256]{2,1,0:T(8,128)(2,1)} %x_ref.1) | copy-start | bytes 3145732
  2.9 21.6 %all-to-all-start = ((bf16[4,2,2048]{2,1,0:T(2,128)(2,1)}), bf16[4,2,2048]{2,1,0:T(2,128)(2,1)S(1)}, u32[]{:S(2)}, u32[]{:S(2)}) async-start(bf16[4,2,2048]{2,1,0:T(2,128)(2,1)} %reshape.84), calls=%async_computation | async-start | bytes 65536 | tf_op jit(solution)/shard_map/all_to_all | solution.py:32
  11.1 3.3 %copy-start.10 = (s32[1,16,16]{2,1,0:T(8,128)S(1)}, s32[1,16,16]{2,1,0:T(8,128)}, u32[]{:S(2)}) copy-start(s32[1,16,16]{2,1,0:T(8,128)} %param.13) | copy-start | bytes 3076
  11.1 3.3 %copy-start.11 = (s32[1,16]{1,0:T(1,128)S(1)}, s32[1,16]{1,0:T(1,128)}, u32[]{:S(2)}) copy-start(s32[1,16]{1,0:T(1,128)} %param.12) | copy-start | bytes 196
  11.1 3.4 %copy-start.9 = (s32[1,16,16]{2,1,0:T(8,128)S(1)}, s32[1,16,16]{2,1,0:T(8,128)}, u32[]{:S(2)}) copy-start(s32[1,16,16]{2,1,0:T(8,128)} %param.11) | copy-start | bytes 3076
  19.6 3.0 %copy-start.5 = (bf16[256,8,256]{2,1,0:T(8,128)(2,1)S(1)}, bf16[256,8,256]{2,1,0:T(8,128)(2,1)}, u32[]{:S(2)}) copy-start(bf16[256,8,256]{2,1,0:T(8,128)(2,1)} %param.8) | copy-start | bytes 3145732
  32.3 6.0 %copy-start.6 = (f32[4,128,128]{2,1,0:T(8,128)S(1)}, f32[4,128,128]{2,1,0:T(8,128)}, u32[]{:S(2)}) copy-start(f32[4,128,128]{2,1,0:T(8,128)} %fusion.3) | copy-start | bytes 786436
  32.3 6.8 %copy-start.7 = (s32[4,512]{1,0:T(4,128)S(1)}, s32[4,512]{1,0:T(4,128)}, u32[]{:S(2)}) copy-start(s32[4,512]{1,0:T(4,128)} %get-tuple-element.27) | copy-start | bytes 24580
  32.3 6.8 %copy-start.8 = (s32[4,512]{1,0:T(4,128)S(1)}, s32[4,512]{1,0:T(4,128)}, u32[]{:S(2)}) copy-start(s32[4,512]{1,0:T(4,128)} %get-tuple-element.28) | copy-start | bytes 24580
  32.3 8.0 %copy-start.4 = (bf16[32,8,8,256]{3,1,2,0:T(8,128)(2,1)S(1)}, bf16[32,8,8,256]{3,1,2,0:T(8,128)(2,1)}, u32[]{:S(2)}) copy-start(bf16[32,8,8,256]{3,1,2,0:T(8,128)(2,1)} %copy.41) | copy-start | bytes 3145732
  33.9 19.1 %all-to-all-start.1 = ((bf16[32,64,256]{2,0,1:T(8,128)(2,1)}), bf16[32,64,256]{2,0,1:T(8,128)(2,1)S(1)}, u32[]{:S(2)}, u32[]{:S(2)}) async-start(bf16[32,64,256]{2,0,1:T(8,128)(2,1)} %copy.32), calls=%async_computation.1 | async-start | bytes 2097152 | tf_op jit(solution)/shard_map/all_to_all | solution.py:144
  55.5 8.6 %copy-start.1 = (bf16[32,8,8,256]{3,1,2,0:T(8,128)(2,1)S(1)}, bf16[32,8,8,256]{3,1,2,0:T(8,128)(2,1)}, u32[]{:S(2)}) copy-start(bf16[32,8,8,256]{3,1,2,0:T(8,128)(2,1)} %copy.37) | copy-start | bytes 3145732
  63.0 2.4 %copy-start.3 = (bf16[256,1024]{1,0:T(8,128)(2,1)S(1)}, bf16[256,1024]{1,0:T(8,128)(2,1)}, u32[]{:S(2)}) copy-start(bf16[256,1024]{1,0:T(8,128)(2,1)} %shard_map.74) | copy-start | bytes 1572868
  65.4 22.1 %collective-permute-start = (bf16[2,256,512]{2,1,0:T(8,128)(2,1)S(1)}, bf16[2,256,512]{2,1,0:T(8,128)(2,1)S(1)}, u32[]{:S(2)}, u32[]{:S(2)}) collective-permute-start(bf16[2,256,512]{2,1,0:T(8,128)(2,1)S(1)} %get-tuple-element.5), channel_id=1, source_target_pairs={{0,1},{1,2},{2,3},{3,0},{4,5},{5,6},{6,7},{7,4},{8,9},{9,10},{10,1... | collective-permute-start | bytes 1572872 | tf_op jit(solution)/shard_map/ppermute | solution.py:164
  67.5 21.8 %collective-permute-start.1 = (bf16[2,256,512]{2,1,0:T(8,128)(2,1)S(1)}, bf16[2,256,512]{2,1,0:T(8,128)(2,1)S(1)}, u32[]{:S(2)}, u32[]{:S(2)}) collective-permute-start(bf16[2,256,512]{2,1,0:T(8,128)(2,1)S(1)} %get-tuple-element.6), channel_id=1, source_target_pairs={{1,0},{2,1},{3,2},{0,3},{5,4},{6,5},{7,6},{4,7},{9,8},{10,9},{11,1... | collective-permute-start | bytes 1572872 | tf_op jit(solution)/shard_map/ppermute | solution.py:165

commit v13 on v11

--- a/solution.py
+++ b/solution.py
@@ -80,10 +80,16 @@
 
 
 OBS_STEP = 256
-def observe_dev_call(state, index, weight):
+def observe_dev_call(state, index, weight, extra=None):
     members, cells = state.shape
     count = index.shape[1]
-    def kernel(f_ref, i_ref, w_ref, o_ref):
+    carry = extra is not None
+
+    def kernel(f_ref, i_ref, w_ref, *rest):
+        if carry:
+            x_ref, o_ref = rest
+        else:
+            (o_ref,) = rest
         cell_ids = lax.broadcasted_iota(jnp.int32, (cells, OBS_STEP), 0)
         f = f_ref[...]
         summed = jnp.zeros((members, OBS_STEP), jnp.float32)
@@ -93,18 +99,36 @@
             summed = summed + w_ref[k:k + 1, :] * picked
         ens = summed.astype(jnp.bfloat16).astype(jnp.float32)
         mean = jnp.sum(ens, axis=0, keepdims=True) / members
-        o_ref[...] = (ens - mean).astype(jnp.bfloat16)
+        dev = (ens - mean).astype(jnp.bfloat16)
+        if carry:
+            o_ref[0] = dev
+            o_ref[1] = x_ref[...]
+        else:
+            o_ref[...] = dev
+
+    in_specs = [
+        pl.BlockSpec((members, cells), lambda j: (0, 0)),
+        pl.BlockSpec((4, OBS_STEP), lambda j: (0, j)),
+        pl.BlockSpec((4, OBS_STEP), lambda j: (0, j)),
+    ]
+    operands = [state, index, weight]
+    if carry:
+        in_specs.append(pl.BlockSpec((members, OBS_STEP), lambda j: (0, j)))
+        operands.append(extra)
+        out_spec = pl.BlockSpec((2, members, OBS_STEP), lambda j: (0, 0, j))
+        out_shape = jax.ShapeDtypeStruct((2, members, count), jnp.bfloat16)
+    else:
+        out_spec = pl.BlockSpec((members, OBS_STEP), lambda j: (0, j))
+        out_shape = jax.ShapeDtypeStruct((members, count), jnp.bfloat16)
     return pl.pallas_call(
         kernel,
         grid=(count // OBS_STEP,),
-        in_specs=[
-            pl.BlockSpec((members, cells), lambda j: (0, 0)),
-            pl.BlockSpec((4, OBS_STEP), lambda j: (0, j)),
-            pl.BlockSpec((4, OBS_STEP), lambda j: (0, j)),
-        ],
-        out_specs=pl.BlockSpec((members, OBS_STEP), lambda j: (0, j)),
-        out_shape=jax.ShapeDtypeStruct((members, count), jnp.bfloat16),
-    )(state, index, weight)
+        in_specs=in_specs,
+        out_specs=out_spec,
+        out_shape=out_shape,
+    )(*operands)
+
+
 def anomaly_from_mean(state_values):
     centred = state_values.astype(jnp.float32)
     return (centred - jnp.mean(centred, axis=-2, keepdims=True)).astype(jnp.bfloat16)
@@ -138,18 +162,19 @@
     )
     halo = HALO_BLK * BLK
     innov_flat = innov.reshape(members, patch_gridpoints)
-    edge_index = jnp.concatenate([local_index[:, :halo], local_index[:, -halo:]], axis=1)
-    edge_weight = jnp.concatenate([local_weight[:, :halo], local_weight[:, -halo:]], axis=1)
-    edge_dev = observe_dev_call(region_state, edge_index, edge_weight)
-    edge_innov = jnp.concatenate([innov_flat[:, :halo], innov_flat[:, -halo:]], axis=1)
-    edges = jnp.stack([edge_dev, edge_innov])
     lon_size = lax.axis_size("lon")
     up = [(i, (i + 1) % lon_size) for i in range(lon_size)]
     down = [(j, i) for i, j in up]
-    west = lax.ppermute(edges[:, :, halo:], "lon", up)
-    east = lax.ppermute(edges[:, :, :halo], "lon", down)
+    last_edge = observe_dev_call(
+        region_state, local_index[:, -halo:], local_weight[:, -halo:], innov_flat[:, -halo:]
+    )
+    west = lax.ppermute(last_edge, "lon", up)
+    first_edge = observe_dev_call(
+        region_state, local_index[:, :halo], local_weight[:, :halo], innov_flat[:, :halo]
+    )
+    east = lax.ppermute(first_edge, "lon", down)
     middle_dev = observe_dev_call(region_state, local_index[:, halo:-halo], local_weight[:, halo:-halo])
-    obs_dev = jnp.concatenate([edge_dev[:, :halo], middle_dev, edge_dev[:, halo:]], axis=1)
+    obs_dev = jnp.concatenate([first_edge[0], middle_dev, last_edge[0]], axis=1)
     model_anomaly = anomaly_from_mean(region_state)
     halo_blocks = halo // BLK
     block_count = patch_gridpoints // BLK

time: 110 us -> 109 us (level)
  blocking collectives: 20 us -> 17.8 us
  Pallas kernels: 34.1 us -> 36.3 us
  other arithmetic: 8.45 us -> 6.4 us
  local copies, waits for them, and re-layouts: 17.8 us -> 19.7 us
    pallas_call x2 -> x3, Pallas kernels: 14.8 us -> 17 us  [observe_dev_call(): pl.pallas_call(kernel, grid=(count // OBS_STEP,), in_specs=in_specs, out_...]
    all_to_all x1, blocking collectives: 20 us -> 17.8 us  [body(): lax.all_to_all(result.reshape(members, band_rows, patch_meridian_lines),...]
    concatenate x3 -> x1, other arithmetic: 3.36 us -> 2.16 us  [body(): obs_dev = jnp.concatenate([first_edge[0], middle_dev, last_edge[0]], axis=1)]
    unnamed x30 -> x26, local copies, waits for them, and re-layouts: 4.59 us -> 4.58 us
  transfers between devices with their start and end apart: 4 -> 4, of which waited for: 3 -> 2; matrix products, arithmetic and copies ran while one was open for 8% -> 11% of each run, Pallas kernels for 14% -> 19%
where the time goes in v13:
time: 109 us; the launch traced here: 108 us
  Pallas kernels  36.3 us (33%)
  local copies, waits for them, and re-layouts  19.7 us (18%)
  blocking collectives  17.8 us (16%)
  starting transfers between devices  13.9 us (13%)
  waiting for transfers between devices  13.9 us (13%)
  other arithmetic  6.4 us (6%)
    all_to_all x1, blocking collectives, body(): lax.all_to_all(result.reshape(members, band_rows, patch_meridian_lines),...  17.8 us
    pallas_call x3, Pallas kernels, observe_dev_call(): pl.pallas_call(kernel, grid=(count // OBS_STEP,), in_specs=in_specs, out_...  17 us
    pallas_call x2, Pallas kernels, update_call(): pl.pallas_call(kernel, grid_spec=grid_spec, out_shape=jax.ShapeDtypeStruc...  14.8 us
    all_to_all x1, waiting for transfers between devices, body(): lax.all_to_all(prediction_increment, 'wide', split_axis=1, concat_axis=0,...  12.4 us
    all_to_all x1, starting transfers between devices, column_halo(): got = lax.all_to_all(spread, axis, 0, 0, tiled=False)  6.32 us
    unnamed x26, local copies, waits for them, and re-layouts  4.58 us
    pallas_call x1, Pallas kernels, forecast_call(): pl.pallas_call(kernel, out_shape=jax.ShapeDtypeStruct(state.shape, jnp.bf...  4.46 us
    all_to_all x1, starting transfers between devices, body(): lax.all_to_all(prediction_increment, 'wide', split_axis=1, concat_axis=0,...  3.72 us
  transfers between devices with their start and end apart: 4, of which 2 were waited for; matrix products, arithmetic and copies ran while one was open for 11% of the time, Pallas kernels for 19%

profile of v13, /device:TPU:0, one launch (start us, length us, event | category | flops | bytes accessed | tf_op | source)
XLA Modules:
  0.0 108.2 jit_solution(9169012612702374693)
XLA Ops:
  0.0 0.0 copy-start
  0.0 0.0 copy-start.5
  0.0 0.0 copy-start.6
  0.0 0.0 copy-start.4
  0.0 0.0 copy-start.3
  0.0 1.5 %fusion.5 = (bf16[32,64,1]{2,1,0:T(8,128)(2,1)S(1)}, bf16[32,64,1]{2,1,0:T(8,128)(2,1)S(1)}) fusion(bf16[32,64,256]{2,1,0:T(8,128)(2,1)} %x_ref.1), kind=kLoop, calls=%fused_computation.32 | loop fusion | bytes 16384 | tf_op jit(solution)/shard_map/slice | solution.py:30
  1.6 0.3 copy.26
  1.9 0.3 copy.27
  2.2 0.7 reshape.84
  2.9 6.3 %all-to-all-start = ((bf16[4,2,2048]{2,1,0:T(2,128)(2,1)}), bf16[4,2,2048]{2,1,0:T(2,128)(2,1)S(1)}, u32[]{:S(2)}, u32[]{:S(2)}) async-start(bf16[4,2,2048]{2,1,0:T(2,128)(2,1)} %reshape.84), calls=%async_computation | async-start | bytes 65536 | tf_op jit(solution)/shard_map/all_to_all | solution.py:32
  9.2 0.0 copy-done.5
  9.3 0.0 copy-done.6
  9.3 0.1 fusion.3
  9.3 0.0 copy-done.4
  9.3 0.1 select_reduce_fusion
  9.5 0.1 fusion.8
  9.6 0.1 pad_add_fusion
  9.7 0.0 copy-done
  9.7 0.8 subtract_bitcast_fusion
  10.5 0.1 slice.98
  10.6 0.7 reshape.82.code_ref
  11.2 0.6 reshape.78.code_ref
  11.9 0.6 slice.100.i_ref
  12.5 0.6 slice.101.w_ref
  13.1 0.0 copy-done.3
  13.1 0.3 copy.32
  13.4 0.0 copy-start.2
  13.4 1.5 %all-to-all-done = bf16[4,2,2048]{2,1,0:T(2,128)(2,1)S(1)} async-done(((bf16[4,2,2048]{2,1,0:T(2,128)(2,1)}), bf16[4,2,2048]{2,1,0:T(2,128)(2,1)S(1)}, u32[]{:S(2)}, u32[]{:S(2)}) %all-to-all-start) | async-done | bytes 32800 | tf_op jit(solution)/shard_map/all_to_all | solution.py:32
  14.9 0.1 reshape.85
  15.0 1.1 %copy.22 = bf16[1,32,64,2]{3,2,1,0:T(8,128)(2,1)} copy(bf16[1,32,64,2]{2,1,3,0:T(8,128)(2,1)S(1)} %get-tuple-element.13) | data formatting | bytes 16384 | tf_op jit(solution)/shard_map/jit(dynamic_index_in_dim)/dynamic_slice | solution.py:34
  16.1 0.3 copy.21
  16.5 1.0 slice.86.w_ref
  17.5 4.5 %shard_map.73 = bf16[32,64,256]{2,1,0:T(8,128)(2,1)} custom-call(bf16[32,64,256]{2,1,0:T(8,128)(2,1)} %x_ref.1, bf16[32,64,1]{2,1,0:T(8,128)(2,1)} %slice.86.w_ref, bf16[32,64,1]{2,1,0:T(8,128)(2,1)} %bitcast.62), custom_call_target="tpu_custom_call" | custom-call | tf_op jit(solution)/shard_map/pallas_call | solution.py:57
  21.9 2.8 %copy.23 = bf16[32,64,256]{2,0,1:T(8,128)(2,1)} copy(bf16[32,64,256]{2,1,0:T(8,128)(2,1)} %shard_map.73) | data formatting | bytes 2097152 | tf_op jit(solution)/shard_map/pallas_call | solution.py:57
  24.7 3.7 %all-to-all-start.1 = ((bf16[32,64,256]{2,0,1:T(8,128)(2,1)}), bf16[32,64,256]{2,0,1:T(8,128)(2,1)S(1)}, u32[]{:S(2)}, u32[]{:S(2)}) async-start(bf16[32,64,256]{2,0,1:T(8,128)(2,1)} %copy.23), calls=%async_computation.1 | async-start | bytes 2097152 | tf_op jit(solution)/shard_map/all_to_all | solution.py:153
  28.4 0.1 fusion.2
  28.6 0.8 concatenate.22.taper_ref
  29.3 0.6 fusion.7
  29.9 0.6 fusion.6
  30.5 0.0 copy-done.2
  30.5 0.9 fusion.4
  31.4 12.4 %all-to-all-done.1 = bf16[32,64,256]{2,0,1:T(8,128)(2,1)S(1)} async-done(((bf16[32,64,256]{2,0,1:T(8,128)(2,1)}), bf16[32,64,256]{2,0,1:T(8,128)(2,1)S(1)}, u32[]{:S(2)}, u32[]{:S(2)}) %all-to-all-start.1) | async-done | bytes 1048608 | tf_op jit(solution)/shard_map/all_to_all | solution.py:153
  43.8 0.6 convert_reduce_fusion
  44.5 0.6 copy.24
  45.1 1.3 %copy.28 = bf16[32,8,8,256]{3,1,2,0:T(8,128)(2,1)} copy(bf16[32,8,8,256]{3,2,1,0:T(8,128)(2,1)S(1)} %bitcast.56) | data formatting | bytes 2097152
  46.4 0.0 copy-start.1
  46.4 4.9 %shard_map.74 = bf16[2,256,512]{2,1,0:T(8,128)(2,1)} custom-call(bf16[256,2048]{1,0:T(8,128)(2,1)} %bitcast.49, s32[4,512]{1,0:T(4,128)} %get-tuple-element.17.i_ref, f32[4,512]{1,0:T(4,128)} %get-tuple-element.15.w_ref, bf16[256,512]{1,0:T(8,128)(2,1)} %get-tuple-element.5.rest_0_), custom_call_target="tpu_custom_call" | custom-call | tf_op jit(solution)/shard_map/pallas_call | solution.py:123
  51.3 0.7 collective-permute-start
  52.0 4.8 %shard_map.75 = bf16[2,256,512]{2,1,0:T(8,128)(2,1)} custom-call(bf16[256,2048]{1,0:T(8,128)(2,1)} %bitcast.50, s32[4,512]{1,0:T(4,128)} %get-tuple-element.18.i_ref, f32[4,512]{1,0:T(4,128)} %get-tuple-element.16.w_ref, bf16[256,512]{1,0:T(8,128)(2,1)} %get-tuple-element.6.rest_0_), custom_call_target="tpu_custom_call" | custom-call | tf_op jit(solution)/shard_map/pallas_call | solution.py:123
  56.8 1.1 slice_bitcast_fusion
  57.8 3.1 %collective-permute-start.1 = (bf16[2,256,512]{2,1,0:T(8,128)(2,1)}, bf16[2,256,512]{2,1,0:T(8,128)(2,1)S(1)}, u32[]{:S(2)}, u32[]{:S(2)}) collective-permute-start(bf16[2,256,512]{2,1,0:T(8,128)(2,1)} %shard_map.75), channel_id=1, source_target_pairs={{1,0},{2,1},{3,2},{0,3},{5,4},{6,5},{7,6},{4,7},{9,8},{10,9},{11,1... | collective-permute-start | bytes 1572872 | tf_op jit(solution)/shard_map/ppermute | solution.py:175
  61.0 0.0 copy-done.1
  61.0 1.2 %subtract_convert_fusion.s_ref = bf16[256,2048]{1,0:T(8,128)(2,1)} fusion(bf16[256,2048]{1,0:T(8,128)(2,1)S(1)} %bitcast.53, f32[2048]{0:T(1024)S(1)} %bitcast.70), kind=kLoop, calls=%fused_computation | loop fusion | flops 1572864 | bytes 2105344 | tf_op jit(solution)/shard_map/convert_element_type | solution.py:134
  62.2 7.4 %shard_map.76 = bf16[256,1024]{1,0:T(8,128)(2,1)} custom-call(bf16[256,2048]{1,0:T(8,128)(2,1)} %bitcast.51, s32[4,1024]{1,0:T(4,128)} %slice.100.i_ref, f32[4,1024]{1,0:T(4,128)} %slice.101.w_ref), custom_call_target="tpu_custom_call" | custom-call | tf_op jit(solution)/shard_map/pallas_call | solution.py:123
  69.6 2.2 %pad_maximum_fusion.o_ref = bf16[256,2048]{1,0:T(8,128)(2,1)} fusion(bf16[256,512]{1,0:T(8,128)(2,1)S(1)} %get-tuple-element.23, bf16[256,1024]{1,0:T(8,128)(2,1)} %shard_map.76, bf16[256,512]{1,0:T(8,128)(2,1)S(1)} %get-tuple-element.24), kind=kLoop, calls=%fused_computation.2 | loop fusion | flops 3145728 | bytes 2097152 | tf_op jit(solution)/shard_map/concatenate | solution.py:177
  71.8 8.4 %shard_map.77.rest_0_ = f32[256,2048]{1,0:T(8,128)} custom-call(s32[256]{0:T(256)} %reshape.82.code_ref, bf16[256,2048]{1,0:T(8,128)(2,1)} %subtract_convert_fusion.s_ref, bf16[256,2048]{1,0:T(8,128)(2,1)} %pad_maximum_fusion.o_ref, bf16[256,2048]{1,0:T(8,128)(2,1)} %bitcast.60, f32[5,128,128]{2,1,0:T(8,128)} %concatenate.22.taper_ref), custom_call_target="tpu_custom_call" | custom-call | flops 4294967296 | bytes 4194304 | tf_op jit(solution)/shard_map/pallas_call | solution.py:286
  80.2 0.0 collective-permute-done
  80.2 0.0 collective-permute-done.1
  80.3 1.1 %pad_maximum_fusion.1 = (bf16[256,1024]{1,0:T(8,128)(2,1)}, bf16[256,1024]{1,0:T(8,128)(2,1)}) fusion(bf16[256,512]{1,0:T(8,128)(2,1)S(1)} %get-tuple-element.12, bf16[256,512]{1,0:T(8,128)(2,1)S(1)} %get-tuple-element.10, bf16[256,512]{1,0:T(8,128)(2,1)S(1)} %get-tuple-element.11, bf16[256,512]{1,0:T(8,128)(2,1)S(1)} %get-tuple-element.9), kind=kLoop, calls=%fused_computation.4 | loop fusion | flops 2097152 | bytes 2097152 | tf_op jit(solution)/shard_map/concatenate | solution.py:189
  81.4 6.4 %shard_map.78 = bf16[256,2048]{1,0:T(8,128)(2,1)} custom-call(s32[128]{0:T(128)} %reshape.78.code_ref, bf16[256,2048]{1,0:T(8,128)(2,1)} %subtract_convert_fusion.s_ref, bf16[256,1024]{1,0:T(8,128)(2,1)} %get-tuple-element.21.o_ref, bf16[256,1024]{1,0:T(8,128)(2,1)} %get-tuple-element.22.i_ref, f32[5,128,128]{2,1,0:T(8,128)} %concatenate.22.taper_ref, ...), custom_call_target="tpu_custom_call" | custom-call | flops 2147483648 | bytes 4194304 | tf_op jit(solution)/shard_map/pallas_call | solution.py:286
  87.8 1.5 %copy.33 = bf16[32,8,8,256]{3,2,1,0:T(8,128)(2,1)S(1)} copy(bf16[32,8,8,256]{3,1,2,0:T(8,128)(2,1)} %bitcast.64) | data formatting | bytes 2097152
  89.4 17.8 %all_to_all.38 = bf16[256,8,256]{2,1,0:T(8,128)(2,1)S(1)} all-to-all(bf16[256,8,256]{2,1,0:T(8,128)(2,1)S(1)} %bitcast.57), channel_id=1, replica_groups=mesh['wide'=8,'lon'=4] {'wide'}, dimensions={0} | all-to-all | bytes 2097152 | tf_op jit(solution)/shard_map/all_to_all | solution.py:203
  107.1 1.1 %copy.36 = bf16[8,32,8,256]{3,2,0,1:T(8,128)(2,1)} copy(bf16[8,32,8,256]{3,2,1,0:T(8,128)(2,1)S(1)} %bitcast.58) | data formatting | bytes 2097152 | tf_op jit(solution)/shard_map/all_to_all | solution.py:203
  (13 shorter events, 0.2 us)
Async XLA Ops:
  0.0 9.7 %copy-start = (f32[4,64,256]{2,1,0:T(8,128)S(1)}, f32[4,64,256]{2,1,0:T(8,128)}, u32[]{:S(2)}) copy-start(f32[4,64,256]{2,1,0:T(8,128)} %param.10) | copy-start | bytes 786436
  0.0 9.2 %copy-start.5 = (s32[1,16,16]{2,1,0:T(8,128)S(1)}, s32[1,16,16]{2,1,0:T(8,128)}, u32[]{:S(2)}) copy-start(s32[1,16,16]{2,1,0:T(8,128)} %param.13) | copy-start | bytes 3076
  0.0 9.3 %copy-start.6 = (s32[1,16]{1,0:T(1,128)S(1)}, s32[1,16]{1,0:T(1,128)}, u32[]{:S(2)}) copy-start(s32[1,16]{1,0:T(1,128)} %param.12) | copy-start | bytes 196
  0.0 9.3 %copy-start.4 = (s32[1,16,16]{2,1,0:T(8,128)S(1)}, s32[1,16,16]{2,1,0:T(8,128)}, u32[]{:S(2)}) copy-start(s32[1,16,16]{2,1,0:T(8,128)} %param.11) | copy-start | bytes 3076
  0.0 13.1 %copy-start.3 = (bf16[256,8,256]{2,1,0:T(8,128)(2,1)S(1)}, bf16[256,8,256]{2,1,0:T(8,128)(2,1)}, u32[]{:S(2)}) copy-start(bf16[256,8,256]{2,1,0:T(8,128)(2,1)} %param.8) | copy-start | bytes 3145732
  2.9 12.0 %all-to-all-start = ((bf16[4,2,2048]{2,1,0:T(2,128)(2,1)}), bf16[4,2,2048]{2,1,0:T(2,128)(2,1)S(1)}, u32[]{:S(2)}, u32[]{:S(2)}) async-start(bf16[4,2,2048]{2,1,0:T(2,128)(2,1)} %reshape.84), calls=%async_computation | async-start | bytes 65536 | tf_op jit(solution)/shard_map/all_to_all | solution.py:32
  13.4 17.1 %copy-start.2 = (bf16[32,8,8,256]{3,1,2,0:T(8,128)(2,1)}, bf16[32,8,8,256]{3,1,2,0:T(8,128)(2,1)S(1)}, u32[]{:S(2)}) copy-start(bf16[32,8,8,256]{3,1,2,0:T(8,128)(2,1)S(1)} %copy.32) | copy-start | bytes 3145732
  24.7 19.1 %all-to-all-start.1 = ((bf16[32,64,256]{2,0,1:T(8,128)(2,1)}), bf16[32,64,256]{2,0,1:T(8,128)(2,1)S(1)}, u32[]{:S(2)}, u32[]{:S(2)}) async-start(bf16[32,64,256]{2,0,1:T(8,128)(2,1)} %copy.23), calls=%async_computation.1 | async-start | bytes 2097152 | tf_op jit(solution)/shard_map/all_to_all | solution.py:153
  46.4 14.6 %copy-start.1 = (bf16[32,8,8,256]{3,1,2,0:T(8,128)(2,1)S(1)}, bf16[32,8,8,256]{3,1,2,0:T(8,128)(2,1)}, u32[]{:S(2)}) copy-start(bf16[32,8,8,256]{3,1,2,0:T(8,128)(2,1)} %copy.28) | copy-start | bytes 3145732
  51.3 28.9 %collective-permute-start = (bf16[2,256,512]{2,1,0:T(8,128)(2,1)}, bf16[2,256,512]{2,1,0:T(8,128)(2,1)S(1)}, u32[]{:S(2)}, u32[]{:S(2)}) collective-permute-start(bf16[2,256,512]{2,1,0:T(8,128)(2,1)} %shard_map.74), channel_id=1, source_target_pairs={{0,1},{1,2},{2,3},{3,0},{4,5},{5,6},{6,7},{7,4},{8,9},{9,10},{10,1... | collective-permute-start | bytes 1572872 | tf_op jit(solution)/shard_map/ppermute | solution.py:171
  57.8 22.4 %collective-permute-start.1 = (bf16[2,256,512]{2,1,0:T(8,128)(2,1)}, bf16[2,256,512]{2,1,0:T(8,128)(2,1)S(1)}, u32[]{:S(2)}, u32[]{:S(2)}) collective-permute-start(bf16[2,256,512]{2,1,0:T(8,128)(2,1)} %shard_map.75), channel_id=1, source_target_pairs={{1,0},{2,1},{3,2},{0,3},{5,4},{6,5},{7,6},{4,7},{9,8},{10,9},{11,1... | collective-permute-start | bytes 1572872 | tf_op jit(solution)/shard_map/ppermute | solution.py:175

commit v14 on v13

--- a/solution.py
+++ b/solution.py
@@ -175,7 +175,6 @@
     east = lax.ppermute(first_edge, "lon", down)
     middle_dev = observe_dev_call(region_state, local_index[:, halo:-halo], local_weight[:, halo:-halo])
     obs_dev = jnp.concatenate([first_edge[0], middle_dev, last_edge[0]], axis=1)
-    model_anomaly = anomaly_from_mean(region_state)
     halo_blocks = halo // BLK
     block_count = patch_gridpoints // BLK
     candidate_count = block_count + 2 * halo_blocks
@@ -184,17 +183,21 @@
     halo_code = jnp.concatenate([code[:, :halo_blocks], code[:, halo_blocks + block_count:]], axis=1)
     tiles = taper_table(BLK, members)
     partial = update_call(
-        own_code.reshape(-1), model_anomaly, None, None, obs_dev, innov_flat, tiles, block_count, block_count
-    )
-    halo_obs = jnp.concatenate([west[0], east[0]], axis=1)
-    halo_innov = jnp.concatenate([west[1], east[1]], axis=1)
+        own_code.reshape(-1),
+        region_state,
+        None,
+        [(first_edge, 0), (middle_dev, None), (last_edge, 0)],
+        [(innov_flat, None)],
+        tiles,
+        block_count,
+        block_count,
+    )
     result = update_call(
         halo_code.reshape(-1),
-        model_anomaly,
+        region_state,
         partial,
-        region_state,
-        halo_obs,
-        halo_innov,
+        [(west, 0), (east, 0)],
+        [(west, 1), (east, 1)],
         tiles,
         block_count,
         2 * halo_blocks,
@@ -231,47 +234,76 @@
 GROUP = 4
 
 
-def update_call(code, state, partial, anchor, cand_obs, cand_innov, tiles, block_count, candidate_count, group=GROUP):
-    members, cells = state.shape
+def piece_spec(array):
+    if array.ndim == 3:
+        return pl.BlockSpec(array.shape, lambda g, code: (0, 0, 0))
+    return pl.BlockSpec(array.shape, lambda g, code: (0, 0))
+
+
+def piece_value(ref, pick):
+    return ref[...] if pick is None else ref[pick]
+
+
+def update_call(code, forecast, partial, obs_pieces, innov_pieces, tiles, block_count, candidate_count, group=GROUP):
+    members, cells = forecast.shape
     rows = group * BLK
     width = candidate_count * BLK
-    final = anchor is not None
-
-    def kernel(code_ref, s_ref, o_ref, i_ref, taper_ref, *rest):
+    final = partial is not None
+    obs_arrays = [a for a, _ in obs_pieces]
+    innov_arrays = [a for a, _ in innov_pieces]
+    n_obs = len(obs_pieces)
+    n_innov = len(innov_pieces)
+
+    def kernel(code_ref, f_ref, taper_ref, *rest):
+        obs_refs = rest[:n_obs]
+        innov_refs = rest[n_obs:n_obs + n_innov]
+        rest = rest[n_obs + n_innov:]
         if final:
-            part_ref, f_ref, out_ref, cov_scr, tap_scr = rest
+            part_ref, out_ref, cov_scr, tap_scr = rest
         else:
             out_ref, cov_scr, tap_scr = rest
         g = pl.program_id(0)
-        cov_scr[...] = lax.dot_general(
-            s_ref[...], o_ref[...], (((0,), (0,)), ((), ())), preferred_element_type=jnp.float32
-        )
+        forecast_block = f_ref[...].astype(jnp.float32)
+        mean = jnp.sum(forecast_block, axis=0, keepdims=True) / members
+        state = (forecast_block - mean).astype(jnp.bfloat16)
+        offset = 0
+        for ref, (_, pick) in zip(obs_refs, obs_pieces):
+            piece = piece_value(ref, pick)
+            span = piece.shape[1]
+            cov_scr[:, offset:offset + span] = lax.dot_general(
+                state, piece, (((0,), (0,)), ((), ())), preferred_element_type=jnp.float32
+            )
+            offset += span
         for sl in range(group):
             s = g * group + sl
             for b in range(candidate_count):
                 c = code_ref[s * candidate_count + b]
                 tile = cov_scr[sl * BLK:(sl + 1) * BLK, b * BLK:(b + 1) * BLK] * taper_ref[c]
                 tap_scr[sl * BLK:(sl + 1) * BLK, b * BLK:(b + 1) * BLK] = tile.astype(jnp.bfloat16)
-        change = lax.dot_general(
-            i_ref[...], tap_scr[...], (((1,), (1,)), ((), ())), preferred_element_type=jnp.float32
-        )
+        change = None
+        offset = 0
+        for ref, (_, pick) in zip(innov_refs, innov_pieces):
+            piece = piece_value(ref, pick)
+            span = piece.shape[1]
+            term = lax.dot_general(
+                piece, tap_scr[:, offset:offset + span], (((1,), (1,)), ((), ())),
+                preferred_element_type=jnp.float32,
+            )
+            change = term if change is None else change + term
+            offset += span
         if final:
             total = part_ref[...] + change
-            out_ref[...] = (f_ref[...].astype(jnp.float32) + total).astype(jnp.bfloat16)
+            out_ref[...] = (forecast_block + total).astype(jnp.bfloat16)
         else:
             out_ref[...] = change
 
     col_spec = pl.BlockSpec((members, rows), lambda g, code: (0, g))
-    in_specs = [
-        col_spec,
-        pl.BlockSpec((members, width), lambda g, code: (0, 0)),
-        pl.BlockSpec((members, width), lambda g, code: (0, 0)),
-        pl.BlockSpec(tiles.shape, lambda g, code: (0, 0, 0)),
-    ]
-    operands = [state, cand_obs, cand_innov, tiles]
+    in_specs = [col_spec, pl.BlockSpec(tiles.shape, lambda g, code: (0, 0, 0))]
+    in_specs += [piece_spec(a) for a in obs_arrays] + [piece_spec(a) for a in innov_arrays]
+    operands = [forecast, tiles] + obs_arrays + innov_arrays
     if final:
-        in_specs += [col_spec, col_spec]
-        operands += [partial, anchor]
+        in_specs.append(col_spec)
+        operands.append(partial)
     grid_spec = pltpu.PrefetchScalarGridSpec(
         num_scalar_prefetch=1,
         grid=(block_count // group,),

time: 109 us -> 106 us (0.972)
  other arithmetic: 6.4 us -> 1.23 us
    concatenate x2 -> x0, other arithmetic: 3.3 us -> none  [the longest x1 2.16 us: body(): obs_dev = jnp.concatenate([first_edge[0], middle_dev, last_edge[0]], axis=1)]
    unnamed x26 -> x27, local copies, waits for them, and re-layouts: 4.58 us -> 6.15 us
    convert_element_type x1 -> x0, other arithmetic: 1.24 us -> none  [anomaly_from_mean(): (centred - jnp.mean(centred, axis=-2, keepdims=True)).astype(jnp.bfloat16)]
    squeeze x3 -> x0, local copies, waits for them, and re-layouts: 1.13 us -> none  [the longest x1 1.06 us: body(): obs_dev = jnp.concatenate([first_edge[0], middle_dev, last_edge[0]], axis=1)]
  transfers between devices with their start and end apart: 4 -> 4, of which waited for: 2 -> 2; matrix products, arithmetic and copies ran while one was open for 11% -> 7% of each run, Pallas kernels for 19% -> 20%
where the time goes in v14:
time: 106 us; the launch traced here: 105 us
  Pallas kernels  37.1 us (35%)
  local copies, waits for them, and re-layouts  20.2 us (19%)
  blocking collectives  17.8 us (17%)
  waiting for transfers between devices  14.8 us (14%)
  starting transfers between devices  13.9 us (13%)
  other arithmetic  1.23 us (1%)
    all_to_all x1, blocking collectives, body(): lax.all_to_all(result.reshape(members, band_rows, patch_meridian_lines),...  17.8 us
    pallas_call x3, Pallas kernels, observe_dev_call(): pl.pallas_call(kernel, grid=(count // OBS_STEP,), in_specs=in_specs, out_...  16.9 us
    pallas_call x2, Pallas kernels, update_call(): pl.pallas_call(kernel, grid_spec=grid_spec, out_shape=jax.ShapeDtypeStruc...  15.6 us
    all_to_all x1, waiting for transfers between devices, body(): lax.all_to_all(prediction_increment, 'wide', split_axis=1, concat_axis=0,...  13.3 us
    all_to_all x1, starting transfers between devices, column_halo(): got = lax.all_to_all(spread, axis, 0, 0, tiled=False)  6.32 us
    unnamed x27, local copies, waits for them, and re-layouts  6.15 us
    pallas_call x1, Pallas kernels, forecast_call(): pl.pallas_call(kernel, out_shape=jax.ShapeDtypeStruct(state.shape, jnp.bf...  4.46 us
    all_to_all x1, starting transfers between devices, body(): lax.all_to_all(prediction_increment, 'wide', split_axis=1, concat_axis=0,...  3.72 us
  transfers between devices with their start and end apart: 4, of which 2 were waited for; matrix products, arithmetic and copies ran while one was open for 7% of the time, Pallas kernels for 20%

profile of v14, /device:TPU:0, one launch (start us, length us, event | category | flops | bytes accessed | tf_op | source)
XLA Modules:
  0.0 105.1 jit_solution(15368296862915716753)
XLA Ops:
  0.0 0.0 copy-start
  0.0 0.0 copy-start.4
  0.0 0.0 copy-start.5
  0.0 0.0 copy-start.3
  0.0 0.0 copy-start.2
  0.0 1.5 %fusion.5 = (bf16[32,64,1]{2,1,0:T(8,128)(2,1)S(1)}, bf16[32,64,1]{2,1,0:T(8,128)(2,1)S(1)}) fusion(bf16[32,64,256]{2,1,0:T(8,128)(2,1)} %x_ref.1), kind=kLoop, calls=%fused_computation.20 | loop fusion | bytes 16384 | tf_op jit(solution)/shard_map/slice | solution.py:30
  1.6 0.3 copy.26
  1.9 0.3 copy.27
  2.2 0.7 reshape.74
  2.9 6.3 %all-to-all-start = ((bf16[4,2,2048]{2,1,0:T(2,128)(2,1)}), bf16[4,2,2048]{2,1,0:T(2,128)(2,1)S(1)}, u32[]{:S(2)}, u32[]{:S(2)}) async-start(bf16[4,2,2048]{2,1,0:T(2,128)(2,1)} %reshape.74), calls=%async_computation | async-start | bytes 65536 | tf_op jit(solution)/shard_map/all_to_all | solution.py:32
  9.2 0.0 copy-done.4
  9.2 0.0 copy-done.5
  9.2 0.1 fusion.3
  9.3 0.0 copy-done.3
  9.3 0.1 select_reduce_fusion
  9.5 0.1 fusion.8
  9.5 0.0 copy-done
  9.5 0.8 subtract_bitcast_fusion
  10.3 0.1 pad_add_fusion
  10.4 0.1 slice.70
  10.5 0.7 reshape.72.code_ref
  11.1 0.7 reshape.68.code_ref
  11.8 0.6 slice.71.i_ref
  12.4 0.6 slice.72.w_ref
  13.1 0.0 copy-done.2
  13.1 0.3 copy.31
  13.4 0.0 copy-start.1
  13.4 1.5 %all-to-all-done = bf16[4,2,2048]{2,1,0:T(2,128)(2,1)S(1)} async-done(((bf16[4,2,2048]{2,1,0:T(2,128)(2,1)}), bf16[4,2,2048]{2,1,0:T(2,128)(2,1)S(1)}, u32[]{:S(2)}, u32[]{:S(2)}) %all-to-all-start) | async-done | bytes 32800 | tf_op jit(solution)/shard_map/all_to_all | solution.py:32
  14.9 0.1 reshape.75
  15.0 1.1 %copy.22 = bf16[1,32,64,2]{3,2,1,0:T(8,128)(2,1)} copy(bf16[1,32,64,2]{2,1,3,0:T(8,128)(2,1)S(1)} %get-tuple-element.9) | data formatting | bytes 16384 | tf_op jit(solution)/shard_map/jit(dynamic_index_in_dim)/dynamic_slice | solution.py:34
  16.1 0.3 copy.21
  16.5 1.0 slice.62.w_ref
  17.5 4.5 %shard_map.73 = bf16[32,64,256]{2,1,0:T(8,128)(2,1)} custom-call(bf16[32,64,256]{2,1,0:T(8,128)(2,1)} %x_ref.1, bf16[32,64,1]{2,1,0:T(8,128)(2,1)} %slice.62.w_ref, bf16[32,64,1]{2,1,0:T(8,128)(2,1)} %bitcast.45), custom_call_target="tpu_custom_call" | custom-call | tf_op jit(solution)/shard_map/pallas_call | solution.py:57
  21.9 2.8 %copy.23 = bf16[32,64,256]{2,0,1:T(8,128)(2,1)} copy(bf16[32,64,256]{2,1,0:T(8,128)(2,1)} %shard_map.73) | data formatting | bytes 2097152 | tf_op jit(solution)/shard_map/pallas_call | solution.py:57
  24.7 3.7 %all-to-all-start.1 = ((bf16[32,64,256]{2,0,1:T(8,128)(2,1)}), bf16[32,64,256]{2,0,1:T(8,128)(2,1)S(1)}, u32[]{:S(2)}, u32[]{:S(2)}) async-start(bf16[32,64,256]{2,0,1:T(8,128)(2,1)} %copy.23), calls=%async_computation.1 | async-start | bytes 2097152 | tf_op jit(solution)/shard_map/all_to_all | solution.py:153
  28.5 0.6 fusion.7
  29.1 0.6 fusion.6
  29.7 0.0 copy-done.1
  29.7 0.9 fusion.4
  30.6 13.3 %all-to-all-done.1 = bf16[32,64,256]{2,0,1:T(8,128)(2,1)S(1)} async-done(((bf16[32,64,256]{2,0,1:T(8,128)(2,1)}), bf16[32,64,256]{2,0,1:T(8,128)(2,1)S(1)}, u32[]{:S(2)}, u32[]{:S(2)}) %all-to-all-start.1) | async-done | bytes 1048608 | tf_op jit(solution)/shard_map/all_to_all | solution.py:153
  43.8 0.6 copy.24
  44.5 1.3 %copy.28 = bf16[32,8,8,256]{3,1,2,0:T(8,128)(2,1)} copy(bf16[32,8,8,256]{3,2,1,0:T(8,128)(2,1)S(1)} %bitcast.39) | data formatting | bytes 2097152
  45.8 4.8 %shard_map.74.rest_2_ = bf16[2,256,512]{2,1,0:T(8,128)(2,1)} custom-call(bf16[256,2048]{1,0:T(8,128)(2,1)} %bitcast.33, s32[4,512]{1,0:T(4,128)} %get-tuple-element.14.i_ref, f32[4,512]{1,0:T(4,128)} %get-tuple-element.12.w_ref, bf16[256,512]{1,0:T(8,128)(2,1)} %get-tuple-element.6.rest_0_), custom_call_target="tpu_custom_call" | custom-call | tf_op jit(solution)/shard_map/pallas_call | solution.py:123
  50.5 0.7 collective-permute-start
  51.3 4.8 %shard_map.75.rest_0_ = bf16[2,256,512]{2,1,0:T(8,128)(2,1)} custom-call(bf16[256,2048]{1,0:T(8,128)(2,1)} %bitcast.34, s32[4,512]{1,0:T(4,128)} %get-tuple-element.13.i_ref, f32[4,512]{1,0:T(4,128)} %get-tuple-element.11.w_ref, bf16[256,512]{1,0:T(8,128)(2,1)} %get-tuple-element.5.rest_0_), custom_call_target="tpu_custom_call" | custom-call | tf_op jit(solution)/shard_map/pallas_call | solution.py:123
  56.0 3.1 %collective-permute-start.1 = (bf16[2,256,512]{2,1,0:T(8,128)(2,1)}, bf16[2,256,512]{2,1,0:T(8,128)(2,1)S(1)}, u32[]{:S(2)}, u32[]{:S(2)}) collective-permute-start(bf16[2,256,512]{2,1,0:T(8,128)(2,1)} %shard_map.75.rest_0_), channel_id=1, source_target_pairs={{1,0},{2,1},{3,2},{0,3},{5,4},{6,5},{7,6},{4,7},{9,8},{10,9},{11,1... | collective-permute-start | bytes 1572872 | tf_op jit(solution)/shard_map/ppermute | solution.py:175
  59.1 0.1 fusion.2
  59.3 0.8 concatenate.11.taper_ref
  60.0 7.4 %shard_map.76.rest_1_ = bf16[256,1024]{1,0:T(8,128)(2,1)} custom-call(bf16[256,2048]{1,0:T(8,128)(2,1)} %bitcast.35, s32[4,1024]{1,0:T(4,128)} %slice.71.i_ref, f32[4,1024]{1,0:T(4,128)} %slice.72.w_ref), custom_call_target="tpu_custom_call" | custom-call | tf_op jit(solution)/shard_map/pallas_call | solution.py:123
  67.4 8.8 %shard_map.77.rest_4_ = f32[256,2048]{1,0:T(8,128)} custom-call(s32[256]{0:T(256)} %reshape.72.code_ref, bf16[256,2048]{1,0:T(8,128)(2,1)} %bitcast.36, f32[5,128,128]{2,1,0:T(8,128)} %concatenate.11.taper_ref, bf16[2,256,512]{2,1,0:T(8,128)(2,1)} %shard_map.75.rest_0_, bf16[256,1024]{1,0:T(8,128)(2,1)} %shard_map.76.rest_1_, ...), custom_call_target="tpu_custom_call" | custom-call | flops 4294967296 | bytes 4194304 | tf_op jit(solution)/shard_map/pallas_call | solution.py:318
  76.2 0.0 collective-permute-done.rest_0_.rest_2_
  76.2 0.0 copy-start.6
  76.2 0.0 collective-permute-done.1.rest_1_.rest_3_
  76.2 0.8 copy-done.6
  77.0 0.0 copy-start.7
  77.0 0.8 copy-done.7
  77.8 6.9 %shard_map.78 = bf16[256,2048]{1,0:T(8,128)(2,1)} custom-call(s32[128]{0:T(128)} %reshape.68.code_ref, bf16[256,2048]{1,0:T(8,128)(2,1)} %bitcast.37, f32[5,128,128]{2,1,0:T(8,128)} %concatenate.11.taper_ref, bf16[2,256,512]{2,1,0:T(8,128)(2,1)} %copy-done.6, bf16[2,256,512]{2,1,0:T(8,128)(2,1)} %copy-done.7, bf16[2,256,512]{2,1,0:T(8,128)(2,1)} %copy-done.6, ...), custom_call_target="tpu_custom_call" | custom-call | flops 2147483648 | bytes 4194304 | tf_op jit(solution)/shard_map/pallas_call | solution.py:318
  84.7 1.5 %copy.32 = bf16[32,8,8,256]{3,2,1,0:T(8,128)(2,1)S(1)} copy(bf16[32,8,8,256]{3,1,2,0:T(8,128)(2,1)} %bitcast.47) | data formatting | bytes 2097152
  86.2 17.8 %all_to_all.38 = bf16[256,8,256]{2,1,0:T(8,128)(2,1)S(1)} all-to-all(bf16[256,8,256]{2,1,0:T(8,128)(2,1)S(1)} %bitcast.40), channel_id=1, replica_groups=mesh['wide'=8,'lon'=4] {'wide'}, dimensions={0} | all-to-all | bytes 2097152 | tf_op jit(solution)/shard_map/all_to_all | solution.py:206
  104.0 1.1 %copy.34 = bf16[8,32,8,256]{3,2,0,1:T(8,128)(2,1)} copy(bf16[8,32,8,256]{3,2,1,0:T(8,128)(2,1)S(1)} %bitcast.41) | data formatting | bytes 2097152 | tf_op jit(solution)/shard_map/all_to_all | solution.py:206
  (9 shorter events, 0.1 us)
Async XLA Ops:
  0.0 9.5 %copy-start = (f32[4,64,256]{2,1,0:T(8,128)S(1)}, f32[4,64,256]{2,1,0:T(8,128)}, u32[]{:S(2)}) copy-start(f32[4,64,256]{2,1,0:T(8,128)} %param.10) | copy-start | bytes 786436
  0.0 9.2 %copy-start.4 = (s32[1,16,16]{2,1,0:T(8,128)S(1)}, s32[1,16,16]{2,1,0:T(8,128)}, u32[]{:S(2)}) copy-start(s32[1,16,16]{2,1,0:T(8,128)} %param.13) | copy-start | bytes 3076
  0.0 9.2 %copy-start.5 = (s32[1,16]{1,0:T(1,128)S(1)}, s32[1,16]{1,0:T(1,128)}, u32[]{:S(2)}) copy-start(s32[1,16]{1,0:T(1,128)} %param.12) | copy-start | bytes 196
  0.0 9.3 %copy-start.3 = (s32[1,16,16]{2,1,0:T(8,128)S(1)}, s32[1,16,16]{2,1,0:T(8,128)}, u32[]{:S(2)}) copy-start(s32[1,16,16]{2,1,0:T(8,128)} %param.11) | copy-start | bytes 3076
  0.0 13.0 %copy-start.2 = (bf16[256,8,256]{2,1,0:T(8,128)(2,1)S(1)}, bf16[256,8,256]{2,1,0:T(8,128)(2,1)}, u32[]{:S(2)}) copy-start(bf16[256,8,256]{2,1,0:T(8,128)(2,1)} %param.8) | copy-start | bytes 3145732
  2.9 12.0 %all-to-all-start = ((bf16[4,2,2048]{2,1,0:T(2,128)(2,1)}), bf16[4,2,2048]{2,1,0:T(2,128)(2,1)S(1)}, u32[]{:S(2)}, u32[]{:S(2)}) async-start(bf16[4,2,2048]{2,1,0:T(2,128)(2,1)} %reshape.74), calls=%async_computation | async-start | bytes 65536 | tf_op jit(solution)/shard_map/all_to_all | solution.py:32
  13.4 16.3 %copy-start.1 = (bf16[32,8,8,256]{3,1,2,0:T(8,128)(2,1)}, bf16[32,8,8,256]{3,1,2,0:T(8,128)(2,1)S(1)}, u32[]{:S(2)}) copy-start(bf16[32,8,8,256]{3,1,2,0:T(8,128)(2,1)S(1)} %copy.31) | copy-start | bytes 3145732
  24.7 19.1 %all-to-all-start.1 = ((bf16[32,64,256]{2,0,1:T(8,128)(2,1)}), bf16[32,64,256]{2,0,1:T(8,128)(2,1)S(1)}, u32[]{:S(2)}, u32[]{:S(2)}) async-start(bf16[32,64,256]{2,0,1:T(8,128)(2,1)} %copy.23), calls=%async_computation.1 | async-start | bytes 2097152 | tf_op jit(solution)/shard_map/all_to_all | solution.py:153
  50.5 25.7 %collective-permute-start = (bf16[2,256,512]{2,1,0:T(8,128)(2,1)}, bf16[2,256,512]{2,1,0:T(8,128)(2,1)S(1)}, u32[]{:S(2)}, u32[]{:S(2)}) collective-permute-start(bf16[2,256,512]{2,1,0:T(8,128)(2,1)} %shard_map.74.rest_2_), channel_id=1, source_target_pairs={{0,1},{1,2},{2,3},{3,0},{4,5},{5,6},{6,7},{7,4},{8,9},{9,10},{10,1... | collective-permute-start | bytes 1572872 | tf_op jit(solution)/shard_map/ppermute | solution.py:171
  56.0 20.2 %collective-permute-start.1 = (bf16[2,256,512]{2,1,0:T(8,128)(2,1)}, bf16[2,256,512]{2,1,0:T(8,128)(2,1)S(1)}, u32[]{:S(2)}, u32[]{:S(2)}) collective-permute-start(bf16[2,256,512]{2,1,0:T(8,128)(2,1)} %shard_map.75.rest_0_), channel_id=1, source_target_pairs={{1,0},{2,1},{3,2},{0,3},{5,4},{6,5},{7,6},{4,7},{9,8},{10,9},{11,1... | collective-permute-start | bytes 1572872 | tf_op jit(solution)/shard_map/ppermute | solution.py:175
  76.2 0.8 copy-start.6
  77.0 0.8 copy-start.7

commit v15 on v14

--- a/solution.py
+++ b/solution.py
@@ -26,26 +26,29 @@
 
 def column_halo(value, axis):
     size = lax.axis_size(axis)
-    here = lax.axis_index(axis)
     edges = jnp.concatenate([value[..., :1], value[..., -1:]], axis=-1)
     spread = jnp.broadcast_to(edges[None], (size,) + edges.shape)
-    got = lax.all_to_all(spread, axis, 0, 0, tiled=False)
-    west = lax.dynamic_index_in_dim(got, (here - 1) % size, 0, keepdims=False)[..., 1:2]
-    east = lax.dynamic_index_in_dim(got, (here + 1) % size, 0, keepdims=False)[..., 0:1]
-    return west, east
-
-
-def forecast_call(state, west, east):
+    return lax.all_to_all(spread, axis, 0, 0, tiled=False)
+
+
+def forecast_call(state, received, here):
     members, rows, cols = state.shape
-
-    def kernel(x_ref, w_ref, e_ref, o_ref):
+    size = received.shape[0]
+    position = jnp.reshape(here, (1,)).astype(jnp.int32)
+
+    def kernel(pos_ref, x_ref, h_ref, o_ref):
         col = lax.broadcasted_iota(jnp.int32, (rows, cols), 1)
         row = lax.broadcasted_iota(jnp.int32, (rows, cols), 0)
+        t = pos_ref[0]
+        west_from = (t + size - 1) % size
+        east_from = (t + 1) % size
 
         def one(m, carry):
             x = x_ref[m].astype(jnp.float32)
-            east_n = jnp.where(col == cols - 1, e_ref[m].astype(jnp.float32), pltpu.roll(x, cols - 1, 1))
-            west_n = jnp.where(col == 0, w_ref[m].astype(jnp.float32), pltpu.roll(x, 1, 1))
+            west_col = h_ref[west_from, m][:, 1:2].astype(jnp.float32)
+            east_col = h_ref[east_from, m][:, 0:1].astype(jnp.float32)
+            east_n = jnp.where(col == cols - 1, east_col, pltpu.roll(x, cols - 1, 1))
+            west_n = jnp.where(col == 0, west_col, pltpu.roll(x, 1, 1))
             north = jnp.where(row == rows - 1, 0.0, pltpu.roll(x, rows - 1, 0))
             south = jnp.where(row == 0, 0.0, pltpu.roll(x, 1, 0))
             spread = east_n + west_n + north + south - 4.0 * x
@@ -54,7 +57,18 @@
 
         lax.fori_loop(0, members, one, 0, unroll=4)
 
-    return pl.pallas_call(kernel, out_shape=jax.ShapeDtypeStruct(state.shape, jnp.bfloat16))(state, west, east)
+    grid_spec = pltpu.PrefetchScalarGridSpec(
+        num_scalar_prefetch=1,
+        grid=(1,),
+        in_specs=[
+            pl.BlockSpec(state.shape, lambda i, p: (0, 0, 0)),
+            pl.BlockSpec(received.shape, lambda i, p: (0, 0, 0, 0)),
+        ],
+        out_specs=pl.BlockSpec(state.shape, lambda i, p: (0, 0, 0)),
+    )
+    return pl.pallas_call(
+        kernel, grid_spec=grid_spec, out_shape=jax.ShapeDtypeStruct(state.shape, jnp.bfloat16)
+    )(position, state, received)
 
 
 def observe_region(state, index, weight):
@@ -144,8 +158,8 @@
 
 
 def body(background_ensemble, innov, obs_index, obs_weight, obs_list, tile_count, taper_class):
-    west_col, east_col = column_halo(background_ensemble, "lon")
-    prediction_increment = forecast_call(background_ensemble, west_col, east_col)
+    received = column_halo(background_ensemble, "lon")
+    prediction_increment = forecast_call(background_ensemble, received, lax.axis_index("lon"))
     ensemble_lines_here, whole_parallel_set, patch_meridian_lines = prediction_increment.shape
     members = innov.shape[0]
     band_rows = innov.shape[1]

time: 106 us -> 106 us (level)
    all_to_all x0 -> x1, local copies, waits for them, and re-layouts: none -> 1.98 us  [column_halo(): return lax.all_to_all(spread, axis, 0, 0, tiled=False)]
    dynamic_slice x3 -> x0, local copies, waits for them, and re-layouts: 1.45 us -> none  [the longest x2 1.11 us: column_halo(): lax.dynamic_index_in_dim(got, (here + 1) % size, 0, keepdims=False)]
where the time goes in v15:
time: 106 us; the launch traced here: 105 us
  Pallas kernels  37.5 us (35%)
  local copies, waits for them, and re-layouts  19.7 us (19%)
  blocking collectives  17.8 us (17%)
  waiting for transfers between devices  14.9 us (14%)
  starting transfers between devices  13.9 us (13%)
  other arithmetic  1.23 us (1%)
    all_to_all x1, blocking collectives, body(): lax.all_to_all(result.reshape(members, band_rows, patch_meridian_lines),...  17.8 us
    pallas_call x3, Pallas kernels, observe_dev_call(): pl.pallas_call(kernel, grid=(count // OBS_STEP,), in_specs=in_specs, out_...  17 us
    pallas_call x2, Pallas kernels, update_call(): pl.pallas_call(kernel, grid_spec=grid_spec, out_shape=jax.ShapeDtypeStruc...  15.6 us
    all_to_all x1, waiting for transfers between devices, body(): lax.all_to_all(prediction_increment, 'wide', split_axis=1, concat_axis=0,...  13.3 us
    all_to_all x1, starting transfers between devices, column_halo(): return lax.all_to_all(spread, axis, 0, 0, tiled=False)  6.32 us
    unnamed x27, local copies, waits for them, and re-layouts  6.16 us
    pallas_call x1, Pallas kernels, forecast_call(): pl.pallas_call(kernel, grid_spec=grid_spec, out_shape=jax.ShapeDtypeStruc...  4.97 us
    all_to_all x1, starting transfers between devices, body(): lax.all_to_all(prediction_increment, 'wide', split_axis=1, concat_axis=0,...  3.72 us
  transfers between devices with their start and end apart: 4, of which 2 were waited for; matrix products, arithmetic and copies ran while one was open for 7% of the time, Pallas kernels for 20%

profile of v15, /device:TPU:0, one launch (start us, length us, event | category | flops | bytes accessed | tf_op | source)
XLA Modules:
  0.0 105.0 jit_solution(12650238280845715908)
XLA Ops:
  0.0 0.0 copy-start
  0.0 0.0 copy-start.4
  0.0 0.0 copy-start.5
  0.0 0.0 copy-start.3
  0.0 0.0 copy-start.2
  0.0 1.5 %fusion.5 = (bf16[32,64,1]{2,1,0:T(8,128)(2,1)S(1)}, bf16[32,64,1]{2,1,0:T(8,128)(2,1)S(1)}) fusion(bf16[32,64,256]{2,1,0:T(8,128)(2,1)} %x_ref.1), kind=kLoop, calls=%fused_computation.18 | loop fusion | bytes 16384 | tf_op jit(solution)/shard_map/slice | solution.py:29
  1.6 0.3 copy.24
  1.9 0.3 copy.25
  2.2 0.7 reshape.78
  2.9 6.3 %all-to-all-start = ((bf16[4,2,2048]{2,1,0:T(2,128)(2,1)}), bf16[4,2,2048]{2,1,0:T(2,128)(2,1)S(1)}, u32[]{:S(2)}, u32[]{:S(2)}) async-start(bf16[4,2,2048]{2,1,0:T(2,128)(2,1)} %reshape.78), calls=%async_computation | async-start | bytes 65536 | tf_op jit(solution)/shard_map/all_to_all | solution.py:31
  9.2 0.0 copy-done.4
  9.2 0.0 copy-done.5
  9.2 0.1 fusion.3
  9.3 0.0 copy-done.3
  9.3 0.1 select_reduce_fusion
  9.5 0.1 fusion.8
  9.5 0.0 copy-done
  9.5 0.8 subtract_bitcast_fusion
  10.3 0.1 pad_add_fusion
  10.4 0.1 slice.60
  10.5 0.7 reshape.76.code_ref
  11.1 0.6 reshape.71.code_ref
  11.8 0.6 slice.61.i_ref
  12.4 0.6 slice.62.w_ref
  13.0 0.0 copy-done.2
  13.0 0.3 copy.29
  13.3 0.0 copy-start.1
  13.3 1.6 %all-to-all-done = bf16[4,2,2048]{2,1,0:T(2,128)(2,1)S(1)} async-done(((bf16[4,2,2048]{2,1,0:T(2,128)(2,1)}), bf16[4,2,2048]{2,1,0:T(2,128)(2,1)S(1)}, u32[]{:S(2)}, u32[]{:S(2)}) %all-to-all-start) | async-done | bytes 32800 | tf_op jit(solution)/shard_map/all_to_all | solution.py:31
  14.9 0.1 reshape.79
  15.0 2.0 %copy.20.h_ref = bf16[4,32,64,2]{3,2,1,0:T(8,128)(2,1)} copy(bf16[4,32,64,2]{2,1,3,0:T(8,128)(2,1)S(1)} %bitcast.44) | data formatting | bytes 65536 | tf_op jit(solution)/shard_map/all_to_all | solution.py:31
  17.0 5.0 %shard_map.73 = bf16[32,64,256]{2,1,0:T(8,128)(2,1)} custom-call(s32[1]{0:T(128)} %bitcast.3.pos_ref, bf16[32,64,256]{2,1,0:T(8,128)(2,1)} %x_ref.1, bf16[4,32,64,2]{3,2,1,0:T(8,128)(2,1)} %copy.20.h_ref), custom_call_target="tpu_custom_call" | custom-call | tf_op jit(solution)/shard_map/pallas_call | solution.py:69
  21.9 2.8 %copy.21 = bf16[32,64,256]{2,0,1:T(8,128)(2,1)} copy(bf16[32,64,256]{2,1,0:T(8,128)(2,1)} %shard_map.73) | data formatting | bytes 2097152 | tf_op jit(solution)/shard_map/pallas_call | solution.py:69
  24.7 3.7 %all-to-all-start.1 = ((bf16[32,64,256]{2,0,1:T(8,128)(2,1)}), bf16[32,64,256]{2,0,1:T(8,128)(2,1)S(1)}, u32[]{:S(2)}, u32[]{:S(2)}) async-start(bf16[32,64,256]{2,0,1:T(8,128)(2,1)} %copy.21), calls=%async_computation.1 | async-start | bytes 2097152 | tf_op jit(solution)/shard_map/all_to_all | solution.py:167
  28.5 0.6 fusion.7
  29.1 0.6 fusion.6
  29.7 0.0 copy-done.1
  29.7 0.9 fusion.4
  30.6 13.3 %all-to-all-done.1 = bf16[32,64,256]{2,0,1:T(8,128)(2,1)S(1)} async-done(((bf16[32,64,256]{2,0,1:T(8,128)(2,1)}), bf16[32,64,256]{2,0,1:T(8,128)(2,1)S(1)}, u32[]{:S(2)}, u32[]{:S(2)}) %all-to-all-start.1) | async-done | bytes 1048608 | tf_op jit(solution)/shard_map/all_to_all | solution.py:167
  43.9 0.6 copy.22
  44.5 1.3 %copy.26 = bf16[32,8,8,256]{3,1,2,0:T(8,128)(2,1)} copy(bf16[32,8,8,256]{3,2,1,0:T(8,128)(2,1)S(1)} %bitcast.37) | data formatting | bytes 2097152
  45.8 4.8 %shard_map.74.rest_2_ = bf16[2,256,512]{2,1,0:T(8,128)(2,1)} custom-call(bf16[256,2048]{1,0:T(8,128)(2,1)} %bitcast.31, s32[4,512]{1,0:T(4,128)} %get-tuple-element.12.i_ref, f32[4,512]{1,0:T(4,128)} %get-tuple-element.10.w_ref, bf16[256,512]{1,0:T(8,128)(2,1)} %get-tuple-element.6.rest_0_), custom_call_target="tpu_custom_call" | custom-call | tf_op jit(solution)/shard_map/pallas_call | solution.py:137
  50.5 0.7 collective-permute-start
  51.3 4.8 %shard_map.75.rest_0_ = bf16[2,256,512]{2,1,0:T(8,128)(2,1)} custom-call(bf16[256,2048]{1,0:T(8,128)(2,1)} %bitcast.32, s32[4,512]{1,0:T(4,128)} %get-tuple-element.11.i_ref, f32[4,512]{1,0:T(4,128)} %get-tuple-element.9.w_ref, bf16[256,512]{1,0:T(8,128)(2,1)} %get-tuple-element.5.rest_0_), custom_call_target="tpu_custom_call" | custom-call | tf_op jit(solution)/shard_map/pallas_call | solution.py:137
  56.1 3.1 %collective-permute-start.1 = (bf16[2,256,512]{2,1,0:T(8,128)(2,1)}, bf16[2,256,512]{2,1,0:T(8,128)(2,1)S(1)}, u32[]{:S(2)}, u32[]{:S(2)}) collective-permute-start(bf16[2,256,512]{2,1,0:T(8,128)(2,1)} %shard_map.75.rest_0_), channel_id=1, source_target_pairs={{1,0},{2,1},{3,2},{0,3},{5,4},{6,5},{7,6},{4,7},{9,8},{10,9},{11,1... | collective-permute-start | bytes 1572872 | tf_op jit(solution)/shard_map/ppermute | solution.py:189
  59.2 0.1 fusion.2
  59.3 0.8 concatenate.11.taper_ref
  60.0 7.4 %shard_map.76.rest_1_ = bf16[256,1024]{1,0:T(8,128)(2,1)} custom-call(bf16[256,2048]{1,0:T(8,128)(2,1)} %bitcast.33, s32[4,1024]{1,0:T(4,128)} %slice.61.i_ref, f32[4,1024]{1,0:T(4,128)} %slice.62.w_ref), custom_call_target="tpu_custom_call" | custom-call | tf_op jit(solution)/shard_map/pallas_call | solution.py:137
  67.5 8.8 %shard_map.77.rest_4_ = f32[256,2048]{1,0:T(8,128)} custom-call(s32[256]{0:T(256)} %reshape.76.code_ref, bf16[256,2048]{1,0:T(8,128)(2,1)} %bitcast.34, f32[5,128,128]{2,1,0:T(8,128)} %concatenate.11.taper_ref, bf16[2,256,512]{2,1,0:T(8,128)(2,1)} %shard_map.75.rest_0_, bf16[256,1024]{1,0:T(8,128)(2,1)} %shard_map.76.rest_1_, ...), custom_call_target="tpu_custom_call" | custom-call | flops 4294967296 | bytes 4194304 | tf_op jit(solution)/shard_map/pallas_call | solution.py:332
  76.3 0.0 collective-permute-done.rest_0_.rest_2_
  76.3 0.0 copy-start.6
  76.3 0.0 collective-permute-done.1.rest_1_.rest_3_
  76.3 0.8 copy-done.6
  77.1 0.0 copy-start.7
  77.1 0.8 copy-done.7
  77.9 6.8 %shard_map.78 = bf16[256,2048]{1,0:T(8,128)(2,1)} custom-call(s32[128]{0:T(128)} %reshape.71.code_ref, bf16[256,2048]{1,0:T(8,128)(2,1)} %bitcast.35, f32[5,128,128]{2,1,0:T(8,128)} %concatenate.11.taper_ref, bf16[2,256,512]{2,1,0:T(8,128)(2,1)} %copy-done.6, bf16[2,256,512]{2,1,0:T(8,128)(2,1)} %copy-done.7, bf16[2,256,512]{2,1,0:T(8,128)(2,1)} %copy-done.6, ...), custom_call_target="tpu_custom_call" | custom-call | flops 2147483648 | bytes 4194304 | tf_op jit(solution)/shard_map/pallas_call | solution.py:332
  84.6 1.5 %copy.30 = bf16[32,8,8,256]{3,2,1,0:T(8,128)(2,1)S(1)} copy(bf16[32,8,8,256]{3,1,2,0:T(8,128)(2,1)} %bitcast.43) | data formatting | bytes 2097152
  86.2 17.8 %all_to_all.38 = bf16[256,8,256]{2,1,0:T(8,128)(2,1)S(1)} all-to-all(bf16[256,8,256]{2,1,0:T(8,128)(2,1)S(1)} %bitcast.38), channel_id=1, replica_groups=mesh['wide'=8,'lon'=4] {'wide'}, dimensions={0} | all-to-all | bytes 2097152 | tf_op jit(solution)/shard_map/all_to_all | solution.py:220
  104.0 1.1 %copy.32 = bf16[8,32,8,256]{3,2,0,1:T(8,128)(2,1)} copy(bf16[8,32,8,256]{3,2,1,0:T(8,128)(2,1)S(1)} %bitcast.39) | data formatting | bytes 2097152 | tf_op jit(solution)/shard_map/all_to_all | solution.py:220
  (8 shorter events, 0.1 us)
Async XLA Ops:
  0.0 9.5 %copy-start = (f32[4,64,256]{2,1,0:T(8,128)S(1)}, f32[4,64,256]{2,1,0:T(8,128)}, u32[]{:S(2)}) copy-start(f32[4,64,256]{2,1,0:T(8,128)} %param.10) | copy-start | bytes 786436
  0.0 9.2 %copy-start.4 = (s32[1,16,16]{2,1,0:T(8,128)S(1)}, s32[1,16,16]{2,1,0:T(8,128)}, u32[]{:S(2)}) copy-start(s32[1,16,16]{2,1,0:T(8,128)} %param.13) | copy-start | bytes 3076
  0.0 9.2 %copy-start.5 = (s32[1,16]{1,0:T(1,128)S(1)}, s32[1,16]{1,0:T(1,128)}, u32[]{:S(2)}) copy-start(s32[1,16]{1,0:T(1,128)} %param.12) | copy-start | bytes 196
  0.0 9.3 %copy-start.3 = (s32[1,16,16]{2,1,0:T(8,128)S(1)}, s32[1,16,16]{2,1,0:T(8,128)}, u32[]{:S(2)}) copy-start(s32[1,16,16]{2,1,0:T(8,128)} %param.11) | copy-start | bytes 3076
  0.0 13.0 %copy-start.2 = (bf16[256,8,256]{2,1,0:T(8,128)(2,1)S(1)}, bf16[256,8,256]{2,1,0:T(8,128)(2,1)}, u32[]{:S(2)}) copy-start(bf16[256,8,256]{2,1,0:T(8,128)(2,1)} %param.8) | copy-start | bytes 3145732
  2.9 12.0 %all-to-all-start = ((bf16[4,2,2048]{2,1,0:T(2,128)(2,1)}), bf16[4,2,2048]{2,1,0:T(2,128)(2,1)S(1)}, u32[]{:S(2)}, u32[]{:S(2)}) async-start(bf16[4,2,2048]{2,1,0:T(2,128)(2,1)} %reshape.78), calls=%async_computation | async-start | bytes 65536 | tf_op jit(solution)/shard_map/all_to_all | solution.py:31
  13.3 16.4 %copy-start.1 = (bf16[32,8,8,256]{3,1,2,0:T(8,128)(2,1)}, bf16[32,8,8,256]{3,1,2,0:T(8,128)(2,1)S(1)}, u32[]{:S(2)}) copy-start(bf16[32,8,8,256]{3,1,2,0:T(8,128)(2,1)S(1)} %copy.29) | copy-start | bytes 3145732
  24.7 19.1 %all-to-all-start.1 = ((bf16[32,64,256]{2,0,1:T(8,128)(2,1)}), bf16[32,64,256]{2,0,1:T(8,128)(2,1)S(1)}, u32[]{:S(2)}, u32[]{:S(2)}) async-start(bf16[32,64,256]{2,0,1:T(8,128)(2,1)} %copy.21), calls=%async_computation.1 | async-start | bytes 2097152 | tf_op jit(solution)/shard_map/all_to_all | solution.py:167
  50.5 25.7 %collective-permute-start = (bf16[2,256,512]{2,1,0:T(8,128)(2,1)}, bf16[2,256,512]{2,1,0:T(8,128)(2,1)S(1)}, u32[]{:S(2)}, u32[]{:S(2)}) collective-permute-start(bf16[2,256,512]{2,1,0:T(8,128)(2,1)} %shard_map.74.rest_2_), channel_id=1, source_target_pairs={{0,1},{1,2},{2,3},{3,0},{4,5},{5,6},{6,7},{7,4},{8,9},{9,10},{10,1... | collective-permute-start | bytes 1572872 | tf_op jit(solution)/shard_map/ppermute | solution.py:185
  56.1 20.2 %collective-permute-start.1 = (bf16[2,256,512]{2,1,0:T(8,128)(2,1)}, bf16[2,256,512]{2,1,0:T(8,128)(2,1)S(1)}, u32[]{:S(2)}, u32[]{:S(2)}) collective-permute-start(bf16[2,256,512]{2,1,0:T(8,128)(2,1)} %shard_map.75.rest_0_), channel_id=1, source_target_pairs={{1,0},{2,1},{3,2},{0,3},{5,4},{6,5},{7,6},{4,7},{9,8},{10,9},{11,1... | collective-permute-start | bytes 1572872 | tf_op jit(solution)/shard_map/ppermute | solution.py:189
  76.3 0.8 copy-start.6
  77.1 0.8 copy-start.7

commit v16 on v15

--- a/solution.py
+++ b/solution.py
@@ -52,10 +52,11 @@
             north = jnp.where(row == rows - 1, 0.0, pltpu.roll(x, rows - 1, 0))
             south = jnp.where(row == 0, 0.0, pltpu.roll(x, 1, 0))
             spread = east_n + west_n + north + south - 4.0 * x
-            o_ref[m] = (x + 0.2 * spread - 0.3 * (east_n - west_n)).astype(jnp.bfloat16)
+            o_ref[:, m, :] = (x + 0.2 * spread - 0.3 * (east_n - west_n)).astype(jnp.bfloat16)
             return carry
 
-        lax.fori_loop(0, members, one, 0, unroll=4)
+        for m in range(members):
+            one(m, 0)
 
     grid_spec = pltpu.PrefetchScalarGridSpec(
         num_scalar_prefetch=1,
@@ -64,10 +65,10 @@
             pl.BlockSpec(state.shape, lambda i, p: (0, 0, 0)),
             pl.BlockSpec(received.shape, lambda i, p: (0, 0, 0, 0)),
         ],
-        out_specs=pl.BlockSpec(state.shape, lambda i, p: (0, 0, 0)),
+        out_specs=pl.BlockSpec((rows, members, cols), lambda i, p: (0, 0, 0)),
     )
     return pl.pallas_call(
-        kernel, grid_spec=grid_spec, out_shape=jax.ShapeDtypeStruct(state.shape, jnp.bfloat16)
+        kernel, grid_spec=grid_spec, out_shape=jax.ShapeDtypeStruct((rows, members, cols), jnp.bfloat16)
     )(position, state, received)
 
 
@@ -160,12 +161,12 @@
 def body(background_ensemble, innov, obs_index, obs_weight, obs_list, tile_count, taper_class):
     received = column_halo(background_ensemble, "lon")
     prediction_increment = forecast_call(background_ensemble, received, lax.axis_index("lon"))
-    ensemble_lines_here, whole_parallel_set, patch_meridian_lines = prediction_increment.shape
+    whole_parallel_set, ensemble_lines_here, patch_meridian_lines = prediction_increment.shape
     members = innov.shape[0]
     band_rows = innov.shape[1]
     patch_gridpoints = band_rows * patch_meridian_lines
-    region = lax.all_to_all(prediction_increment, "wide", split_axis=1, concat_axis=0, tiled=True)
-    region_state = region.reshape(members, patch_gridpoints)
+    region = lax.all_to_all(prediction_increment, "wide", split_axis=0, concat_axis=1, tiled=True)
+    region_state = region.transpose(1, 0, 2).reshape(members, patch_gridpoints)
     first_row = lax.axis_index("wide") * band_rows
     local_index = lax.dynamic_slice_in_dim(obs_index, first_row, band_rows, 1).reshape(
         4, patch_gridpoints

time: 106 us -> 104 us (0.981)
  local copies, waits for them, and re-layouts: 19.7 us -> 16.8 us
  Pallas kernels: 37.5 us -> 38.9 us
    pallas_call x1 -> x0, local copies, waits for them, and re-layouts: 2.78 us -> none  [forecast_call(): pl.pallas_call(kernel, grid_spec=grid_spec, out_shape=jax.ShapeDtypeStruc...]
    pallas_call x1, Pallas kernels: 4.97 us -> 6.37 us  [forecast_call(): pl.pallas_call(kernel, grid_spec=grid_spec, out_shape=jax.ShapeDtypeStruc...]
where the time goes in v16:
time: 104 us
  Pallas kernels  38.9 us (37%)
  blocking collectives  17.8 us (17%)
  local copies, waits for them, and re-layouts  16.8 us (16%)
  waiting for transfers between devices  14.9 us (14%)
  starting transfers between devices  13.9 us (13%)
  other arithmetic  1.23 us (1%)
    all_to_all x1, blocking collectives, body(): lax.all_to_all(result.reshape(members, band_rows, patch_meridian_lines),...  17.8 us
    pallas_call x3, Pallas kernels, observe_dev_call(): pl.pallas_call(kernel, grid=(count // OBS_STEP,), in_specs=in_specs, out_...  17 us
    pallas_call x2, Pallas kernels, update_call(): pl.pallas_call(kernel, grid_spec=grid_spec, out_shape=jax.ShapeDtypeStruc...  15.6 us
    all_to_all x1, waiting for transfers between devices, body(): lax.all_to_all(prediction_increment, 'wide', split_axis=0, concat_axis=1,...  13.3 us
    pallas_call x1, Pallas kernels, forecast_call(): pl.pallas_call(kernel, grid_spec=grid_spec, out_shape=jax.ShapeDtypeStruc...  6.37 us
    all_to_all x1, starting transfers between devices, column_halo(): return lax.all_to_all(spread, axis, 0, 0, tiled=False)  6.32 us
    unnamed x27, local copies, waits for them, and re-layouts  6.16 us
    all_to_all x1, starting transfers between devices, body(): lax.all_to_all(prediction_increment, 'wide', split_axis=0, concat_axis=1,...  3.72 us
  transfers between devices with their start and end apart: 4, of which 2 were waited for; matrix products, arithmetic and copies ran while one was open for 7% of the time, Pallas kernels for 20%

profile of v16, /device:TPU:0, one launch (start us, length us, event | category | flops | bytes accessed | tf_op | source)
XLA Modules:
  0.0 103.7 jit_solution(18406913880135906515)
XLA Ops:
  0.0 0.0 copy-start
  0.0 0.0 copy-start.4
  0.0 0.0 copy-start.5
  0.0 0.0 copy-start.3
  0.0 0.0 copy-start.2
  0.0 1.5 %fusion.5 = (bf16[32,64,1]{2,1,0:T(8,128)(2,1)S(1)}, bf16[32,64,1]{2,1,0:T(8,128)(2,1)S(1)}) fusion(bf16[32,64,256]{2,1,0:T(8,128)(2,1)} %x_ref.1), kind=kLoop, calls=%fused_computation.18 | loop fusion | bytes 16384 | tf_op jit(solution)/shard_map/slice | solution.py:29
  1.6 0.3 copy.22
  1.9 0.3 copy.23
  2.2 0.7 reshape.77
  2.9 6.3 %all-to-all-start = ((bf16[4,2,2048]{2,1,0:T(2,128)(2,1)}), bf16[4,2,2048]{2,1,0:T(2,128)(2,1)S(1)}, u32[]{:S(2)}, u32[]{:S(2)}) async-start(bf16[4,2,2048]{2,1,0:T(2,128)(2,1)} %reshape.77), calls=%async_computation | async-start | bytes 65536 | tf_op jit(solution)/shard_map/all_to_all | solution.py:31
  9.2 0.0 copy-done.4
  9.2 0.0 copy-done.5
  9.2 0.1 fusion.3
  9.3 0.0 copy-done.3
  9.3 0.1 select_reduce_fusion
  9.5 0.1 fusion.8
  9.5 0.0 copy-done
  9.5 0.8 subtract_bitcast_fusion
  10.3 0.1 pad_add_fusion
  10.4 0.1 slice.60
  10.5 0.7 reshape.75.code_ref
  11.1 0.6 reshape.70.code_ref
  11.8 0.6 slice.61.i_ref
  12.4 0.6 slice.62.w_ref
  13.0 0.0 copy-done.2
  13.0 0.3 copy.27
  13.3 0.0 copy-start.1
  13.3 1.6 %all-to-all-done = bf16[4,2,2048]{2,1,0:T(2,128)(2,1)S(1)} async-done(((bf16[4,2,2048]{2,1,0:T(2,128)(2,1)}), bf16[4,2,2048]{2,1,0:T(2,128)(2,1)S(1)}, u32[]{:S(2)}, u32[]{:S(2)}) %all-to-all-start) | async-done | bytes 32800 | tf_op jit(solution)/shard_map/all_to_all | solution.py:31
  14.9 0.1 reshape.78
  15.0 2.0 %copy.19.h_ref = bf16[4,32,64,2]{3,2,1,0:T(8,128)(2,1)} copy(bf16[4,32,64,2]{2,1,3,0:T(8,128)(2,1)S(1)} %bitcast.47) | data formatting | bytes 65536 | tf_op jit(solution)/shard_map/all_to_all | solution.py:31
  17.0 6.4 %shard_map.73 = bf16[64,32,256]{2,1,0:T(8,128)(2,1)} custom-call(s32[1]{0:T(128)} %bitcast.3.pos_ref, bf16[32,64,256]{2,1,0:T(8,128)(2,1)} %x_ref.1, bf16[4,32,64,2]{3,2,1,0:T(8,128)(2,1)} %copy.19.h_ref), custom_call_target="tpu_custom_call" | custom-call | tf_op jit(solution)/shard_map/pallas_call | solution.py:70
  23.3 3.7 %all-to-all-start.1 = ((bf16[64,32,256]{2,1,0:T(8,128)(2,1)}), bf16[64,32,256]{2,1,0:T(8,128)(2,1)S(1)}, u32[]{:S(2)}, u32[]{:S(2)}) async-start(bf16[64,32,256]{2,1,0:T(8,128)(2,1)} %shard_map.73), calls=%async_computation.1 | async-start | bytes 2097152 | tf_op jit(solution)/shard_map/all_to_all | solution.py:168
  27.1 0.6 fusion.7
  27.7 0.6 fusion.6
  28.3 0.0 copy-done.1
  28.3 0.8 fusion.4
  29.2 13.3 %all-to-all-done.1 = bf16[64,32,256]{2,1,0:T(8,128)(2,1)S(1)} async-done(((bf16[64,32,256]{2,1,0:T(8,128)(2,1)}), bf16[64,32,256]{2,1,0:T(8,128)(2,1)S(1)}, u32[]{:S(2)}, u32[]{:S(2)}) %all-to-all-start.1) | async-done | bytes 1048608 | tf_op jit(solution)/shard_map/all_to_all | solution.py:168
  42.5 0.6 copy.20
  43.1 1.3 %copy.24 = bf16[32,8,8,256]{3,1,2,0:T(8,128)(2,1)} copy(bf16[32,8,8,256]{3,2,1,0:T(8,128)(2,1)S(1)} %bitcast.40) | data formatting | bytes 2097152
  44.4 4.8 %shard_map.74.rest_2_ = bf16[2,256,512]{2,1,0:T(8,128)(2,1)} custom-call(bf16[256,2048]{1,0:T(8,128)(2,1)} %bitcast.34, s32[4,512]{1,0:T(4,128)} %get-tuple-element.12.i_ref, f32[4,512]{1,0:T(4,128)} %get-tuple-element.10.w_ref, bf16[256,512]{1,0:T(8,128)(2,1)} %get-tuple-element.6.rest_0_), custom_call_target="tpu_custom_call" | custom-call | tf_op jit(solution)/shard_map/pallas_call | solution.py:138
  49.2 0.7 collective-permute-start
  49.9 4.8 %shard_map.75.rest_0_ = bf16[2,256,512]{2,1,0:T(8,128)(2,1)} custom-call(bf16[256,2048]{1,0:T(8,128)(2,1)} %bitcast.35, s32[4,512]{1,0:T(4,128)} %get-tuple-element.11.i_ref, f32[4,512]{1,0:T(4,128)} %get-tuple-element.9.w_ref, bf16[256,512]{1,0:T(8,128)(2,1)} %get-tuple-element.5.rest_0_), custom_call_target="tpu_custom_call" | custom-call | tf_op jit(solution)/shard_map/pallas_call | solution.py:138
  54.7 3.1 %collective-permute-start.1 = (bf16[2,256,512]{2,1,0:T(8,128)(2,1)}, bf16[2,256,512]{2,1,0:T(8,128)(2,1)S(1)}, u32[]{:S(2)}, u32[]{:S(2)}) collective-permute-start(bf16[2,256,512]{2,1,0:T(8,128)(2,1)} %shard_map.75.rest_0_), channel_id=1, source_target_pairs={{1,0},{2,1},{3,2},{0,3},{5,4},{6,5},{7,6},{4,7},{9,8},{10,9},{11,1... | collective-permute-start | bytes 1572872 | tf_op jit(solution)/shard_map/ppermute | solution.py:190
  57.8 0.1 fusion.2
  57.9 0.8 concatenate.11.taper_ref
  58.7 7.4 %shard_map.76.rest_1_ = bf16[256,1024]{1,0:T(8,128)(2,1)} custom-call(bf16[256,2048]{1,0:T(8,128)(2,1)} %bitcast.36, s32[4,1024]{1,0:T(4,128)} %slice.61.i_ref, f32[4,1024]{1,0:T(4,128)} %slice.62.w_ref), custom_call_target="tpu_custom_call" | custom-call | tf_op jit(solution)/shard_map/pallas_call | solution.py:138
  66.1 8.8 %shard_map.77.rest_4_ = f32[256,2048]{1,0:T(8,128)} custom-call(s32[256]{0:T(256)} %reshape.75.code_ref, bf16[256,2048]{1,0:T(8,128)(2,1)} %bitcast.37, f32[5,128,128]{2,1,0:T(8,128)} %concatenate.11.taper_ref, bf16[2,256,512]{2,1,0:T(8,128)(2,1)} %shard_map.75.rest_0_, bf16[256,1024]{1,0:T(8,128)(2,1)} %shard_map.76.rest_1_, ...), custom_call_target="tpu_custom_call" | custom-call | flops 4294967296 | bytes 4194304 | tf_op jit(solution)/shard_map/pallas_call | solution.py:333
  74.9 0.0 collective-permute-done.rest_0_.rest_2_
  74.9 0.0 copy-start.6
  74.9 0.0 collective-permute-done.1.rest_1_.rest_3_
  74.9 0.8 copy-done.6
  75.7 0.0 copy-start.7
  75.7 0.8 copy-done.7
  76.5 6.8 %shard_map.78 = bf16[256,2048]{1,0:T(8,128)(2,1)} custom-call(s32[128]{0:T(128)} %reshape.70.code_ref, bf16[256,2048]{1,0:T(8,128)(2,1)} %bitcast.38, f32[5,128,128]{2,1,0:T(8,128)} %concatenate.11.taper_ref, bf16[2,256,512]{2,1,0:T(8,128)(2,1)} %copy-done.6, bf16[2,256,512]{2,1,0:T(8,128)(2,1)} %copy-done.7, bf16[2,256,512]{2,1,0:T(8,128)(2,1)} %copy-done.6, ...), custom_call_target="tpu_custom_call" | custom-call | flops 2147483648 | bytes 4194304 | tf_op jit(solution)/shard_map/pallas_call | solution.py:333
  83.3 1.5 %copy.28 = bf16[32,8,8,256]{3,2,1,0:T(8,128)(2,1)S(1)} copy(bf16[32,8,8,256]{3,1,2,0:T(8,128)(2,1)} %bitcast.46) | data formatting | bytes 2097152
  84.8 17.8 %all_to_all.41 = bf16[256,8,256]{2,1,0:T(8,128)(2,1)S(1)} all-to-all(bf16[256,8,256]{2,1,0:T(8,128)(2,1)S(1)} %bitcast.41), channel_id=1, replica_groups=mesh['wide'=8,'lon'=4] {'wide'}, dimensions={0} | all-to-all | bytes 2097152 | tf_op jit(solution)/shard_map/all_to_all | solution.py:221
  102.6 1.1 %copy.30 = bf16[8,32,8,256]{3,2,0,1:T(8,128)(2,1)} copy(bf16[8,32,8,256]{3,2,1,0:T(8,128)(2,1)S(1)} %bitcast.42) | data formatting | bytes 2097152 | tf_op jit(solution)/shard_map/all_to_all | solution.py:221
  (8 shorter events, 0.1 us)
Async XLA Ops:
  0.0 9.5 %copy-start = (f32[4,64,256]{2,1,0:T(8,128)S(1)}, f32[4,64,256]{2,1,0:T(8,128)}, u32[]{:S(2)}) copy-start(f32[4,64,256]{2,1,0:T(8,128)} %param.10) | copy-start | bytes 786436
  0.0 9.2 %copy-start.4 = (s32[1,16,16]{2,1,0:T(8,128)S(1)}, s32[1,16,16]{2,1,0:T(8,128)}, u32[]{:S(2)}) copy-start(s32[1,16,16]{2,1,0:T(8,128)} %param.13) | copy-start | bytes 3076
  0.0 9.2 %copy-start.5 = (s32[1,16]{1,0:T(1,128)S(1)}, s32[1,16]{1,0:T(1,128)}, u32[]{:S(2)}) copy-start(s32[1,16]{1,0:T(1,128)} %param.12) | copy-start | bytes 196
  0.0 9.3 %copy-start.3 = (s32[1,16,16]{2,1,0:T(8,128)S(1)}, s32[1,16,16]{2,1,0:T(8,128)}, u32[]{:S(2)}) copy-start(s32[1,16,16]{2,1,0:T(8,128)} %param.11) | copy-start | bytes 3076
  0.0 13.0 %copy-start.2 = (bf16[256,8,256]{2,1,0:T(8,128)(2,1)S(1)}, bf16[256,8,256]{2,1,0:T(8,128)(2,1)}, u32[]{:S(2)}) copy-start(bf16[256,8,256]{2,1,0:T(8,128)(2,1)} %param.8) | copy-start | bytes 3145732
  2.9 12.0 %all-to-all-start = ((bf16[4,2,2048]{2,1,0:T(2,128)(2,1)}), bf16[4,2,2048]{2,1,0:T(2,128)(2,1)S(1)}, u32[]{:S(2)}, u32[]{:S(2)}) async-start(bf16[4,2,2048]{2,1,0:T(2,128)(2,1)} %reshape.77), calls=%async_computation | async-start | bytes 65536 | tf_op jit(solution)/shard_map/all_to_all | solution.py:31
  13.3 15.0 %copy-start.1 = (bf16[32,8,8,256]{3,1,2,0:T(8,128)(2,1)}, bf16[32,8,8,256]{3,1,2,0:T(8,128)(2,1)S(1)}, u32[]{:S(2)}) copy-start(bf16[32,8,8,256]{3,1,2,0:T(8,128)(2,1)S(1)} %copy.27) | copy-start | bytes 3145732
  23.3 19.1 %all-to-all-start.1 = ((bf16[64,32,256]{2,1,0:T(8,128)(2,1)}), bf16[64,32,256]{2,1,0:T(8,128)(2,1)S(1)}, u32[]{:S(2)}, u32[]{:S(2)}) async-start(bf16[64,32,256]{2,1,0:T(8,128)(2,1)} %shard_map.73), calls=%async_computation.1 | async-start | bytes 2097152 | tf_op jit(solution)/shard_map/all_to_all | solution.py:168
  49.2 25.7 %collective-permute-start = (bf16[2,256,512]{2,1,0:T(8,128)(2,1)}, bf16[2,256,512]{2,1,0:T(8,128)(2,1)S(1)}, u32[]{:S(2)}, u32[]{:S(2)}) collective-permute-start(bf16[2,256,512]{2,1,0:T(8,128)(2,1)} %shard_map.74.rest_2_), channel_id=1, source_target_pairs={{0,1},{1,2},{2,3},{3,0},{4,5},{5,6},{6,7},{7,4},{8,9},{9,10},{10,1... | collective-permute-start | bytes 1572872 | tf_op jit(solution)/shard_map/ppermute | solution.py:186
  54.7 20.2 %collective-permute-start.1 = (bf16[2,256,512]{2,1,0:T(8,128)(2,1)}, bf16[2,256,512]{2,1,0:T(8,128)(2,1)S(1)}, u32[]{:S(2)}, u32[]{:S(2)}) collective-permute-start(bf16[2,256,512]{2,1,0:T(8,128)(2,1)} %shard_map.75.rest_0_), channel_id=1, source_target_pairs={{1,0},{2,1},{3,2},{0,3},{5,4},{6,5},{7,6},{4,7},{9,8},{10,9},{11,1... | collective-permute-start | bytes 1572872 | tf_op jit(solution)/shard_map/ppermute | solution.py:190
  74.9 0.8 copy-start.6
  75.7 0.8 copy-start.7

commit v17 on v16

--- a/solution.py
+++ b/solution.py
@@ -206,6 +206,7 @@
         tiles,
         block_count,
         block_count,
+        group=8,
     )
     result = update_call(
         halo_code.reshape(-1),

time: 104 us -> 104 us (level)
  no operation moved by 1% of the time
where the time goes in v17:
time: 104 us; the launch traced here: 103 us
  Pallas kernels  38.7 us (37%)
  blocking collectives  17.8 us (17%)
  local copies, waits for them, and re-layouts  16.8 us (16%)
  waiting for transfers between devices  14.9 us (14%)
  starting transfers between devices  13.9 us (13%)
  other arithmetic  1.23 us (1%)
    all_to_all x1, blocking collectives, body(): lax.all_to_all(result.reshape(members, band_rows, patch_meridian_lines),...  17.8 us
    pallas_call x3, Pallas kernels, observe_dev_call(): pl.pallas_call(kernel, grid=(count // OBS_STEP,), in_specs=in_specs, out_...  17 us
    pallas_call x2, Pallas kernels, update_call(): pl.pallas_call(kernel, grid_spec=grid_spec, out_shape=jax.ShapeDtypeStruc...  15.3 us
    all_to_all x1, waiting for transfers between devices, body(): lax.all_to_all(prediction_increment, 'wide', split_axis=0, concat_axis=1,...  13.3 us
    pallas_call x1, Pallas kernels, forecast_call(): pl.pallas_call(kernel, grid_spec=grid_spec, out_shape=jax.ShapeDtypeStruc...  6.37 us
    all_to_all x1, starting transfers between devices, column_halo(): return lax.all_to_all(spread, axis, 0, 0, tiled=False)  6.32 us
    unnamed x27, local copies, waits for them, and re-layouts  6.16 us
    all_to_all x1, starting transfers between devices, body(): lax.all_to_all(prediction_increment, 'wide', split_axis=0, concat_axis=1,...  3.72 us
  transfers between devices with their start and end apart: 4, of which 2 were waited for; matrix products, arithmetic and copies ran while one was open for 7% of the time, Pallas kernels for 20%

profile of v17, /device:TPU:0, one launch (start us, length us, event | category | flops | bytes accessed | tf_op | source)
XLA Modules:
  0.0 103.5 jit_solution(3645751307608244672)
XLA Ops:
  0.0 0.0 copy-start
  0.0 0.0 copy-start.4
  0.0 0.0 copy-start.5
  0.0 0.0 copy-start.3
  0.0 0.0 copy-start.2
  0.0 1.5 %fusion.5 = (bf16[32,64,1]{2,1,0:T(8,128)(2,1)S(1)}, bf16[32,64,1]{2,1,0:T(8,128)(2,1)S(1)}) fusion(bf16[32,64,256]{2,1,0:T(8,128)(2,1)} %x_ref.1), kind=kLoop, calls=%fused_computation.18 | loop fusion | bytes 16384 | tf_op jit(solution)/shard_map/slice | solution.py:29
  1.6 0.3 copy.22
  1.9 0.3 copy.23
  2.2 0.7 reshape.77
  2.9 6.3 %all-to-all-start = ((bf16[4,2,2048]{2,1,0:T(2,128)(2,1)}), bf16[4,2,2048]{2,1,0:T(2,128)(2,1)S(1)}, u32[]{:S(2)}, u32[]{:S(2)}) async-start(bf16[4,2,2048]{2,1,0:T(2,128)(2,1)} %reshape.77), calls=%async_computation | async-start | bytes 65536 | tf_op jit(solution)/shard_map/all_to_all | solution.py:31
  9.2 0.0 copy-done.4
  9.2 0.0 copy-done.5
  9.2 0.1 fusion.3
  9.3 0.0 copy-done.3
  9.3 0.1 select_reduce_fusion
  9.5 0.1 fusion.8
  9.5 0.0 copy-done
  9.5 0.8 subtract_bitcast_fusion
  10.3 0.1 pad_add_fusion
  10.4 0.1 slice.60
  10.5 0.7 reshape.75.code_ref
  11.1 0.6 reshape.70.code_ref
  11.8 0.6 slice.61.i_ref
  12.4 0.6 slice.62.w_ref
  13.0 0.0 copy-done.2
  13.0 0.3 copy.27
  13.3 0.0 copy-start.1
  13.3 1.6 %all-to-all-done = bf16[4,2,2048]{2,1,0:T(2,128)(2,1)S(1)} async-done(((bf16[4,2,2048]{2,1,0:T(2,128)(2,1)}), bf16[4,2,2048]{2,1,0:T(2,128)(2,1)S(1)}, u32[]{:S(2)}, u32[]{:S(2)}) %all-to-all-start) | async-done | bytes 32800 | tf_op jit(solution)/shard_map/all_to_all | solution.py:31
  14.9 0.1 reshape.78
  15.0 2.0 %copy.19.h_ref = bf16[4,32,64,2]{3,2,1,0:T(8,128)(2,1)} copy(bf16[4,32,64,2]{2,1,3,0:T(8,128)(2,1)S(1)} %bitcast.47) | data formatting | bytes 65536 | tf_op jit(solution)/shard_map/all_to_all | solution.py:31
  17.0 6.4 %shard_map.73 = bf16[64,32,256]{2,1,0:T(8,128)(2,1)} custom-call(s32[1]{0:T(128)} %bitcast.3.pos_ref, bf16[32,64,256]{2,1,0:T(8,128)(2,1)} %x_ref.1, bf16[4,32,64,2]{3,2,1,0:T(8,128)(2,1)} %copy.19.h_ref), custom_call_target="tpu_custom_call" | custom-call | tf_op jit(solution)/shard_map/pallas_call | solution.py:70
  23.3 3.7 %all-to-all-start.1 = ((bf16[64,32,256]{2,1,0:T(8,128)(2,1)}), bf16[64,32,256]{2,1,0:T(8,128)(2,1)S(1)}, u32[]{:S(2)}, u32[]{:S(2)}) async-start(bf16[64,32,256]{2,1,0:T(8,128)(2,1)} %shard_map.73), calls=%async_computation.1 | async-start | bytes 2097152 | tf_op jit(solution)/shard_map/all_to_all | solution.py:168
  27.1 0.6 fusion.7
  27.7 0.6 fusion.6
  28.3 0.0 copy-done.1
  28.3 0.8 fusion.4
  29.2 13.3 %all-to-all-done.1 = bf16[64,32,256]{2,1,0:T(8,128)(2,1)S(1)} async-done(((bf16[64,32,256]{2,1,0:T(8,128)(2,1)}), bf16[64,32,256]{2,1,0:T(8,128)(2,1)S(1)}, u32[]{:S(2)}, u32[]{:S(2)}) %all-to-all-start.1) | async-done | bytes 1048608 | tf_op jit(solution)/shard_map/all_to_all | solution.py:168
  42.5 0.6 copy.20
  43.1 1.3 %copy.24 = bf16[32,8,8,256]{3,1,2,0:T(8,128)(2,1)} copy(bf16[32,8,8,256]{3,2,1,0:T(8,128)(2,1)S(1)} %bitcast.40) | data formatting | bytes 2097152
  44.4 4.8 %shard_map.74.rest_2_ = bf16[2,256,512]{2,1,0:T(8,128)(2,1)} custom-call(bf16[256,2048]{1,0:T(8,128)(2,1)} %bitcast.34, s32[4,512]{1,0:T(4,128)} %get-tuple-element.12.i_ref, f32[4,512]{1,0:T(4,128)} %get-tuple-element.10.w_ref, bf16[256,512]{1,0:T(8,128)(2,1)} %get-tuple-element.6.rest_0_), custom_call_target="tpu_custom_call" | custom-call | tf_op jit(solution)/shard_map/pallas_call | solution.py:138
  49.2 0.7 collective-permute-start
  49.9 4.8 %shard_map.75.rest_0_ = bf16[2,256,512]{2,1,0:T(8,128)(2,1)} custom-call(bf16[256,2048]{1,0:T(8,128)(2,1)} %bitcast.35, s32[4,512]{1,0:T(4,128)} %get-tuple-element.11.i_ref, f32[4,512]{1,0:T(4,128)} %get-tuple-element.9.w_ref, bf16[256,512]{1,0:T(8,128)(2,1)} %get-tuple-element.5.rest_0_), custom_call_target="tpu_custom_call" | custom-call | tf_op jit(solution)/shard_map/pallas_call | solution.py:138
  54.7 3.1 %collective-permute-start.1 = (bf16[2,256,512]{2,1,0:T(8,128)(2,1)}, bf16[2,256,512]{2,1,0:T(8,128)(2,1)S(1)}, u32[]{:S(2)}, u32[]{:S(2)}) collective-permute-start(bf16[2,256,512]{2,1,0:T(8,128)(2,1)} %shard_map.75.rest_0_), channel_id=1, source_target_pairs={{1,0},{2,1},{3,2},{0,3},{5,4},{6,5},{7,6},{4,7},{9,8},{10,9},{11,1... | collective-permute-start | bytes 1572872 | tf_op jit(solution)/shard_map/ppermute | solution.py:190
  57.8 0.1 fusion.2
  57.9 0.8 concatenate.11.taper_ref
  58.7 7.4 %shard_map.76.rest_1_ = bf16[256,1024]{1,0:T(8,128)(2,1)} custom-call(bf16[256,2048]{1,0:T(8,128)(2,1)} %bitcast.36, s32[4,1024]{1,0:T(4,128)} %slice.61.i_ref, f32[4,1024]{1,0:T(4,128)} %slice.62.w_ref), custom_call_target="tpu_custom_call" | custom-call | tf_op jit(solution)/shard_map/pallas_call | solution.py:138
  66.1 8.6 %shard_map.77.rest_4_ = f32[256,2048]{1,0:T(8,128)} custom-call(s32[256]{0:T(256)} %reshape.75.code_ref, bf16[256,2048]{1,0:T(8,128)(2,1)} %bitcast.37, f32[5,128,128]{2,1,0:T(8,128)} %concatenate.11.taper_ref, bf16[2,256,512]{2,1,0:T(8,128)(2,1)} %shard_map.75.rest_0_, bf16[256,1024]{1,0:T(8,128)(2,1)} %shard_map.76.rest_1_, ...), custom_call_target="tpu_custom_call" | custom-call | flops 4294967296 | bytes 4194304 | tf_op jit(solution)/shard_map/pallas_call | solution.py:334
  74.6 0.0 collective-permute-done.rest_0_.rest_2_
  74.6 0.0 copy-start.6
  74.6 0.0 collective-permute-done.1.rest_1_.rest_3_
  74.7 0.8 copy-done.6
  75.4 0.0 copy-start.7
  75.4 0.8 copy-done.7
  76.3 6.8 %shard_map.78 = bf16[256,2048]{1,0:T(8,128)(2,1)} custom-call(s32[128]{0:T(128)} %reshape.70.code_ref, bf16[256,2048]{1,0:T(8,128)(2,1)} %bitcast.38, f32[5,128,128]{2,1,0:T(8,128)} %concatenate.11.taper_ref, bf16[2,256,512]{2,1,0:T(8,128)(2,1)} %copy-done.6, bf16[2,256,512]{2,1,0:T(8,128)(2,1)} %copy-done.7, bf16[2,256,512]{2,1,0:T(8,128)(2,1)} %copy-done.6, ...), custom_call_target="tpu_custom_call" | custom-call | flops 2147483648 | bytes 4194304 | tf_op jit(solution)/shard_map/pallas_call | solution.py:334
  83.0 1.5 %copy.28 = bf16[32,8,8,256]{3,2,1,0:T(8,128)(2,1)S(1)} copy(bf16[32,8,8,256]{3,1,2,0:T(8,128)(2,1)} %bitcast.46) | data formatting | bytes 2097152
  84.5 17.8 %all_to_all.41 = bf16[256,8,256]{2,1,0:T(8,128)(2,1)S(1)} all-to-all(bf16[256,8,256]{2,1,0:T(8,128)(2,1)S(1)} %bitcast.41), channel_id=1, replica_groups=mesh['wide'=8,'lon'=4] {'wide'}, dimensions={0} | all-to-all | bytes 2097152 | tf_op jit(solution)/shard_map/all_to_all | solution.py:222
  102.4 1.1 %copy.30 = bf16[8,32,8,256]{3,2,0,1:T(8,128)(2,1)} copy(bf16[8,32,8,256]{3,2,1,0:T(8,128)(2,1)S(1)} %bitcast.42) | data formatting | bytes 2097152 | tf_op jit(solution)/shard_map/all_to_all | solution.py:222
  (8 shorter events, 0.1 us)
Async XLA Ops:
  0.0 9.5 %copy-start = (f32[4,64,256]{2,1,0:T(8,128)S(1)}, f32[4,64,256]{2,1,0:T(8,128)}, u32[]{:S(2)}) copy-start(f32[4,64,256]{2,1,0:T(8,128)} %param.10) | copy-start | bytes 786436
  0.0 9.2 %copy-start.4 = (s32[1,16,16]{2,1,0:T(8,128)S(1)}, s32[1,16,16]{2,1,0:T(8,128)}, u32[]{:S(2)}) copy-start(s32[1,16,16]{2,1,0:T(8,128)} %param.13) | copy-start | bytes 3076
  0.0 9.2 %copy-start.5 = (s32[1,16]{1,0:T(1,128)S(1)}, s32[1,16]{1,0:T(1,128)}, u32[]{:S(2)}) copy-start(s32[1,16]{1,0:T(1,128)} %param.12) | copy-start | bytes 196
  0.0 9.3 %copy-start.3 = (s32[1,16,16]{2,1,0:T(8,128)S(1)}, s32[1,16,16]{2,1,0:T(8,128)}, u32[]{:S(2)}) copy-start(s32[1,16,16]{2,1,0:T(8,128)} %param.11) | copy-start | bytes 3076
  0.0 13.0 %copy-start.2 = (bf16[256,8,256]{2,1,0:T(8,128)(2,1)S(1)}, bf16[256,8,256]{2,1,0:T(8,128)(2,1)}, u32[]{:S(2)}) copy-start(bf16[256,8,256]{2,1,0:T(8,128)(2,1)} %param.8) | copy-start | bytes 3145732
  2.9 12.0 %all-to-all-start = ((bf16[4,2,2048]{2,1,0:T(2,128)(2,1)}), bf16[4,2,2048]{2,1,0:T(2,128)(2,1)S(1)}, u32[]{:S(2)}, u32[]{:S(2)}) async-start(bf16[4,2,2048]{2,1,0:T(2,128)(2,1)} %reshape.77), calls=%async_computation | async-start | bytes 65536 | tf_op jit(solution)/shard_map/all_to_all | solution.py:31
  13.3 15.0 %copy-start.1 = (bf16[32,8,8,256]{3,1,2,0:T(8,128)(2,1)}, bf16[32,8,8,256]{3,1,2,0:T(8,128)(2,1)S(1)}, u32[]{:S(2)}) copy-start(bf16[32,8,8,256]{3,1,2,0:T(8,128)(2,1)S(1)} %copy.27) | copy-start | bytes 3145732
  23.3 19.1 %all-to-all-start.1 = ((bf16[64,32,256]{2,1,0:T(8,128)(2,1)}), bf16[64,32,256]{2,1,0:T(8,128)(2,1)S(1)}, u32[]{:S(2)}, u32[]{:S(2)}) async-start(bf16[64,32,256]{2,1,0:T(8,128)(2,1)} %shard_map.73), calls=%async_computation.1 | async-start | bytes 2097152 | tf_op jit(solution)/shard_map/all_to_all | solution.py:168
  49.2 25.5 %collective-permute-start = (bf16[2,256,512]{2,1,0:T(8,128)(2,1)}, bf16[2,256,512]{2,1,0:T(8,128)(2,1)S(1)}, u32[]{:S(2)}, u32[]{:S(2)}) collective-permute-start(bf16[2,256,512]{2,1,0:T(8,128)(2,1)} %shard_map.74.rest_2_), channel_id=1, source_target_pairs={{0,1},{1,2},{2,3},{3,0},{4,5},{5,6},{6,7},{7,4},{8,9},{9,10},{10,1... | collective-permute-start | bytes 1572872 | tf_op jit(solution)/shard_map/ppermute | solution.py:186
  54.7 20.0 %collective-permute-start.1 = (bf16[2,256,512]{2,1,0:T(8,128)(2,1)}, bf16[2,256,512]{2,1,0:T(8,128)(2,1)S(1)}, u32[]{:S(2)}, u32[]{:S(2)}) collective-permute-start(bf16[2,256,512]{2,1,0:T(8,128)(2,1)} %shard_map.75.rest_0_), channel_id=1, source_target_pairs={{1,0},{2,1},{3,2},{0,3},{5,4},{6,5},{7,6},{4,7},{9,8},{10,9},{11,1... | collective-permute-start | bytes 1572872 | tf_op jit(solution)/shard_map/ppermute | solution.py:190
  74.6 0.8 copy-start.6
  75.4 0.8 copy-start.7

commit v18 on v17

--- a/solution.py
+++ b/solution.py
@@ -1,4 +1,6 @@
 import math
+
+import numpy as np
 
 import jax
 import jax.numpy as jnp
@@ -238,13 +240,13 @@
 
 
 def taper_table(tile_width, members):
-    row_ids = lax.broadcasted_iota(jnp.float32, (tile_width, tile_width), 0)
-    col_ids = lax.broadcasted_iota(jnp.float32, (tile_width, tile_width), 1)
-    offset = row_ids - col_ids
-    length = 8.0 * jnp.exp2(jnp.arange(4, dtype=jnp.float32))
+    offset = np.arange(tile_width, dtype=np.float32)[:, None] - np.arange(tile_width, dtype=np.float32)[None, :]
+    length = np.float32(8.0) * np.exp2(np.arange(4, dtype=np.float32))
     scaled = offset[None] / length[:, None, None]
-    tiles = (1.0 / (1.0 + scaled * scaled)) / (members - 1.0)
-    return jnp.concatenate([tiles, jnp.zeros((1, tile_width, tile_width), jnp.float32)], axis=0)
+    one = np.float32(1.0)
+    tiles = (one / (one + scaled * scaled)) / np.float32(members - 1.0)
+    zero = np.zeros((1, tile_width, tile_width), np.float32)
+    return jnp.asarray(np.concatenate([tiles, zero], axis=0).astype(np.float32))
 
 
 GROUP = 4

time: 104 us -> 106 us (1.019)
  waiting for transfers between devices: 14.9 us -> 17.6 us
    all_to_all x1, waiting for transfers between devices: 1.58 us -> 4.25 us  [column_halo(): return lax.all_to_all(spread, axis, 0, 0, tiled=False)]
  transfers between devices with their start and end apart: 4 -> 4, of which waited for: 2 -> 2; matrix products, arithmetic and copies ran while one was open for 7% -> 6% of each run, Pallas kernels for 20% -> 20%
where the time goes in v18:
time: 106 us; the launch traced here: 105 us
  Pallas kernels  38.7 us (37%)
  blocking collectives  17.8 us (17%)
  waiting for transfers between devices  17.6 us (17%)
  local copies, waits for them, and re-layouts  16.1 us (15%)
  starting transfers between devices  13.9 us (13%)
  other arithmetic  1.08 us (1%)
    all_to_all x1, blocking collectives, body(): lax.all_to_all(result.reshape(members, band_rows, patch_meridian_lines),...  17.8 us
    pallas_call x3, Pallas kernels, observe_dev_call(): pl.pallas_call(kernel, grid=(count // OBS_STEP,), in_specs=in_specs, out_...  17 us
    pallas_call x2, Pallas kernels, update_call(): pl.pallas_call(kernel, grid_spec=grid_spec, out_shape=jax.ShapeDtypeStruc...  15.3 us
    all_to_all x1, waiting for transfers between devices, body(): lax.all_to_all(prediction_increment, 'wide', split_axis=0, concat_axis=1,...  13.4 us
    pallas_call x1, Pallas kernels, forecast_call(): pl.pallas_call(kernel, grid_spec=grid_spec, out_shape=jax.ShapeDtypeStruc...  6.37 us
    all_to_all x1, starting transfers between devices, column_halo(): return lax.all_to_all(spread, axis, 0, 0, tiled=False)  6.32 us
    unnamed x27, local copies, waits for them, and re-layouts  6.18 us
    all_to_all x1, waiting for transfers between devices, column_halo(): return lax.all_to_all(spread, axis, 0, 0, tiled=False)  4.25 us
  transfers between devices with their start and end apart: 4, of which 2 were waited for; matrix products, arithmetic and copies ran while one was open for 6% of the time, Pallas kernels for 20%

profile of v18, /device:TPU:0, one launch (start us, length us, event | category | flops | bytes accessed | tf_op | source)
XLA Modules:
  0.0 105.2 jit_solution(17096082482967531680)
XLA Ops:
  0.0 0.0 copy-start
  0.0 0.0 copy-start.4
  0.0 0.0 copy-start.5
  0.0 0.0 copy-start.3
  0.0 0.0 copy-start.2
  0.0 1.5 %fusion.2 = (bf16[32,64,1]{2,1,0:T(8,128)(2,1)S(1)}, bf16[32,64,1]{2,1,0:T(8,128)(2,1)S(1)}) fusion(bf16[32,64,256]{2,1,0:T(8,128)(2,1)} %x_ref.1), kind=kLoop, calls=%fused_computation.12 | loop fusion | bytes 16384 | tf_op jit(solution)/shard_map/slice | solution.py:31
  1.6 0.3 copy.23
  1.9 0.3 copy.24
  2.2 0.7 reshape.64
  2.9 6.3 %all-to-all-start = ((bf16[4,2,2048]{2,1,0:T(2,128)(2,1)}), bf16[4,2,2048]{2,1,0:T(2,128)(2,1)S(1)}, u32[]{:S(2)}, u32[]{:S(2)}) async-start(bf16[4,2,2048]{2,1,0:T(2,128)(2,1)} %reshape.64), calls=%async_computation | async-start | bytes 65536 | tf_op jit(solution)/shard_map/all_to_all | solution.py:33
  9.2 0.0 copy-done.4
  9.2 0.0 copy-done.5
  9.2 0.1 fusion
  9.3 0.0 copy-done.3
  9.3 0.1 select_reduce_fusion
  9.5 0.0 copy-done
  9.5 0.8 subtract_bitcast_fusion
  10.3 0.0 copy-done.2
  10.3 0.3 copy.28
  10.6 0.0 copy-start.1
  10.6 4.3 %all-to-all-done = bf16[4,2,2048]{2,1,0:T(2,128)(2,1)S(1)} async-done(((bf16[4,2,2048]{2,1,0:T(2,128)(2,1)}), bf16[4,2,2048]{2,1,0:T(2,128)(2,1)S(1)}, u32[]{:S(2)}, u32[]{:S(2)}) %all-to-all-start) | async-done | bytes 32800 | tf_op jit(solution)/shard_map/all_to_all | solution.py:33
  14.9 0.1 reshape.65
  15.0 2.0 %copy.20.h_ref = bf16[4,32,64,2]{3,2,1,0:T(8,128)(2,1)} copy(bf16[4,32,64,2]{2,1,3,0:T(8,128)(2,1)S(1)} %bitcast.47) | data formatting | bytes 65536 | tf_op jit(solution)/shard_map/all_to_all | solution.py:33
  17.0 6.4 %shard_map.82 = bf16[64,32,256]{2,1,0:T(8,128)(2,1)} custom-call(s32[1]{0:T(128)} %bitcast.3.pos_ref, bf16[32,64,256]{2,1,0:T(8,128)(2,1)} %x_ref.1, bf16[4,32,64,2]{3,2,1,0:T(8,128)(2,1)} %copy.20.h_ref), custom_call_target="tpu_custom_call" | custom-call | tf_op jit(solution)/shard_map/pallas_call | solution.py:72
  23.3 3.7 %all-to-all-start.1 = ((bf16[64,32,256]{2,1,0:T(8,128)(2,1)}), bf16[64,32,256]{2,1,0:T(8,128)(2,1)S(1)}, u32[]{:S(2)}, u32[]{:S(2)}) async-start(bf16[64,32,256]{2,1,0:T(8,128)(2,1)} %shard_map.82), calls=%async_computation.1 | async-start | bytes 2097152 | tf_op jit(solution)/shard_map/all_to_all | solution.py:170
  27.1 0.6 fusion.4
  27.7 0.6 fusion.3
  28.3 0.0 copy-done.1
  28.3 0.8 fusion.1
  29.1 13.4 %all-to-all-done.1 = bf16[64,32,256]{2,1,0:T(8,128)(2,1)S(1)} async-done(((bf16[64,32,256]{2,1,0:T(8,128)(2,1)}), bf16[64,32,256]{2,1,0:T(8,128)(2,1)S(1)}, u32[]{:S(2)}, u32[]{:S(2)}) %all-to-all-start.1) | async-done | bytes 1048608 | tf_op jit(solution)/shard_map/all_to_all | solution.py:170
  42.5 0.6 copy.21
  43.1 1.3 %copy.25 = bf16[32,8,8,256]{3,1,2,0:T(8,128)(2,1)} copy(bf16[32,8,8,256]{3,2,1,0:T(8,128)(2,1)S(1)} %bitcast.40) | data formatting | bytes 2097152
  44.4 4.8 %shard_map.83.rest_2_ = bf16[2,256,512]{2,1,0:T(8,128)(2,1)} custom-call(bf16[256,2048]{1,0:T(8,128)(2,1)} %bitcast.34, s32[4,512]{1,0:T(4,128)} %get-tuple-element.12.i_ref, f32[4,512]{1,0:T(4,128)} %get-tuple-element.10.w_ref, bf16[256,512]{1,0:T(8,128)(2,1)} %get-tuple-element.6.rest_0_), custom_call_target="tpu_custom_call" | custom-call | tf_op jit(solution)/shard_map/pallas_call | solution.py:140
  49.2 0.7 collective-permute-start
  49.9 4.8 %shard_map.84.rest_0_ = bf16[2,256,512]{2,1,0:T(8,128)(2,1)} custom-call(bf16[256,2048]{1,0:T(8,128)(2,1)} %bitcast.35, s32[4,512]{1,0:T(4,128)} %get-tuple-element.11.i_ref, f32[4,512]{1,0:T(4,128)} %get-tuple-element.9.w_ref, bf16[256,512]{1,0:T(8,128)(2,1)} %get-tuple-element.5.rest_0_), custom_call_target="tpu_custom_call" | custom-call | tf_op jit(solution)/shard_map/pallas_call | solution.py:140
  54.7 3.1 %collective-permute-start.1 = (bf16[2,256,512]{2,1,0:T(8,128)(2,1)}, bf16[2,256,512]{2,1,0:T(8,128)(2,1)S(1)}, u32[]{:S(2)}, u32[]{:S(2)}) collective-permute-start(bf16[2,256,512]{2,1,0:T(8,128)(2,1)} %shard_map.84.rest_0_), channel_id=1, source_target_pairs={{1,0},{2,1},{3,2},{0,3},{5,4},{6,5},{7,6},{4,7},{9,8},{10,9},{11,1... | collective-permute-start | bytes 1572872 | tf_op jit(solution)/shard_map/ppermute | solution.py:192
  57.8 0.1 fusion.5
  57.8 0.1 slice.60
  57.9 0.6 slice.61.i_ref
  58.5 0.6 slice.62.w_ref
  59.1 0.6 reshape.62.code_ref
  59.8 0.1 pad_add_fusion
  59.8 0.6 reshape.57.code_ref
  60.4 7.4 %shard_map.85.rest_1_ = bf16[256,1024]{1,0:T(8,128)(2,1)} custom-call(bf16[256,2048]{1,0:T(8,128)(2,1)} %bitcast.36, s32[4,1024]{1,0:T(4,128)} %slice.61.i_ref, f32[4,1024]{1,0:T(4,128)} %slice.62.w_ref), custom_call_target="tpu_custom_call" | custom-call | tf_op jit(solution)/shard_map/pallas_call | solution.py:140
  67.8 8.6 %shard_map.86.rest_4_ = f32[256,2048]{1,0:T(8,128)} custom-call(s32[256]{0:T(256)} %reshape.62.code_ref, bf16[256,2048]{1,0:T(8,128)(2,1)} %bitcast.37, f32[5,128,128]{2,1,0:T(8,128)} %constant.26.clone.taper_ref, bf16[2,256,512]{2,1,0:T(8,128)(2,1)} %shard_map.84.rest_0_, bf16[256,1024]{1,0:T(8,128)(2,1)} %shard_map.85.rest_1_, ...), custom_call_target="tpu_custom_call" | custom-call | flops 4294967296 | bytes 4194304 | tf_op jit(solution)/shard_map/pallas_call | solution.py:336
  76.4 0.0 collective-permute-done.rest_0_.rest_2_
  76.4 0.0 copy-start.6
  76.4 0.0 collective-permute-done.1.rest_1_.rest_3_
  76.4 0.8 copy-done.6
  77.2 0.0 copy-start.7
  77.2 0.8 copy-done.7
  78.0 6.8 %shard_map.87 = bf16[256,2048]{1,0:T(8,128)(2,1)} custom-call(s32[128]{0:T(128)} %reshape.57.code_ref, bf16[256,2048]{1,0:T(8,128)(2,1)} %bitcast.38, f32[5,128,128]{2,1,0:T(8,128)} %constant.26.clone.taper_ref, bf16[2,256,512]{2,1,0:T(8,128)(2,1)} %copy-done.6, bf16[2,256,512]{2,1,0:T(8,128)(2,1)} %copy-done.7, bf16[2,256,512]{2,1,0:T(8,128)(2,1)} %copy-done.6, ...), custom_call_target="tpu_custom_call" | custom-call | flops 2147483648 | bytes 4194304 | tf_op jit(solution)/shard_map/pallas_call | solution.py:336
  84.8 1.5 %copy.29 = bf16[32,8,8,256]{3,2,1,0:T(8,128)(2,1)S(1)} copy(bf16[32,8,8,256]{3,1,2,0:T(8,128)(2,1)} %bitcast.46) | data formatting | bytes 2097152
  86.3 17.8 %all_to_all.41 = bf16[256,8,256]{2,1,0:T(8,128)(2,1)S(1)} all-to-all(bf16[256,8,256]{2,1,0:T(8,128)(2,1)S(1)} %bitcast.41), channel_id=1, replica_groups=mesh['wide'=8,'lon'=4] {'wide'}, dimensions={0} | all-to-all | bytes 2097152 | tf_op jit(solution)/shard_map/all_to_all | solution.py:224
  104.1 1.1 %copy.31 = bf16[8,32,8,256]{3,2,0,1:T(8,128)(2,1)} copy(bf16[8,32,8,256]{3,2,1,0:T(8,128)(2,1)S(1)} %bitcast.42) | data formatting | bytes 2097152 | tf_op jit(solution)/shard_map/all_to_all | solution.py:224
  (6 shorter events, 0.1 us)
Async XLA Ops:
  0.0 9.5 %copy-start = (f32[4,64,256]{2,1,0:T(8,128)S(1)}, f32[4,64,256]{2,1,0:T(8,128)}, u32[]{:S(2)}) copy-start(f32[4,64,256]{2,1,0:T(8,128)} %param.11) | copy-start | bytes 786436
  0.0 9.2 %copy-start.4 = (s32[1,16,16]{2,1,0:T(8,128)S(1)}, s32[1,16,16]{2,1,0:T(8,128)}, u32[]{:S(2)}) copy-start(s32[1,16,16]{2,1,0:T(8,128)} %param.14) | copy-start | bytes 3076
  0.0 9.2 %copy-start.5 = (s32[1,16]{1,0:T(1,128)S(1)}, s32[1,16]{1,0:T(1,128)}, u32[]{:S(2)}) copy-start(s32[1,16]{1,0:T(1,128)} %param.13) | copy-start | bytes 196
  0.0 9.3 %copy-start.3 = (s32[1,16,16]{2,1,0:T(8,128)S(1)}, s32[1,16,16]{2,1,0:T(8,128)}, u32[]{:S(2)}) copy-start(s32[1,16,16]{2,1,0:T(8,128)} %param.12) | copy-start | bytes 3076
  0.0 10.3 %copy-start.2 = (bf16[256,8,256]{2,1,0:T(8,128)(2,1)S(1)}, bf16[256,8,256]{2,1,0:T(8,128)(2,1)}, u32[]{:S(2)}) copy-start(bf16[256,8,256]{2,1,0:T(8,128)(2,1)} %param.9) | copy-start | bytes 3145732
  2.9 12.0 %all-to-all-start = ((bf16[4,2,2048]{2,1,0:T(2,128)(2,1)}), bf16[4,2,2048]{2,1,0:T(2,128)(2,1)S(1)}, u32[]{:S(2)}, u32[]{:S(2)}) async-start(bf16[4,2,2048]{2,1,0:T(2,128)(2,1)} %reshape.64), calls=%async_computation | async-start | bytes 65536 | tf_op jit(solution)/shard_map/all_to_all | solution.py:33
  10.6 17.7 %copy-start.1 = (bf16[32,8,8,256]{3,1,2,0:T(8,128)(2,1)}, bf16[32,8,8,256]{3,1,2,0:T(8,128)(2,1)S(1)}, u32[]{:S(2)}) copy-start(bf16[32,8,8,256]{3,1,2,0:T(8,128)(2,1)S(1)} %copy.28) | copy-start | bytes 3145732
  23.3 19.1 %all-to-all-start.1 = ((bf16[64,32,256]{2,1,0:T(8,128)(2,1)}), bf16[64,32,256]{2,1,0:T(8,128)(2,1)S(1)}, u32[]{:S(2)}, u32[]{:S(2)}) async-start(bf16[64,32,256]{2,1,0:T(8,128)(2,1)} %shard_map.82), calls=%async_computation.1 | async-start | bytes 2097152 | tf_op jit(solution)/shard_map/all_to_all | solution.py:170
  49.2 27.3 %collective-permute-start = (bf16[2,256,512]{2,1,0:T(8,128)(2,1)}, bf16[2,256,512]{2,1,0:T(8,128)(2,1)S(1)}, u32[]{:S(2)}, u32[]{:S(2)}) collective-permute-start(bf16[2,256,512]{2,1,0:T(8,128)(2,1)} %shard_map.83.rest_2_), channel_id=1, source_target_pairs={{0,1},{1,2},{2,3},{3,0},{4,5},{5,6},{6,7},{7,4},{8,9},{9,10},{10,1... | collective-permute-start | bytes 1572872 | tf_op jit(solution)/shard_map/ppermute | solution.py:188
  54.7 21.7 %collective-permute-start.1 = (bf16[2,256,512]{2,1,0:T(8,128)(2,1)}, bf16[2,256,512]{2,1,0:T(8,128)(2,1)S(1)}, u32[]{:S(2)}, u32[]{:S(2)}) collective-permute-start(bf16[2,256,512]{2,1,0:T(8,128)(2,1)} %shard_map.84.rest_0_), channel_id=1, source_target_pairs={{1,0},{2,1},{3,2},{0,3},{5,4},{6,5},{7,6},{4,7},{9,8},{10,9},{11,1... | collective-permute-start | bytes 1572872 | tf_op jit(solution)/shard_map/ppermute | solution.py:192
  76.4 0.8 copy-start.6
  77.2 0.8 copy-start.7

commit v19 on v17

--- a/solution.py
+++ b/solution.py
@@ -43,7 +43,7 @@
         west_from = (t + size - 1) % size
         east_from = (t + 1) % size
 
-        def one(m, carry):
+        def one(m):
             x = x_ref[m].astype(jnp.float32)
             west_col = h_ref[west_from, m][:, 1:2].astype(jnp.float32)
             east_col = h_ref[east_from, m][:, 0:1].astype(jnp.float32)
@@ -52,11 +52,15 @@
             north = jnp.where(row == rows - 1, 0.0, pltpu.roll(x, rows - 1, 0))
             south = jnp.where(row == 0, 0.0, pltpu.roll(x, 1, 0))
             spread = east_n + west_n + north + south - 4.0 * x
-            o_ref[:, m, :] = (x + 0.2 * spread - 0.3 * (east_n - west_n)).astype(jnp.bfloat16)
+            return (x + 0.2 * spread - 0.3 * (east_n - west_n)).astype(jnp.bfloat16)
+
+        def group(i, carry):
+            base = pl.multiple_of(i * 8, 8)
+            values = jnp.stack([one(base + j) for j in range(8)], axis=1)
+            o_ref[:, pl.ds(base, 8), :] = values
             return carry
 
-        for m in range(members):
-            one(m, 0)
+        lax.fori_loop(0, members // 8, group, 0)
 
     grid_spec = pltpu.PrefetchScalarGridSpec(
         num_scalar_prefetch=1,

time: 104 us -> 104 us (level)
  no operation moved by 1% of the time
where the time goes in v19:
time: 104 us
  Pallas kernels  39.1 us (38%)
  blocking collectives  17.8 us (17%)
  local copies, waits for them, and re-layouts  16.8 us (16%)
  waiting for transfers between devices  14.9 us (14%)
  starting transfers between devices  13.9 us (13%)
  other arithmetic  1.23 us (1%)
    all_to_all x1, blocking collectives, body(): lax.all_to_all(result.reshape(members, band_rows, patch_meridian_lines),...  17.8 us
    pallas_call x3, Pallas kernels, observe_dev_call(): pl.pallas_call(kernel, grid=(count // OBS_STEP,), in_specs=in_specs, out_...  17 us
    pallas_call x2, Pallas kernels, update_call(): pl.pallas_call(kernel, grid_spec=grid_spec, out_shape=jax.ShapeDtypeStruc...  15.3 us
    all_to_all x1, waiting for transfers between devices, body(): lax.all_to_all(prediction_increment, 'wide', split_axis=0, concat_axis=1,...  13.3 us
    pallas_call x1, Pallas kernels, forecast_call(): pl.pallas_call(kernel, grid_spec=grid_spec, out_shape=jax.ShapeDtypeStruc...  6.77 us
    all_to_all x1, starting transfers between devices, column_halo(): return lax.all_to_all(spread, axis, 0, 0, tiled=False)  6.32 us
    unnamed x27, local copies, waits for them, and re-layouts  6.16 us
    all_to_all x1, starting transfers between devices, body(): lax.all_to_all(prediction_increment, 'wide', split_axis=0, concat_axis=1,...  3.72 us
  transfers between devices with their start and end apart: 4, of which 2 were waited for; matrix products, arithmetic and copies ran while one was open for 7% of the time, Pallas kernels for 20%

profile of v19, /device:TPU:0, one launch (start us, length us, event | category | flops | bytes accessed | tf_op | source)
XLA Modules:
  0.0 103.9 jit_solution(9190131649021243671)
XLA Ops:
  0.0 0.0 copy-start
  0.0 0.0 copy-start.4
  0.0 0.0 copy-start.5
  0.0 0.0 copy-start.3
  0.0 0.0 copy-start.2
  0.0 1.5 %fusion.5 = (bf16[32,64,1]{2,1,0:T(8,128)(2,1)S(1)}, bf16[32,64,1]{2,1,0:T(8,128)(2,1)S(1)}) fusion(bf16[32,64,256]{2,1,0:T(8,128)(2,1)} %x_ref.1), kind=kLoop, calls=%fused_computation.18 | loop fusion | bytes 16384 | tf_op jit(solution)/shard_map/slice | solution.py:29
  1.6 0.3 copy.22
  1.9 0.3 copy.23
  2.2 0.7 reshape.77
  2.9 6.3 %all-to-all-start = ((bf16[4,2,2048]{2,1,0:T(2,128)(2,1)}), bf16[4,2,2048]{2,1,0:T(2,128)(2,1)S(1)}, u32[]{:S(2)}, u32[]{:S(2)}) async-start(bf16[4,2,2048]{2,1,0:T(2,128)(2,1)} %reshape.77), calls=%async_computation | async-start | bytes 65536 | tf_op jit(solution)/shard_map/all_to_all | solution.py:31
  9.2 0.0 copy-done.4
  9.2 0.0 copy-done.5
  9.2 0.1 fusion.3
  9.3 0.0 copy-done.3
  9.3 0.1 select_reduce_fusion
  9.5 0.1 fusion.8
  9.5 0.0 copy-done
  9.5 0.8 subtract_bitcast_fusion
  10.3 0.1 pad_add_fusion
  10.4 0.1 slice.60
  10.5 0.7 reshape.75.code_ref
  11.1 0.6 reshape.70.code_ref
  11.8 0.6 slice.61.i_ref
  12.4 0.6 slice.62.w_ref
  13.0 0.0 copy-done.2
  13.0 0.3 copy.27
  13.3 0.0 copy-start.1
  13.3 1.6 %all-to-all-done = bf16[4,2,2048]{2,1,0:T(2,128)(2,1)S(1)} async-done(((bf16[4,2,2048]{2,1,0:T(2,128)(2,1)}), bf16[4,2,2048]{2,1,0:T(2,128)(2,1)S(1)}, u32[]{:S(2)}, u32[]{:S(2)}) %all-to-all-start) | async-done | bytes 32800 | tf_op jit(solution)/shard_map/all_to_all | solution.py:31
  14.9 0.1 reshape.78
  15.0 2.0 %copy.19.h_ref = bf16[4,32,64,2]{3,2,1,0:T(8,128)(2,1)} copy(bf16[4,32,64,2]{2,1,3,0:T(8,128)(2,1)S(1)} %bitcast.47) | data formatting | bytes 65536 | tf_op jit(solution)/shard_map/all_to_all | solution.py:31
  17.0 6.8 %shard_map.73 = bf16[64,32,256]{2,1,0:T(8,128)(2,1)} custom-call(s32[1]{0:T(128)} %bitcast.3.pos_ref, bf16[32,64,256]{2,1,0:T(8,128)(2,1)} %x_ref.1, bf16[4,32,64,2]{3,2,1,0:T(8,128)(2,1)} %copy.19.h_ref), custom_call_target="tpu_custom_call" | custom-call | tf_op jit(solution)/shard_map/pallas_call | solution.py:74
  23.7 3.7 %all-to-all-start.1 = ((bf16[64,32,256]{2,1,0:T(8,128)(2,1)}), bf16[64,32,256]{2,1,0:T(8,128)(2,1)S(1)}, u32[]{:S(2)}, u32[]{:S(2)}) async-start(bf16[64,32,256]{2,1,0:T(8,128)(2,1)} %shard_map.73), calls=%async_computation.1 | async-start | bytes 2097152 | tf_op jit(solution)/shard_map/all_to_all | solution.py:172
  27.5 0.6 fusion.7
  28.1 0.6 fusion.6
  28.7 0.0 copy-done.1
  28.7 0.8 fusion.4
  29.5 13.3 %all-to-all-done.1 = bf16[64,32,256]{2,1,0:T(8,128)(2,1)S(1)} async-done(((bf16[64,32,256]{2,1,0:T(8,128)(2,1)}), bf16[64,32,256]{2,1,0:T(8,128)(2,1)S(1)}, u32[]{:S(2)}, u32[]{:S(2)}) %all-to-all-start.1) | async-done | bytes 1048608 | tf_op jit(solution)/shard_map/all_to_all | solution.py:172
  42.9 0.6 copy.20
  43.5 1.3 %copy.24 = bf16[32,8,8,256]{3,1,2,0:T(8,128)(2,1)} copy(bf16[32,8,8,256]{3,2,1,0:T(8,128)(2,1)S(1)} %bitcast.40) | data formatting | bytes 2097152
  44.8 4.8 %shard_map.74.rest_2_ = bf16[2,256,512]{2,1,0:T(8,128)(2,1)} custom-call(bf16[256,2048]{1,0:T(8,128)(2,1)} %bitcast.34, s32[4,512]{1,0:T(4,128)} %get-tuple-element.12.i_ref, f32[4,512]{1,0:T(4,128)} %get-tuple-element.10.w_ref, bf16[256,512]{1,0:T(8,128)(2,1)} %get-tuple-element.6.rest_0_), custom_call_target="tpu_custom_call" | custom-call | tf_op jit(solution)/shard_map/pallas_call | solution.py:142
  49.6 0.7 collective-permute-start
  50.3 4.8 %shard_map.75.rest_0_ = bf16[2,256,512]{2,1,0:T(8,128)(2,1)} custom-call(bf16[256,2048]{1,0:T(8,128)(2,1)} %bitcast.35, s32[4,512]{1,0:T(4,128)} %get-tuple-element.11.i_ref, f32[4,512]{1,0:T(4,128)} %get-tuple-element.9.w_ref, bf16[256,512]{1,0:T(8,128)(2,1)} %get-tuple-element.5.rest_0_), custom_call_target="tpu_custom_call" | custom-call | tf_op jit(solution)/shard_map/pallas_call | solution.py:142
  55.1 3.1 %collective-permute-start.1 = (bf16[2,256,512]{2,1,0:T(8,128)(2,1)}, bf16[2,256,512]{2,1,0:T(8,128)(2,1)S(1)}, u32[]{:S(2)}, u32[]{:S(2)}) collective-permute-start(bf16[2,256,512]{2,1,0:T(8,128)(2,1)} %shard_map.75.rest_0_), channel_id=1, source_target_pairs={{1,0},{2,1},{3,2},{0,3},{5,4},{6,5},{7,6},{4,7},{9,8},{10,9},{11,1... | collective-permute-start | bytes 1572872 | tf_op jit(solution)/shard_map/ppermute | solution.py:194
  58.2 0.1 fusion.2
  58.3 0.8 concatenate.11.taper_ref
  59.1 7.4 %shard_map.76.rest_1_ = bf16[256,1024]{1,0:T(8,128)(2,1)} custom-call(bf16[256,2048]{1,0:T(8,128)(2,1)} %bitcast.36, s32[4,1024]{1,0:T(4,128)} %slice.61.i_ref, f32[4,1024]{1,0:T(4,128)} %slice.62.w_ref), custom_call_target="tpu_custom_call" | custom-call | tf_op jit(solution)/shard_map/pallas_call | solution.py:142
  66.5 8.6 %shard_map.77.rest_4_ = f32[256,2048]{1,0:T(8,128)} custom-call(s32[256]{0:T(256)} %reshape.75.code_ref, bf16[256,2048]{1,0:T(8,128)(2,1)} %bitcast.37, f32[5,128,128]{2,1,0:T(8,128)} %concatenate.11.taper_ref, bf16[2,256,512]{2,1,0:T(8,128)(2,1)} %shard_map.75.rest_0_, bf16[256,1024]{1,0:T(8,128)(2,1)} %shard_map.76.rest_1_, ...), custom_call_target="tpu_custom_call" | custom-call | flops 4294967296 | bytes 4194304 | tf_op jit(solution)/shard_map/pallas_call | solution.py:338
  75.0 0.0 collective-permute-done.rest_0_.rest_2_
  75.0 0.0 copy-start.6
  75.0 0.0 collective-permute-done.1.rest_1_.rest_3_
  75.1 0.8 copy-done.6
  75.8 0.0 copy-start.7
  75.8 0.8 copy-done.7
  76.7 6.8 %shard_map.78 = bf16[256,2048]{1,0:T(8,128)(2,1)} custom-call(s32[128]{0:T(128)} %reshape.70.code_ref, bf16[256,2048]{1,0:T(8,128)(2,1)} %bitcast.38, f32[5,128,128]{2,1,0:T(8,128)} %concatenate.11.taper_ref, bf16[2,256,512]{2,1,0:T(8,128)(2,1)} %copy-done.6, bf16[2,256,512]{2,1,0:T(8,128)(2,1)} %copy-done.7, bf16[2,256,512]{2,1,0:T(8,128)(2,1)} %copy-done.6, ...), custom_call_target="tpu_custom_call" | custom-call | flops 2147483648 | bytes 4194304 | tf_op jit(solution)/shard_map/pallas_call | solution.py:338
  83.4 1.5 %copy.28 = bf16[32,8,8,256]{3,2,1,0:T(8,128)(2,1)S(1)} copy(bf16[32,8,8,256]{3,1,2,0:T(8,128)(2,1)} %bitcast.46) | data formatting | bytes 2097152
  84.9 17.8 %all_to_all.41 = bf16[256,8,256]{2,1,0:T(8,128)(2,1)S(1)} all-to-all(bf16[256,8,256]{2,1,0:T(8,128)(2,1)S(1)} %bitcast.41), channel_id=1, replica_groups=mesh['wide'=8,'lon'=4] {'wide'}, dimensions={0} | all-to-all | bytes 2097152 | tf_op jit(solution)/shard_map/all_to_all | solution.py:226
  102.8 1.1 %copy.30 = bf16[8,32,8,256]{3,2,0,1:T(8,128)(2,1)} copy(bf16[8,32,8,256]{3,2,1,0:T(8,128)(2,1)S(1)} %bitcast.42) | data formatting | bytes 2097152 | tf_op jit(solution)/shard_map/all_to_all | solution.py:226
  (8 shorter events, 0.1 us)
Async XLA Ops:
  0.0 9.5 %copy-start = (f32[4,64,256]{2,1,0:T(8,128)S(1)}, f32[4,64,256]{2,1,0:T(8,128)}, u32[]{:S(2)}) copy-start(f32[4,64,256]{2,1,0:T(8,128)} %param.10) | copy-start | bytes 786436
  0.0 9.2 %copy-start.4 = (s32[1,16,16]{2,1,0:T(8,128)S(1)}, s32[1,16,16]{2,1,0:T(8,128)}, u32[]{:S(2)}) copy-start(s32[1,16,16]{2,1,0:T(8,128)} %param.13) | copy-start | bytes 3076
  0.0 9.2 %copy-start.5 = (s32[1,16]{1,0:T(1,128)S(1)}, s32[1,16]{1,0:T(1,128)}, u32[]{:S(2)}) copy-start(s32[1,16]{1,0:T(1,128)} %param.12) | copy-start | bytes 196
  0.0 9.3 %copy-start.3 = (s32[1,16,16]{2,1,0:T(8,128)S(1)}, s32[1,16,16]{2,1,0:T(8,128)}, u32[]{:S(2)}) copy-start(s32[1,16,16]{2,1,0:T(8,128)} %param.11) | copy-start | bytes 3076
  0.0 13.0 %copy-start.2 = (bf16[256,8,256]{2,1,0:T(8,128)(2,1)S(1)}, bf16[256,8,256]{2,1,0:T(8,128)(2,1)}, u32[]{:S(2)}) copy-start(bf16[256,8,256]{2,1,0:T(8,128)(2,1)} %param.8) | copy-start | bytes 3145732
  2.9 12.0 %all-to-all-start = ((bf16[4,2,2048]{2,1,0:T(2,128)(2,1)}), bf16[4,2,2048]{2,1,0:T(2,128)(2,1)S(1)}, u32[]{:S(2)}, u32[]{:S(2)}) async-start(bf16[4,2,2048]{2,1,0:T(2,128)(2,1)} %reshape.77), calls=%async_computation | async-start | bytes 65536 | tf_op jit(solution)/shard_map/all_to_all | solution.py:31
  13.3 15.4 %copy-start.1 = (bf16[32,8,8,256]{3,1,2,0:T(8,128)(2,1)}, bf16[32,8,8,256]{3,1,2,0:T(8,128)(2,1)S(1)}, u32[]{:S(2)}) copy-start(bf16[32,8,8,256]{3,1,2,0:T(8,128)(2,1)S(1)} %copy.27) | copy-start | bytes 3145732
  23.7 19.1 %all-to-all-start.1 = ((bf16[64,32,256]{2,1,0:T(8,128)(2,1)}), bf16[64,32,256]{2,1,0:T(8,128)(2,1)S(1)}, u32[]{:S(2)}, u32[]{:S(2)}) async-start(bf16[64,32,256]{2,1,0:T(8,128)(2,1)} %shard_map.73), calls=%async_computation.1 | async-start | bytes 2097152 | tf_op jit(solution)/shard_map/all_to_all | solution.py:172
  49.6 25.5 %collective-permute-start = (bf16[2,256,512]{2,1,0:T(8,128)(2,1)}, bf16[2,256,512]{2,1,0:T(8,128)(2,1)S(1)}, u32[]{:S(2)}, u32[]{:S(2)}) collective-permute-start(bf16[2,256,512]{2,1,0:T(8,128)(2,1)} %shard_map.74.rest_2_), channel_id=1, source_target_pairs={{0,1},{1,2},{2,3},{3,0},{4,5},{5,6},{6,7},{7,4},{8,9},{9,10},{10,1... | collective-permute-start | bytes 1572872 | tf_op jit(solution)/shard_map/ppermute | solution.py:190
  55.1 20.0 %collective-permute-start.1 = (bf16[2,256,512]{2,1,0:T(8,128)(2,1)}, bf16[2,256,512]{2,1,0:T(8,128)(2,1)S(1)}, u32[]{:S(2)}, u32[]{:S(2)}) collective-permute-start(bf16[2,256,512]{2,1,0:T(8,128)(2,1)} %shard_map.75.rest_0_), channel_id=1, source_target_pairs={{1,0},{2,1},{3,2},{0,3},{5,4},{6,5},{7,6},{4,7},{9,8},{10,9},{11,1... | collective-permute-start | bytes 1572872 | tf_op jit(solution)/shard_map/ppermute | solution.py:194
  75.0 0.8 copy-start.6
  75.8 0.8 copy-start.7

commit v20 on v17

--- a/solution.py
+++ b/solution.py
@@ -26,7 +26,7 @@
 
 def column_halo(value, axis):
     size = lax.axis_size(axis)
-    edges = jnp.concatenate([value[..., :1], value[..., -1:]], axis=-1)
+    edges = jnp.stack([value[..., 0], value[..., -1]]).transpose(0, 2, 1)
     spread = jnp.broadcast_to(edges[None], (size,) + edges.shape)
     return lax.all_to_all(spread, axis, 0, 0, tiled=False)
 
@@ -45,8 +45,8 @@
 
         def one(m, carry):
             x = x_ref[m].astype(jnp.float32)
-            west_col = h_ref[west_from, m][:, 1:2].astype(jnp.float32)
-            east_col = h_ref[east_from, m][:, 0:1].astype(jnp.float32)
+            west_col = h_ref[west_from, 1][:, m:m + 1].astype(jnp.float32)
+            east_col = h_ref[east_from, 0][:, m:m + 1].astype(jnp.float32)
             east_n = jnp.where(col == cols - 1, east_col, pltpu.roll(x, cols - 1, 1))
             west_n = jnp.where(col == 0, west_col, pltpu.roll(x, 1, 1))
             north = jnp.where(row == rows - 1, 0.0, pltpu.roll(x, rows - 1, 0))

time: 104 us -> 102 us (0.981)
  local copies, waits for them, and re-layouts: 16.8 us -> 15.6 us
    all_to_all x1, local copies, waits for them, and re-layouts: 1.98 us -> 0.77 us  [column_halo(): return lax.all_to_all(spread, axis, 0, 0, tiled=False)]
where the time goes in v20:
time: 102 us; the launch traced here: 101 us
  Pallas kernels  37.9 us (37%)
  blocking collectives  17.8 us (17%)
  local copies, waits for them, and re-layouts  15.6 us (15%)
  waiting for transfers between devices  14.9 us (15%)
  starting transfers between devices  13.9 us (14%)
  other arithmetic  1.23 us (1%)
    all_to_all x1, blocking collectives, body(): lax.all_to_all(result.reshape(members, band_rows, patch_meridian_lines),...  17.8 us
    pallas_call x3, Pallas kernels, observe_dev_call(): pl.pallas_call(kernel, grid=(count // OBS_STEP,), in_specs=in_specs, out_...  17 us
    pallas_call x2, Pallas kernels, update_call(): pl.pallas_call(kernel, grid_spec=grid_spec, out_shape=jax.ShapeDtypeStruc...  15.3 us
    all_to_all x1, waiting for transfers between devices, body(): lax.all_to_all(prediction_increment, 'wide', split_axis=0, concat_axis=1,...  13.3 us
    all_to_all x1, starting transfers between devices, column_halo(): return lax.all_to_all(spread, axis, 0, 0, tiled=False)  6.32 us
    unnamed x27, local copies, waits for them, and re-layouts  6.16 us
    pallas_call x1, Pallas kernels, forecast_call(): pl.pallas_call(kernel, grid_spec=grid_spec, out_shape=jax.ShapeDtypeStruc...  5.6 us
    all_to_all x1, starting transfers between devices, body(): lax.all_to_all(prediction_increment, 'wide', split_axis=0, concat_axis=1,...  3.72 us
  transfers between devices with their start and end apart: 4, of which 2 were waited for; matrix products, arithmetic and copies ran while one was open for 7% of the time, Pallas kernels for 20%

profile of v20, /device:TPU:0, one launch (start us, length us, event | category | flops | bytes accessed | tf_op | source)
XLA Modules:
  0.0 101.5 jit_solution(1008738646895264032)
XLA Ops:
  0.0 0.0 copy-start
  0.0 0.0 copy-start.4
  0.0 0.0 copy-start.5
  0.0 0.0 copy-start.3
  0.0 0.0 copy-start.2
  0.0 1.5 %fusion.5 = (bf16[32,64,1]{2,1,0:T(8,128)(2,1)S(1)}, bf16[32,64,1]{2,1,0:T(8,128)(2,1)S(1)}) fusion(bf16[32,64,256]{2,1,0:T(8,128)(2,1)} %x_ref.1), kind=kLoop, calls=%fused_computation.18 | loop fusion | bytes 16384 | tf_op jit(solution)/shard_map/slice | solution.py:29
  1.6 0.3 copy.27
  1.9 0.3 copy.28
  2.2 0.7 reshape.77
  2.9 6.3 %all-to-all-start = ((bf16[4,2,2048]{2,1,0:T(2,128)(2,1)}), bf16[4,2,2048]{2,1,0:T(2,128)(2,1)S(1)}, u32[]{:S(2)}, u32[]{:S(2)}) async-start(bf16[4,2,2048]{2,1,0:T(2,128)(2,1)} %reshape.77), calls=%async_computation | async-start | bytes 65536 | tf_op jit(solution)/shard_map/all_to_all | solution.py:31
  9.2 0.0 copy-done.4
  9.2 0.0 copy-done.5
  9.2 0.1 fusion.3
  9.3 0.0 copy-done.3
  9.3 0.1 select_reduce_fusion
  9.5 0.1 fusion.8
  9.5 0.0 copy-done
  9.5 0.8 subtract_bitcast_fusion
  10.3 0.1 pad_add_fusion
  10.4 0.1 slice.60
  10.5 0.7 reshape.75.code_ref
  11.1 0.6 reshape.70.code_ref
  11.7 0.6 slice.61.i_ref
  12.3 0.6 slice.62.w_ref
  12.9 0.0 copy-done.2
  12.9 0.3 copy.32
  13.3 0.0 copy-start.1
  13.3 1.6 %all-to-all-done = bf16[4,2,2048]{2,1,0:T(2,128)(2,1)S(1)} async-done(((bf16[4,2,2048]{2,1,0:T(2,128)(2,1)}), bf16[4,2,2048]{2,1,0:T(2,128)(2,1)S(1)}, u32[]{:S(2)}, u32[]{:S(2)}) %all-to-all-start) | async-done | bytes 32800 | tf_op jit(solution)/shard_map/all_to_all | solution.py:31
  14.9 0.1 reshape.78
  15.0 0.8 copy.24.h_ref
  15.8 5.6 %shard_map.73 = bf16[64,32,256]{2,1,0:T(8,128)(2,1)} custom-call(s32[1]{0:T(128)} %bitcast.3.pos_ref, bf16[32,64,256]{2,1,0:T(8,128)(2,1)} %x_ref.1, bf16[4,2,64,32]{3,2,1,0:T(8,128)(2,1)} %copy.24.h_ref), custom_call_target="tpu_custom_call" | custom-call | tf_op jit(solution)/shard_map/pallas_call | solution.py:70
  21.4 3.7 %all-to-all-start.1 = ((bf16[64,32,256]{2,1,0:T(8,128)(2,1)}), bf16[64,32,256]{2,1,0:T(8,128)(2,1)S(1)}, u32[]{:S(2)}, u32[]{:S(2)}) async-start(bf16[64,32,256]{2,1,0:T(8,128)(2,1)} %shard_map.73), calls=%async_computation.1 | async-start | bytes 2097152 | tf_op jit(solution)/shard_map/all_to_all | solution.py:168
  25.1 0.6 fusion.7
  25.7 0.6 fusion.6
  26.3 0.0 copy-done.1
  26.3 0.8 fusion.4
  27.2 13.3 %all-to-all-done.1 = bf16[64,32,256]{2,1,0:T(8,128)(2,1)S(1)} async-done(((bf16[64,32,256]{2,1,0:T(8,128)(2,1)}), bf16[64,32,256]{2,1,0:T(8,128)(2,1)S(1)}, u32[]{:S(2)}, u32[]{:S(2)}) %all-to-all-start.1) | async-done | bytes 1048608 | tf_op jit(solution)/shard_map/all_to_all | solution.py:168
  40.5 0.6 copy.25
  41.1 1.3 %copy.29 = bf16[32,8,8,256]{3,1,2,0:T(8,128)(2,1)} copy(bf16[32,8,8,256]{3,2,1,0:T(8,128)(2,1)S(1)} %bitcast.44) | data formatting | bytes 2097152
  42.4 4.8 %shard_map.74.rest_2_ = bf16[2,256,512]{2,1,0:T(8,128)(2,1)} custom-call(bf16[256,2048]{1,0:T(8,128)(2,1)} %bitcast.38, s32[4,512]{1,0:T(4,128)} %get-tuple-element.12.i_ref, f32[4,512]{1,0:T(4,128)} %get-tuple-element.10.w_ref, bf16[256,512]{1,0:T(8,128)(2,1)} %get-tuple-element.6.rest_0_), custom_call_target="tpu_custom_call" | custom-call | tf_op jit(solution)/shard_map/pallas_call | solution.py:138
  47.2 0.7 collective-permute-start
  47.9 4.8 %shard_map.75.rest_0_ = bf16[2,256,512]{2,1,0:T(8,128)(2,1)} custom-call(bf16[256,2048]{1,0:T(8,128)(2,1)} %bitcast.39, s32[4,512]{1,0:T(4,128)} %get-tuple-element.11.i_ref, f32[4,512]{1,0:T(4,128)} %get-tuple-element.9.w_ref, bf16[256,512]{1,0:T(8,128)(2,1)} %get-tuple-element.5.rest_0_), custom_call_target="tpu_custom_call" | custom-call | tf_op jit(solution)/shard_map/pallas_call | solution.py:138
  52.7 3.1 %collective-permute-start.1 = (bf16[2,256,512]{2,1,0:T(8,128)(2,1)}, bf16[2,256,512]{2,1,0:T(8,128)(2,1)S(1)}, u32[]{:S(2)}, u32[]{:S(2)}) collective-permute-start(bf16[2,256,512]{2,1,0:T(8,128)(2,1)} %shard_map.75.rest_0_), channel_id=1, source_target_pairs={{1,0},{2,1},{3,2},{0,3},{5,4},{6,5},{7,6},{4,7},{9,8},{10,9},{11,1... | collective-permute-start | bytes 1572872 | tf_op jit(solution)/shard_map/ppermute | solution.py:190
  55.8 0.1 fusion.2
  55.9 0.8 concatenate.7.taper_ref
  56.7 7.4 %shard_map.76.rest_1_ = bf16[256,1024]{1,0:T(8,128)(2,1)} custom-call(bf16[256,2048]{1,0:T(8,128)(2,1)} %bitcast.40, s32[4,1024]{1,0:T(4,128)} %slice.61.i_ref, f32[4,1024]{1,0:T(4,128)} %slice.62.w_ref), custom_call_target="tpu_custom_call" | custom-call | tf_op jit(solution)/shard_map/pallas_call | solution.py:138
  64.1 8.6 %shard_map.77.rest_4_ = f32[256,2048]{1,0:T(8,128)} custom-call(s32[256]{0:T(256)} %reshape.75.code_ref, bf16[256,2048]{1,0:T(8,128)(2,1)} %bitcast.41, f32[5,128,128]{2,1,0:T(8,128)} %concatenate.7.taper_ref, bf16[2,256,512]{2,1,0:T(8,128)(2,1)} %shard_map.75.rest_0_, bf16[256,1024]{1,0:T(8,128)(2,1)} %shard_map.76.rest_1_, ...), custom_call_target="tpu_custom_call" | custom-call | flops 4294967296 | bytes 4194304 | tf_op jit(solution)/shard_map/pallas_call | solution.py:334
  72.7 0.0 collective-permute-done.rest_0_.rest_2_
  72.7 0.0 copy-start.6
  72.7 0.0 collective-permute-done.1.rest_1_.rest_3_
  72.7 0.8 copy-done.6
  73.5 0.0 copy-start.7
  73.5 0.8 copy-done.7
  74.3 6.8 %shard_map.78 = bf16[256,2048]{1,0:T(8,128)(2,1)} custom-call(s32[128]{0:T(128)} %reshape.70.code_ref, bf16[256,2048]{1,0:T(8,128)(2,1)} %bitcast.42, f32[5,128,128]{2,1,0:T(8,128)} %concatenate.7.taper_ref, bf16[2,256,512]{2,1,0:T(8,128)(2,1)} %copy-done.6, bf16[2,256,512]{2,1,0:T(8,128)(2,1)} %copy-done.7, bf16[2,256,512]{2,1,0:T(8,128)(2,1)} %copy-done.6, ...), custom_call_target="tpu_custom_call" | custom-call | flops 2147483648 | bytes 4194304 | tf_op jit(solution)/shard_map/pallas_call | solution.py:334
  81.0 1.5 %copy.33 = bf16[32,8,8,256]{3,2,1,0:T(8,128)(2,1)S(1)} copy(bf16[32,8,8,256]{3,1,2,0:T(8,128)(2,1)} %bitcast.50) | data formatting | bytes 2097152
  82.6 17.8 %all_to_all.41 = bf16[256,8,256]{2,1,0:T(8,128)(2,1)S(1)} all-to-all(bf16[256,8,256]{2,1,0:T(8,128)(2,1)S(1)} %bitcast.45), channel_id=1, replica_groups=mesh['wide'=8,'lon'=4] {'wide'}, dimensions={0} | all-to-all | bytes 2097152 | tf_op jit(solution)/shard_map/all_to_all | solution.py:222
  100.4 1.1 %copy.35 = bf16[8,32,8,256]{3,2,0,1:T(8,128)(2,1)} copy(bf16[8,32,8,256]{3,2,1,0:T(8,128)(2,1)S(1)} %bitcast.46) | data formatting | bytes 2097152 | tf_op jit(solution)/shard_map/all_to_all | solution.py:222
  (8 shorter events, 0.1 us)
Async XLA Ops:
  0.0 9.5 %copy-start = (f32[4,64,256]{2,1,0:T(8,128)S(1)}, f32[4,64,256]{2,1,0:T(8,128)}, u32[]{:S(2)}) copy-start(f32[4,64,256]{2,1,0:T(8,128)} %param.10) | copy-start | bytes 786436
  0.0 9.2 %copy-start.4 = (s32[1,16,16]{2,1,0:T(8,128)S(1)}, s32[1,16,16]{2,1,0:T(8,128)}, u32[]{:S(2)}) copy-start(s32[1,16,16]{2,1,0:T(8,128)} %param.13) | copy-start | bytes 3076
  0.0 9.2 %copy-start.5 = (s32[1,16]{1,0:T(1,128)S(1)}, s32[1,16]{1,0:T(1,128)}, u32[]{:S(2)}) copy-start(s32[1,16]{1,0:T(1,128)} %param.12) | copy-start | bytes 196
  0.0 9.3 %copy-start.3 = (s32[1,16,16]{2,1,0:T(8,128)S(1)}, s32[1,16,16]{2,1,0:T(8,128)}, u32[]{:S(2)}) copy-start(s32[1,16,16]{2,1,0:T(8,128)} %param.11) | copy-start | bytes 3076
  0.0 12.9 %copy-start.2 = (bf16[256,8,256]{2,1,0:T(8,128)(2,1)S(1)}, bf16[256,8,256]{2,1,0:T(8,128)(2,1)}, u32[]{:S(2)}) copy-start(bf16[256,8,256]{2,1,0:T(8,128)(2,1)} %param.8) | copy-start | bytes 3145732
  2.9 12.0 %all-to-all-start = ((bf16[4,2,2048]{2,1,0:T(2,128)(2,1)}), bf16[4,2,2048]{2,1,0:T(2,128)(2,1)S(1)}, u32[]{:S(2)}, u32[]{:S(2)}) async-start(bf16[4,2,2048]{2,1,0:T(2,128)(2,1)} %reshape.77), calls=%async_computation | async-start | bytes 65536 | tf_op jit(solution)/shard_map/all_to_all | solution.py:31
  13.3 13.1 %copy-start.1 = (bf16[32,8,8,256]{3,1,2,0:T(8,128)(2,1)}, bf16[32,8,8,256]{3,1,2,0:T(8,128)(2,1)S(1)}, u32[]{:S(2)}) copy-start(bf16[32,8,8,256]{3,1,2,0:T(8,128)(2,1)S(1)} %copy.32) | copy-start | bytes 3145732
  21.4 19.1 %all-to-all-start.1 = ((bf16[64,32,256]{2,1,0:T(8,128)(2,1)}), bf16[64,32,256]{2,1,0:T(8,128)(2,1)S(1)}, u32[]{:S(2)}, u32[]{:S(2)}) async-start(bf16[64,32,256]{2,1,0:T(8,128)(2,1)} %shard_map.73), calls=%async_computation.1 | async-start | bytes 2097152 | tf_op jit(solution)/shard_map/all_to_all | solution.py:168
  47.2 25.5 %collective-permute-start = (bf16[2,256,512]{2,1,0:T(8,128)(2,1)}, bf16[2,256,512]{2,1,0:T(8,128)(2,1)S(1)}, u32[]{:S(2)}, u32[]{:S(2)}) collective-permute-start(bf16[2,256,512]{2,1,0:T(8,128)(2,1)} %shard_map.74.rest_2_), channel_id=1, source_target_pairs={{0,1},{1,2},{2,3},{3,0},{4,5},{5,6},{6,7},{7,4},{8,9},{9,10},{10,1... | collective-permute-start | bytes 1572872 | tf_op jit(solution)/shard_map/ppermute | solution.py:186
  52.7 20.0 %collective-permute-start.1 = (bf16[2,256,512]{2,1,0:T(8,128)(2,1)}, bf16[2,256,512]{2,1,0:T(8,128)(2,1)S(1)}, u32[]{:S(2)}, u32[]{:S(2)}) collective-permute-start(bf16[2,256,512]{2,1,0:T(8,128)(2,1)} %shard_map.75.rest_0_), channel_id=1, source_target_pairs={{1,0},{2,1},{3,2},{0,3},{5,4},{6,5},{7,6},{4,7},{9,8},{10,9},{11,1... | collective-permute-start | bytes 1572872 | tf_op jit(solution)/shard_map/ppermute | solution.py:190
  72.7 0.8 copy-start.6
  73.5 0.8 copy-start.7

commit v21 on v20

--- a/solution.py
+++ b/solution.py
@@ -27,8 +27,10 @@
 def column_halo(value, axis):
     size = lax.axis_size(axis)
     edges = jnp.stack([value[..., 0], value[..., -1]]).transpose(0, 2, 1)
-    spread = jnp.broadcast_to(edges[None], (size,) + edges.shape)
-    return lax.all_to_all(spread, axis, 0, 0, tiled=False)
+    flat = edges.reshape(2, -1)
+    spread = jnp.broadcast_to(flat[None], (size,) + flat.shape)
+    got = lax.all_to_all(spread, axis, 0, 0, tiled=False)
+    return got.reshape((size,) + edges.shape)
 
 
 def forecast_call(state, received, here):

time: 102 us -> 102 us (level)
    unnamed x27 -> x24, local copies, waits for them, and re-layouts: 6.16 us -> 5.31 us
where the time goes in v21:
time: 102 us; the launch traced here: 101 us
  Pallas kernels  37.9 us (37%)
  blocking collectives  17.8 us (17%)
  local copies, waits for them, and re-layouts  15.6 us (15%)
  waiting for transfers between devices  14.9 us (15%)
  starting transfers between devices  13.9 us (14%)
  other arithmetic  1.23 us (1%)
    all_to_all x1, blocking collectives, body(): lax.all_to_all(result.reshape(members, band_rows, patch_meridian_lines),...  17.8 us
    pallas_call x3, Pallas kernels, observe_dev_call(): pl.pallas_call(kernel, grid=(count // OBS_STEP,), in_specs=in_specs, out_...  17 us
    pallas_call x2, Pallas kernels, update_call(): pl.pallas_call(kernel, grid_spec=grid_spec, out_shape=jax.ShapeDtypeStruc...  15.3 us
    all_to_all x1, waiting for transfers between devices, body(): lax.all_to_all(prediction_increment, 'wide', split_axis=0, concat_axis=1,...  13.3 us
    all_to_all x1, starting transfers between devices, column_halo(): got = lax.all_to_all(spread, axis, 0, 0, tiled=False)  6.32 us
    pallas_call x1, Pallas kernels, forecast_call(): pl.pallas_call(kernel, grid_spec=grid_spec, out_shape=jax.ShapeDtypeStruc...  5.6 us
    unnamed x24, local copies, waits for them, and re-layouts  5.31 us
    all_to_all x1, starting transfers between devices, body(): lax.all_to_all(prediction_increment, 'wide', split_axis=0, concat_axis=1,...  3.72 us
  transfers between devices with their start and end apart: 4, of which 2 were waited for; matrix products, arithmetic and copies ran while one was open for 7% of the time, Pallas kernels for 20%

profile of v21, /device:TPU:0, one launch (start us, length us, event | category | flops | bytes accessed | tf_op | source)
XLA Modules:
  0.0 101.5 jit_solution(7663244967839027107)
XLA Ops:
  0.0 0.0 copy-start
  0.0 0.0 copy-start.4
  0.0 0.0 copy-start.5
  0.0 0.0 copy-start.3
  0.0 0.0 copy-start.2
  0.0 1.5 %fusion.5 = (bf16[32,64,1]{2,1,0:T(8,128)(2,1)S(1)}, bf16[32,64,1]{2,1,0:T(8,128)(2,1)S(1)}) fusion(bf16[32,64,256]{2,1,0:T(8,128)(2,1)} %x_ref.1), kind=kLoop, calls=%fused_computation.18 | loop fusion | bytes 16384 | tf_op jit(solution)/shard_map/slice | solution.py:29
  1.6 0.3 copy.21
  1.9 0.3 copy.22
  2.1 0.1 copy.18
  2.2 0.1 broadcast_in_dim.32
  2.4 0.6 broadcast_in_dim.33
  3.0 6.3 %all-to-all-start = ((bf16[4,2,2048]{2,1,0:T(2,128)(2,1)}), bf16[4,2,2048]{2,1,0:T(2,128)(2,1)S(1)}, u32[]{:S(2)}, u32[]{:S(2)}) async-start(bf16[4,2,2048]{2,1,0:T(2,128)(2,1)} %broadcast_in_dim.33), calls=%async_computation | async-start | bytes 65536 | tf_op jit(solution)/shard_map/all_to_all | solution.py:32
  9.3 0.0 copy-done.4
  9.3 0.0 copy-done.5
  9.3 0.1 fusion.3
  9.4 0.0 copy-done.3
  9.4 0.1 select_reduce_fusion
  9.6 0.1 fusion.8
  9.6 0.0 copy-done
  9.6 0.8 subtract_bitcast_fusion
  10.4 0.1 pad_add_fusion
  10.5 0.1 slice.60
  10.6 0.7 reshape.79.code_ref
  11.2 0.6 reshape.73.code_ref
  11.8 0.6 slice.61.i_ref
  12.4 0.6 slice.62.w_ref
  13.0 0.0 copy-done.2
  13.1 0.3 copy.26
  13.4 0.0 copy-start.1
  13.4 1.6 %all-to-all-done = bf16[4,2,2048]{2,1,0:T(2,128)(2,1)S(1)} async-done(((bf16[4,2,2048]{2,1,0:T(2,128)(2,1)}), bf16[4,2,2048]{2,1,0:T(2,128)(2,1)S(1)}, u32[]{:S(2)}, u32[]{:S(2)}) %all-to-all-start) | async-done | bytes 32800 | tf_op jit(solution)/shard_map/all_to_all | solution.py:32
  15.0 0.8 reshape.75.h_ref
  15.8 5.6 %shard_map.73 = bf16[64,32,256]{2,1,0:T(8,128)(2,1)} custom-call(s32[1]{0:T(128)} %bitcast.3.pos_ref, bf16[32,64,256]{2,1,0:T(8,128)(2,1)} %x_ref.1, bf16[4,2,64,32]{3,2,1,0:T(8,128)(2,1)} %reshape.75.h_ref), custom_call_target="tpu_custom_call" | custom-call | tf_op jit(solution)/shard_map/pallas_call | solution.py:72
  21.4 3.7 %all-to-all-start.1 = ((bf16[64,32,256]{2,1,0:T(8,128)(2,1)}), bf16[64,32,256]{2,1,0:T(8,128)(2,1)S(1)}, u32[]{:S(2)}, u32[]{:S(2)}) async-start(bf16[64,32,256]{2,1,0:T(8,128)(2,1)} %shard_map.73), calls=%async_computation.1 | async-start | bytes 2097152 | tf_op jit(solution)/shard_map/all_to_all | solution.py:170
  25.1 0.6 fusion.7
  25.7 0.6 fusion.6
  26.3 0.0 copy-done.1
  26.3 0.8 fusion.4
  27.2 13.3 %all-to-all-done.1 = bf16[64,32,256]{2,1,0:T(8,128)(2,1)S(1)} async-done(((bf16[64,32,256]{2,1,0:T(8,128)(2,1)}), bf16[64,32,256]{2,1,0:T(8,128)(2,1)S(1)}, u32[]{:S(2)}, u32[]{:S(2)}) %all-to-all-start.1) | async-done | bytes 1048608 | tf_op jit(solution)/shard_map/all_to_all | solution.py:170
  40.5 0.6 copy.19
  41.1 1.3 %copy.23 = bf16[32,8,8,256]{3,1,2,0:T(8,128)(2,1)} copy(bf16[32,8,8,256]{3,2,1,0:T(8,128)(2,1)S(1)} %bitcast.41) | data formatting | bytes 2097152
  42.4 4.8 %shard_map.74.rest_2_ = bf16[2,256,512]{2,1,0:T(8,128)(2,1)} custom-call(bf16[256,2048]{1,0:T(8,128)(2,1)} %bitcast.35, s32[4,512]{1,0:T(4,128)} %get-tuple-element.12.i_ref, f32[4,512]{1,0:T(4,128)} %get-tuple-element.10.w_ref, bf16[256,512]{1,0:T(8,128)(2,1)} %get-tuple-element.6.rest_0_), custom_call_target="tpu_custom_call" | custom-call | tf_op jit(solution)/shard_map/pallas_call | solution.py:140
  47.2 0.7 collective-permute-start
  47.9 4.8 %shard_map.75.rest_0_ = bf16[2,256,512]{2,1,0:T(8,128)(2,1)} custom-call(bf16[256,2048]{1,0:T(8,128)(2,1)} %bitcast.36, s32[4,512]{1,0:T(4,128)} %get-tuple-element.11.i_ref, f32[4,512]{1,0:T(4,128)} %get-tuple-element.9.w_ref, bf16[256,512]{1,0:T(8,128)(2,1)} %get-tuple-element.5.rest_0_), custom_call_target="tpu_custom_call" | custom-call | tf_op jit(solution)/shard_map/pallas_call | solution.py:140
  52.7 3.1 %collective-permute-start.1 = (bf16[2,256,512]{2,1,0:T(8,128)(2,1)}, bf16[2,256,512]{2,1,0:T(8,128)(2,1)S(1)}, u32[]{:S(2)}, u32[]{:S(2)}) collective-permute-start(bf16[2,256,512]{2,1,0:T(8,128)(2,1)} %shard_map.75.rest_0_), channel_id=1, source_target_pairs={{1,0},{2,1},{3,2},{0,3},{5,4},{6,5},{7,6},{4,7},{9,8},{10,9},{11,1... | collective-permute-start | bytes 1572872 | tf_op jit(solution)/shard_map/ppermute | solution.py:192
  55.8 0.1 fusion.2
  55.9 0.8 concatenate.7.taper_ref
  56.7 7.4 %shard_map.76.rest_1_ = bf16[256,1024]{1,0:T(8,128)(2,1)} custom-call(bf16[256,2048]{1,0:T(8,128)(2,1)} %bitcast.37, s32[4,1024]{1,0:T(4,128)} %slice.61.i_ref, f32[4,1024]{1,0:T(4,128)} %slice.62.w_ref), custom_call_target="tpu_custom_call" | custom-call | tf_op jit(solution)/shard_map/pallas_call | solution.py:140
  64.1 8.6 %shard_map.77.rest_4_ = f32[256,2048]{1,0:T(8,128)} custom-call(s32[256]{0:T(256)} %reshape.79.code_ref, bf16[256,2048]{1,0:T(8,128)(2,1)} %bitcast.38, f32[5,128,128]{2,1,0:T(8,128)} %concatenate.7.taper_ref, bf16[2,256,512]{2,1,0:T(8,128)(2,1)} %shard_map.75.rest_0_, bf16[256,1024]{1,0:T(8,128)(2,1)} %shard_map.76.rest_1_, ...), custom_call_target="tpu_custom_call" | custom-call | flops 4294967296 | bytes 4194304 | tf_op jit(solution)/shard_map/pallas_call | solution.py:336
  72.7 0.0 collective-permute-done.rest_0_.rest_2_
  72.7 0.0 copy-start.6
  72.7 0.0 collective-permute-done.1.rest_1_.rest_3_
  72.7 0.8 copy-done.6
  73.5 0.0 copy-start.7
  73.5 0.8 copy-done.7
  74.3 6.8 %shard_map.78 = bf16[256,2048]{1,0:T(8,128)(2,1)} custom-call(s32[128]{0:T(128)} %reshape.73.code_ref, bf16[256,2048]{1,0:T(8,128)(2,1)} %bitcast.39, f32[5,128,128]{2,1,0:T(8,128)} %concatenate.7.taper_ref, bf16[2,256,512]{2,1,0:T(8,128)(2,1)} %copy-done.6, bf16[2,256,512]{2,1,0:T(8,128)(2,1)} %copy-done.7, bf16[2,256,512]{2,1,0:T(8,128)(2,1)} %copy-done.6, ...), custom_call_target="tpu_custom_call" | custom-call | flops 2147483648 | bytes 4194304 | tf_op jit(solution)/shard_map/pallas_call | solution.py:336
  81.0 1.5 %copy.27 = bf16[32,8,8,256]{3,2,1,0:T(8,128)(2,1)S(1)} copy(bf16[32,8,8,256]{3,1,2,0:T(8,128)(2,1)} %bitcast.47) | data formatting | bytes 2097152
  82.6 17.8 %all_to_all.41 = bf16[256,8,256]{2,1,0:T(8,128)(2,1)S(1)} all-to-all(bf16[256,8,256]{2,1,0:T(8,128)(2,1)S(1)} %bitcast.42), channel_id=1, replica_groups=mesh['wide'=8,'lon'=4] {'wide'}, dimensions={0} | all-to-all | bytes 2097152 | tf_op jit(solution)/shard_map/all_to_all | solution.py:224
  100.4 1.1 %copy.29 = bf16[8,32,8,256]{3,2,0,1:T(8,128)(2,1)} copy(bf16[8,32,8,256]{3,2,1,0:T(8,128)(2,1)S(1)} %bitcast.43) | data formatting | bytes 2097152 | tf_op jit(solution)/shard_map/all_to_all | solution.py:224
  (7 shorter events, 0.1 us)
Async XLA Ops:
  0.0 9.6 %copy-start = (f32[4,64,256]{2,1,0:T(8,128)S(1)}, f32[4,64,256]{2,1,0:T(8,128)}, u32[]{:S(2)}) copy-start(f32[4,64,256]{2,1,0:T(8,128)} %param.10) | copy-start | bytes 786436
  0.0 9.3 %copy-start.4 = (s32[1,16,16]{2,1,0:T(8,128)S(1)}, s32[1,16,16]{2,1,0:T(8,128)}, u32[]{:S(2)}) copy-start(s32[1,16,16]{2,1,0:T(8,128)} %param.13) | copy-start | bytes 3076
  0.0 9.3 %copy-start.5 = (s32[1,16]{1,0:T(1,128)S(1)}, s32[1,16]{1,0:T(1,128)}, u32[]{:S(2)}) copy-start(s32[1,16]{1,0:T(1,128)} %param.12) | copy-start | bytes 196
  0.0 9.4 %copy-start.3 = (s32[1,16,16]{2,1,0:T(8,128)S(1)}, s32[1,16,16]{2,1,0:T(8,128)}, u32[]{:S(2)}) copy-start(s32[1,16,16]{2,1,0:T(8,128)} %param.11) | copy-start | bytes 3076
  0.0 13.0 %copy-start.2 = (bf16[256,8,256]{2,1,0:T(8,128)(2,1)S(1)}, bf16[256,8,256]{2,1,0:T(8,128)(2,1)}, u32[]{:S(2)}) copy-start(bf16[256,8,256]{2,1,0:T(8,128)(2,1)} %param.8) | copy-start | bytes 3145732
  3.0 12.0 %all-to-all-start = ((bf16[4,2,2048]{2,1,0:T(2,128)(2,1)}), bf16[4,2,2048]{2,1,0:T(2,128)(2,1)S(1)}, u32[]{:S(2)}, u32[]{:S(2)}) async-start(bf16[4,2,2048]{2,1,0:T(2,128)(2,1)} %broadcast_in_dim.33), calls=%async_computation | async-start | bytes 65536 | tf_op jit(solution)/shard_map/all_to_all | solution.py:32
  13.4 13.0 %copy-start.1 = (bf16[32,8,8,256]{3,1,2,0:T(8,128)(2,1)}, bf16[32,8,8,256]{3,1,2,0:T(8,128)(2,1)S(1)}, u32[]{:S(2)}) copy-start(bf16[32,8,8,256]{3,1,2,0:T(8,128)(2,1)S(1)} %copy.26) | copy-start | bytes 3145732
  21.4 19.1 %all-to-all-start.1 = ((bf16[64,32,256]{2,1,0:T(8,128)(2,1)}), bf16[64,32,256]{2,1,0:T(8,128)(2,1)S(1)}, u32[]{:S(2)}, u32[]{:S(2)}) async-start(bf16[64,32,256]{2,1,0:T(8,128)(2,1)} %shard_map.73), calls=%async_computation.1 | async-start | bytes 2097152 | tf_op jit(solution)/shard_map/all_to_all | solution.py:170
  47.2 25.5 %collective-permute-start = (bf16[2,256,512]{2,1,0:T(8,128)(2,1)}, bf16[2,256,512]{2,1,0:T(8,128)(2,1)S(1)}, u32[]{:S(2)}, u32[]{:S(2)}) collective-permute-start(bf16[2,256,512]{2,1,0:T(8,128)(2,1)} %shard_map.74.rest_2_), channel_id=1, source_target_pairs={{0,1},{1,2},{2,3},{3,0},{4,5},{5,6},{6,7},{7,4},{8,9},{9,10},{10,1... | collective-permute-start | bytes 1572872 | tf_op jit(solution)/shard_map/ppermute | solution.py:188
  52.7 20.0 %collective-permute-start.1 = (bf16[2,256,512]{2,1,0:T(8,128)(2,1)}, bf16[2,256,512]{2,1,0:T(8,128)(2,1)S(1)}, u32[]{:S(2)}, u32[]{:S(2)}) collective-permute-start(bf16[2,256,512]{2,1,0:T(8,128)(2,1)} %shard_map.75.rest_0_), channel_id=1, source_target_pairs={{1,0},{2,1},{3,2},{0,3},{5,4},{6,5},{7,6},{4,7},{9,8},{10,9},{11,1... | collective-permute-start | bytes 1572872 | tf_op jit(solution)/shard_map/ppermute | solution.py:192
  72.7 0.8 copy-start.6
  73.5 0.8 copy-start.7

commit v22 on v20

--- a/solution.py
+++ b/solution.py
@@ -94,7 +94,7 @@
     return result.transpose(1, 0, 2).reshape(members, count)
 
 
-OBS_STEP = 256
+OBS_STEP = 512
 def observe_dev_call(state, index, weight, extra=None):
     members, cells = state.shape
     count = index.shape[1]
@@ -217,7 +217,7 @@
         tiles,
         block_count,
         2 * halo_blocks,
-        group=8,
+        group=16,
     )
     return lax.all_to_all(
         result.reshape(members, band_rows, patch_meridian_lines),

time: 102 us -> 102 us (level)
  no operation moved by 1% of the time
where the time goes in v22:
time: 102 us; the launch traced here: 101 us
  Pallas kernels  37.4 us (37%)
  blocking collectives  18.2 us (18%)
  local copies, waits for them, and re-layouts  15.6 us (15%)
  waiting for transfers between devices  14.9 us (15%)
  starting transfers between devices  13.9 us (14%)
  other arithmetic  1.23 us (1%)
    all_to_all x1, blocking collectives, body(): lax.all_to_all(result.reshape(members, band_rows, patch_meridian_lines),...  18.2 us
    pallas_call x3, Pallas kernels, observe_dev_call(): pl.pallas_call(kernel, grid=(count // OBS_STEP,), in_specs=in_specs, out_...  16.5 us
    pallas_call x2, Pallas kernels, update_call(): pl.pallas_call(kernel, grid_spec=grid_spec, out_shape=jax.ShapeDtypeStruc...  15.4 us
    all_to_all x1, waiting for transfers between devices, body(): lax.all_to_all(prediction_increment, 'wide', split_axis=0, concat_axis=1,...  13.3 us
    all_to_all x1, starting transfers between devices, column_halo(): return lax.all_to_all(spread, axis, 0, 0, tiled=False)  6.32 us
    unnamed x27, local copies, waits for them, and re-layouts  6.16 us
    pallas_call x1, Pallas kernels, forecast_call(): pl.pallas_call(kernel, grid_spec=grid_spec, out_shape=jax.ShapeDtypeStruc...  5.6 us
    all_to_all x1, starting transfers between devices, body(): lax.all_to_all(prediction_increment, 'wide', split_axis=0, concat_axis=1,...  3.72 us
  transfers between devices with their start and end apart: 4, of which 2 were waited for; matrix products, arithmetic and copies ran while one was open for 7% of the time, Pallas kernels for 20%

profile of v22, /device:TPU:0, one launch (start us, length us, event | category | flops | bytes accessed | tf_op | source)
XLA Modules:
  0.0 101.4 jit_solution(15870945656079772788)
XLA Ops:
  0.0 0.0 copy-start
  0.0 0.0 copy-start.4
  0.0 0.0 copy-start.5
  0.0 0.0 copy-start.3
  0.0 0.0 copy-start.2
  0.0 1.5 %fusion.5 = (bf16[32,64,1]{2,1,0:T(8,128)(2,1)S(1)}, bf16[32,64,1]{2,1,0:T(8,128)(2,1)S(1)}) fusion(bf16[32,64,256]{2,1,0:T(8,128)(2,1)} %x_ref.1), kind=kLoop, calls=%fused_computation.18 | loop fusion | bytes 16384 | tf_op jit(solution)/shard_map/slice | solution.py:29
  1.6 0.3 copy.27
  1.9 0.3 copy.28
  2.2 0.7 reshape.77
  2.9 6.3 %all-to-all-start = ((bf16[4,2,2048]{2,1,0:T(2,128)(2,1)}), bf16[4,2,2048]{2,1,0:T(2,128)(2,1)S(1)}, u32[]{:S(2)}, u32[]{:S(2)}) async-start(bf16[4,2,2048]{2,1,0:T(2,128)(2,1)} %reshape.77), calls=%async_computation | async-start | bytes 65536 | tf_op jit(solution)/shard_map/all_to_all | solution.py:31
  9.2 0.0 copy-done.4
  9.2 0.0 copy-done.5
  9.2 0.1 fusion.3
  9.3 0.0 copy-done.3
  9.3 0.1 select_reduce_fusion
  9.5 0.1 fusion.8
  9.5 0.0 copy-done
  9.5 0.8 subtract_bitcast_fusion
  10.3 0.1 pad_add_fusion
  10.4 0.1 slice.60
  10.5 0.7 reshape.75.code_ref
  11.1 0.6 reshape.70.code_ref
  11.7 0.6 slice.61.i_ref
  12.3 0.6 slice.62.w_ref
  12.9 0.0 copy-done.2
  12.9 0.3 copy.32
  13.3 0.0 copy-start.1
  13.3 1.6 %all-to-all-done = bf16[4,2,2048]{2,1,0:T(2,128)(2,1)S(1)} async-done(((bf16[4,2,2048]{2,1,0:T(2,128)(2,1)}), bf16[4,2,2048]{2,1,0:T(2,128)(2,1)S(1)}, u32[]{:S(2)}, u32[]{:S(2)}) %all-to-all-start) | async-done | bytes 32800 | tf_op jit(solution)/shard_map/all_to_all | solution.py:31
  14.9 0.1 reshape.78
  15.0 0.8 copy.24.h_ref
  15.8 5.6 %shard_map.73 = bf16[64,32,256]{2,1,0:T(8,128)(2,1)} custom-call(s32[1]{0:T(128)} %bitcast.3.pos_ref, bf16[32,64,256]{2,1,0:T(8,128)(2,1)} %x_ref.1, bf16[4,2,64,32]{3,2,1,0:T(8,128)(2,1)} %copy.24.h_ref), custom_call_target="tpu_custom_call" | custom-call | tf_op jit(solution)/shard_map/pallas_call | solution.py:70
  21.4 3.7 %all-to-all-start.1 = ((bf16[64,32,256]{2,1,0:T(8,128)(2,1)}), bf16[64,32,256]{2,1,0:T(8,128)(2,1)S(1)}, u32[]{:S(2)}, u32[]{:S(2)}) async-start(bf16[64,32,256]{2,1,0:T(8,128)(2,1)} %shard_map.73), calls=%async_computation.1 | async-start | bytes 2097152 | tf_op jit(solution)/shard_map/all_to_all | solution.py:168
  25.1 0.6 fusion.7
  25.7 0.6 fusion.6
  26.3 0.0 copy-done.1
  26.3 0.8 fusion.4
  27.2 13.3 %all-to-all-done.1 = bf16[64,32,256]{2,1,0:T(8,128)(2,1)S(1)} async-done(((bf16[64,32,256]{2,1,0:T(8,128)(2,1)}), bf16[64,32,256]{2,1,0:T(8,128)(2,1)S(1)}, u32[]{:S(2)}, u32[]{:S(2)}) %all-to-all-start.1) | async-done | bytes 1048608 | tf_op jit(solution)/shard_map/all_to_all | solution.py:168
  40.5 0.6 copy.25
  41.1 1.3 %copy.29 = bf16[32,8,8,256]{3,1,2,0:T(8,128)(2,1)} copy(bf16[32,8,8,256]{3,2,1,0:T(8,128)(2,1)S(1)} %bitcast.44) | data formatting | bytes 2097152
  42.4 4.7 %shard_map.74.rest_2_ = bf16[2,256,512]{2,1,0:T(8,128)(2,1)} custom-call(bf16[256,2048]{1,0:T(8,128)(2,1)} %bitcast.38, s32[4,512]{1,0:T(4,128)} %get-tuple-element.12.i_ref, f32[4,512]{1,0:T(4,128)} %get-tuple-element.10.w_ref, bf16[256,512]{1,0:T(8,128)(2,1)} %get-tuple-element.6.rest_0_), custom_call_target="tpu_custom_call" | custom-call | tf_op jit(solution)/shard_map/pallas_call | solution.py:138
  47.1 0.7 collective-permute-start
  47.8 4.7 %shard_map.75.rest_0_ = bf16[2,256,512]{2,1,0:T(8,128)(2,1)} custom-call(bf16[256,2048]{1,0:T(8,128)(2,1)} %bitcast.39, s32[4,512]{1,0:T(4,128)} %get-tuple-element.11.i_ref, f32[4,512]{1,0:T(4,128)} %get-tuple-element.9.w_ref, bf16[256,512]{1,0:T(8,128)(2,1)} %get-tuple-element.5.rest_0_), custom_call_target="tpu_custom_call" | custom-call | tf_op jit(solution)/shard_map/pallas_call | solution.py:138
  52.5 3.1 %collective-permute-start.1 = (bf16[2,256,512]{2,1,0:T(8,128)(2,1)}, bf16[2,256,512]{2,1,0:T(8,128)(2,1)S(1)}, u32[]{:S(2)}, u32[]{:S(2)}) collective-permute-start(bf16[2,256,512]{2,1,0:T(8,128)(2,1)} %shard_map.75.rest_0_), channel_id=1, source_target_pairs={{1,0},{2,1},{3,2},{0,3},{5,4},{6,5},{7,6},{4,7},{9,8},{10,9},{11,1... | collective-permute-start | bytes 1572872 | tf_op jit(solution)/shard_map/ppermute | solution.py:190
  55.5 0.1 fusion.2
  55.7 0.8 concatenate.7.taper_ref
  56.4 7.2 %shard_map.76.rest_1_ = bf16[256,1024]{1,0:T(8,128)(2,1)} custom-call(bf16[256,2048]{1,0:T(8,128)(2,1)} %bitcast.40, s32[4,1024]{1,0:T(4,128)} %slice.61.i_ref, f32[4,1024]{1,0:T(4,128)} %slice.62.w_ref), custom_call_target="tpu_custom_call" | custom-call | tf_op jit(solution)/shard_map/pallas_call | solution.py:138
  63.6 8.6 %shard_map.77.rest_4_ = f32[256,2048]{1,0:T(8,128)} custom-call(s32[256]{0:T(256)} %reshape.75.code_ref, bf16[256,2048]{1,0:T(8,128)(2,1)} %bitcast.41, f32[5,128,128]{2,1,0:T(8,128)} %concatenate.7.taper_ref, bf16[2,256,512]{2,1,0:T(8,128)(2,1)} %shard_map.75.rest_0_, bf16[256,1024]{1,0:T(8,128)(2,1)} %shard_map.76.rest_1_, ...), custom_call_target="tpu_custom_call" | custom-call | flops 4294967296 | bytes 4194304 | tf_op jit(solution)/shard_map/pallas_call | solution.py:334
  72.2 0.0 collective-permute-done.rest_0_.rest_2_
  72.2 0.0 copy-start.6
  72.2 0.0 collective-permute-done.1.rest_1_.rest_3_
  72.2 0.8 copy-done.6
  73.0 0.0 copy-start.7
  73.0 0.8 copy-done.7
  73.8 6.8 %shard_map.78 = bf16[256,2048]{1,0:T(8,128)(2,1)} custom-call(s32[128]{0:T(128)} %reshape.70.code_ref, bf16[256,2048]{1,0:T(8,128)(2,1)} %bitcast.42, f32[5,128,128]{2,1,0:T(8,128)} %concatenate.7.taper_ref, bf16[2,256,512]{2,1,0:T(8,128)(2,1)} %copy-done.6, bf16[2,256,512]{2,1,0:T(8,128)(2,1)} %copy-done.7, bf16[2,256,512]{2,1,0:T(8,128)(2,1)} %copy-done.6, ...), custom_call_target="tpu_custom_call" | custom-call | flops 2147483648 | bytes 4194304 | tf_op jit(solution)/shard_map/pallas_call | solution.py:334
  80.6 1.5 %copy.33 = bf16[32,8,8,256]{3,2,1,0:T(8,128)(2,1)S(1)} copy(bf16[32,8,8,256]{3,1,2,0:T(8,128)(2,1)} %bitcast.50) | data formatting | bytes 2097152
  82.1 18.2 %all_to_all.41 = bf16[256,8,256]{2,1,0:T(8,128)(2,1)S(1)} all-to-all(bf16[256,8,256]{2,1,0:T(8,128)(2,1)S(1)} %bitcast.45), channel_id=1, replica_groups=mesh['wide'=8,'lon'=4] {'wide'}, dimensions={0} | all-to-all | bytes 2097152 | tf_op jit(solution)/shard_map/all_to_all | solution.py:222
  100.3 1.1 %copy.35 = bf16[8,32,8,256]{3,2,0,1:T(8,128)(2,1)} copy(bf16[8,32,8,256]{3,2,1,0:T(8,128)(2,1)S(1)} %bitcast.46) | data formatting | bytes 2097152 | tf_op jit(solution)/shard_map/all_to_all | solution.py:222
  (8 shorter events, 0.1 us)
Async XLA Ops:
  0.0 9.5 %copy-start = (f32[4,64,256]{2,1,0:T(8,128)S(1)}, f32[4,64,256]{2,1,0:T(8,128)}, u32[]{:S(2)}) copy-start(f32[4,64,256]{2,1,0:T(8,128)} %param.10) | copy-start | bytes 786436
  0.0 9.2 %copy-start.4 = (s32[1,16,16]{2,1,0:T(8,128)S(1)}, s32[1,16,16]{2,1,0:T(8,128)}, u32[]{:S(2)}) copy-start(s32[1,16,16]{2,1,0:T(8,128)} %param.13) | copy-start | bytes 3076
  0.0 9.2 %copy-start.5 = (s32[1,16]{1,0:T(1,128)S(1)}, s32[1,16]{1,0:T(1,128)}, u32[]{:S(2)}) copy-start(s32[1,16]{1,0:T(1,128)} %param.12) | copy-start | bytes 196
  0.0 9.3 %copy-start.3 = (s32[1,16,16]{2,1,0:T(8,128)S(1)}, s32[1,16,16]{2,1,0:T(8,128)}, u32[]{:S(2)}) copy-start(s32[1,16,16]{2,1,0:T(8,128)} %param.11) | copy-start | bytes 3076
  0.0 12.9 %copy-start.2 = (bf16[256,8,256]{2,1,0:T(8,128)(2,1)S(1)}, bf16[256,8,256]{2,1,0:T(8,128)(2,1)}, u32[]{:S(2)}) copy-start(bf16[256,8,256]{2,1,0:T(8,128)(2,1)} %param.8) | copy-start | bytes 3145732
  2.9 12.0 %all-to-all-start = ((bf16[4,2,2048]{2,1,0:T(2,128)(2,1)}), bf16[4,2,2048]{2,1,0:T(2,128)(2,1)S(1)}, u32[]{:S(2)}, u32[]{:S(2)}) async-start(bf16[4,2,2048]{2,1,0:T(2,128)(2,1)} %reshape.77), calls=%async_computation | async-start | bytes 65536 | tf_op jit(solution)/shard_map/all_to_all | solution.py:31
  13.3 13.1 %copy-start.1 = (bf16[32,8,8,256]{3,1,2,0:T(8,128)(2,1)}, bf16[32,8,8,256]{3,1,2,0:T(8,128)(2,1)S(1)}, u32[]{:S(2)}) copy-start(bf16[32,8,8,256]{3,1,2,0:T(8,128)(2,1)S(1)} %copy.32) | copy-start | bytes 3145732
  21.4 19.1 %all-to-all-start.1 = ((bf16[64,32,256]{2,1,0:T(8,128)(2,1)}), bf16[64,32,256]{2,1,0:T(8,128)(2,1)S(1)}, u32[]{:S(2)}, u32[]{:S(2)}) async-start(bf16[64,32,256]{2,1,0:T(8,128)(2,1)} %shard_map.73), calls=%async_computation.1 | async-start | bytes 2097152 | tf_op jit(solution)/shard_map/all_to_all | solution.py:168
  47.1 25.1 %collective-permute-start = (bf16[2,256,512]{2,1,0:T(8,128)(2,1)}, bf16[2,256,512]{2,1,0:T(8,128)(2,1)S(1)}, u32[]{:S(2)}, u32[]{:S(2)}) collective-permute-start(bf16[2,256,512]{2,1,0:T(8,128)(2,1)} %shard_map.74.rest_2_), channel_id=1, source_target_pairs={{0,1},{1,2},{2,3},{3,0},{4,5},{5,6},{6,7},{7,4},{8,9},{9,10},{10,1... | collective-permute-start | bytes 1572872 | tf_op jit(solution)/shard_map/ppermute | solution.py:186
  52.5 19.7 %collective-permute-start.1 = (bf16[2,256,512]{2,1,0:T(8,128)(2,1)}, bf16[2,256,512]{2,1,0:T(8,128)(2,1)S(1)}, u32[]{:S(2)}, u32[]{:S(2)}) collective-permute-start(bf16[2,256,512]{2,1,0:T(8,128)(2,1)} %shard_map.75.rest_0_), channel_id=1, source_target_pairs={{1,0},{2,1},{3,2},{0,3},{5,4},{6,5},{7,6},{4,7},{9,8},{10,9},{11,1... | collective-permute-start | bytes 1572872 | tf_op jit(solution)/shard_map/ppermute | solution.py:190
  72.2 0.8 copy-start.6
  73.0 0.8 copy-start.7

commit v23 on v20

--- a/solution.py
+++ b/solution.py
@@ -96,7 +96,8 @@
 
 OBS_STEP = 256
 def observe_dev_call(state, index, weight, extra=None):
-    members, cells = state.shape
+    band, members, cols = state.shape
+    cells = band * cols
     count = index.shape[1]
     carry = extra is not None
 
@@ -106,11 +107,14 @@
         else:
             (o_ref,) = rest
         cell_ids = lax.broadcasted_iota(jnp.int32, (cells, OBS_STEP), 0)
-        f = f_ref[...]
         summed = jnp.zeros((members, OBS_STEP), jnp.float32)
         for k in range(4):
             selector = (cell_ids == i_ref[k:k + 1, :]).astype(jnp.bfloat16)
-            picked = jnp.dot(f, selector, preferred_element_type=jnp.float32)
+            picked = jnp.dot(f_ref[0], selector[:cols], preferred_element_type=jnp.float32)
+            for r in range(1, band):
+                picked = picked + jnp.dot(
+                    f_ref[r], selector[r * cols:(r + 1) * cols], preferred_element_type=jnp.float32
+                )
             summed = summed + w_ref[k:k + 1, :] * picked
         ens = summed.astype(jnp.bfloat16).astype(jnp.float32)
         mean = jnp.sum(ens, axis=0, keepdims=True) / members
@@ -122,7 +126,7 @@
             o_ref[...] = dev
 
     in_specs = [
-        pl.BlockSpec((members, cells), lambda j: (0, 0)),
+        pl.BlockSpec(state.shape, lambda j: (0, 0, 0)),
         pl.BlockSpec((4, OBS_STEP), lambda j: (0, j)),
         pl.BlockSpec((4, OBS_STEP), lambda j: (0, j)),
     ]
@@ -166,7 +170,7 @@
     band_rows = innov.shape[1]
     patch_gridpoints = band_rows * patch_meridian_lines
     region = lax.all_to_all(prediction_increment, "wide", split_axis=0, concat_axis=1, tiled=True)
-    region_state = region.transpose(1, 0, 2).reshape(members, patch_gridpoints)
+    region_state = region
     first_row = lax.axis_index("wide") * band_rows
     local_index = lax.dynamic_slice_in_dim(obs_index, first_row, band_rows, 1).reshape(
         4, patch_gridpoints
@@ -261,8 +265,10 @@
 
 
 def update_call(code, forecast, partial, obs_pieces, innov_pieces, tiles, block_count, candidate_count, group=GROUP):
-    members, cells = forecast.shape
+    band, members, cols = forecast.shape
+    cells = band * cols
     rows = group * BLK
+    band_step = rows // cols
     width = candidate_count * BLK
     final = partial is not None
     obs_arrays = [a for a, _ in obs_pieces]
@@ -279,7 +285,7 @@
         else:
             out_ref, cov_scr, tap_scr = rest
         g = pl.program_id(0)
-        forecast_block = f_ref[...].astype(jnp.float32)
+        forecast_block = jnp.concatenate([f_ref[r] for r in range(band_step)], axis=1).astype(jnp.float32)
         mean = jnp.sum(forecast_block, axis=0, keepdims=True) / members
         state = (forecast_block - mean).astype(jnp.bfloat16)
         offset = 0
@@ -314,7 +320,8 @@
             out_ref[...] = change
 
     col_spec = pl.BlockSpec((members, rows), lambda g, code: (0, g))
-    in_specs = [col_spec, pl.BlockSpec(tiles.shape, lambda g, code: (0, 0, 0))]
+    band_spec = pl.BlockSpec((band_step, members, cols), lambda g, code: (g, 0, 0))
+    in_specs = [band_spec, pl.BlockSpec(tiles.shape, lambda g, code: (0, 0, 0))]
     in_specs += [piece_spec(a) for a in obs_arrays] + [piece_spec(a) for a in innov_arrays]
     operands = [forecast, tiles] + obs_arrays + innov_arrays
     if final:

time: 102 us -> 101 us (level)
    unnamed x27 -> x26, local copies, waits for them, and re-layouts: 6.16 us -> 4.88 us
  transfers between devices with their start and end apart: 4 -> 4, of which waited for: 2 -> 2; matrix products, arithmetic and copies ran while one was open for 7% -> 7% of each run, Pallas kernels for 20% -> 21%
where the time goes in v23:
time: 101 us
  Pallas kernels  37.8 us (37%)
  blocking collectives  17.9 us (18%)
  waiting for transfers between devices  14.9 us (15%)
  local copies, waits for them, and re-layouts  14.8 us (15%)
  starting transfers between devices  13.9 us (14%)
  other arithmetic  1.23 us (1%)
    all_to_all x1, blocking collectives, body(): lax.all_to_all(result.reshape(members, band_rows, patch_meridian_lines),...  17.9 us
    pallas_call x3, Pallas kernels, observe_dev_call(): pl.pallas_call(kernel, grid=(count // OBS_STEP,), in_specs=in_specs, out_...  16.9 us
    pallas_call x2, Pallas kernels, update_call(): pl.pallas_call(kernel, grid_spec=grid_spec, out_shape=jax.ShapeDtypeStruc...  15.4 us
    all_to_all x1, waiting for transfers between devices, body(): lax.all_to_all(prediction_increment, 'wide', split_axis=0, concat_axis=1,...  13.3 us
    all_to_all x1, starting transfers between devices, column_halo(): return lax.all_to_all(spread, axis, 0, 0, tiled=False)  6.32 us
    pallas_call x1, Pallas kernels, forecast_call(): pl.pallas_call(kernel, grid_spec=grid_spec, out_shape=jax.ShapeDtypeStruc...  5.6 us
    unnamed x26, local copies, waits for them, and re-layouts  4.88 us
    all_to_all x1, starting transfers between devices, body(): lax.all_to_all(prediction_increment, 'wide', split_axis=0, concat_axis=1,...  3.72 us
  transfers between devices with their start and end apart: 4, of which 2 were waited for; matrix products, arithmetic and copies ran while one was open for 7% of the time, Pallas kernels for 21%

profile of v23, /device:TPU:0, one launch (start us, length us, event | category | flops | bytes accessed | tf_op | source)
XLA Modules:
  0.0 100.6 jit_solution(8894946173898982295)
XLA Ops:
  0.0 0.0 copy-start
  0.0 0.0 copy-start.4
  0.0 0.0 copy-start.5
  0.0 0.0 copy-start.3
  0.0 0.0 copy-start.2
  0.0 1.5 %fusion.5 = (bf16[32,64,1]{2,1,0:T(8,128)(2,1)S(1)}, bf16[32,64,1]{2,1,0:T(8,128)(2,1)S(1)}) fusion(bf16[32,64,256]{2,1,0:T(8,128)(2,1)} %x_ref.1), kind=kLoop, calls=%fused_computation.18 | loop fusion | bytes 16384 | tf_op jit(solution)/shard_map/slice | solution.py:29
  1.6 0.3 copy.27
  1.9 0.3 copy.28
  2.2 0.7 reshape.73
  2.9 6.3 %all-to-all-start = ((bf16[4,2,2048]{2,1,0:T(2,128)(2,1)}), bf16[4,2,2048]{2,1,0:T(2,128)(2,1)S(1)}, u32[]{:S(2)}, u32[]{:S(2)}) async-start(bf16[4,2,2048]{2,1,0:T(2,128)(2,1)} %reshape.73), calls=%async_computation | async-start | bytes 65536 | tf_op jit(solution)/shard_map/all_to_all | solution.py:31
  9.2 0.0 copy-done.4
  9.2 0.0 copy-done.5
  9.2 0.1 fusion.3
  9.3 0.0 copy-done.3
  9.3 0.1 select_reduce_fusion
  9.5 0.1 fusion.8
  9.5 0.0 copy-done
  9.5 0.8 subtract_bitcast_fusion
  10.3 0.1 pad_add_fusion
  10.4 0.1 slice.60
  10.5 0.7 reshape.71.code_ref
  11.1 0.6 reshape.67.code_ref
  11.7 0.6 slice.61.i_ref
  12.3 0.6 slice.62.w_ref
  12.9 0.0 copy-done.2
  12.9 0.3 copy.31
  13.3 0.0 copy-start.1
  13.3 1.6 %all-to-all-done = bf16[4,2,2048]{2,1,0:T(2,128)(2,1)S(1)} async-done(((bf16[4,2,2048]{2,1,0:T(2,128)(2,1)}), bf16[4,2,2048]{2,1,0:T(2,128)(2,1)S(1)}, u32[]{:S(2)}, u32[]{:S(2)}) %all-to-all-start) | async-done | bytes 32800 | tf_op jit(solution)/shard_map/all_to_all | solution.py:31
  14.9 0.1 reshape.74
  15.0 0.8 copy.24.h_ref
  15.8 5.6 %shard_map.73 = bf16[64,32,256]{2,1,0:T(8,128)(2,1)} custom-call(s32[1]{0:T(128)} %bitcast.3.pos_ref, bf16[32,64,256]{2,1,0:T(8,128)(2,1)} %x_ref.1, bf16[4,2,64,32]{3,2,1,0:T(8,128)(2,1)} %copy.24.h_ref), custom_call_target="tpu_custom_call" | custom-call | tf_op jit(solution)/shard_map/pallas_call | solution.py:70
  21.4 3.7 %all-to-all-start.1 = ((bf16[64,32,256]{2,1,0:T(8,128)(2,1)}), bf16[64,32,256]{2,1,0:T(8,128)(2,1)S(1)}, u32[]{:S(2)}, u32[]{:S(2)}) async-start(bf16[64,32,256]{2,1,0:T(8,128)(2,1)} %shard_map.73), calls=%async_computation.1 | async-start | bytes 2097152 | tf_op jit(solution)/shard_map/all_to_all | solution.py:172
  25.1 0.6 fusion.7
  25.7 0.6 fusion.6
  26.3 0.0 copy-done.1
  26.3 0.8 fusion.4
  27.2 13.3 %all-to-all-done.1 = bf16[64,32,256]{2,1,0:T(8,128)(2,1)S(1)} async-done(((bf16[64,32,256]{2,1,0:T(8,128)(2,1)}), bf16[64,32,256]{2,1,0:T(8,128)(2,1)S(1)}, u32[]{:S(2)}, u32[]{:S(2)}) %all-to-all-start.1) | async-done | bytes 1048608 | tf_op jit(solution)/shard_map/all_to_all | solution.py:172
  40.5 1.1 %copy.25 = bf16[8,8,32,256]{3,2,0,1:T(8,128)(2,1)} copy(bf16[8,8,32,256]{3,2,1,0:T(8,128)(2,1)S(1)} %bitcast.39) | data formatting | bytes 2097152 | tf_op jit(solution)/shard_map/all_to_all | solution.py:172
  41.6 4.8 %shard_map.74.rest_2_ = bf16[2,256,512]{2,1,0:T(8,128)(2,1)} custom-call(bf16[8,256,256]{2,1,0:T(8,128)(2,1)} %bitcast.34, s32[4,512]{1,0:T(4,128)} %get-tuple-element.12.i_ref, f32[4,512]{1,0:T(4,128)} %get-tuple-element.10.w_ref, bf16[256,512]{1,0:T(8,128)(2,1)} %get-tuple-element.6.rest_0_), custom_call_target="tpu_custom_call" | custom-call | tf_op jit(solution)/shard_map/pallas_call | solution.py:142
  46.3 0.7 collective-permute-start
  47.0 4.8 %shard_map.75.rest_0_ = bf16[2,256,512]{2,1,0:T(8,128)(2,1)} custom-call(bf16[8,256,256]{2,1,0:T(8,128)(2,1)} %bitcast.35, s32[4,512]{1,0:T(4,128)} %get-tuple-element.11.i_ref, f32[4,512]{1,0:T(4,128)} %get-tuple-element.9.w_ref, bf16[256,512]{1,0:T(8,128)(2,1)} %get-tuple-element.5.rest_0_), custom_call_target="tpu_custom_call" | custom-call | tf_op jit(solution)/shard_map/pallas_call | solution.py:142
  51.8 3.1 %collective-permute-start.1 = (bf16[2,256,512]{2,1,0:T(8,128)(2,1)}, bf16[2,256,512]{2,1,0:T(8,128)(2,1)S(1)}, u32[]{:S(2)}, u32[]{:S(2)}) collective-permute-start(bf16[2,256,512]{2,1,0:T(8,128)(2,1)} %shard_map.75.rest_0_), channel_id=1, source_target_pairs={{1,0},{2,1},{3,2},{0,3},{5,4},{6,5},{7,6},{4,7},{9,8},{10,9},{11,1... | collective-permute-start | bytes 1572872 | tf_op jit(solution)/shard_map/ppermute | solution.py:194
  54.9 0.1 fusion.2
  55.0 0.8 concatenate.7.taper_ref
  55.8 7.4 %shard_map.76.rest_1_ = bf16[256,1024]{1,0:T(8,128)(2,1)} custom-call(bf16[8,256,256]{2,1,0:T(8,128)(2,1)} %bitcast.36, s32[4,1024]{1,0:T(4,128)} %slice.61.i_ref, f32[4,1024]{1,0:T(4,128)} %slice.62.w_ref), custom_call_target="tpu_custom_call" | custom-call | tf_op jit(solution)/shard_map/pallas_call | solution.py:142
  63.1 8.6 %shard_map.77.rest_4_ = f32[256,2048]{1,0:T(8,128)} custom-call(s32[256]{0:T(256)} %reshape.71.code_ref, bf16[8,256,256]{2,1,0:T(8,128)(2,1)} %bitcast.37, f32[5,128,128]{2,1,0:T(8,128)} %concatenate.7.taper_ref, bf16[2,256,512]{2,1,0:T(8,128)(2,1)} %shard_map.75.rest_0_, bf16[256,1024]{1,0:T(8,128)(2,1)} %shard_map.76.rest_1_, ...), custom_call_target="tpu_custom_call" | custom-call | flops 4294967296 | bytes 4194304 | tf_op jit(solution)/shard_map/pallas_call | solution.py:341
  71.7 0.0 collective-permute-done.rest_0_.rest_2_
  71.7 0.0 copy-start.6
  71.7 0.0 collective-permute-done.1.rest_1_.rest_3_
  71.7 0.8 copy-done.6
  72.5 0.0 copy-start.7
  72.5 0.8 copy-done.7
  73.3 6.8 %shard_map.78 = bf16[256,2048]{1,0:T(8,128)(2,1)} custom-call(s32[128]{0:T(128)} %reshape.67.code_ref, bf16[8,256,256]{2,1,0:T(8,128)(2,1)} %bitcast.38, f32[5,128,128]{2,1,0:T(8,128)} %concatenate.7.taper_ref, bf16[2,256,512]{2,1,0:T(8,128)(2,1)} %copy-done.6, bf16[2,256,512]{2,1,0:T(8,128)(2,1)} %copy-done.7, bf16[2,256,512]{2,1,0:T(8,128)(2,1)} %copy-done.6, ...), custom_call_target="tpu_custom_call" | custom-call | flops 2147483648 | bytes 4194304 | tf_op jit(solution)/shard_map/pallas_call | solution.py:341
  80.1 1.5 %copy.32 = bf16[32,8,8,256]{3,2,1,0:T(8,128)(2,1)S(1)} copy(bf16[32,8,8,256]{3,1,2,0:T(8,128)(2,1)} %bitcast.45) | data formatting | bytes 2097152
  81.7 17.9 %all_to_all.41 = bf16[256,8,256]{2,1,0:T(8,128)(2,1)S(1)} all-to-all(bf16[256,8,256]{2,1,0:T(8,128)(2,1)S(1)} %bitcast.40), channel_id=1, replica_groups=mesh['wide'=8,'lon'=4] {'wide'}, dimensions={0} | all-to-all | bytes 2097152 | tf_op jit(solution)/shard_map/all_to_all | solution.py:226
  99.5 1.1 %copy.34 = bf16[8,32,8,256]{3,2,0,1:T(8,128)(2,1)} copy(bf16[8,32,8,256]{3,2,1,0:T(8,128)(2,1)S(1)} %bitcast.41) | data formatting | bytes 2097152 | tf_op jit(solution)/shard_map/all_to_all | solution.py:226
  (8 shorter events, 0.1 us)
Async XLA Ops:
  0.0 9.5 %copy-start = (f32[4,64,256]{2,1,0:T(8,128)S(1)}, f32[4,64,256]{2,1,0:T(8,128)}, u32[]{:S(2)}) copy-start(f32[4,64,256]{2,1,0:T(8,128)} %param.10) | copy-start | bytes 786436
  0.0 9.2 %copy-start.4 = (s32[1,16,16]{2,1,0:T(8,128)S(1)}, s32[1,16,16]{2,1,0:T(8,128)}, u32[]{:S(2)}) copy-start(s32[1,16,16]{2,1,0:T(8,128)} %param.13) | copy-start | bytes 3076
  0.0 9.2 %copy-start.5 = (s32[1,16]{1,0:T(1,128)S(1)}, s32[1,16]{1,0:T(1,128)}, u32[]{:S(2)}) copy-start(s32[1,16]{1,0:T(1,128)} %param.12) | copy-start | bytes 196
  0.0 9.3 %copy-start.3 = (s32[1,16,16]{2,1,0:T(8,128)S(1)}, s32[1,16,16]{2,1,0:T(8,128)}, u32[]{:S(2)}) copy-start(s32[1,16,16]{2,1,0:T(8,128)} %param.11) | copy-start | bytes 3076
  0.0 12.9 %copy-start.2 = (bf16[256,8,256]{2,1,0:T(8,128)(2,1)S(1)}, bf16[256,8,256]{2,1,0:T(8,128)(2,1)}, u32[]{:S(2)}) copy-start(bf16[256,8,256]{2,1,0:T(8,128)(2,1)} %param.8) | copy-start | bytes 3145732
  2.9 12.0 %all-to-all-start = ((bf16[4,2,2048]{2,1,0:T(2,128)(2,1)}), bf16[4,2,2048]{2,1,0:T(2,128)(2,1)S(1)}, u32[]{:S(2)}, u32[]{:S(2)}) async-start(bf16[4,2,2048]{2,1,0:T(2,128)(2,1)} %reshape.73), calls=%async_computation | async-start | bytes 65536 | tf_op jit(solution)/shard_map/all_to_all | solution.py:31
  13.3 13.1 %copy-start.1 = (bf16[32,8,8,256]{3,1,2,0:T(8,128)(2,1)}, bf16[32,8,8,256]{3,1,2,0:T(8,128)(2,1)S(1)}, u32[]{:S(2)}) copy-start(bf16[32,8,8,256]{3,1,2,0:T(8,128)(2,1)S(1)} %copy.31) | copy-start | bytes 3145732
  21.4 19.1 %all-to-all-start.1 = ((bf16[64,32,256]{2,1,0:T(8,128)(2,1)}), bf16[64,32,256]{2,1,0:T(8,128)(2,1)S(1)}, u32[]{:S(2)}, u32[]{:S(2)}) async-start(bf16[64,32,256]{2,1,0:T(8,128)(2,1)} %shard_map.73), calls=%async_computation.1 | async-start | bytes 2097152 | tf_op jit(solution)/shard_map/all_to_all | solution.py:172
  46.3 25.4 %collective-permute-start = (bf16[2,256,512]{2,1,0:T(8,128)(2,1)}, bf16[2,256,512]{2,1,0:T(8,128)(2,1)S(1)}, u32[]{:S(2)}, u32[]{:S(2)}) collective-permute-start(bf16[2,256,512]{2,1,0:T(8,128)(2,1)} %shard_map.74.rest_2_), channel_id=1, source_target_pairs={{0,1},{1,2},{2,3},{3,0},{4,5},{5,6},{6,7},{7,4},{8,9},{9,10},{10,1... | collective-permute-start | bytes 1572872 | tf_op jit(solution)/shard_map/ppermute | solution.py:190
  51.8 19.9 %collective-permute-start.1 = (bf16[2,256,512]{2,1,0:T(8,128)(2,1)}, bf16[2,256,512]{2,1,0:T(8,128)(2,1)S(1)}, u32[]{:S(2)}, u32[]{:S(2)}) collective-permute-start(bf16[2,256,512]{2,1,0:T(8,128)(2,1)} %shard_map.75.rest_0_), channel_id=1, source_target_pairs={{1,0},{2,1},{3,2},{0,3},{5,4},{6,5},{7,6},{4,7},{9,8},{10,9},{11,1... | collective-permute-start | bytes 1572872 | tf_op jit(solution)/shard_map/ppermute | solution.py:194
  71.7 0.8 copy-start.6
  72.5 0.8 copy-start.7

commit v24 on v23

--- a/solution.py
+++ b/solution.py
@@ -276,15 +276,26 @@
     n_obs = len(obs_pieces)
     n_innov = len(innov_pieces)
 
-    def kernel(code_ref, f_ref, taper_ref, *rest):
+    def kernel(code_ref, f_ref, *rest):
         obs_refs = rest[:n_obs]
         innov_refs = rest[n_obs:n_obs + n_innov]
         rest = rest[n_obs + n_innov:]
         if final:
-            part_ref, out_ref, cov_scr, tap_scr = rest
+            part_ref, out_ref, cov_scr, tap_scr, taper_ref = rest
         else:
-            out_ref, cov_scr, tap_scr = rest
+            out_ref, cov_scr, tap_scr, taper_ref = rest
         g = pl.program_id(0)
+
+        @pl.when(g == 0)
+        def _():
+            row_ids = lax.broadcasted_iota(jnp.int32, (BLK, BLK), 0)
+            col_ids = lax.broadcasted_iota(jnp.int32, (BLK, BLK), 1)
+            offset = (row_ids - col_ids).astype(jnp.float32)
+            for k in range(4):
+                scaled = offset / (8.0 * 2.0 ** k)
+                taper_ref[k] = (1.0 / (1.0 + scaled * scaled)) / (members - 1.0)
+            taper_ref[4] = jnp.zeros((BLK, BLK), jnp.float32)
+
         forecast_block = jnp.concatenate([f_ref[r] for r in range(band_step)], axis=1).astype(jnp.float32)
         mean = jnp.sum(forecast_block, axis=0, keepdims=True) / members
         state = (forecast_block - mean).astype(jnp.bfloat16)
@@ -321,9 +332,9 @@
 
     col_spec = pl.BlockSpec((members, rows), lambda g, code: (0, g))
     band_spec = pl.BlockSpec((band_step, members, cols), lambda g, code: (g, 0, 0))
-    in_specs = [band_spec, pl.BlockSpec(tiles.shape, lambda g, code: (0, 0, 0))]
+    in_specs = [band_spec]
     in_specs += [piece_spec(a) for a in obs_arrays] + [piece_spec(a) for a in innov_arrays]
-    operands = [forecast, tiles] + obs_arrays + innov_arrays
+    operands = [forecast] + obs_arrays + innov_arrays
     if final:
         in_specs.append(col_spec)
         operands.append(partial)
@@ -335,6 +346,7 @@
         scratch_shapes=[
             pltpu.VMEM((rows, width), jnp.float32),
             pltpu.VMEM((rows, width), jnp.bfloat16),
+            pltpu.VMEM((5, BLK, BLK), jnp.float32),
         ],
     )
     out_type = jnp.bfloat16 if final else jnp.float32

time: 101 us -> 103 us (1.020)
  waiting for transfers between devices: 14.9 us -> 17.6 us
    all_to_all x1, waiting for transfers between devices: 1.61 us -> 4.25 us  [column_halo(): return lax.all_to_all(spread, axis, 0, 0, tiled=False)]
  transfers between devices with their start and end apart: 4 -> 4, of which waited for: 2 -> 2; matrix products, arithmetic and copies ran while one was open for 7% -> 6% of each run, Pallas kernels for 21% -> 20%
where the time goes in v24:
time: 103 us; the launch traced here: 102 us
  Pallas kernels  37.8 us (37%)
  blocking collectives  17.8 us (17%)
  waiting for transfers between devices  17.6 us (17%)
  local copies, waits for them, and re-layouts  14 us (14%)
  starting transfers between devices  13.9 us (13%)
  other arithmetic  1.08 us (1%)
    all_to_all x1, blocking collectives, body(): lax.all_to_all(result.reshape(members, band_rows, patch_meridian_lines),...  17.8 us
    pallas_call x3, Pallas kernels, observe_dev_call(): pl.pallas_call(kernel, grid=(count // OBS_STEP,), in_specs=in_specs, out_...  16.9 us
    pallas_call x2, Pallas kernels, update_call(): pl.pallas_call(kernel, grid_spec=grid_spec, out_shape=jax.ShapeDtypeStruc...  15.3 us
    all_to_all x1, waiting for transfers between devices, body(): lax.all_to_all(prediction_increment, 'wide', split_axis=0, concat_axis=1,...  13.4 us
    all_to_all x1, starting transfers between devices, column_halo(): return lax.all_to_all(spread, axis, 0, 0, tiled=False)  6.32 us
    pallas_call x1, Pallas kernels, forecast_call(): pl.pallas_call(kernel, grid_spec=grid_spec, out_shape=jax.ShapeDtypeStruc...  5.6 us
    unnamed x26, local copies, waits for them, and re-layouts  4.9 us
    all_to_all x1, waiting for transfers between devices, column_halo(): return lax.all_to_all(spread, axis, 0, 0, tiled=False)  4.25 us
  transfers between devices with their start and end apart: 4, of which 2 were waited for; matrix products, arithmetic and copies ran while one was open for 6% of the time, Pallas kernels for 20%

profile of v24, /device:TPU:0, one launch (start us, length us, event | category | flops | bytes accessed | tf_op | source)
XLA Modules:
  0.0 102.3 jit_solution(17670031564576894393)
XLA Ops:
  0.0 0.0 copy-start
  0.0 0.0 copy-start.4
  0.0 0.0 copy-start.5
  0.0 0.0 copy-start.3
  0.0 0.0 copy-start.2
  0.0 1.5 %fusion.2 = (bf16[32,64,1]{2,1,0:T(8,128)(2,1)S(1)}, bf16[32,64,1]{2,1,0:T(8,128)(2,1)S(1)}) fusion(bf16[32,64,256]{2,1,0:T(8,128)(2,1)} %x_ref.1), kind=kLoop, calls=%fused_computation.12 | loop fusion | bytes 16384 | tf_op jit(solution)/shard_map/slice | solution.py:29
  1.6 0.3 copy.27
  1.9 0.3 copy.28
  2.2 0.7 reshape.60
  2.9 6.3 %all-to-all-start = ((bf16[4,2,2048]{2,1,0:T(2,128)(2,1)}), bf16[4,2,2048]{2,1,0:T(2,128)(2,1)S(1)}, u32[]{:S(2)}, u32[]{:S(2)}) async-start(bf16[4,2,2048]{2,1,0:T(2,128)(2,1)} %reshape.60), calls=%async_computation | async-start | bytes 65536 | tf_op jit(solution)/shard_map/all_to_all | solution.py:31
  9.2 0.0 copy-done.4
  9.2 0.0 copy-done.5
  9.2 0.1 fusion
  9.3 0.0 copy-done.3
  9.3 0.1 select_reduce_fusion
  9.5 0.0 copy-done
  9.5 0.8 subtract_bitcast_fusion
  10.3 0.0 copy-done.2
  10.3 0.3 copy.31
  10.6 0.0 copy-start.1
  10.6 4.3 %all-to-all-done = bf16[4,2,2048]{2,1,0:T(2,128)(2,1)S(1)} async-done(((bf16[4,2,2048]{2,1,0:T(2,128)(2,1)}), bf16[4,2,2048]{2,1,0:T(2,128)(2,1)S(1)}, u32[]{:S(2)}, u32[]{:S(2)}) %all-to-all-start) | async-done | bytes 32800 | tf_op jit(solution)/shard_map/all_to_all | solution.py:31
  14.9 0.1 reshape.61
  15.0 0.8 copy.24.h_ref
  15.8 5.6 %shard_map.73 = bf16[64,32,256]{2,1,0:T(8,128)(2,1)} custom-call(s32[1]{0:T(128)} %bitcast.3.pos_ref, bf16[32,64,256]{2,1,0:T(8,128)(2,1)} %x_ref.1, bf16[4,2,64,32]{3,2,1,0:T(8,128)(2,1)} %copy.24.h_ref), custom_call_target="tpu_custom_call" | custom-call | tf_op jit(solution)/shard_map/pallas_call | solution.py:70
  21.4 3.7 %all-to-all-start.1 = ((bf16[64,32,256]{2,1,0:T(8,128)(2,1)}), bf16[64,32,256]{2,1,0:T(8,128)(2,1)S(1)}, u32[]{:S(2)}, u32[]{:S(2)}) async-start(bf16[64,32,256]{2,1,0:T(8,128)(2,1)} %shard_map.73), calls=%async_computation.1 | async-start | bytes 2097152 | tf_op jit(solution)/shard_map/all_to_all | solution.py:172
  25.1 0.6 fusion.4
  25.7 0.6 fusion.3
  26.3 0.0 copy-done.1
  26.3 0.8 fusion.1
  27.1 13.4 %all-to-all-done.1 = bf16[64,32,256]{2,1,0:T(8,128)(2,1)S(1)} async-done(((bf16[64,32,256]{2,1,0:T(8,128)(2,1)}), bf16[64,32,256]{2,1,0:T(8,128)(2,1)S(1)}, u32[]{:S(2)}, u32[]{:S(2)}) %all-to-all-start.1) | async-done | bytes 1048608 | tf_op jit(solution)/shard_map/all_to_all | solution.py:172
  40.5 1.1 %copy.25 = bf16[8,8,32,256]{3,2,0,1:T(8,128)(2,1)} copy(bf16[8,8,32,256]{3,2,1,0:T(8,128)(2,1)S(1)} %bitcast.39) | data formatting | bytes 2097152 | tf_op jit(solution)/shard_map/all_to_all | solution.py:172
  41.6 4.8 %shard_map.74.rest_2_ = bf16[2,256,512]{2,1,0:T(8,128)(2,1)} custom-call(bf16[8,256,256]{2,1,0:T(8,128)(2,1)} %bitcast.34, s32[4,512]{1,0:T(4,128)} %get-tuple-element.12.i_ref, f32[4,512]{1,0:T(4,128)} %get-tuple-element.10.w_ref, bf16[256,512]{1,0:T(8,128)(2,1)} %get-tuple-element.6.rest_0_), custom_call_target="tpu_custom_call" | custom-call | tf_op jit(solution)/shard_map/pallas_call | solution.py:142
  46.3 0.7 collective-permute-start
  47.0 4.8 %shard_map.75.rest_0_ = bf16[2,256,512]{2,1,0:T(8,128)(2,1)} custom-call(bf16[8,256,256]{2,1,0:T(8,128)(2,1)} %bitcast.35, s32[4,512]{1,0:T(4,128)} %get-tuple-element.11.i_ref, f32[4,512]{1,0:T(4,128)} %get-tuple-element.9.w_ref, bf16[256,512]{1,0:T(8,128)(2,1)} %get-tuple-element.5.rest_0_), custom_call_target="tpu_custom_call" | custom-call | tf_op jit(solution)/shard_map/pallas_call | solution.py:142
  51.8 3.1 %collective-permute-start.1 = (bf16[2,256,512]{2,1,0:T(8,128)(2,1)}, bf16[2,256,512]{2,1,0:T(8,128)(2,1)S(1)}, u32[]{:S(2)}, u32[]{:S(2)}) collective-permute-start(bf16[2,256,512]{2,1,0:T(8,128)(2,1)} %shard_map.75.rest_0_), channel_id=1, source_target_pairs={{1,0},{2,1},{3,2},{0,3},{5,4},{6,5},{7,6},{4,7},{9,8},{10,9},{11,1... | collective-permute-start | bytes 1572872 | tf_op jit(solution)/shard_map/ppermute | solution.py:194
  54.9 0.1 fusion.5
  55.0 0.1 slice.60
  55.0 0.6 slice.61.i_ref
  55.6 0.6 slice.62.w_ref
  56.2 0.6 reshape.58.code_ref
  56.9 0.1 pad_add_fusion
  57.0 0.6 reshape.54.code_ref
  57.6 7.4 %shard_map.76.rest_1_ = bf16[256,1024]{1,0:T(8,128)(2,1)} custom-call(bf16[8,256,256]{2,1,0:T(8,128)(2,1)} %bitcast.36, s32[4,1024]{1,0:T(4,128)} %slice.61.i_ref, f32[4,1024]{1,0:T(4,128)} %slice.62.w_ref), custom_call_target="tpu_custom_call" | custom-call | tf_op jit(solution)/shard_map/pallas_call | solution.py:142
  64.9 8.5 %shard_map.77.rest_4_ = f32[256,2048]{1,0:T(8,128)} custom-call(s32[256]{0:T(256)} %reshape.58.code_ref, bf16[8,256,256]{2,1,0:T(8,128)(2,1)} %bitcast.37, bf16[2,256,512]{2,1,0:T(8,128)(2,1)} %shard_map.75.rest_0_, bf16[256,1024]{1,0:T(8,128)(2,1)} %shard_map.76.rest_1_, bf16[2,256,512]{2,1,0:T(8,128)(2,1)} %shard_map.74.rest_2_, bf16[256,2048]{1,0:T(8,128)(2,1)} %bitcast.43), custom_call_target="tpu_custom_call" | custom-call | flops 4294967296 | bytes 4194304 | tf_op jit(solution)/shard_map/pallas_call | solution.py:353
  73.4 0.0 collective-permute-done.rest_0_.rest_2_
  73.4 0.0 copy-start.6
  73.5 0.0 collective-permute-done.1.rest_1_.rest_3_
  73.5 0.8 copy-done.6
  74.2 0.0 copy-start.7
  74.2 0.8 copy-done.7
  75.1 6.8 %shard_map.78 = bf16[256,2048]{1,0:T(8,128)(2,1)} custom-call(s32[128]{0:T(128)} %reshape.54.code_ref, bf16[8,256,256]{2,1,0:T(8,128)(2,1)} %bitcast.38, bf16[2,256,512]{2,1,0:T(8,128)(2,1)} %copy-done.6, bf16[2,256,512]{2,1,0:T(8,128)(2,1)} %copy-done.7, bf16[2,256,512]{2,1,0:T(8,128)(2,1)} %copy-done.6, bf16[2,256,512]{2,1,0:T(8,128)(2,1)} %copy-done.7, ...), custom_call_target="tpu_custom_call" | custom-call | flops 2147483648 | bytes 4194304 | tf_op jit(solution)/shard_map/pallas_call | solution.py:353
  81.8 1.5 %copy.32 = bf16[32,8,8,256]{3,2,1,0:T(8,128)(2,1)S(1)} copy(bf16[32,8,8,256]{3,1,2,0:T(8,128)(2,1)} %bitcast.45) | data formatting | bytes 2097152
  83.4 17.8 %all_to_all.41 = bf16[256,8,256]{2,1,0:T(8,128)(2,1)S(1)} all-to-all(bf16[256,8,256]{2,1,0:T(8,128)(2,1)S(1)} %bitcast.40), channel_id=1, replica_groups=mesh['wide'=8,'lon'=4] {'wide'}, dimensions={0} | all-to-all | bytes 2097152 | tf_op jit(solution)/shard_map/all_to_all | solution.py:226
  101.2 1.1 %copy.34 = bf16[8,32,8,256]{3,2,0,1:T(8,128)(2,1)} copy(bf16[8,32,8,256]{3,2,1,0:T(8,128)(2,1)S(1)} %bitcast.41) | data formatting | bytes 2097152 | tf_op jit(solution)/shard_map/all_to_all | solution.py:226
  (6 shorter events, 0.1 us)
Async XLA Ops:
  0.0 9.5 %copy-start = (f32[4,64,256]{2,1,0:T(8,128)S(1)}, f32[4,64,256]{2,1,0:T(8,128)}, u32[]{:S(2)}) copy-start(f32[4,64,256]{2,1,0:T(8,128)} %param.10) | copy-start | bytes 786436
  0.0 9.2 %copy-start.4 = (s32[1,16,16]{2,1,0:T(8,128)S(1)}, s32[1,16,16]{2,1,0:T(8,128)}, u32[]{:S(2)}) copy-start(s32[1,16,16]{2,1,0:T(8,128)} %param.13) | copy-start | bytes 3076
  0.0 9.2 %copy-start.5 = (s32[1,16]{1,0:T(1,128)S(1)}, s32[1,16]{1,0:T(1,128)}, u32[]{:S(2)}) copy-start(s32[1,16]{1,0:T(1,128)} %param.12) | copy-start | bytes 196
  0.0 9.3 %copy-start.3 = (s32[1,16,16]{2,1,0:T(8,128)S(1)}, s32[1,16,16]{2,1,0:T(8,128)}, u32[]{:S(2)}) copy-start(s32[1,16,16]{2,1,0:T(8,128)} %param.11) | copy-start | bytes 3076
  0.0 10.3 %copy-start.2 = (bf16[256,8,256]{2,1,0:T(8,128)(2,1)S(1)}, bf16[256,8,256]{2,1,0:T(8,128)(2,1)}, u32[]{:S(2)}) copy-start(bf16[256,8,256]{2,1,0:T(8,128)(2,1)} %param.8) | copy-start | bytes 3145732
  2.9 12.0 %all-to-all-start = ((bf16[4,2,2048]{2,1,0:T(2,128)(2,1)}), bf16[4,2,2048]{2,1,0:T(2,128)(2,1)S(1)}, u32[]{:S(2)}, u32[]{:S(2)}) async-start(bf16[4,2,2048]{2,1,0:T(2,128)(2,1)} %reshape.60), calls=%async_computation | async-start | bytes 65536 | tf_op jit(solution)/shard_map/all_to_all | solution.py:31
  10.6 15.7 %copy-start.1 = (bf16[32,8,8,256]{3,1,2,0:T(8,128)(2,1)}, bf16[32,8,8,256]{3,1,2,0:T(8,128)(2,1)S(1)}, u32[]{:S(2)}) copy-start(bf16[32,8,8,256]{3,1,2,0:T(8,128)(2,1)S(1)} %copy.31) | copy-start | bytes 3145732
  21.4 19.1 %all-to-all-start.1 = ((bf16[64,32,256]{2,1,0:T(8,128)(2,1)}), bf16[64,32,256]{2,1,0:T(8,128)(2,1)S(1)}, u32[]{:S(2)}, u32[]{:S(2)}) async-start(bf16[64,32,256]{2,1,0:T(8,128)(2,1)} %shard_map.73), calls=%async_computation.1 | async-start | bytes 2097152 | tf_op jit(solution)/shard_map/all_to_all | solution.py:172
  46.3 27.1 %collective-permute-start = (bf16[2,256,512]{2,1,0:T(8,128)(2,1)}, bf16[2,256,512]{2,1,0:T(8,128)(2,1)S(1)}, u32[]{:S(2)}, u32[]{:S(2)}) collective-permute-start(bf16[2,256,512]{2,1,0:T(8,128)(2,1)} %shard_map.74.rest_2_), channel_id=1, source_target_pairs={{0,1},{1,2},{2,3},{3,0},{4,5},{5,6},{6,7},{7,4},{8,9},{9,10},{10,1... | collective-permute-start | bytes 1572872 | tf_op jit(solution)/shard_map/ppermute | solution.py:190
  51.8 21.7 %collective-permute-start.1 = (bf16[2,256,512]{2,1,0:T(8,128)(2,1)}, bf16[2,256,512]{2,1,0:T(8,128)(2,1)S(1)}, u32[]{:S(2)}, u32[]{:S(2)}) collective-permute-start(bf16[2,256,512]{2,1,0:T(8,128)(2,1)} %shard_map.75.rest_0_), channel_id=1, source_target_pairs={{1,0},{2,1},{3,2},{0,3},{5,4},{6,5},{7,6},{4,7},{9,8},{10,9},{11,1... | collective-permute-start | bytes 1572872 | tf_op jit(solution)/shard_map/ppermute | solution.py:194
  73.4 0.8 copy-start.6
  74.2 0.8 copy-start.7

commit v25 on v23

--- a/solution.py
+++ b/solution.py
@@ -95,7 +95,7 @@
 
 
 OBS_STEP = 256
-def observe_dev_call(state, index, weight, extra=None):
+def observe_dev_call(state, index, weight, extra=None, step=OBS_STEP):
     band, members, cols = state.shape
     cells = band * cols
     count = index.shape[1]
@@ -106,8 +106,8 @@
             x_ref, o_ref = rest
         else:
             (o_ref,) = rest
-        cell_ids = lax.broadcasted_iota(jnp.int32, (cells, OBS_STEP), 0)
-        summed = jnp.zeros((members, OBS_STEP), jnp.float32)
+        cell_ids = lax.broadcasted_iota(jnp.int32, (cells, step), 0)
+        summed = jnp.zeros((members, step), jnp.float32)
         for k in range(4):
             selector = (cell_ids == i_ref[k:k + 1, :]).astype(jnp.bfloat16)
             picked = jnp.dot(f_ref[0], selector[:cols], preferred_element_type=jnp.float32)
@@ -127,21 +127,21 @@
 
     in_specs = [
         pl.BlockSpec(state.shape, lambda j: (0, 0, 0)),
-        pl.BlockSpec((4, OBS_STEP), lambda j: (0, j)),
-        pl.BlockSpec((4, OBS_STEP), lambda j: (0, j)),
+        pl.BlockSpec((4, step), lambda j: (0, j)),
+        pl.BlockSpec((4, step), lambda j: (0, j)),
     ]
     operands = [state, index, weight]
     if carry:
-        in_specs.append(pl.BlockSpec((members, OBS_STEP), lambda j: (0, j)))
+        in_specs.append(pl.BlockSpec((members, step), lambda j: (0, j)))
         operands.append(extra)
-        out_spec = pl.BlockSpec((2, members, OBS_STEP), lambda j: (0, 0, j))
+        out_spec = pl.BlockSpec((2, members, step), lambda j: (0, 0, j))
         out_shape = jax.ShapeDtypeStruct((2, members, count), jnp.bfloat16)
     else:
-        out_spec = pl.BlockSpec((members, OBS_STEP), lambda j: (0, j))
+        out_spec = pl.BlockSpec((members, step), lambda j: (0, j))
         out_shape = jax.ShapeDtypeStruct((members, count), jnp.bfloat16)
     return pl.pallas_call(
         kernel,
-        grid=(count // OBS_STEP,),
+        grid=(count // step,),
         in_specs=in_specs,
         out_specs=out_spec,
         out_shape=out_shape,
@@ -192,7 +192,7 @@
         region_state, local_index[:, :halo], local_weight[:, :halo], innov_flat[:, :halo]
     )
     east = lax.ppermute(first_edge, "lon", down)
-    middle_dev = observe_dev_call(region_state, local_index[:, halo:-halo], local_weight[:, halo:-halo])
+    middle_dev = observe_dev_call(region_state, local_index[:, halo:-halo], local_weight[:, halo:-halo], step=512)
     obs_dev = jnp.concatenate([first_edge[0], middle_dev, last_edge[0]], axis=1)
     halo_blocks = halo // BLK
     block_count = patch_gridpoints // BLK

time: 101 us -> 101 us (level)
  transfers between devices with their start and end apart: 4 -> 4, of which waited for: 2 -> 2; matrix products, arithmetic and copies ran while one was open for 7% -> 7% of each run, Pallas kernels for 21% -> 20%
where the time goes in v25:
time: 101 us
  Pallas kernels  37.6 us (37%)
  blocking collectives  18.1 us (18%)
  waiting for transfers between devices  14.9 us (15%)
  local copies, waits for them, and re-layouts  14.8 us (15%)
  starting transfers between devices  13.9 us (14%)
  other arithmetic  1.23 us (1%)
    all_to_all x1, blocking collectives, body(): lax.all_to_all(result.reshape(members, band_rows, patch_meridian_lines),...  18.1 us
    pallas_call x3, Pallas kernels, observe_dev_call(): pl.pallas_call(kernel, grid=(count // step,), in_specs=in_specs, out_spec...  16.6 us
    pallas_call x2, Pallas kernels, update_call(): pl.pallas_call(kernel, grid_spec=grid_spec, out_shape=jax.ShapeDtypeStruc...  15.4 us
    all_to_all x1, waiting for transfers between devices, body(): lax.all_to_all(prediction_increment, 'wide', split_axis=0, concat_axis=1,...  13.3 us
    all_to_all x1, starting transfers between devices, column_halo(): return lax.all_to_all(spread, axis, 0, 0, tiled=False)  6.32 us
    pallas_call x1, Pallas kernels, forecast_call(): pl.pallas_call(kernel, grid_spec=grid_spec, out_shape=jax.ShapeDtypeStruc...  5.6 us
    unnamed x26, local copies, waits for them, and re-layouts  4.88 us
    all_to_all x1, starting transfers between devices, body(): lax.all_to_all(prediction_increment, 'wide', split_axis=0, concat_axis=1,...  3.72 us
  transfers between devices with their start and end apart: 4, of which 2 were waited for; matrix products, arithmetic and copies ran while one was open for 7% of the time, Pallas kernels for 20%

profile of v25, /device:TPU:0, one launch (start us, length us, event | category | flops | bytes accessed | tf_op | source)
XLA Modules:
  0.0 100.6 jit_solution(14629103415971197811)
XLA Ops:
  0.0 0.0 copy-start
  0.0 0.0 copy-start.4
  0.0 0.0 copy-start.5
  0.0 0.0 copy-start.3
  0.0 0.0 copy-start.2
  0.0 1.5 %fusion.5 = (bf16[32,64,1]{2,1,0:T(8,128)(2,1)S(1)}, bf16[32,64,1]{2,1,0:T(8,128)(2,1)S(1)}) fusion(bf16[32,64,256]{2,1,0:T(8,128)(2,1)} %x_ref.1), kind=kLoop, calls=%fused_computation.18 | loop fusion | bytes 16384 | tf_op jit(solution)/shard_map/slice | solution.py:29
  1.6 0.3 copy.27
  1.9 0.3 copy.28
  2.2 0.7 reshape.73
  2.9 6.3 %all-to-all-start = ((bf16[4,2,2048]{2,1,0:T(2,128)(2,1)}), bf16[4,2,2048]{2,1,0:T(2,128)(2,1)S(1)}, u32[]{:S(2)}, u32[]{:S(2)}) async-start(bf16[4,2,2048]{2,1,0:T(2,128)(2,1)} %reshape.73), calls=%async_computation | async-start | bytes 65536 | tf_op jit(solution)/shard_map/all_to_all | solution.py:31
  9.2 0.0 copy-done.4
  9.2 0.0 copy-done.5
  9.2 0.1 fusion.3
  9.3 0.0 copy-done.3
  9.3 0.1 select_reduce_fusion
  9.5 0.1 fusion.8
  9.5 0.0 copy-done
  9.5 0.8 subtract_bitcast_fusion
  10.3 0.1 pad_add_fusion
  10.4 0.1 slice.60
  10.5 0.7 reshape.71.code_ref
  11.1 0.6 reshape.67.code_ref
  11.7 0.6 slice.61.i_ref
  12.3 0.6 slice.62.w_ref
  12.9 0.0 copy-done.2
  12.9 0.3 copy.31
  13.3 0.0 copy-start.1
  13.3 1.6 %all-to-all-done = bf16[4,2,2048]{2,1,0:T(2,128)(2,1)S(1)} async-done(((bf16[4,2,2048]{2,1,0:T(2,128)(2,1)}), bf16[4,2,2048]{2,1,0:T(2,128)(2,1)S(1)}, u32[]{:S(2)}, u32[]{:S(2)}) %all-to-all-start) | async-done | bytes 32800 | tf_op jit(solution)/shard_map/all_to_all | solution.py:31
  14.9 0.1 reshape.74
  15.0 0.8 copy.24.h_ref
  15.8 5.6 %shard_map.73 = bf16[64,32,256]{2,1,0:T(8,128)(2,1)} custom-call(s32[1]{0:T(128)} %bitcast.3.pos_ref, bf16[32,64,256]{2,1,0:T(8,128)(2,1)} %x_ref.1, bf16[4,2,64,32]{3,2,1,0:T(8,128)(2,1)} %copy.24.h_ref), custom_call_target="tpu_custom_call" | custom-call | tf_op jit(solution)/shard_map/pallas_call | solution.py:70
  21.4 3.7 %all-to-all-start.1 = ((bf16[64,32,256]{2,1,0:T(8,128)(2,1)}), bf16[64,32,256]{2,1,0:T(8,128)(2,1)S(1)}, u32[]{:S(2)}, u32[]{:S(2)}) async-start(bf16[64,32,256]{2,1,0:T(8,128)(2,1)} %shard_map.73), calls=%async_computation.1 | async-start | bytes 2097152 | tf_op jit(solution)/shard_map/all_to_all | solution.py:172
  25.1 0.6 fusion.7
  25.7 0.6 fusion.6
  26.3 0.0 copy-done.1
  26.3 0.8 fusion.4
  27.2 13.3 %all-to-all-done.1 = bf16[64,32,256]{2,1,0:T(8,128)(2,1)S(1)} async-done(((bf16[64,32,256]{2,1,0:T(8,128)(2,1)}), bf16[64,32,256]{2,1,0:T(8,128)(2,1)S(1)}, u32[]{:S(2)}, u32[]{:S(2)}) %all-to-all-start.1) | async-done | bytes 1048608 | tf_op jit(solution)/shard_map/all_to_all | solution.py:172
  40.5 1.1 %copy.25 = bf16[8,8,32,256]{3,2,0,1:T(8,128)(2,1)} copy(bf16[8,8,32,256]{3,2,1,0:T(8,128)(2,1)S(1)} %bitcast.39) | data formatting | bytes 2097152 | tf_op jit(solution)/shard_map/all_to_all | solution.py:172
  41.6 4.8 %shard_map.74.rest_2_ = bf16[2,256,512]{2,1,0:T(8,128)(2,1)} custom-call(bf16[8,256,256]{2,1,0:T(8,128)(2,1)} %bitcast.34, s32[4,512]{1,0:T(4,128)} %get-tuple-element.12.i_ref, f32[4,512]{1,0:T(4,128)} %get-tuple-element.10.w_ref, bf16[256,512]{1,0:T(8,128)(2,1)} %get-tuple-element.6.rest_0_), custom_call_target="tpu_custom_call" | custom-call | tf_op jit(solution)/shard_map/pallas_call | solution.py:142
  46.3 0.7 collective-permute-start
  47.0 4.8 %shard_map.75.rest_0_ = bf16[2,256,512]{2,1,0:T(8,128)(2,1)} custom-call(bf16[8,256,256]{2,1,0:T(8,128)(2,1)} %bitcast.35, s32[4,512]{1,0:T(4,128)} %get-tuple-element.11.i_ref, f32[4,512]{1,0:T(4,128)} %get-tuple-element.9.w_ref, bf16[256,512]{1,0:T(8,128)(2,1)} %get-tuple-element.5.rest_0_), custom_call_target="tpu_custom_call" | custom-call | tf_op jit(solution)/shard_map/pallas_call | solution.py:142
  51.8 3.1 %collective-permute-start.1 = (bf16[2,256,512]{2,1,0:T(8,128)(2,1)}, bf16[2,256,512]{2,1,0:T(8,128)(2,1)S(1)}, u32[]{:S(2)}, u32[]{:S(2)}) collective-permute-start(bf16[2,256,512]{2,1,0:T(8,128)(2,1)} %shard_map.75.rest_0_), channel_id=1, source_target_pairs={{1,0},{2,1},{3,2},{0,3},{5,4},{6,5},{7,6},{4,7},{9,8},{10,9},{11,1... | collective-permute-start | bytes 1572872 | tf_op jit(solution)/shard_map/ppermute | solution.py:194
  54.9 0.1 fusion.2
  55.0 0.8 concatenate.7.taper_ref
  55.8 7.1 %shard_map.76.rest_1_ = bf16[256,1024]{1,0:T(8,128)(2,1)} custom-call(bf16[8,256,256]{2,1,0:T(8,128)(2,1)} %bitcast.36, s32[4,1024]{1,0:T(4,128)} %slice.61.i_ref, f32[4,1024]{1,0:T(4,128)} %slice.62.w_ref), custom_call_target="tpu_custom_call" | custom-call | tf_op jit(solution)/shard_map/pallas_call | solution.py:142
  62.9 8.6 %shard_map.77.rest_4_ = f32[256,2048]{1,0:T(8,128)} custom-call(s32[256]{0:T(256)} %reshape.71.code_ref, bf16[8,256,256]{2,1,0:T(8,128)(2,1)} %bitcast.37, f32[5,128,128]{2,1,0:T(8,128)} %concatenate.7.taper_ref, bf16[2,256,512]{2,1,0:T(8,128)(2,1)} %shard_map.75.rest_0_, bf16[256,1024]{1,0:T(8,128)(2,1)} %shard_map.76.rest_1_, ...), custom_call_target="tpu_custom_call" | custom-call | flops 4294967296 | bytes 4194304 | tf_op jit(solution)/shard_map/pallas_call | solution.py:341
  71.5 0.0 collective-permute-done.rest_0_.rest_2_
  71.5 0.0 copy-start.6
  71.5 0.0 collective-permute-done.1.rest_1_.rest_3_
  71.5 0.8 copy-done.6
  72.3 0.0 copy-start.7
  72.3 0.8 copy-done.7
  73.1 6.8 %shard_map.78 = bf16[256,2048]{1,0:T(8,128)(2,1)} custom-call(s32[128]{0:T(128)} %reshape.67.code_ref, bf16[8,256,256]{2,1,0:T(8,128)(2,1)} %bitcast.38, f32[5,128,128]{2,1,0:T(8,128)} %concatenate.7.taper_ref, bf16[2,256,512]{2,1,0:T(8,128)(2,1)} %copy-done.6, bf16[2,256,512]{2,1,0:T(8,128)(2,1)} %copy-done.7, bf16[2,256,512]{2,1,0:T(8,128)(2,1)} %copy-done.6, ...), custom_call_target="tpu_custom_call" | custom-call | flops 2147483648 | bytes 4194304 | tf_op jit(solution)/shard_map/pallas_call | solution.py:341
  79.9 1.5 %copy.32 = bf16[32,8,8,256]{3,2,1,0:T(8,128)(2,1)S(1)} copy(bf16[32,8,8,256]{3,1,2,0:T(8,128)(2,1)} %bitcast.45) | data formatting | bytes 2097152
  81.4 18.1 %all_to_all.41 = bf16[256,8,256]{2,1,0:T(8,128)(2,1)S(1)} all-to-all(bf16[256,8,256]{2,1,0:T(8,128)(2,1)S(1)} %bitcast.40), channel_id=1, replica_groups=mesh['wide'=8,'lon'=4] {'wide'}, dimensions={0} | all-to-all | bytes 2097152 | tf_op jit(solution)/shard_map/all_to_all | solution.py:226
  99.5 1.1 %copy.34 = bf16[8,32,8,256]{3,2,0,1:T(8,128)(2,1)} copy(bf16[8,32,8,256]{3,2,1,0:T(8,128)(2,1)S(1)} %bitcast.41) | data formatting | bytes 2097152 | tf_op jit(solution)/shard_map/all_to_all | solution.py:226
  (8 shorter events, 0.1 us)
Async XLA Ops:
  0.0 9.5 %copy-start = (f32[4,64,256]{2,1,0:T(8,128)S(1)}, f32[4,64,256]{2,1,0:T(8,128)}, u32[]{:S(2)}) copy-start(f32[4,64,256]{2,1,0:T(8,128)} %param.10) | copy-start | bytes 786436
  0.0 9.2 %copy-start.4 = (s32[1,16,16]{2,1,0:T(8,128)S(1)}, s32[1,16,16]{2,1,0:T(8,128)}, u32[]{:S(2)}) copy-start(s32[1,16,16]{2,1,0:T(8,128)} %param.13) | copy-start | bytes 3076
  0.0 9.2 %copy-start.5 = (s32[1,16]{1,0:T(1,128)S(1)}, s32[1,16]{1,0:T(1,128)}, u32[]{:S(2)}) copy-start(s32[1,16]{1,0:T(1,128)} %param.12) | copy-start | bytes 196
  0.0 9.3 %copy-start.3 = (s32[1,16,16]{2,1,0:T(8,128)S(1)}, s32[1,16,16]{2,1,0:T(8,128)}, u32[]{:S(2)}) copy-start(s32[1,16,16]{2,1,0:T(8,128)} %param.11) | copy-start | bytes 3076
  0.0 12.9 %copy-start.2 = (bf16[256,8,256]{2,1,0:T(8,128)(2,1)S(1)}, bf16[256,8,256]{2,1,0:T(8,128)(2,1)}, u32[]{:S(2)}) copy-start(bf16[256,8,256]{2,1,0:T(8,128)(2,1)} %param.8) | copy-start | bytes 3145732
  2.9 12.0 %all-to-all-start = ((bf16[4,2,2048]{2,1,0:T(2,128)(2,1)}), bf16[4,2,2048]{2,1,0:T(2,128)(2,1)S(1)}, u32[]{:S(2)}, u32[]{:S(2)}) async-start(bf16[4,2,2048]{2,1,0:T(2,128)(2,1)} %reshape.73), calls=%async_computation | async-start | bytes 65536 | tf_op jit(solution)/shard_map/all_to_all | solution.py:31
  13.3 13.1 %copy-start.1 = (bf16[32,8,8,256]{3,1,2,0:T(8,128)(2,1)}, bf16[32,8,8,256]{3,1,2,0:T(8,128)(2,1)S(1)}, u32[]{:S(2)}) copy-start(bf16[32,8,8,256]{3,1,2,0:T(8,128)(2,1)S(1)} %copy.31) | copy-start | bytes 3145732
  21.4 19.1 %all-to-all-start.1 = ((bf16[64,32,256]{2,1,0:T(8,128)(2,1)}), bf16[64,32,256]{2,1,0:T(8,128)(2,1)S(1)}, u32[]{:S(2)}, u32[]{:S(2)}) async-start(bf16[64,32,256]{2,1,0:T(8,128)(2,1)} %shard_map.73), calls=%async_computation.1 | async-start | bytes 2097152 | tf_op jit(solution)/shard_map/all_to_all | solution.py:172
  46.3 25.2 %collective-permute-start = (bf16[2,256,512]{2,1,0:T(8,128)(2,1)}, bf16[2,256,512]{2,1,0:T(8,128)(2,1)S(1)}, u32[]{:S(2)}, u32[]{:S(2)}) collective-permute-start(bf16[2,256,512]{2,1,0:T(8,128)(2,1)} %shard_map.74.rest_2_), channel_id=1, source_target_pairs={{0,1},{1,2},{2,3},{3,0},{4,5},{5,6},{6,7},{7,4},{8,9},{9,10},{10,1... | collective-permute-start | bytes 1572872 | tf_op jit(solution)/shard_map/ppermute | solution.py:190
  51.8 19.7 %collective-permute-start.1 = (bf16[2,256,512]{2,1,0:T(8,128)(2,1)}, bf16[2,256,512]{2,1,0:T(8,128)(2,1)S(1)}, u32[]{:S(2)}, u32[]{:S(2)}) collective-permute-start(bf16[2,256,512]{2,1,0:T(8,128)(2,1)} %shard_map.75.rest_0_), channel_id=1, source_target_pairs={{1,0},{2,1},{3,2},{0,3},{5,4},{6,5},{7,6},{4,7},{9,8},{10,9},{11,1... | collective-permute-start | bytes 1572872 | tf_op jit(solution)/shard_map/ppermute | solution.py:194
  71.5 0.8 copy-start.6
  72.3 0.8 copy-start.7

commit v26 on v25

--- a/solution.py
+++ b/solution.py
@@ -210,7 +210,7 @@
         tiles,
         block_count,
         block_count,
-        group=8,
+        group=16,
     )
     result = update_call(
         halo_code.reshape(-1),

time: 101 us -> 101 us (level)
  transfers between devices with their start and end apart: 4 -> 4, of which waited for: 2 -> 2; matrix products, arithmetic and copies ran while one was open for 7% -> 7% of each run, Pallas kernels for 20% -> 21%
where the time goes in v26:
time: 101 us
  Pallas kernels  37.8 us (37%)
  blocking collectives  17.9 us (18%)
  waiting for transfers between devices  14.9 us (15%)
  local copies, waits for them, and re-layouts  14.8 us (15%)
  starting transfers between devices  13.9 us (14%)
  other arithmetic  1.23 us (1%)
    all_to_all x1, blocking collectives, body(): lax.all_to_all(result.reshape(members, band_rows, patch_meridian_lines),...  17.9 us
    pallas_call x3, Pallas kernels, observe_dev_call(): pl.pallas_call(kernel, grid=(count // step,), in_specs=in_specs, out_spec...  16.6 us
    pallas_call x2, Pallas kernels, update_call(): pl.pallas_call(kernel, grid_spec=grid_spec, out_shape=jax.ShapeDtypeStruc...  15.5 us
    all_to_all x1, waiting for transfers between devices, body(): lax.all_to_all(prediction_increment, 'wide', split_axis=0, concat_axis=1,...  13.3 us
    all_to_all x1, starting transfers between devices, column_halo(): return lax.all_to_all(spread, axis, 0, 0, tiled=False)  6.32 us
    pallas_call x1, Pallas kernels, forecast_call(): pl.pallas_call(kernel, grid_spec=grid_spec, out_shape=jax.ShapeDtypeStruc...  5.6 us
    unnamed x26, local copies, waits for them, and re-layouts  4.89 us
    all_to_all x1, starting transfers between devices, body(): lax.all_to_all(prediction_increment, 'wide', split_axis=0, concat_axis=1,...  3.72 us
  transfers between devices with their start and end apart: 4, of which 2 were waited for; matrix products, arithmetic and copies ran while one was open for 7% of the time, Pallas kernels for 21%

profile of v26, /device:TPU:0, one launch (start us, length us, event | category | flops | bytes accessed | tf_op | source)
XLA Modules:
  0.0 100.6 jit_solution(1869889115984505885)
XLA Ops:
  0.0 0.0 copy-start
  0.0 0.0 copy-start.4
  0.0 0.0 copy-start.5
  0.0 0.0 copy-start.3
  0.0 0.0 copy-start.2
  0.0 1.5 %fusion.5 = (bf16[32,64,1]{2,1,0:T(8,128)(2,1)S(1)}, bf16[32,64,1]{2,1,0:T(8,128)(2,1)S(1)}) fusion(bf16[32,64,256]{2,1,0:T(8,128)(2,1)} %x_ref.1), kind=kLoop, calls=%fused_computation.18 | loop fusion | bytes 16384 | tf_op jit(solution)/shard_map/slice | solution.py:29
  1.6 0.3 copy.27
  1.9 0.3 copy.28
  2.2 0.7 reshape.73
  2.9 6.3 %all-to-all-start = ((bf16[4,2,2048]{2,1,0:T(2,128)(2,1)}), bf16[4,2,2048]{2,1,0:T(2,128)(2,1)S(1)}, u32[]{:S(2)}, u32[]{:S(2)}) async-start(bf16[4,2,2048]{2,1,0:T(2,128)(2,1)} %reshape.73), calls=%async_computation | async-start | bytes 65536 | tf_op jit(solution)/shard_map/all_to_all | solution.py:31
  9.2 0.0 copy-done.4
  9.2 0.0 copy-done.5
  9.2 0.1 fusion.3
  9.3 0.0 copy-done.3
  9.3 0.1 select_reduce_fusion
  9.5 0.1 fusion.8
  9.5 0.0 copy-done
  9.5 0.8 subtract_bitcast_fusion
  10.3 0.1 pad_add_fusion
  10.4 0.1 slice.60
  10.5 0.7 reshape.71.code_ref
  11.1 0.6 reshape.67.code_ref
  11.7 0.6 slice.61.i_ref
  12.3 0.6 slice.62.w_ref
  12.9 0.0 copy-done.2
  12.9 0.3 copy.31
  13.3 0.0 copy-start.1
  13.3 1.6 %all-to-all-done = bf16[4,2,2048]{2,1,0:T(2,128)(2,1)S(1)} async-done(((bf16[4,2,2048]{2,1,0:T(2,128)(2,1)}), bf16[4,2,2048]{2,1,0:T(2,128)(2,1)S(1)}, u32[]{:S(2)}, u32[]{:S(2)}) %all-to-all-start) | async-done | bytes 32800 | tf_op jit(solution)/shard_map/all_to_all | solution.py:31
  14.9 0.1 reshape.74
  15.0 0.8 copy.24.h_ref
  15.8 5.6 %shard_map.73 = bf16[64,32,256]{2,1,0:T(8,128)(2,1)} custom-call(s32[1]{0:T(128)} %bitcast.3.pos_ref, bf16[32,64,256]{2,1,0:T(8,128)(2,1)} %x_ref.1, bf16[4,2,64,32]{3,2,1,0:T(8,128)(2,1)} %copy.24.h_ref), custom_call_target="tpu_custom_call" | custom-call | tf_op jit(solution)/shard_map/pallas_call | solution.py:70
  21.4 3.7 %all-to-all-start.1 = ((bf16[64,32,256]{2,1,0:T(8,128)(2,1)}), bf16[64,32,256]{2,1,0:T(8,128)(2,1)S(1)}, u32[]{:S(2)}, u32[]{:S(2)}) async-start(bf16[64,32,256]{2,1,0:T(8,128)(2,1)} %shard_map.73), calls=%async_computation.1 | async-start | bytes 2097152 | tf_op jit(solution)/shard_map/all_to_all | solution.py:172
  25.1 0.6 fusion.7
  25.7 0.6 fusion.6
  26.3 0.0 copy-done.1
  26.3 0.8 fusion.4
  27.2 13.3 %all-to-all-done.1 = bf16[64,32,256]{2,1,0:T(8,128)(2,1)S(1)} async-done(((bf16[64,32,256]{2,1,0:T(8,128)(2,1)}), bf16[64,32,256]{2,1,0:T(8,128)(2,1)S(1)}, u32[]{:S(2)}, u32[]{:S(2)}) %all-to-all-start.1) | async-done | bytes 1048608 | tf_op jit(solution)/shard_map/all_to_all | solution.py:172
  40.5 1.1 %copy.25 = bf16[8,8,32,256]{3,2,0,1:T(8,128)(2,1)} copy(bf16[8,8,32,256]{3,2,1,0:T(8,128)(2,1)S(1)} %bitcast.39) | data formatting | bytes 2097152 | tf_op jit(solution)/shard_map/all_to_all | solution.py:172
  41.6 4.8 %shard_map.74.rest_2_ = bf16[2,256,512]{2,1,0:T(8,128)(2,1)} custom-call(bf16[8,256,256]{2,1,0:T(8,128)(2,1)} %bitcast.34, s32[4,512]{1,0:T(4,128)} %get-tuple-element.12.i_ref, f32[4,512]{1,0:T(4,128)} %get-tuple-element.10.w_ref, bf16[256,512]{1,0:T(8,128)(2,1)} %get-tuple-element.6.rest_0_), custom_call_target="tpu_custom_call" | custom-call | tf_op jit(solution)/shard_map/pallas_call | solution.py:142
  46.3 0.7 collective-permute-start
  47.0 4.8 %shard_map.75.rest_0_ = bf16[2,256,512]{2,1,0:T(8,128)(2,1)} custom-call(bf16[8,256,256]{2,1,0:T(8,128)(2,1)} %bitcast.35, s32[4,512]{1,0:T(4,128)} %get-tuple-element.11.i_ref, f32[4,512]{1,0:T(4,128)} %get-tuple-element.9.w_ref, bf16[256,512]{1,0:T(8,128)(2,1)} %get-tuple-element.5.rest_0_), custom_call_target="tpu_custom_call" | custom-call | tf_op jit(solution)/shard_map/pallas_call | solution.py:142
  51.8 3.1 %collective-permute-start.1 = (bf16[2,256,512]{2,1,0:T(8,128)(2,1)}, bf16[2,256,512]{2,1,0:T(8,128)(2,1)S(1)}, u32[]{:S(2)}, u32[]{:S(2)}) collective-permute-start(bf16[2,256,512]{2,1,0:T(8,128)(2,1)} %shard_map.75.rest_0_), channel_id=1, source_target_pairs={{1,0},{2,1},{3,2},{0,3},{5,4},{6,5},{7,6},{4,7},{9,8},{10,9},{11,1... | collective-permute-start | bytes 1572872 | tf_op jit(solution)/shard_map/ppermute | solution.py:194
  54.9 0.1 fusion.2
  55.0 0.8 concatenate.7.taper_ref
  55.8 7.1 %shard_map.76.rest_1_ = bf16[256,1024]{1,0:T(8,128)(2,1)} custom-call(bf16[8,256,256]{2,1,0:T(8,128)(2,1)} %bitcast.36, s32[4,1024]{1,0:T(4,128)} %slice.61.i_ref, f32[4,1024]{1,0:T(4,128)} %slice.62.w_ref), custom_call_target="tpu_custom_call" | custom-call | tf_op jit(solution)/shard_map/pallas_call | solution.py:142
  62.9 8.8 %shard_map.77.rest_4_ = f32[256,2048]{1,0:T(8,128)} custom-call(s32[256]{0:T(256)} %reshape.71.code_ref, bf16[8,256,256]{2,1,0:T(8,128)(2,1)} %bitcast.37, f32[5,128,128]{2,1,0:T(8,128)} %concatenate.7.taper_ref, bf16[2,256,512]{2,1,0:T(8,128)(2,1)} %shard_map.75.rest_0_, bf16[256,1024]{1,0:T(8,128)(2,1)} %shard_map.76.rest_1_, ...), custom_call_target="tpu_custom_call" | custom-call | flops 4294967296 | bytes 4194304 | tf_op jit(solution)/shard_map/pallas_call | solution.py:341
  71.7 0.0 collective-permute-done.rest_0_.rest_2_
  71.7 0.0 copy-start.6
  71.7 0.0 collective-permute-done.1.rest_1_.rest_3_
  71.7 0.8 copy-done.6
  72.5 0.0 copy-start.7
  72.5 0.8 copy-done.7
  73.3 6.8 %shard_map.78 = bf16[256,2048]{1,0:T(8,128)(2,1)} custom-call(s32[128]{0:T(128)} %reshape.67.code_ref, bf16[8,256,256]{2,1,0:T(8,128)(2,1)} %bitcast.38, f32[5,128,128]{2,1,0:T(8,128)} %concatenate.7.taper_ref, bf16[2,256,512]{2,1,0:T(8,128)(2,1)} %copy-done.6, bf16[2,256,512]{2,1,0:T(8,128)(2,1)} %copy-done.7, bf16[2,256,512]{2,1,0:T(8,128)(2,1)} %copy-done.6, ...), custom_call_target="tpu_custom_call" | custom-call | flops 2147483648 | bytes 4194304 | tf_op jit(solution)/shard_map/pallas_call | solution.py:341
  80.1 1.5 %copy.32 = bf16[32,8,8,256]{3,2,1,0:T(8,128)(2,1)S(1)} copy(bf16[32,8,8,256]{3,1,2,0:T(8,128)(2,1)} %bitcast.45) | data formatting | bytes 2097152
  81.6 17.9 %all_to_all.41 = bf16[256,8,256]{2,1,0:T(8,128)(2,1)S(1)} all-to-all(bf16[256,8,256]{2,1,0:T(8,128)(2,1)S(1)} %bitcast.40), channel_id=1, replica_groups=mesh['wide'=8,'lon'=4] {'wide'}, dimensions={0} | all-to-all | bytes 2097152 | tf_op jit(solution)/shard_map/all_to_all | solution.py:226
  99.5 1.1 %copy.34 = bf16[8,32,8,256]{3,2,0,1:T(8,128)(2,1)} copy(bf16[8,32,8,256]{3,2,1,0:T(8,128)(2,1)S(1)} %bitcast.41) | data formatting | bytes 2097152 | tf_op jit(solution)/shard_map/all_to_all | solution.py:226
  (8 shorter events, 0.1 us)
Async XLA Ops:
  0.0 9.5 %copy-start = (f32[4,64,256]{2,1,0:T(8,128)S(1)}, f32[4,64,256]{2,1,0:T(8,128)}, u32[]{:S(2)}) copy-start(f32[4,64,256]{2,1,0:T(8,128)} %param.10) | copy-start | bytes 786436
  0.0 9.2 %copy-start.4 = (s32[1,16,16]{2,1,0:T(8,128)S(1)}, s32[1,16,16]{2,1,0:T(8,128)}, u32[]{:S(2)}) copy-start(s32[1,16,16]{2,1,0:T(8,128)} %param.13) | copy-start | bytes 3076
  0.0 9.2 %copy-start.5 = (s32[1,16]{1,0:T(1,128)S(1)}, s32[1,16]{1,0:T(1,128)}, u32[]{:S(2)}) copy-start(s32[1,16]{1,0:T(1,128)} %param.12) | copy-start | bytes 196
  0.0 9.3 %copy-start.3 = (s32[1,16,16]{2,1,0:T(8,128)S(1)}, s32[1,16,16]{2,1,0:T(8,128)}, u32[]{:S(2)}) copy-start(s32[1,16,16]{2,1,0:T(8,128)} %param.11) | copy-start | bytes 3076
  0.0 12.9 %copy-start.2 = (bf16[256,8,256]{2,1,0:T(8,128)(2,1)S(1)}, bf16[256,8,256]{2,1,0:T(8,128)(2,1)}, u32[]{:S(2)}) copy-start(bf16[256,8,256]{2,1,0:T(8,128)(2,1)} %param.8) | copy-start | bytes 3145732
  2.9 12.0 %all-to-all-start = ((bf16[4,2,2048]{2,1,0:T(2,128)(2,1)}), bf16[4,2,2048]{2,1,0:T(2,128)(2,1)S(1)}, u32[]{:S(2)}, u32[]{:S(2)}) async-start(bf16[4,2,2048]{2,1,0:T(2,128)(2,1)} %reshape.73), calls=%async_computation | async-start | bytes 65536 | tf_op jit(solution)/shard_map/all_to_all | solution.py:31
  13.3 13.1 %copy-start.1 = (bf16[32,8,8,256]{3,1,2,0:T(8,128)(2,1)}, bf16[32,8,8,256]{3,1,2,0:T(8,128)(2,1)S(1)}, u32[]{:S(2)}) copy-start(bf16[32,8,8,256]{3,1,2,0:T(8,128)(2,1)S(1)} %copy.31) | copy-start | bytes 3145732
  21.4 19.1 %all-to-all-start.1 = ((bf16[64,32,256]{2,1,0:T(8,128)(2,1)}), bf16[64,32,256]{2,1,0:T(8,128)(2,1)S(1)}, u32[]{:S(2)}, u32[]{:S(2)}) async-start(bf16[64,32,256]{2,1,0:T(8,128)(2,1)} %shard_map.73), calls=%async_computation.1 | async-start | bytes 2097152 | tf_op jit(solution)/shard_map/all_to_all | solution.py:172
  46.3 25.4 %collective-permute-start = (bf16[2,256,512]{2,1,0:T(8,128)(2,1)}, bf16[2,256,512]{2,1,0:T(8,128)(2,1)S(1)}, u32[]{:S(2)}, u32[]{:S(2)}) collective-permute-start(bf16[2,256,512]{2,1,0:T(8,128)(2,1)} %shard_map.74.rest_2_), channel_id=1, source_target_pairs={{0,1},{1,2},{2,3},{3,0},{4,5},{5,6},{6,7},{7,4},{8,9},{9,10},{10,1... | collective-permute-start | bytes 1572872 | tf_op jit(solution)/shard_map/ppermute | solution.py:190
  51.8 19.9 %collective-permute-start.1 = (bf16[2,256,512]{2,1,0:T(8,128)(2,1)}, bf16[2,256,512]{2,1,0:T(8,128)(2,1)S(1)}, u32[]{:S(2)}, u32[]{:S(2)}) collective-permute-start(bf16[2,256,512]{2,1,0:T(8,128)(2,1)} %shard_map.75.rest_0_), channel_id=1, source_target_pairs={{1,0},{2,1},{3,2},{0,3},{5,4},{6,5},{7,6},{4,7},{9,8},{10,9},{11,1... | collective-permute-start | bytes 1572872 | tf_op jit(solution)/shard_map/ppermute | solution.py:194
  71.7 0.8 copy-start.6
  72.5 0.8 copy-start.7
